TPU v7x, 32 devices: a whole 2x2x4 slice. The times are simulated.
32 devices in a mesh: tile: 8 (over z, x), lev: 4 (over y, core).
Axes of the slice: x: 2, y: 2, z: 4, core: 2. Of those that a mesh axis runs over, the one named last changes fastest.
Arguments:
- obs_adjoint: float32 [16, 4096], P('lev', 'tile'), may hold values from -6 to 6
- foot_obs: int32 [8, 8, 128], P('tile'), may hold values from 0 to 511
- foot_cell: int32 [8, 8, 128], P('tile'), may hold values from 0 to 4095
- foot_weight: float32 [8, 8, 128], P('tile'), may hold values from 0.2 to 1
- counts: int32 [8, 8], P('tile'), may hold values from 0 to 128, as said below
- ensemble: bfloat16 [16, 80, 128, 256], P('lev', None, 'tile'), may hold values from -6 to 6
- vert_root: bfloat16 [16, 16], replicated, may hold values from -0.5 to 3
- radius: int32 [16], P('lev'), may hold values from 1 to 16, as said below
- alpha: float32 [16, 80, 128, 256], P('lev', None, 'tile'), may hold values from -32 to 32
Outputs:
- gradient: float32 [16, 80, 128, 256], P('lev', None, 'tile')
- r_factor: float32 [80, 80], replicated
Inputs may be any that keep to these rules, and one draw needn't show every extreme that they name: The live slots of a block are its first counts[s, d] slots. In every draw some destination tile has 128 live slots from every sender tile. Some level group has radius 16 in every draw.
All inputs are finite; a program needn't handle non-finite values.
Results may differ from a plain program's by a relative error of at most 0.0003.
The roundings to bfloat16 on the way count: a program that leaves them out, or rounds other values in their place, can miss the bound.
Values may be sent and summed in bfloat16 or wider, within the bound.
No kernel may reach another device: no remote copies, remote signals or barrier semaphores. Data moves between devices by JAX's collectives and lax.ppermute only.
A program may use at most 128 MiB of HBM per device.

v0:
```python
import jax
import jax.numpy as jnp
from jax import lax
from jax.sharding import PartitionSpec as P

HALO = 16


def extended(cells, sides, width):
    for axis, dim in sides:
        count = lax.axis_size(axis)
        ends = count - 1
        head = lax.slice_in_dim(cells, 0, width, axis=dim)
        tail = lax.slice_in_dim(cells, cells.shape[dim] - width, cells.shape[dim], axis=dim)
        cells = jnp.concatenate(
            [
                lax.ppermute(tail, axis, [(i, (i + 1) % count) for i in range(ends)]),
                cells,
                lax.ppermute(head, axis, [((i + 1) % count, i) for i in range(ends)]),
            ],
            axis=dim,
        )
    return cells


def taps_table(radius, offsets):
    reach_max = radius.astype(jnp.float32)[:, None, None]
    distance = jnp.abs(offsets).astype(jnp.float32)[None]
    weights = jnp.where(
        distance <= reach_max, (reach_max + 1.0 - distance) / (reach_max + 1.0), 0.0
    )
    return weights.astype(jnp.bfloat16)


def shards(
    obs_adjoint, foot_obs, foot_cell, foot_weight, counts, ensemble, vert_root, radius, alpha
):
    lev_dev, members, col_count, row_count = alpha.shape
    tile_count = lax.axis_size("tile")
    group_count = lax.axis_size("lev")
    capacity = foot_obs.shape[2]
    slot_index = lax.broadcasted_iota(jnp.int32, (tile_count, capacity), 1)
    live_mask = (slot_index < counts[0][:, None]).astype(jnp.float32)
    values = jnp.take(obs_adjoint, foot_obs[0], axis=1)
    payload = values * (foot_weight[0] * live_mask)[None]
    arrived, cell_index = (
        lax.all_to_all(payload, "tile", split_axis=1, concat_axis=1, tiled=True),
        lax.all_to_all(foot_cell, "tile", split_axis=1, concat_axis=1, tiled=True),
    )
    forcing = jnp.zeros((lev_dev, col_count * row_count), jnp.float32)
    forcing = forcing.at[:, cell_index.reshape(-1)].add(arrived.reshape(lev_dev, -1))
    forcing = forcing.reshape(lev_dev, col_count, row_count)
    member_forcing = (ensemble * forcing[:, None]).astype(jnp.bfloat16)
    regrouped = lax.all_to_all(member_forcing, "lev", split_axis=1, concat_axis=0, tiled=True)
    local_mix = jnp.einsum(
        "lk,lmxy->kmxy", vert_root, regrouped, preferred_element_type=jnp.float32
    )
    level_mix = lax.all_to_all(
        local_mix.astype(jnp.bfloat16), "lev", split_axis=0, concat_axis=1, tiled=True
    )
    row_iota = jnp.arange(row_count, dtype=jnp.int32)
    taps_rows = taps_table(radius, row_iota[:, None] - row_iota[None, :])
    wide_iota = jnp.arange(col_count + 2 * HALO, dtype=jnp.int32)
    col_iota = jnp.arange(col_count, dtype=jnp.int32)
    taps_cols = taps_table(radius, wide_iota[:, None] - HALO - col_iota[None, :])
    smoothed = jnp.einsum(
        "kmxy,kyz->kmxz", level_mix, taps_rows, preferred_element_type=jnp.float32
    )
    smooth_wide = extended(smoothed.astype(jnp.bfloat16), (("tile", 2),), HALO)
    smooth_x = jnp.einsum(
        "kmey,kex->kmxy", smooth_wide, taps_cols, preferred_element_type=jnp.float32
    )
    gradient = alpha + smooth_x
    panel = gradient.reshape(lev_dev, members, col_count * row_count)
    total_cells = float(lev_dev * group_count * col_count * tile_count * row_count)
    gram_local = (
        jnp.einsum("kmc,knc->mn", panel, panel, precision=lax.Precision.HIGHEST) / total_cells
    )
    gram_total = lax.psum(gram_local, ("tile", "lev"))
    r_factor = jnp.linalg.cholesky(gram_total).T
    return (gradient, r_factor)


def solution(mesh):
    return jax.shard_map(
        shards,
        mesh=mesh,
        in_specs=(
            P("lev", "tile"),
            P("tile", None, None),
            P("tile", None, None),
            P("tile", None, None),
            P("tile", None),
            P("lev", None, "tile", None),
            P(),
            P("lev"),
            P("lev", None, "tile", None),
        ),
        out_specs=(P("lev", None, "tile", None), P()),
        check_vma=False,
    )
```

profile of v0, /device:TPU:0, one launch (start us, length us, event | category | flops | bytes accessed | tf_op | source)
XLA Modules:
  0.0 299.8 jit_solution(4316643736802365267)
XLA Ops:
  0.6 0.0 copy-start
  0.6 7.3 %all-to-all-start = ((s32[1,8,128]{2,0,1:T(1,128)}), s32[1,8,128]{2,0,1:T(1,128)S(1)}, u32[]{:S(2)}, u32[]{:S(2)}) async-start(s32[1,8,128]{2,0,1:T(1,128)} %bitcast.74), calls=%async_computation | async-start | bytes 8192 | tf_op jit(solution)/shard_map/all_to_all | solution.py:48
  7.9 0.7 compare_and_fusion
  8.6 0.7 fusion.25
  9.3 0.8 copy.33
  10.1 2.8 gather_fusion
  13.0 0.2 copy.34
  13.1 0.8 select_bitcast_fusion.1
  13.9 0.6 multiply_bitcast_fusion
  14.5 0.0 all-to-all-done
  14.5 6.0 %all-to-all-start.1 = ((f32[4,8,128]{2,0,1:T(4,128)}), f32[4,8,128]{2,0,1:T(4,128)S(1)}, u32[]{:S(2)}, u32[]{:S(2)}) async-start(f32[4,8,128]{2,0,1:T(4,128)} %multiply_bitcast_fusion), calls=%async_computation.1 | async-start | bytes 32768 | tf_op jit(solution)/shard_map/all_to_all | solution.py:47
  20.5 6.6 %all-to-all-done.1 = f32[4,8,128]{2,0,1:T(4,128)S(1)} async-done(((f32[4,8,128]{2,0,1:T(4,128)}), f32[4,8,128]{2,0,1:T(4,128)S(1)}, u32[]{:S(2)}, u32[]{:S(2)}) %all-to-all-start.1) | async-done | bytes 16416 | tf_op jit(solution)/shard_map/all_to_all | solution.py:47
  27.1 0.2 copy.35
  27.3 6.5 %scatter_custom_fusion = f32[4,4096]{0,1:T(8,128)S(1)} fusion(s32[1024]{0:T(1024)S(1)} %bitcast.75, f32[1024,4]{1,0:T(8,128)S(1)} %copy.35, f32[]{:T(128)} %constant.57.clone.1), kind=kCustom, calls=%fused_computation.16 | custom fusion | flops 4096 | bytes 65540 | tf_op jit(solution)/shard_map/scatter-add | solution.py:51
  33.9 0.6 copy.36
  34.5 2.4 multiply_convert_fusion
  37.0 33.9 %all_to_all.46 = bf16[4,80,16,256]{3,2,0,1:T(8,128)(2,1)S(1)} all-to-all(bf16[4,80,16,256]{3,2,0,1:T(8,128)(2,1)S(1)} %multiply_convert_fusion), channel_id=1, replica_groups=mesh['tile'=8,'lev'=4] {'lev'}, dimensions={1} | all-to-all | bytes 5242880 | tf_op jit(solution)/shard_map/all_to_all | solution.py:54
  70.9 1.4 copy.52
  72.2 2.8 all_to_all.37
  75.0 0.0 copy-done
  75.0 2.6 convert_bitcast_fusion
  77.6 2.4 copy.39
  80.0 0.0 copy-start.1
  80.0 3.8 %all-to-all-start.3 = ((bf16[16,20,16,256]{3,2,1,0:T(8,128)(2,1)}), bf16[16,20,16,256]{3,2,1,0:T(8,128)(2,1)S(1)}, u32[]{:S(2)}, u32[]{:S(2)}) async-start(bf16[16,20,16,256]{3,2,1,0:T(8,128)(2,1)} %copy.39), calls=%async_computation.3 | async-start | bytes 5242880 | tf_op jit(solution)/shard_map/all_to_all | solution.py:58
  83.8 0.0 copy-done.1
  83.9 31.2 %all-to-all-done.3 = bf16[16,20,16,256]{3,2,1,0:T(8,128)(2,1)S(1)} async-done(((bf16[16,20,16,256]{3,2,1,0:T(8,128)(2,1)}), bf16[16,20,16,256]{3,2,1,0:T(8,128)(2,1)S(1)}, u32[]{:S(2)}, u32[]{:S(2)}) %all-to-all-start.3) | async-done | bytes 2621472 | tf_op jit(solution)/shard_map/all_to_all | solution.py:58
  115.1 0.0 slice-start
  115.1 0.2 copy.40
  115.3 0.0 slice-start.1
  115.3 1.0 convolution_convert_fusion
  116.3 1.4 collective-permute-start.1
  117.7 4.9 %collective-permute-start = (bf16[4,80,16,256]{3,2,1,0:T(8,128)(2,1)S(1)}, bf16[4,80,16,256]{3,2,1,0:T(8,128)(2,1)S(1)}, u32[]{:S(2)}, u32[]{:S(2)}) collective-permute-start(bf16[4,80,16,256]{3,2,1,0:T(8,128)(2,1)S(1)} %convolution_convert_fusion), channel_id=1, source_target_pairs={{0,4},{4,8},{8,12},{12,16},{16,20},{20,24},{24,28},{1,5},{5,9},{9,... | collective-permute-start | bytes 7864328 | tf_op jit(solution)/shard_map/ppermute | solution.py:17
  122.6 54.1 %collective-permute-done.1 = bf16[4,80,16,256]{3,2,1,0:T(8,128)(2,1)S(1)} collective-permute-done((bf16[4,80,16,256]{3,2,1,0:T(8,128)(2,1)S(1)}, bf16[4,80,16,256]{3,2,1,0:T(8,128)(2,1)S(1)}, u32[]{:S(2)}, u32[]{:S(2)}) %collective-permute-start.1) | collective-permute-done | bytes 2621472 | tf_op jit(solution)/shard_map/ppermute | solution.py:19
  176.7 55.1 %collective-permute-done = bf16[4,80,16,256]{3,2,1,0:T(8,128)(2,1)S(1)} collective-permute-done((bf16[4,80,16,256]{3,2,1,0:T(8,128)(2,1)S(1)}, bf16[4,80,16,256]{3,2,1,0:T(8,128)(2,1)S(1)}, u32[]{:S(2)}, u32[]{:S(2)}) %collective-permute-start) | collective-permute-done | bytes 2621472 | tf_op jit(solution)/shard_map/ppermute | solution.py:17
  231.8 0.0 slice-done
  231.8 0.0 slice-done.1
  231.8 3.5 %bitcast_add_fusion = f32[4,80,16,256]{3,2,1,0:T(8,128)} fusion(f32[4,80,16,256]{3,2,1,0:T(8,128)S(1)} %bitcast.78, bf16[4,80,16,256]{3,2,1,0:T(8,128)(2,1)S(1)} %collective-permute-done.1, bf16[4,80,16,256]{3,2,1,0:T(8,128)(2,1)S(1)} %convolution_convert_fusion, bf16[4,80,16,256]{3,2,1,0:T(8,128)(2,1)S(1)} %collective-permute-done, ...), kind=kOutput, calls=%fused_computation.8 | convolution fusion | flops 150748160 | bytes 18353184 | tf_op jit(solution)/shard_map/kmey,kex->kmxy/dot_general | solution.py:70
  235.4 6.8 %reshape.159 = f32[4,80,4096]{2,1,0:T(8,128)} reshape(f32[4,80,16,256]{3,2,1,0:T(8,128)} %bitcast_add_fusion) | data formatting | bytes 10485760 | tf_op jit(solution)/shard_map/reshape | solution.py:74
  242.2 8.3 %fusion.8 = f32[80,80]{0,1:T(8,128)S(1)} fusion(f32[4,80,4096]{2,1,0:T(8,128)} %reshape.159), kind=kOutput, calls=%fused_computation.14 | convolution fusion | flops 1258297600 | bytes 5268480 | tf_op jit(solution)/shard_map/kmc,knc->mn/dot_general | solution.py:77
  250.5 39.8 %psum.7 = f32[80,80]{0,1:T(8,128)S(1)} all-reduce(f32[80,80]{0,1:T(8,128)S(1)} %fusion.8), channel_id=1, replica_groups=mesh['tile'=8,'lev'=4] {'tile','lev'}, use_global_device_ids=true, to_apply=%region_1.2 | all-reduce | flops 6400 | bytes 51200 | tf_op jit(solution)/shard_map/psum | solution.py:79
  290.3 0.1 copy.42
  290.4 7.3 %cholesky.18 = f32[80,80]{1,0:T(8,128)S(1)} custom-call(f32[80,80]{1,0:T(8,128)S(1)} %fusion.17), custom_call_target="Cholesky" | custom-call | tf_op jit(solution)/shard_map/jit(cholesky)/cholesky | solution.py:80
  297.8 0.6 compare_reduce_fusion
  298.4 0.7 select_bitcast_fusion
  299.1 0.7 copy.43
  (9 shorter events, 0.1 us)
Async XLA Ops:
  0.6 74.4 %copy-start = (bf16[16,16]{1,0:T(8,128)(2,1)S(1)}, bf16[16,16]{1,0:T(8,128)(2,1)}, u32[]{:S(2)}) copy-start(bf16[16,16]{1,0:T(8,128)(2,1)} %param.15) | copy-start | bytes 1540
  0.6 13.9 %all-to-all-start = ((s32[1,8,128]{2,0,1:T(1,128)}), s32[1,8,128]{2,0,1:T(1,128)S(1)}, u32[]{:S(2)}, u32[]{:S(2)}) async-start(s32[1,8,128]{2,0,1:T(1,128)} %bitcast.74), calls=%async_computation | async-start | bytes 8192 | tf_op jit(solution)/shard_map/all_to_all | solution.py:48
  14.5 12.6 %all-to-all-start.1 = ((f32[4,8,128]{2,0,1:T(4,128)}), f32[4,8,128]{2,0,1:T(4,128)S(1)}, u32[]{:S(2)}, u32[]{:S(2)}) async-start(f32[4,8,128]{2,0,1:T(4,128)} %multiply_bitcast_fusion), calls=%async_computation.1 | async-start | bytes 32768 | tf_op jit(solution)/shard_map/all_to_all | solution.py:47
  80.0 3.8 %copy-start.1 = (s32[4]{0:T(128)S(1)}, s32[4]{0:T(128)}, u32[]{:S(2)}) copy-start(s32[4]{0:T(128)} %param.16) | copy-start | bytes 52
  80.0 35.1 %all-to-all-start.3 = ((bf16[16,20,16,256]{3,2,1,0:T(8,128)(2,1)}), bf16[16,20,16,256]{3,2,1,0:T(8,128)(2,1)S(1)}, u32[]{:S(2)}, u32[]{:S(2)}) async-start(bf16[16,20,16,256]{3,2,1,0:T(8,128)(2,1)} %copy.39), calls=%async_computation.3 | async-start | bytes 5242880 | tf_op jit(solution)/shard_map/all_to_all | solution.py:58
  115.1 116.7 %slice-start = ((s8[5242880]{0:T(1024)(128)(4,1)}), s8[4194304]{0:T(1024)(128)(4,1)S(1)}, s32[]{:S(2)}) async-start(s8[5242880]{0:T(1024)(128)(4,1)} %bitcast.77), calls=%async_computation.4 | async-start | bytes 8388608
  115.3 116.5 %slice-start.1 = ((s8[5242880]{0:T(1024)(128)(4,1)}), s8[1048576]{0:T(1024)(128)(4,1)S(1)}, s32[]{:S(2)}) async-start(s8[5242880]{0:T(1024)(128)(4,1)} %bitcast.77), calls=%async_computation.5 | async-start | bytes 2097152
  116.3 60.4 %collective-permute-start.1 = (bf16[4,80,16,256]{3,2,1,0:T(8,128)(2,1)S(1)}, bf16[4,80,16,256]{3,2,1,0:T(8,128)(2,1)S(1)}, u32[]{:S(2)}, u32[]{:S(2)}) collective-permute-start(bf16[4,80,16,256]{3,2,1,0:T(8,128)(2,1)S(1)} %convolution_convert_fusion), channel_id=1, source_target_pairs={{4,0},{8,4},{12,8},{16,12},{20,16},{24,20},{28,24},{5,1},{9,5},{13... | collective-permute-start | bytes 7864328 | tf_op jit(solution)/shard_map/ppermute | solution.py:19
  117.7 114.1 %collective-permute-start = (bf16[4,80,16,256]{3,2,1,0:T(8,128)(2,1)S(1)}, bf16[4,80,16,256]{3,2,1,0:T(8,128)(2,1)S(1)}, u32[]{:S(2)}, u32[]{:S(2)}) collective-permute-start(bf16[4,80,16,256]{3,2,1,0:T(8,128)(2,1)S(1)} %convolution_convert_fusion), channel_id=1, source_target_pairs={{0,4},{4,8},{8,12},{12,16},{16,20},{20,24},{24,28},{1,5},{5,9},{9,... | collective-permute-start | bytes 7864328 | tf_op jit(solution)/shard_map/ppermute | solution.py:17
where the time goes:
time: 301 us; the launch traced here: 300 us
  waiting for transfers between devices  147 us (49%)
  blocking collectives  73.7 us (24%)
  starting transfers between devices  23.4 us (8%)
  other arithmetic  20.5 us (7%)
  local copies, waits for them, and re-layouts  19 us (6%)
  matrix products  15.5 us (5%)
    ppermute x1, waiting for transfers between devices, extended(): lax.ppermute(tail, axis, [(i, (i + 1) % count) for i in range(ends)])  55.1 us
    ppermute x1, waiting for transfers between devices, extended(): lax.ppermute(head, axis, [((i + 1) % count, i) for i in range(ends)])  54.1 us
    psum x1, blocking collectives, shards(): gram_total = lax.psum(gram_local, ('tile', 'lev'))  39.8 us
    all_to_all x1, blocking collectives, shards(): lax.all_to_all(member_forcing, 'lev', split_axis=1, concat_axis=0, tiled=...  33.9 us
    all_to_all x1, waiting for transfers between devices, shards(): lax.all_to_all(local_mix.astype(jnp.bfloat16), 'lev', split_axis=0, conca...  31.2 us
    dot_general x1, matrix products, shards(): jnp.einsum('kmc,knc->mn', panel, panel, precision=lax.Precision.HIGHEST)  8.34 us
    another operation x3, other arithmetic, shards(): r_factor = jnp.linalg.cholesky(gram_total).T  7.98 us
    all_to_all x1, starting transfers between devices, shards(): lax.all_to_all(foot_cell, 'tile', split_axis=1, concat_axis=1, tiled=True)  7.26 us
  transfers between devices with their start and end apart: 5, of which 4 were waited for; matrix products, arithmetic and copies ran while one was open for 2% of the time, Pallas kernels for 0%

commit v1 on v0

v1 whole, which is shorter than its diff:
```python
import jax
import jax.numpy as jnp
from jax import lax
from jax.sharding import PartitionSpec as P

HALO = 16


def taps_table(radius, offsets):
    reach_max = radius.astype(jnp.float32)[:, None, None]
    distance = jnp.abs(offsets).astype(jnp.float32)[None]
    weights = jnp.where(
        distance <= reach_max, (reach_max + 1.0 - distance) / (reach_max + 1.0), 0.0
    )
    return weights.astype(jnp.bfloat16)


def first_hits(cells):
    slots = cells.shape[-1]
    same = cells[..., :, None] == cells[..., None, :]
    later = lax.broadcasted_iota(jnp.int32, (slots, slots), 1) < lax.broadcasted_iota(
        jnp.int32, (slots, slots), 0
    )
    return jnp.logical_not(jnp.any(same & later, axis=-1))


def one_hot(cells, keep, cell_count):
    grid = lax.broadcasted_iota(jnp.int32, cells.shape + (cell_count,), cells.ndim)
    hit = (cells[..., None] == grid) & keep[..., None]
    return hit.astype(jnp.bfloat16)


def shards(
    obs_adjoint, foot_obs, foot_cell, foot_weight, counts, ensemble, vert_root, radius, alpha
):
    lev_dev, members, col_count, row_count = alpha.shape
    tile_count = lax.axis_size("tile")
    group_count = lax.axis_size("lev")
    capacity = foot_obs.shape[2]
    cell_count = col_count * row_count
    slots = tile_count * capacity
    packed = slots < cell_count
    assert HALO <= col_count
    tile = lax.axis_index("tile")

    slot_index = lax.broadcasted_iota(jnp.int32, (tile_count, capacity), 1)
    live_mask = (slot_index < counts[0][:, None]).astype(jnp.float32)
    values = jnp.take(obs_adjoint, foot_obs[0], axis=1)
    payload = values * (foot_weight[0] * live_mask)[None]
    arrived = lax.all_to_all(payload, "tile", split_axis=1, concat_axis=1, tiled=True)
    all_cells = lax.all_gather(foot_cell[0], "tile")
    cells_of = jnp.swapaxes(all_cells, 0, 1).reshape(tile_count, slots)
    cell_index = lax.dynamic_index_in_dim(cells_of, tile, 0, keepdims=False)

    forcing = jnp.zeros((lev_dev, cell_count), jnp.float32)
    forcing = forcing.at[:, cell_index].add(arrived.reshape(lev_dev, -1))
    forcing = forcing.reshape(lev_dev, col_count, row_count)
    member_forcing = (ensemble * forcing[:, None]).astype(jnp.bfloat16)
    member_forcing = member_forcing.reshape(lev_dev, members, cell_count)

    if packed:
        near = jnp.stack(
            [
                lax.dynamic_index_in_dim(cells_of, jnp.maximum(tile - 1, 0), 0, keepdims=False),
                cell_index,
                lax.dynamic_index_in_dim(
                    cells_of, jnp.minimum(tile + 1, tile_count - 1), 0, keepdims=False
                ),
            ]
        )
        hits = one_hot(near, first_hits(near), cell_count)
        member_forcing = jnp.einsum(
            "lmc,sc->lms", member_forcing, hits[1], preferred_element_type=jnp.float32
        ).astype(jnp.bfloat16)

    regrouped = lax.all_to_all(member_forcing, "lev", split_axis=1, concat_axis=0, tiled=True)
    local_mix = jnp.einsum(
        "lk,lmc->kmc", vert_root, regrouped, preferred_element_type=jnp.float32
    )
    level_mix = lax.all_to_all(
        local_mix.astype(jnp.bfloat16), "lev", split_axis=0, concat_axis=1, tiled=True
    )
    ends = tile_count - 1
    from_left = lax.ppermute(level_mix, "tile", [(i, i + 1) for i in range(ends)])
    from_right = lax.ppermute(level_mix, "tile", [(i + 1, i) for i in range(ends)])
    three = jnp.stack([from_left, level_mix, from_right])
    if packed:
        three = jnp.einsum(
            "tkms,tsc->kmtc", three, hits, preferred_element_type=jnp.float32
        ).astype(jnp.bfloat16)
    else:
        three = jnp.moveaxis(three, 0, 2)
    wide_mix = three.reshape(lev_dev, members, 3 * col_count, row_count)

    row_iota = jnp.arange(row_count, dtype=jnp.int32)
    taps_rows = taps_table(radius, row_iota[:, None] - row_iota[None, :])
    wide_iota = jnp.arange(3 * col_count, dtype=jnp.int32)
    col_iota = jnp.arange(col_count, dtype=jnp.int32)
    taps_cols = taps_table(radius, wide_iota[:, None] - col_count - col_iota[None, :])
    smooth_wide = jnp.einsum(
        "kmxy,kyz->kmxz", wide_mix, taps_rows, preferred_element_type=jnp.float32
    ).astype(jnp.bfloat16)
    smooth_x = jnp.einsum(
        "kmey,kex->kmxy", smooth_wide, taps_cols, preferred_element_type=jnp.float32
    )
    gradient = alpha + smooth_x
    panel = gradient.reshape(lev_dev, members, col_count * row_count)
    total_cells = float(lev_dev * group_count * col_count * tile_count * row_count)
    gram_local = (
        jnp.einsum("kmc,knc->mn", panel, panel, precision=lax.Precision.HIGHEST) / total_cells
    )
    gram_total = lax.psum(gram_local, ("tile", "lev"))
    r_factor = jnp.linalg.cholesky(gram_total).T
    return (gradient, r_factor)


def solution(mesh):
    return jax.shard_map(
        shards,
        mesh=mesh,
        in_specs=(
            P("lev", "tile"),
            P("tile", None, None),
            P("tile", None, None),
            P("tile", None, None),
            P("tile", None),
            P("lev", None, "tile", None),
            P(),
            P("lev"),
            P("lev", None, "tile", None),
        ),
        out_specs=(P("lev", None, "tile", None), P()),
        check_vma=False,
    )
```

time: 301 us -> 276 us (0.917)
  waiting for transfers between devices: 147 us -> 37.6 us
  local copies, waits for them, and re-layouts: 19 us -> 63.7 us
  matrix products: 15.5 us -> 37.4 us
  other arithmetic: 20.5 us -> 35.7 us
  blocking collectives: 73.7 us -> 84.2 us
  starting transfers between devices: 23.4 us -> 15.6 us
    ppermute x2, waiting for transfers between devices: 109 us -> 26 us  [the longest x1 26 us: shards(): lax.ppermute(level_mix, 'tile', [(i, i + 1) for i in range(ends)])]
    all_gather x0 -> x1, blocking collectives: none -> 31.1 us  [shards(): all_cells = lax.all_gather(foot_cell[0], 'tile')]
    reshape x1 -> x3, local copies, waits for them, and re-layouts: 0.22 us -> 25.4 us  [the longest x1 22.1 us: shards(): wide_mix = three.reshape(lev_dev, members, 3 * col_count, row_count)]
    convert_element_type x0 -> x2, local copies, waits for them, and re-layouts: none -> 23.6 us  [the longest x1 23.1 us: shards(): three = jnp.einsum('tkms,tsc->kmtc', three, hits, preferred_element_type=...]
    all_to_all x1, blocking collectives: 33.9 us -> 12.8 us  [shards(): lax.all_to_all(member_forcing, 'lev', split_axis=1, concat_axis=0, tiled=...]
    all_to_all x1, waiting for transfers between devices: 31.2 us -> 11.6 us  [shards(): lax.all_to_all(local_mix.astype(jnp.bfloat16), 'lev', split_axis=0, conca...]
    dot_general x2 -> x3, matrix products: 3.58 us -> 21 us  [the longest x1 14.7 us: shards(): jnp.einsum('tkms,tsc->kmtc', three, hits, preferred_element_type=jnp.floa...]
    and x0 -> x1, other arithmetic: none -> 12.4 us  [one_hot(): hit = (cells[..., None] == grid) & keep[..., None]]
  transfers between devices with their start and end apart: 5 -> 4, of which waited for: 4 -> 2; matrix products, arithmetic and copies ran while one was open for 2% -> 6% of each run, Pallas kernels for 0% -> 0%
where the time goes in v1:
time: 276 us; the launch traced here: 275 us
  blocking collectives  84.2 us (31%)
  local copies, waits for them, and re-layouts  63.7 us (23%)
  waiting for transfers between devices  37.6 us (14%)
  matrix products  37.4 us (14%)
  other arithmetic  35.7 us (13%)
  starting transfers between devices  15.6 us (6%)
    psum x1, blocking collectives, shards(): gram_total = lax.psum(gram_local, ('tile', 'lev'))  40.3 us
    all_gather x1, blocking collectives, shards(): all_cells = lax.all_gather(foot_cell[0], 'tile')  31.1 us
    ppermute x1, waiting for transfers between devices, shards(): lax.ppermute(level_mix, 'tile', [(i, i + 1) for i in range(ends)])  26 us
    convert_element_type x1, local copies, waits for them, and re-layouts, shards(): three = jnp.einsum('tkms,tsc->kmtc', three, hits, preferred_element_type=...  23.1 us
    reshape x1, local copies, waits for them, and re-layouts, shards(): wide_mix = three.reshape(lev_dev, members, 3 * col_count, row_count)  22.1 us
    dot_general x1, matrix products, shards(): jnp.einsum('tkms,tsc->kmtc', three, hits, preferred_element_type=jnp.floa...  14.7 us
    all_to_all x1, blocking collectives, shards(): lax.all_to_all(member_forcing, 'lev', split_axis=1, concat_axis=0, tiled=...  12.8 us
    and x1, other arithmetic, one_hot(): hit = (cells[..., None] == grid) & keep[..., None]  12.4 us
  transfers between devices with their start and end apart: 4, of which 2 were waited for; matrix products, arithmetic and copies ran while one was open for 6% of the time, Pallas kernels for 0%

profile of v1, /device:TPU:0, one launch (start us, length us, event | category | flops | bytes accessed | tf_op | source)
XLA Modules:
  0.0 275.2 jit_solution(2542801620730495534)
XLA Ops:
  0.6 0.0 copy-start
  0.6 0.7 fusion.41
  1.3 0.7 compare_and_fusion
  2.0 0.8 copy.64
  2.9 2.8 %gather_fusion = f32[1024,4]{1,0:T(8,128)S(1)} fusion(f32[4,512]{0,1:T(8,128)S(1)} %copy.64, s32[1024]{0:T(1024)S(1)} %fusion.41), kind=kCustom, calls=%fused_computation | custom fusion | bytes 36864 | tf_op jit(solution)/shard_map/jit(_take)/gather | solution.py:48
  5.7 0.2 copy.65
  5.9 0.8 select_bitcast_fusion.1
  6.7 0.6 multiply_bitcast_fusion
  7.3 7.3 %all-to-all-start = ((f32[4,8,128]{2,0,1:T(4,128)}), f32[4,8,128]{2,0,1:T(4,128)S(1)}, u32[]{:S(2)}, u32[]{:S(2)}) async-start(f32[4,8,128]{2,0,1:T(4,128)} %multiply_bitcast_fusion), calls=%async_computation | async-start | bytes 32768 | tf_op jit(solution)/shard_map/all_to_all | solution.py:50
  14.5 0.3 iota_compare_fusion.1
  14.8 31.1 %all_gather.3 = s32[8,8,128]{2,1,0:T(8,128)S(1)} all-gather(s32[1,8,128]{2,1,0:T(8,128)} %param.11), channel_id=1, replica_groups=mesh['tile'=8,'lev'=4] {'tile'}, dimensions={0}, use_global_device_ids=true | all-gather | bytes 36864 | tf_op jit(solution)/shard_map/all_gather | solution.py:51
  46.0 2.6 and_reduce_fusion
  48.6 12.4 %fusion = pred[3,1024,4096]{2,1,0:T(32,128)(4,1)} fusion(s32[3,1024]{1,0:T(4,128)S(1)} %pad_add_fusion, pred[3,1024]{1,0:T(4,128)(4,1)S(1)} %not.7), kind=kLoop, calls=%fused_computation.3 | loop fusion | flops 25165824 | bytes 12598272 | tf_op jit(solution)/shard_map/and | solution.py:29
  61.1 0.0 all-to-all-done
  61.1 0.2 copy.66
  61.3 6.5 %scatter_custom_fusion = f32[4,4096]{0,1:T(8,128)S(1)} fusion(s32[1024]{0:T(1024)S(1)} %bitcast.100, f32[1024,4]{1,0:T(8,128)S(1)} %copy.66, f32[]{:T(128)} %constant.75.clone.1), kind=kCustom, calls=%fused_computation.27 | custom fusion | flops 4096 | bytes 65540 | tf_op jit(solution)/shard_map/scatter-add | solution.py:56
  67.9 0.6 copy.67
  68.5 2.3 multiply_convert_fusion
  70.7 3.1 %reshape.178 = bf16[4,80,4096]{2,1,0:T(8,128)(2,1)} reshape(bf16[4,80,16,256]{3,2,1,0:T(8,128)(2,1)S(1)} %multiply_convert_fusion) | data formatting | bytes 5242880 | tf_op jit(solution)/shard_map/reshape | solution.py:59
  73.9 5.9 %fusion.17 = bf16[4,80,1024]{2,1,0:T(8,128)(2,1)S(1)} fusion(bf16[4,80,4096]{2,1,0:T(8,128)(2,1)} %reshape.178, pred[3,1024,4096]{2,1,0:T(32,128)(4,1)} %fusion), kind=kOutput, calls=%fused_computation.21 | convolution fusion | flops 2684682240 | bytes 7471104 | tf_op jit(solution)/shard_map/lmc,sc->lms/dot_general | solution.py:72
  79.7 0.0 copy-start.2
  79.7 0.5 copy.68
  80.3 12.8 %all_to_all.41 = bf16[4,80,1024]{2,0,1:T(4,128)(2,1)S(1)} all-to-all(bf16[4,80,1024]{2,0,1:T(4,128)(2,1)S(1)} %copy.68), channel_id=1, replica_groups=mesh['tile'=8,'lev'=4] {'lev'}, dimensions={1} | all-to-all | bytes 1310720 | tf_op jit(solution)/shard_map/all_to_all | solution.py:76
  93.1 0.3 copy.69
  93.4 0.2 all_to_all.33
  93.6 0.4 fusion.18
  94.0 1.3 copy.71
  95.2 3.5 %all-to-all-start.2 = ((bf16[16,20,1024]{2,1,0:T(8,128)(2,1)}), bf16[16,20,1024]{2,1,0:T(8,128)(2,1)S(1)}, u32[]{:S(2)}, u32[]{:S(2)}) async-start(bf16[16,20,1024]{2,1,0:T(8,128)(2,1)} %copy.71), calls=%async_computation.2 | async-start | bytes 1572864 | tf_op jit(solution)/shard_map/all_to_all | solution.py:80
  98.8 11.6 %all-to-all-done.2 = bf16[16,20,1024]{2,1,0:T(8,128)(2,1)S(1)} async-done(((bf16[16,20,1024]{2,1,0:T(8,128)(2,1)}), bf16[16,20,1024]{2,1,0:T(8,128)(2,1)S(1)}, u32[]{:S(2)}, u32[]{:S(2)}) %all-to-all-start.2) | async-done | bytes 655392 | tf_op jit(solution)/shard_map/all_to_all | solution.py:80
  110.4 0.5 copy.72
  110.9 0.2 copy.73
  111.1 3.4 %collective-permute-start = (bf16[4,80,1024]{2,1,0:T(8,128)(2,1)S(1)}, bf16[4,80,1024]{2,1,0:T(8,128)(2,1)S(1)}, u32[]{:S(2)}, u32[]{:S(2)}) collective-permute-start(bf16[4,80,1024]{2,1,0:T(8,128)(2,1)S(1)} %copy.73), channel_id=1, source_target_pairs={{0,4},{4,8},{8,12},{12,16},{16,20},{20,24},{24,28},{1,5},{5,9},{9,... | collective-permute-start | bytes 1966088 | tf_op jit(solution)/shard_map/ppermute | solution.py:84
  114.5 1.5 collective-permute-start.1
  116.1 0.2 copy.75
  116.3 26.0 %collective-permute-done = bf16[4,80,1024]{2,1,0:T(8,128)(2,1)S(1)} collective-permute-done((bf16[4,80,1024]{2,1,0:T(8,128)(2,1)S(1)}, bf16[4,80,1024]{2,1,0:T(8,128)(2,1)S(1)}, u32[]{:S(2)}, u32[]{:S(2)}) %collective-permute-start) | collective-permute-done | bytes 655392 | tf_op jit(solution)/shard_map/ppermute | solution.py:84
  142.3 0.0 collective-permute-done.1
  142.3 14.7 %convert_bitcast_fusion = bf16[4,80,3,4096]{3,1,0,2:T(8,128)(2,1)S(1)} fusion(bf16[1,4,80,1024]{3,2,1,0:T(8,128)(2,1)S(1)} %bitcast.103, bf16[1,4,80,1024]{3,2,1,0:T(8,128)(2,1)S(1)} %copy.75, bf16[1,4,80,1024]{3,2,1,0:T(8,128)(2,1)S(1)} %bitcast.102, s32[3,1024]{1,0:T(4,128)S(1)} %pad_add_fusion, pred[3,1024]{1,0:T(4,128)(4,1)S(1)} %not.7), kind=kOutput, calls=%fused_computation.11 | convolution fusion | flops 8088059904 | bytes 9845760 | tf_op jit(solution)/shard_map/tkms,tsc->kmtc/dot_general | solution.py:88
  157.0 23.1 %copy.76 = bf16[4,80,3,4096]{3,2,1,0:T(4,128)(2,1)} copy(bf16[4,80,3,4096]{3,1,0,2:T(8,128)(2,1)S(1)} %convert_bitcast_fusion) | data formatting | bytes 15728640 | tf_op jit(solution)/shard_map/convert_element_type | solution.py:90
  180.1 22.1 %reshape.179 = bf16[4,80,48,256]{3,2,1,0:T(8,128)(2,1)} reshape(bf16[4,80,3,4096]{3,2,1,0:T(4,128)(2,1)} %copy.76) | data formatting | bytes 15728640 | tf_op jit(solution)/shard_map/reshape | solution.py:93
  202.2 8.1 %bitcast_add_fusion = f32[4,80,16,256]{3,2,1,0:T(8,128)} fusion(f32[4,80,16,256]{3,2,1,0:T(8,128)} %param.17, bf16[4,80,48,256]{3,2,1,0:T(8,128)(2,1)} %reshape.179, f32[4]{0:T(128)S(1)} %broadcast_add_fusion, f32[256,256]{1,0:T(8,128)S(1)} %abs_convert_fusion, f32[4]{0:T(128)S(1)} %convert_element_type.55, f32[48,16]{0,1:T(8,128)S(1)} %abs_convert_fusion.1), kind=kOutput, calls=%fused_computation.12 | convolution fusion | flops 2145664000 | bytes 18615328 | tf_op jit(solution)/shard_map/kmey,kex->kmxy/dot_general | solution.py:103
  210.3 6.8 %reshape.180 = f32[4,80,4096]{2,1,0:T(8,128)} reshape(f32[4,80,16,256]{3,2,1,0:T(8,128)} %bitcast_add_fusion) | data formatting | bytes 10485760 | tf_op jit(solution)/shard_map/reshape | solution.py:107
  217.1 8.3 %fusion.19 = f32[80,80]{0,1:T(8,128)S(1)} fusion(f32[4,80,4096]{2,1,0:T(8,128)} %reshape.180), kind=kOutput, calls=%fused_computation.25 | convolution fusion | flops 1258297600 | bytes 5268480 | tf_op jit(solution)/shard_map/kmc,knc->mn/dot_general | solution.py:110
  225.5 40.3 %psum.7 = f32[80,80]{0,1:T(8,128)S(1)} all-reduce(f32[80,80]{0,1:T(8,128)S(1)} %fusion.19), channel_id=1, replica_groups=mesh['tile'=8,'lev'=4] {'tile','lev'}, use_global_device_ids=true, to_apply=%region_2.3 | all-reduce | flops 6400 | bytes 51200 | tf_op jit(solution)/shard_map/psum | solution.py:112
  265.8 0.1 copy.78
  265.9 7.3 %cholesky.18 = f32[80,80]{1,0:T(8,128)S(1)} custom-call(f32[80,80]{1,0:T(8,128)S(1)} %fusion.33), custom_call_target="Cholesky" | custom-call | tf_op jit(solution)/shard_map/jit(cholesky)/cholesky | solution.py:113
  273.2 0.6 compare_reduce_fusion
  273.9 0.7 select_bitcast_fusion
  274.5 0.7 copy.79
  (15 shorter events, 0.2 us)
Async XLA Ops:
  0.6 93.0 %copy-start = (bf16[16,16]{1,0:T(8,128)(2,1)S(1)}, bf16[16,16]{1,0:T(8,128)(2,1)}, u32[]{:S(2)}) copy-start(bf16[16,16]{1,0:T(8,128)(2,1)} %param.15) | copy-start | bytes 1540
  7.3 53.8 %all-to-all-start = ((f32[4,8,128]{2,0,1:T(4,128)}), f32[4,8,128]{2,0,1:T(4,128)S(1)}, u32[]{:S(2)}, u32[]{:S(2)}) async-start(f32[4,8,128]{2,0,1:T(4,128)} %multiply_bitcast_fusion), calls=%async_computation | async-start | bytes 32768 | tf_op jit(solution)/shard_map/all_to_all | solution.py:50
  79.7 19.0 %copy-start.2 = (s32[4]{0:T(128)S(1)}, s32[4]{0:T(128)}, u32[]{:S(2)}) copy-start(s32[4]{0:T(128)} %param.16) | copy-start | bytes 52
  95.2 15.1 %all-to-all-start.2 = ((bf16[16,20,1024]{2,1,0:T(8,128)(2,1)}), bf16[16,20,1024]{2,1,0:T(8,128)(2,1)S(1)}, u32[]{:S(2)}, u32[]{:S(2)}) async-start(bf16[16,20,1024]{2,1,0:T(8,128)(2,1)} %copy.71), calls=%async_computation.2 | async-start | bytes 1572864 | tf_op jit(solution)/shard_map/all_to_all | solution.py:80
  111.1 31.2 %collective-permute-start = (bf16[4,80,1024]{2,1,0:T(8,128)(2,1)S(1)}, bf16[4,80,1024]{2,1,0:T(8,128)(2,1)S(1)}, u32[]{:S(2)}, u32[]{:S(2)}) collective-permute-start(bf16[4,80,1024]{2,1,0:T(8,128)(2,1)S(1)} %copy.73), channel_id=1, source_target_pairs={{0,4},{4,8},{8,12},{12,16},{16,20},{20,24},{24,28},{1,5},{5,9},{9,... | collective-permute-start | bytes 1966088 | tf_op jit(solution)/shard_map/ppermute | solution.py:84
  114.5 27.8 %collective-permute-start.1 = (bf16[4,80,1024]{2,1,0:T(8,128)(2,1)S(1)}, bf16[4,80,1024]{2,1,0:T(8,128)(2,1)S(1)}, u32[]{:S(2)}, u32[]{:S(2)}) collective-permute-start(bf16[4,80,1024]{2,1,0:T(8,128)(2,1)S(1)} %copy.73), channel_id=1, source_target_pairs={{4,0},{8,4},{12,8},{16,12},{20,16},{24,20},{28,24},{5,1},{9,5},{13... | collective-permute-start | bytes 1966088 | tf_op jit(solution)/shard_map/ppermute | solution.py:85
  210.3 64.9 %copy-start.1 = (bf16[16,16]{1,0:T(8,128)(2,1)S(1)}, bf16[16,16]{1,0:T(8,128)(2,1)}, u32[]{:S(2)}) copy-start(bf16[16,16]{1,0:T(8,128)(2,1)} %param.15) | copy-start | bytes 1540

commit v2 on v1

--- a/solution.py
+++ b/solution.py
@@ -41,41 +41,35 @@
     slots = tile_count * capacity
     packed = slots < cell_count
     assert HALO <= col_count
-    tile = lax.axis_index("tile")
 
     slot_index = lax.broadcasted_iota(jnp.int32, (tile_count, capacity), 1)
     live_mask = (slot_index < counts[0][:, None]).astype(jnp.float32)
     values = jnp.take(obs_adjoint, foot_obs[0], axis=1)
     payload = values * (foot_weight[0] * live_mask)[None]
-    arrived = lax.all_to_all(payload, "tile", split_axis=1, concat_axis=1, tiled=True)
-    all_cells = lax.all_gather(foot_cell[0], "tile")
-    cells_of = jnp.swapaxes(all_cells, 0, 1).reshape(tile_count, slots)
-    cell_index = lax.dynamic_index_in_dim(cells_of, tile, 0, keepdims=False)
+    own_cells = foot_cell[0]
+    prev_cells = jnp.concatenate([own_cells[:1], own_cells[:-1]], axis=0)
+    next_cells = jnp.concatenate([own_cells[1:], own_cells[-1:]], axis=0)
+    cell_rows = jnp.stack([prev_cells, own_cells, next_cells]).astype(jnp.float32)
+    outgoing = jnp.concatenate([payload, cell_rows], axis=0)
+    arrived = lax.all_to_all(outgoing, "tile", split_axis=1, concat_axis=1, tiled=True)
+    near = arrived[lev_dev:].astype(jnp.int32).reshape(3, slots)
+    cell_index = near[1]
 
     forcing = jnp.zeros((lev_dev, cell_count), jnp.float32)
-    forcing = forcing.at[:, cell_index].add(arrived.reshape(lev_dev, -1))
+    forcing = forcing.at[:, cell_index].add(arrived[:lev_dev].reshape(lev_dev, -1))
     forcing = forcing.reshape(lev_dev, col_count, row_count)
     member_forcing = (ensemble * forcing[:, None]).astype(jnp.bfloat16)
-    member_forcing = member_forcing.reshape(lev_dev, members, cell_count)
 
     if packed:
-        near = jnp.stack(
-            [
-                lax.dynamic_index_in_dim(cells_of, jnp.maximum(tile - 1, 0), 0, keepdims=False),
-                cell_index,
-                lax.dynamic_index_in_dim(
-                    cells_of, jnp.minimum(tile + 1, tile_count - 1), 0, keepdims=False
-                ),
-            ]
-        )
-        hits = one_hot(near, first_hits(near), cell_count)
+        keep = first_hits(near)
+        hits = one_hot(near, keep, cell_count).reshape(3, slots, col_count, row_count)
         member_forcing = jnp.einsum(
-            "lmc,sc->lms", member_forcing, hits[1], preferred_element_type=jnp.float32
+            "lmxy,sxy->lms", member_forcing, hits[1], preferred_element_type=jnp.float32
         ).astype(jnp.bfloat16)
 
     regrouped = lax.all_to_all(member_forcing, "lev", split_axis=1, concat_axis=0, tiled=True)
     local_mix = jnp.einsum(
-        "lk,lmc->kmc", vert_root, regrouped, preferred_element_type=jnp.float32
+        "lk,lm...->km...", vert_root, regrouped, preferred_element_type=jnp.float32
     )
     level_mix = lax.all_to_all(
         local_mix.astype(jnp.bfloat16), "lev", split_axis=0, concat_axis=1, tiled=True
@@ -86,28 +80,25 @@
     three = jnp.stack([from_left, level_mix, from_right])
     if packed:
         three = jnp.einsum(
-            "tkms,tsc->kmtc", three, hits, preferred_element_type=jnp.float32
+            "tkms,tsxy->tkmxy", three, hits, preferred_element_type=jnp.float32
         ).astype(jnp.bfloat16)
-    else:
-        three = jnp.moveaxis(three, 0, 2)
-    wide_mix = three.reshape(lev_dev, members, 3 * col_count, row_count)
 
     row_iota = jnp.arange(row_count, dtype=jnp.int32)
     taps_rows = taps_table(radius, row_iota[:, None] - row_iota[None, :])
     wide_iota = jnp.arange(3 * col_count, dtype=jnp.int32)
     col_iota = jnp.arange(col_count, dtype=jnp.int32)
     taps_cols = taps_table(radius, wide_iota[:, None] - col_count - col_iota[None, :])
+    taps_cols = taps_cols.reshape(lev_dev, 3, col_count, col_count)
     smooth_wide = jnp.einsum(
-        "kmxy,kyz->kmxz", wide_mix, taps_rows, preferred_element_type=jnp.float32
+        "tkmxy,kyz->tkmxz", three, taps_rows, preferred_element_type=jnp.float32
     ).astype(jnp.bfloat16)
     smooth_x = jnp.einsum(
-        "kmey,kex->kmxy", smooth_wide, taps_cols, preferred_element_type=jnp.float32
+        "tkmey,ktex->kmxy", smooth_wide, taps_cols, preferred_element_type=jnp.float32
     )
     gradient = alpha + smooth_x
-    panel = gradient.reshape(lev_dev, members, col_count * row_count)
     total_cells = float(lev_dev * group_count * col_count * tile_count * row_count)
     gram_local = (
-        jnp.einsum("kmc,knc->mn", panel, panel, precision=lax.Precision.HIGHEST) / total_cells
+        jnp.einsum("kmxy,knxy->mn", gradient, gradient, precision=lax.Precision.HIGHEST) / total_cells
     )
     gram_total = lax.psum(gram_local, ("tile", "lev"))
     r_factor = jnp.linalg.cholesky(gram_total).T

time: 276 us -> 197 us (0.71)
  local copies, waits for them, and re-layouts: 63.7 us -> 10.2 us
  blocking collectives: 84.2 us -> 53 us
  other arithmetic: 35.7 us -> 27.6 us
  matrix products: 37.4 us -> 44.5 us
  waiting for transfers between devices: 37.6 us -> 42.7 us
    reshape x4 -> x2, local copies, waits for them, and re-layouts: 32.2 us -> 0.23 us  [shards(): arrived[:lev_dev].reshape(lev_dev, -1)]
    all_gather x1 -> x0, blocking collectives: 31.1 us -> none  [shards(): all_cells = lax.all_gather(foot_cell[0], 'tile')]
    convert_element_type x2 -> x1, local copies, waits for them, and re-layouts: 23.6 us -> 0.51 us  [shards(): member_forcing = jnp.einsum('lmxy,sxy->lms', member_forcing, hits[1], pre...]
    ppermute x1, waiting for transfers between devices: 26 us -> 12.9 us  [shards(): lax.ppermute(level_mix, 'tile', [(i, i + 1) for i in range(ends)])]
    ppermute x1, waiting for transfers between devices: 0.01 us -> 11.8 us  [shards(): lax.ppermute(level_mix, 'tile', [(i + 1, i) for i in range(ends)])]
    and x1, other arithmetic: 12.4 us -> 3.5 us  [one_hot(): hit = (cells[..., None] == grid) & keep[..., None]]
    dot_general x5, matrix products: 37.4 us -> 44.5 us  [the longest x1 16 us: shards(): jnp.einsum('tkms,tsxy->tkmxy', three, hits, preferred_element_type=jnp.fl...]
    all_to_all x1, waiting for transfers between devices: 0.01 us -> 6.37 us  [shards(): lax.all_to_all(outgoing, 'tile', split_axis=1, concat_axis=1, tiled=True)]
  transfers between devices with their start and end apart: 4 -> 4, of which waited for: 2 -> 4; matrix products, arithmetic and copies ran while one was open for 6% -> 0% of each run, Pallas kernels for 0% -> 0%
where the time goes in v2:
time: 197 us; the launch traced here: 196 us
  blocking collectives  53 us (27%)
  matrix products  44.5 us (23%)
  waiting for transfers between devices  42.7 us (22%)
  other arithmetic  27.6 us (14%)
  starting transfers between devices  16.8 us (9%)
  local copies, waits for them, and re-layouts  10.2 us (5%)
    psum x1, blocking collectives, shards(): gram_total = lax.psum(gram_local, ('tile', 'lev'))  40.1 us
    dot_general x1, matrix products, shards(): jnp.einsum('tkms,tsxy->tkmxy', three, hits, preferred_element_type=jnp.fl...  16 us
    dot_general x1, matrix products, shards(): jnp.einsum('kmxy,knxy->mn', gradient, gradient, precision=lax.Precision.H...  13.8 us
    ppermute x1, waiting for transfers between devices, shards(): lax.ppermute(level_mix, 'tile', [(i, i + 1) for i in range(ends)])  12.9 us
    all_to_all x1, blocking collectives, shards(): lax.all_to_all(member_forcing, 'lev', split_axis=1, concat_axis=0, tiled=...  12.8 us
    ppermute x1, waiting for transfers between devices, shards(): lax.ppermute(level_mix, 'tile', [(i + 1, i) for i in range(ends)])  11.8 us
    all_to_all x1, waiting for transfers between devices, shards(): lax.all_to_all(local_mix.astype(jnp.bfloat16), 'lev', split_axis=0, conca...  11.6 us
    dot_general x1, matrix products, shards(): jnp.einsum('tkmey,ktex->kmxy', smooth_wide, taps_cols, preferred_element_...  10.9 us
  transfers between devices with their start and end apart: 4, of which 4 were waited for; matrix products, arithmetic and copies ran while one was open for 0% of the time, Pallas kernels for 0%

profile of v2, /device:TPU:0, one launch (start us, length us, event | category | flops | bytes accessed | tf_op | source)
XLA Modules:
  0.0 195.7 jit_solution(7878956950496482561)
XLA Ops:
  0.6 0.0 copy-start
  0.6 0.7 compare_and_fusion
  1.3 0.7 fusion.66
  2.0 0.8 slice_bitcast_fusion.4
  2.8 0.8 slice_bitcast_fusion.2
  3.6 0.8 copy.84
  4.4 2.8 %gather_fusion = f32[1024,4]{1,0:T(8,128)S(1)} fusion(f32[4,512]{0,1:T(8,128)S(1)} %copy.84, s32[1024]{0:T(1024)S(1)} %fusion.66), kind=kCustom, calls=%fused_computation | custom fusion | bytes 36864 | tf_op jit(solution)/shard_map/jit(_take)/gather | solution.py:47
  7.2 0.2 copy.85
  7.4 0.8 select_bitcast_fusion.1
  8.2 0.7 add_convert_fusion
  8.9 0.6 pad_maximum_fusion
  9.5 7.3 %all-to-all-start = ((f32[7,8,128]{2,0,1:T(8,128)}), f32[7,8,128]{2,0,1:T(8,128)S(1)}, u32[]{:S(2)}, u32[]{:S(2)}) async-start(f32[7,8,128]{2,0,1:T(8,128)} %pad_maximum_fusion), calls=%async_computation | async-start | bytes 65536 | tf_op jit(solution)/shard_map/all_to_all | solution.py:54
  16.8 0.3 iota_compare_fusion.1
  17.1 6.4 %all-to-all-done = f32[7,8,128]{2,0,1:T(8,128)S(1)} async-done(((f32[7,8,128]{2,0,1:T(8,128)}), f32[7,8,128]{2,0,1:T(8,128)S(1)}, u32[]{:S(2)}, u32[]{:S(2)}) %all-to-all-start) | async-done | bytes 28704 | tf_op jit(solution)/shard_map/all_to_all | solution.py:54
  23.6 0.2 copy.88
  23.8 2.6 %and_reduce_fusion = pred[3,1024]{1,0:T(4,128)(4,1)S(1)} fusion(s32[3,1024]{1,0:T(4,128)S(1)} %bitcast.118, pred[1024,1024]{1,0:T(8,128)(4,1)S(1)} %iota_compare_fusion.1), kind=kLoop, calls=%fused_computation.11 | loop fusion | flops 9434112 | bytes 1063936 | tf_op jit(solution)/shard_map/reduce_or | solution.py:24
  26.5 6.7 %scatter_custom_fusion = f32[4,4096]{0,1:T(8,128)S(1)} fusion(s32[1024]{0:T(1024)S(1)} %bitcast.124, f32[1024,4]{1,0:T(8,128)S(1)} %copy.88, f32[]{:T(128)} %constant.61.clone.1), kind=kCustom, calls=%fused_computation.36 | custom fusion | flops 4096 | bytes 65540 | tf_op jit(solution)/shard_map/scatter-add | solution.py:59
  33.2 0.6 copy.89
  33.8 2.2 %multiply_convert_fusion = bf16[4,80,16,256]{3,2,1,0:T(8,128)(2,1)S(1)} fusion(bf16[4,80,16,256]{3,2,1,0:T(8,128)(2,1)} %param.14, f32[4,16,256]{2,1,0:T(8,128)S(1)} %copy.89), kind=kLoop, calls=%fused_computation.21 | loop fusion | flops 3932160 | bytes 5308416 | tf_op jit(solution)/shard_map/convert_element_type | solution.py:61
  36.0 3.5 %fusion.7 = pred[1,1024,4096]{1,2,0:T(32,128)(4,1)S(1)} fusion(s32[1,1024]{1,0:T(1,128)S(1)} %slice.61, pred[1,1024]{1,0:T(4,128)(4,1)S(1)} %slice.62), kind=kLoop, calls=%fused_computation.10 | loop fusion | flops 8388608 | bytes 4199424 | tf_op jit(solution)/shard_map/and | solution.py:29
  39.5 3.5 %fusion.35 = bf16[4,80,1024]{2,1,0:T(8,128)(2,1)S(1)} fusion(pred[1024,16,256,1]{0,2,1,3:T(32,128)(4,1)S(1)} %bitcast.113, bf16[4,80,16,256]{3,2,1,0:T(8,128)(2,1)S(1)} %multiply_convert_fusion), kind=kOutput, calls=%fused_computation.32 | convolution fusion | flops 2684682240 | bytes 7471104 | tf_op jit(solution)/shard_map/lmxy,sxy->lms/dot_general | solution.py:66
  43.0 0.5 copy.92
  43.5 0.0 copy-start.1
  43.6 12.8 %all_to_all.41 = bf16[4,80,1024]{2,0,1:T(4,128)(2,1)S(1)} all-to-all(bf16[4,80,1024]{2,0,1:T(4,128)(2,1)S(1)} %copy.92), channel_id=1, replica_groups=mesh['tile'=8,'lev'=4] {'lev'}, dimensions={1} | all-to-all | bytes 1310720 | tf_op jit(solution)/shard_map/all_to_all | solution.py:70
  56.4 0.3 copy.93
  56.7 0.2 all_to_all.33
  56.9 0.0 copy-done
  56.9 0.4 fusion.38
  57.3 1.3 copy.95
  58.5 3.5 %all-to-all-start.2 = ((bf16[16,20,1024]{2,1,0:T(8,128)(2,1)}), bf16[16,20,1024]{2,1,0:T(8,128)(2,1)S(1)}, u32[]{:S(2)}, u32[]{:S(2)}) async-start(bf16[16,20,1024]{2,1,0:T(8,128)(2,1)} %copy.95), calls=%async_computation.2 | async-start | bytes 1572864 | tf_op jit(solution)/shard_map/all_to_all | solution.py:74
  62.0 0.0 copy-done.1
  62.1 11.6 %all-to-all-done.2 = bf16[16,20,1024]{2,1,0:T(8,128)(2,1)S(1)} async-done(((bf16[16,20,1024]{2,1,0:T(8,128)(2,1)}), bf16[16,20,1024]{2,1,0:T(8,128)(2,1)S(1)}, u32[]{:S(2)}, u32[]{:S(2)}) %all-to-all-start.2) | async-done | bytes 655392 | tf_op jit(solution)/shard_map/all_to_all | solution.py:74
  73.7 0.5 copy.96
  74.2 0.2 copy.97
  74.4 1.3 collective-permute-start.1
  75.7 4.8 %collective-permute-start = (bf16[4,80,1024]{2,1,0:T(8,128)(2,1)S(1)}, bf16[4,80,1024]{2,1,0:T(8,128)(2,1)S(1)}, u32[]{:S(2)}, u32[]{:S(2)}) collective-permute-start(bf16[4,80,1024]{2,1,0:T(8,128)(2,1)S(1)} %copy.97), channel_id=1, source_target_pairs={{0,4},{4,8},{8,12},{12,16},{16,20},{20,24},{24,28},{1,5},{5,9},{9,... | collective-permute-start | bytes 1966088 | tf_op jit(solution)/shard_map/ppermute | solution.py:78
  80.6 0.2 copy.99
  80.8 11.8 %collective-permute-done.1 = bf16[4,80,1024]{2,1,0:T(8,128)(2,1)S(1)} collective-permute-done((bf16[4,80,1024]{2,1,0:T(8,128)(2,1)S(1)}, bf16[4,80,1024]{2,1,0:T(8,128)(2,1)S(1)}, u32[]{:S(2)}, u32[]{:S(2)}) %collective-permute-start.1) | collective-permute-done | bytes 655392 | tf_op jit(solution)/shard_map/ppermute | solution.py:79
  92.5 12.9 %collective-permute-done = bf16[4,80,1024]{2,1,0:T(8,128)(2,1)S(1)} collective-permute-done((bf16[4,80,1024]{2,1,0:T(8,128)(2,1)S(1)}, bf16[4,80,1024]{2,1,0:T(8,128)(2,1)S(1)}, u32[]{:S(2)}, u32[]{:S(2)}) %collective-permute-start) | collective-permute-done | bytes 655392 | tf_op jit(solution)/shard_map/ppermute | solution.py:78
  105.5 16.0 %fusion.17 = bf16[3,4,80,16,256]{4,2,3,1,0:T(8,128)(2,1)} fusion(s32[16,256]{1,0:T(8,128)S(1)} %multiply_add_fusion, s32[3,1024]{1,0:T(4,128)S(1)} %bitcast.119, pred[3,1024]{1,0:T(4,128)(4,1)S(1)} %not.7, bf16[1,4,80,1024]{3,2,1,0:T(8,128)(2,1)S(1)} %bitcast.126, bf16[1,4,80,1024]{3,2,1,0:T(8,128)(2,1)S(1)} %copy.99, bf16[1,4,80,1024]{3,2,1,0:T(8,128)(2,1)S(1)} %bitcast.127), kind=kOutput, calls=%fused_computation.17 | convolution fusion | flops 8088059904 | bytes 9862144 | tf_op jit(solution)/shard_map/tkms,tsxy->tkmxy/dot_general | solution.py:82
  121.5 10.9 %bitcast_add_fusion = f32[4,80,16,256]{3,2,1,0:T(8,128)} fusion(f32[4,80,16,256]{3,2,1,0:T(8,128)} %param.17, bf16[3,4,80,16,256]{4,2,3,1,0:T(8,128)(2,1)} %fusion.17, f32[4]{0:T(128)S(1)} %broadcast_add_fusion, f32[256,256]{1,0:T(8,128)S(1)} %abs_convert_fusion, f32[4]{0:T(128)S(1)} %convert_element_type.62, f32[3,16,16]{1,2,0:T(8,128)S(1)} %abs_convert_fusion.1), kind=kOutput, calls=%fused_computation.18 | convolution fusion | flops 2145664000 | bytes 18615328 | tf_op jit(solution)/shard_map/tkmey,ktex->kmxy/dot_general | solution.py:95
  132.3 13.8 %fusion.42 = f32[80,80]{0,1:T(8,128)S(1)} fusion(f32[4,80,16,256]{3,2,1,0:T(8,128)} %bitcast_add_fusion), kind=kOutput, calls=%fused_computation.35 | convolution fusion | flops 1258297600 | bytes 5268480 | tf_op jit(solution)/shard_map/kmxy,knxy->mn/dot_general | solution.py:101
  146.1 40.1 %psum.7 = f32[80,80]{0,1:T(8,128)S(1)} all-reduce(f32[80,80]{0,1:T(8,128)S(1)} %fusion.42), channel_id=1, replica_groups=mesh['tile'=8,'lev'=4] {'tile','lev'}, use_global_device_ids=true, to_apply=%region_2.3 | all-reduce | flops 6400 | bytes 51200 | tf_op jit(solution)/shard_map/psum | solution.py:103
  186.3 0.1 copy.104
  186.4 7.3 %cholesky.18 = f32[80,80]{1,0:T(8,128)S(1)} custom-call(f32[80,80]{1,0:T(8,128)S(1)} %fusion.64), custom_call_target="Cholesky" | custom-call | tf_op jit(solution)/shard_map/jit(cholesky)/cholesky | solution.py:104
  193.7 0.6 compare_reduce_fusion
  194.3 0.7 select_bitcast_fusion
  195.0 0.7 copy.105
  (20 shorter events, 0.2 us)
Async XLA Ops:
  0.6 56.3 %copy-start = (bf16[16,16]{1,0:T(8,128)(2,1)S(1)}, bf16[16,16]{1,0:T(8,128)(2,1)}, u32[]{:S(2)}) copy-start(bf16[16,16]{1,0:T(8,128)(2,1)} %param.15) | copy-start | bytes 1540
  9.5 13.9 %all-to-all-start = ((f32[7,8,128]{2,0,1:T(8,128)}), f32[7,8,128]{2,0,1:T(8,128)S(1)}, u32[]{:S(2)}, u32[]{:S(2)}) async-start(f32[7,8,128]{2,0,1:T(8,128)} %pad_maximum_fusion), calls=%async_computation | async-start | bytes 65536 | tf_op jit(solution)/shard_map/all_to_all | solution.py:54
  43.5 18.5 %copy-start.1 = (s32[4]{0:T(128)S(1)}, s32[4]{0:T(128)}, u32[]{:S(2)}) copy-start(s32[4]{0:T(128)} %param.16) | copy-start | bytes 52
  58.5 15.1 %all-to-all-start.2 = ((bf16[16,20,1024]{2,1,0:T(8,128)(2,1)}), bf16[16,20,1024]{2,1,0:T(8,128)(2,1)S(1)}, u32[]{:S(2)}, u32[]{:S(2)}) async-start(bf16[16,20,1024]{2,1,0:T(8,128)(2,1)} %copy.95), calls=%async_computation.2 | async-start | bytes 1572864 | tf_op jit(solution)/shard_map/all_to_all | solution.py:74
  74.4 18.2 %collective-permute-start.1 = (bf16[4,80,1024]{2,1,0:T(8,128)(2,1)S(1)}, bf16[4,80,1024]{2,1,0:T(8,128)(2,1)S(1)}, u32[]{:S(2)}, u32[]{:S(2)}) collective-permute-start(bf16[4,80,1024]{2,1,0:T(8,128)(2,1)S(1)} %copy.97), channel_id=1, source_target_pairs={{4,0},{8,4},{12,8},{16,12},{20,16},{24,20},{28,24},{5,1},{9,5},{13... | collective-permute-start | bytes 1966088 | tf_op jit(solution)/shard_map/ppermute | solution.py:79
  75.7 29.8 %collective-permute-start = (bf16[4,80,1024]{2,1,0:T(8,128)(2,1)S(1)}, bf16[4,80,1024]{2,1,0:T(8,128)(2,1)S(1)}, u32[]{:S(2)}, u32[]{:S(2)}) collective-permute-start(bf16[4,80,1024]{2,1,0:T(8,128)(2,1)S(1)} %copy.97), channel_id=1, source_target_pairs={{0,4},{4,8},{8,12},{12,16},{16,20},{20,24},{24,28},{1,5},{5,9},{9,... | collective-permute-start | bytes 1966088 | tf_op jit(solution)/shard_map/ppermute | solution.py:78

commit v3 on v2

--- a/solution.py
+++ b/solution.py
@@ -30,6 +30,17 @@
     return hit.astype(jnp.bfloat16)
 
 
+def all_sum(value, axes):
+    if any(size & (size - 1) for _, size in axes):
+        return lax.psum(value, tuple(name for name, _ in axes))
+    for name, size in axes:
+        bit = 1
+        while bit < size:
+            value = value + lax.ppermute(value, name, [(i, i ^ bit) for i in range(size)])
+            bit *= 2
+    return value
+
+
 def shards(
     obs_adjoint, foot_obs, foot_cell, foot_weight, counts, ensemble, vert_root, radius, alpha
 ):
@@ -55,17 +66,23 @@
     near = arrived[lev_dev:].astype(jnp.int32).reshape(3, slots)
     cell_index = near[1]
 
-    forcing = jnp.zeros((lev_dev, cell_count), jnp.float32)
-    forcing = forcing.at[:, cell_index].add(arrived[:lev_dev].reshape(lev_dev, -1))
-    forcing = forcing.reshape(lev_dev, col_count, row_count)
-    member_forcing = (ensemble * forcing[:, None]).astype(jnp.bfloat16)
-
     if packed:
+        same = (cell_index[:, None] == cell_index[None, :]).astype(jnp.float32)
+        forcing = jnp.einsum(
+            "ls,st->lt", arrived[:lev_dev].reshape(lev_dev, -1), same,
+            precision=lax.Precision.HIGHEST,
+        )
         keep = first_hits(near)
         hits = one_hot(near, keep, cell_count).reshape(3, slots, col_count, row_count)
-        member_forcing = jnp.einsum(
-            "lmxy,sxy->lms", member_forcing, hits[1], preferred_element_type=jnp.float32
-        ).astype(jnp.bfloat16)
+        picked = jnp.einsum(
+            "lmxy,sxy->lms", ensemble, hits[1], preferred_element_type=jnp.float32
+        )
+        member_forcing = (picked * forcing[:, None]).astype(jnp.bfloat16)
+    else:
+        forcing = jnp.zeros((lev_dev, cell_count), jnp.float32)
+        forcing = forcing.at[:, cell_index].add(arrived[:lev_dev].reshape(lev_dev, -1))
+        forcing = forcing.reshape(lev_dev, col_count, row_count)
+        member_forcing = (ensemble * forcing[:, None]).astype(jnp.bfloat16)
 
     regrouped = lax.all_to_all(member_forcing, "lev", split_axis=1, concat_axis=0, tiled=True)
     local_mix = jnp.einsum(
@@ -100,7 +117,7 @@
     gram_local = (
         jnp.einsum("kmxy,knxy->mn", gradient, gradient, precision=lax.Precision.HIGHEST) / total_cells
     )
-    gram_total = lax.psum(gram_local, ("tile", "lev"))
+    gram_total = all_sum(gram_local, (("lev", group_count), ("tile", tile_count)))
     r_factor = jnp.linalg.cholesky(gram_total).T
     return (gradient, r_factor)
 

time: 197 us -> 169 us (0.86)
  blocking collectives: 53 us -> 12.8 us
  waiting for transfers between devices: 42.7 us -> 55 us
  other arithmetic: 27.6 us -> 21.2 us
  starting transfers between devices: 16.8 us -> 22.2 us
    psum x1 -> x0, blocking collectives: 40.1 us -> none  [shards(): gram_total = lax.psum(gram_local, ('tile', 'lev'))]
    ppermute x0 -> x5, waiting for transfers between devices: none -> 13.2 us  [all_sum(): lax.ppermute(value, name, [(i, i ^ bit) for i in range(size)])]
    scatter-add x1 -> x0, other arithmetic: 6.71 us -> none  [shards(): forcing.at[:, cell_index].add(arrived[:lev_dev].reshape(lev_dev, -1))]
    ppermute x0 -> x5, starting transfers between devices: none -> 5.42 us  [all_sum(): lax.ppermute(value, name, [(i, i ^ bit) for i in range(size)])]
    convert_element_type x1 -> x0, other arithmetic: 2.22 us -> none  [shards(): member_forcing = (ensemble * forcing[:, None]).astype(jnp.bfloat16)]
    dot_general x1 -> x2, matrix products: 3.49 us -> 4.57 us  [the longest x1 3.23 us: shards(): jnp.einsum('lmxy,sxy->lms', ensemble, hits[1], preferred_element_type=jnp...]
  transfers between devices with their start and end apart: 4 -> 9, of which waited for: 4 -> 9; matrix products, arithmetic and copies ran while one was open for 0% -> 1% of each run, Pallas kernels for 0% -> 0%
where the time goes in v3:
time: 169 us
  waiting for transfers between devices  55 us (33%)
  matrix products  46.4 us (27%)
  starting transfers between devices  22.2 us (13%)
  other arithmetic  21.2 us (13%)
  blocking collectives  12.8 us (8%)
  local copies, waits for them, and re-layouts  10.2 us (6%)
    dot_general x1, matrix products, shards(): jnp.einsum('tkms,tsxy->tkmxy', three, hits, preferred_element_type=jnp.fl...  15.9 us
    dot_general x1, matrix products, shards(): jnp.einsum('kmxy,knxy->mn', gradient, gradient, precision=lax.Precision.H...  13.8 us
    ppermute x5, waiting for transfers between devices, all_sum(): lax.ppermute(value, name, [(i, i ^ bit) for i in range(size)])  13.2 us
    ppermute x1, waiting for transfers between devices, shards(): lax.ppermute(level_mix, 'tile', [(i, i + 1) for i in range(ends)])  12.9 us
    all_to_all x1, blocking collectives, shards(): lax.all_to_all(member_forcing, 'lev', split_axis=1, concat_axis=0, tiled=...  12.8 us
    ppermute x1, waiting for transfers between devices, shards(): lax.ppermute(level_mix, 'tile', [(i + 1, i) for i in range(ends)])  12 us
    all_to_all x1, waiting for transfers between devices, shards(): lax.all_to_all(local_mix.astype(jnp.bfloat16), 'lev', split_axis=0, conca...  11.4 us
    dot_general x1, matrix products, shards(): jnp.einsum('tkmey,ktex->kmxy', smooth_wide, taps_cols, preferred_element_...  10.6 us
  transfers between devices with their start and end apart: 9, of which 9 were waited for; matrix products, arithmetic and copies ran while one was open for 1% of the time, Pallas kernels for 0%

profile of v3, /device:TPU:0, one launch (start us, length us, event | category | flops | bytes accessed | tf_op | source)
XLA Modules:
  0.0 168.7 jit_solution(6769631714299450376)
XLA Ops:
  0.6 0.8 compare_and_fusion
  1.5 0.7 fusion.71
  2.2 0.8 slice_bitcast_fusion.6
  2.9 0.8 slice_bitcast_fusion.4
  3.7 0.8 copy.58
  4.6 2.8 %gather_fusion = f32[1024,4]{1,0:T(8,128)S(1)} fusion(f32[4,512]{0,1:T(8,128)S(1)} %copy.58, s32[1024]{0:T(1024)S(1)} %fusion.71), kind=kCustom, calls=%fused_computation | custom fusion | bytes 36864 | tf_op jit(solution)/shard_map/jit(_take)/gather | solution.py:58
  7.4 0.2 copy.59
  7.6 0.8 select_bitcast_fusion.1
  8.3 0.7 add_convert_fusion
  9.1 0.6 pad_maximum_fusion
  9.7 7.3 %all-to-all-start = ((f32[7,8,128]{2,0,1:T(8,128)}), f32[7,8,128]{2,0,1:T(8,128)S(1)}, u32[]{:S(2)}, u32[]{:S(2)}) async-start(f32[7,8,128]{2,0,1:T(8,128)} %pad_maximum_fusion), calls=%async_computation | async-start | bytes 65536 | tf_op jit(solution)/shard_map/all_to_all | solution.py:65
  16.9 1.3 iota_compare_fusion.1
  18.2 5.4 %all-to-all-done = f32[7,8,128]{2,0,1:T(8,128)S(1)} async-done(((f32[7,8,128]{2,0,1:T(8,128)}), f32[7,8,128]{2,0,1:T(8,128)S(1)}, u32[]{:S(2)}, u32[]{:S(2)}) %all-to-all-start) | async-done | bytes 28704 | tf_op jit(solution)/shard_map/all_to_all | solution.py:65
  23.7 4.0 %and_reduce_fusion = pred[3,1024]{1,0:T(4,128)(4,1)S(1)} fusion(s32[3,1024]{1,0:T(4,128)S(1)} %bitcast.120, pred[1024,1024]{1,0:T(8,128)(4,1)} %iota_compare_fusion.1), kind=kLoop, calls=%fused_computation.10 | loop fusion | flops 9434112 | bytes 1063936 | tf_op jit(solution)/shard_map/reduce_or | solution.py:24
  27.7 3.5 %fusion.7 = pred[1,1024,4096]{1,2,0:T(32,128)(4,1)S(1)} fusion(s32[1,1024]{1,0:T(1,128)S(1)} %slice.59, pred[1,1024]{1,0:T(4,128)(4,1)S(1)} %slice.60), kind=kLoop, calls=%fused_computation.9 | loop fusion | flops 8388608 | bytes 4199424 | tf_op jit(solution)/shard_map/and | solution.py:29
  31.2 1.3 fusion.22
  32.6 3.2 %fusion.42 = bf16[4,80,1024]{2,1,0:T(8,128)(2,1)S(1)} fusion(pred[1024,16,256,1]{0,2,1,3:T(32,128)(4,1)S(1)} %bitcast.115, bf16[4,80,16,256]{3,2,1,0:T(8,128)(2,1)S(1)} %copy-done, f32[4,1024]{1,0:T(4,128)S(1)} %fusion.22), kind=kOutput, calls=%fused_computation.34 | convolution fusion | flops 2685009920 | bytes 7487488 | tf_op jit(solution)/shard_map/lmxy,sxy->lms/dot_general | solution.py:77
  35.8 0.5 copy.64
  36.4 12.8 %all_to_all.41 = bf16[4,80,1024]{2,0,1:T(4,128)(2,1)S(1)} all-to-all(bf16[4,80,1024]{2,0,1:T(4,128)(2,1)S(1)} %copy.64), channel_id=1, replica_groups=mesh['tile'=8,'lev'=4] {'lev'}, dimensions={1} | all-to-all | bytes 1310720 | tf_op jit(solution)/shard_map/all_to_all | solution.py:87
  49.2 0.3 copy.65
  49.5 1.0 all_to_all.33
  50.5 1.5 fusion.45
  52.0 1.3 copy.67
  53.3 3.7 %all-to-all-start.2 = ((bf16[16,20,1024]{2,1,0:T(8,128)(2,1)}), bf16[16,20,1024]{2,1,0:T(8,128)(2,1)S(1)}, u32[]{:S(2)}, u32[]{:S(2)}) async-start(bf16[16,20,1024]{2,1,0:T(8,128)(2,1)} %copy.67), calls=%async_computation.2 | async-start | bytes 1572864 | tf_op jit(solution)/shard_map/all_to_all | solution.py:91
  57.0 11.4 %all-to-all-done.2 = bf16[16,20,1024]{2,1,0:T(8,128)(2,1)S(1)} async-done(((bf16[16,20,1024]{2,1,0:T(8,128)(2,1)}), bf16[16,20,1024]{2,1,0:T(8,128)(2,1)S(1)}, u32[]{:S(2)}, u32[]{:S(2)}) %all-to-all-start.2) | async-done | bytes 655392 | tf_op jit(solution)/shard_map/all_to_all | solution.py:91
  68.4 0.5 copy.68
  68.9 0.2 copy.69
  69.1 1.3 collective-permute-start.1
  70.4 4.6 %collective-permute-start = (bf16[4,80,1024]{2,1,0:T(8,128)(2,1)S(1)}, bf16[4,80,1024]{2,1,0:T(8,128)(2,1)S(1)}, u32[]{:S(2)}, u32[]{:S(2)}) collective-permute-start(bf16[4,80,1024]{2,1,0:T(8,128)(2,1)S(1)} %copy.69), channel_id=1, source_target_pairs={{0,4},{4,8},{8,12},{12,16},{16,20},{20,24},{24,28},{1,5},{5,9},{9,... | collective-permute-start | bytes 1966088 | tf_op jit(solution)/shard_map/ppermute | solution.py:95
  75.1 0.2 copy.71
  75.3 12.0 %collective-permute-done.1 = bf16[4,80,1024]{2,1,0:T(8,128)(2,1)S(1)} collective-permute-done((bf16[4,80,1024]{2,1,0:T(8,128)(2,1)S(1)}, bf16[4,80,1024]{2,1,0:T(8,128)(2,1)S(1)}, u32[]{:S(2)}, u32[]{:S(2)}) %collective-permute-start.1) | collective-permute-done | bytes 655392 | tf_op jit(solution)/shard_map/ppermute | solution.py:96
  87.3 12.9 %collective-permute-done = bf16[4,80,1024]{2,1,0:T(8,128)(2,1)S(1)} collective-permute-done((bf16[4,80,1024]{2,1,0:T(8,128)(2,1)S(1)}, bf16[4,80,1024]{2,1,0:T(8,128)(2,1)S(1)}, u32[]{:S(2)}, u32[]{:S(2)}) %collective-permute-start) | collective-permute-done | bytes 655392 | tf_op jit(solution)/shard_map/ppermute | solution.py:95
  100.2 15.9 %fusion.17 = bf16[3,4,80,16,256]{4,2,3,1,0:T(8,128)(2,1)} fusion(s32[16,256]{1,0:T(8,128)S(1)} %multiply_add_fusion, s32[3,1024]{1,0:T(4,128)S(1)} %bitcast.121, pred[3,1024]{1,0:T(4,128)(4,1)S(1)} %not.7, bf16[1,4,80,1024]{3,2,1,0:T(8,128)(2,1)S(1)} %bitcast.126, bf16[1,4,80,1024]{3,2,1,0:T(8,128)(2,1)S(1)} %copy.71, bf16[1,4,80,1024]{3,2,1,0:T(8,128)(2,1)S(1)} %bitcast.127), kind=kOutput, calls=%fused_computation.16 | convolution fusion | flops 8088059904 | bytes 9862144 | tf_op jit(solution)/shard_map/tkms,tsxy->tkmxy/dot_general | solution.py:99
  116.1 10.6 %bitcast_add_fusion = f32[4,80,16,256]{3,2,1,0:T(8,128)} fusion(f32[4,80,16,256]{3,2,1,0:T(8,128)} %param.17, bf16[3,4,80,16,256]{4,2,3,1,0:T(8,128)(2,1)} %fusion.17, f32[4]{0:T(128)S(1)} %broadcast_add_fusion, f32[256,256]{1,0:T(8,128)S(1)} %abs_convert_fusion, f32[4]{0:T(128)S(1)} %convert_element_type.57, f32[3,16,16]{1,2,0:T(8,128)S(1)} %abs_convert_fusion.1), kind=kOutput, calls=%fused_computation.17 | convolution fusion | flops 2145664000 | bytes 18615328 | tf_op jit(solution)/shard_map/tkmey,ktex->kmxy/dot_general | solution.py:112
  126.7 13.8 %fusion.49 = f32[80,80]{0,1:T(8,128)S(1)} fusion(f32[4,80,16,256]{3,2,1,0:T(8,128)} %bitcast_add_fusion), kind=kOutput, calls=%fused_computation.38 | convolution fusion | flops 1258297600 | bytes 5268480 | tf_op jit(solution)/shard_map/kmxy,knxy->mn/dot_general | solution.py:118
  140.7 1.2 collective-permute-done.2
  141.8 0.6 collective-permute-start.3
  142.4 3.4 %collective-permute-done.3 = f32[80,80]{0,1:T(8,128)S(1)} collective-permute-done((f32[80,80]{0,1:T(8,128)S(1)}, f32[80,80]{0,1:T(8,128)S(1)}, u32[]{:S(2)}, u32[]{:S(2)}) %collective-permute-start.3) | collective-permute-done | bytes 25632 | tf_op jit(solution)/shard_map/ppermute | solution.py:39
  145.8 2.5 %collective-permute-start.4 = (f32[80,80]{0,1:T(8,128)S(1)}, f32[80,80]{0,1:T(8,128)S(1)}, u32[]{:S(2)}, u32[]{:S(2)}) collective-permute-start(f32[80,80]{0,1:T(8,128)S(1)} %add.71), channel_id=1, source_target_pairs={{0,4},{4,0},{8,12},{12,8},{16,20},{20,16},{24,28},{28,24},{1,5},{5... | collective-permute-start | bytes 76808 | tf_op jit(solution)/shard_map/ppermute | solution.py:39
  148.3 2.0 %collective-permute-done.4 = f32[80,80]{0,1:T(8,128)S(1)} collective-permute-done((f32[80,80]{0,1:T(8,128)S(1)}, f32[80,80]{0,1:T(8,128)S(1)}, u32[]{:S(2)}, u32[]{:S(2)}) %collective-permute-start.4) | collective-permute-done | bytes 25632 | tf_op jit(solution)/shard_map/ppermute | solution.py:39
  150.3 1.1 collective-permute-start.5
  151.4 3.0 %collective-permute-done.5 = f32[80,80]{0,1:T(8,128)S(1)} collective-permute-done((f32[80,80]{0,1:T(8,128)S(1)}, f32[80,80]{0,1:T(8,128)S(1)}, u32[]{:S(2)}, u32[]{:S(2)}) %collective-permute-start.5) | collective-permute-done | bytes 25632 | tf_op jit(solution)/shard_map/ppermute | solution.py:39
  154.3 1.2 collective-permute-start.6
  155.5 3.7 %collective-permute-done.6 = f32[80,80]{0,1:T(8,128)S(1)} collective-permute-done((f32[80,80]{0,1:T(8,128)S(1)}, f32[80,80]{0,1:T(8,128)S(1)}, u32[]{:S(2)}, u32[]{:S(2)}) %collective-permute-start.6) | collective-permute-done | bytes 25632 | tf_op jit(solution)/shard_map/ppermute | solution.py:39
  159.3 7.3 %cholesky.18 = f32[80,80]{1,0:T(8,128)S(1)} custom-call(f32[80,80]{1,0:T(8,128)S(1)} %fusion.69), custom_call_target="Cholesky" | custom-call | tf_op jit(solution)/shard_map/jit(cholesky)/cholesky | solution.py:121
  166.7 0.6 compare_reduce_fusion
  167.3 0.7 select_bitcast_fusion
  168.0 0.7 copy.77
  (31 shorter events, 0.4 us)
Async XLA Ops:
  0.6 32.0 %copy-start = (bf16[4,80,16,256]{3,2,1,0:T(8,128)(2,1)S(1)}, bf16[4,80,16,256]{3,2,1,0:T(8,128)(2,1)}, u32[]{:S(2)}) copy-start(bf16[4,80,16,256]{3,2,1,0:T(8,128)(2,1)} %param.14) | copy-start | bytes 7864324
  9.7 13.9 %all-to-all-start = ((f32[7,8,128]{2,0,1:T(8,128)}), f32[7,8,128]{2,0,1:T(8,128)S(1)}, u32[]{:S(2)}, u32[]{:S(2)}) async-start(f32[7,8,128]{2,0,1:T(8,128)} %pad_maximum_fusion), calls=%async_computation | async-start | bytes 65536 | tf_op jit(solution)/shard_map/all_to_all | solution.py:65
  35.8 14.7 %copy-start.1 = (bf16[16,16]{1,0:T(8,128)(2,1)S(1)}, bf16[16,16]{1,0:T(8,128)(2,1)}, u32[]{:S(2)}) copy-start(bf16[16,16]{1,0:T(8,128)(2,1)} %param.15) | copy-start | bytes 1540
  36.4 20.6 %copy-start.2 = (s32[4]{0:T(128)S(1)}, s32[4]{0:T(128)}, u32[]{:S(2)}) copy-start(s32[4]{0:T(128)} %param.16) | copy-start | bytes 52
  53.3 15.1 %all-to-all-start.2 = ((bf16[16,20,1024]{2,1,0:T(8,128)(2,1)}), bf16[16,20,1024]{2,1,0:T(8,128)(2,1)S(1)}, u32[]{:S(2)}, u32[]{:S(2)}) async-start(bf16[16,20,1024]{2,1,0:T(8,128)(2,1)} %copy.67), calls=%async_computation.2 | async-start | bytes 1572864 | tf_op jit(solution)/shard_map/all_to_all | solution.py:91
  69.1 18.2 %collective-permute-start.1 = (bf16[4,80,1024]{2,1,0:T(8,128)(2,1)S(1)}, bf16[4,80,1024]{2,1,0:T(8,128)(2,1)S(1)}, u32[]{:S(2)}, u32[]{:S(2)}) collective-permute-start(bf16[4,80,1024]{2,1,0:T(8,128)(2,1)S(1)} %copy.69), channel_id=1, source_target_pairs={{4,0},{8,4},{12,8},{16,12},{20,16},{24,20},{28,24},{5,1},{9,5},{13... | collective-permute-start | bytes 1966088 | tf_op jit(solution)/shard_map/ppermute | solution.py:96
  70.4 29.8 %collective-permute-start = (bf16[4,80,1024]{2,1,0:T(8,128)(2,1)S(1)}, bf16[4,80,1024]{2,1,0:T(8,128)(2,1)S(1)}, u32[]{:S(2)}, u32[]{:S(2)}) collective-permute-start(bf16[4,80,1024]{2,1,0:T(8,128)(2,1)S(1)} %copy.69), channel_id=1, source_target_pairs={{0,4},{4,8},{8,12},{12,16},{16,20},{20,24},{24,28},{1,5},{5,9},{9,... | collective-permute-start | bytes 1966088 | tf_op jit(solution)/shard_map/ppermute | solution.py:95
  140.5 1.3 collective-permute-start.2
  141.8 4.0 %collective-permute-start.3 = (f32[80,80]{0,1:T(8,128)S(1)}, f32[80,80]{0,1:T(8,128)S(1)}, u32[]{:S(2)}, u32[]{:S(2)}) collective-permute-start(f32[80,80]{0,1:T(8,128)S(1)} %add.70), channel_id=1, source_target_pairs={{0,2},{1,3},{2,0},{3,1},{4,6},{5,7},{6,4},{7,5},{8,10},{9,11},{10,... | collective-permute-start | bytes 76808 | tf_op jit(solution)/shard_map/ppermute | solution.py:39
  145.8 4.5 %collective-permute-start.4 = (f32[80,80]{0,1:T(8,128)S(1)}, f32[80,80]{0,1:T(8,128)S(1)}, u32[]{:S(2)}, u32[]{:S(2)}) collective-permute-start(f32[80,80]{0,1:T(8,128)S(1)} %add.71), channel_id=1, source_target_pairs={{0,4},{4,0},{8,12},{12,8},{16,20},{20,16},{24,28},{28,24},{1,5},{5... | collective-permute-start | bytes 76808 | tf_op jit(solution)/shard_map/ppermute | solution.py:39
  150.3 4.0 %collective-permute-start.5 = (f32[80,80]{0,1:T(8,128)S(1)}, f32[80,80]{0,1:T(8,128)S(1)}, u32[]{:S(2)}, u32[]{:S(2)}) collective-permute-start(f32[80,80]{0,1:T(8,128)S(1)} %add.72), channel_id=1, source_target_pairs={{0,8},{4,12},{8,0},{12,4},{16,24},{20,28},{24,16},{28,20},{1,9},{5... | collective-permute-start | bytes 76808 | tf_op jit(solution)/shard_map/ppermute | solution.py:39
  154.3 4.9 %collective-permute-start.6 = (f32[80,80]{0,1:T(8,128)S(1)}, f32[80,80]{0,1:T(8,128)S(1)}, u32[]{:S(2)}, u32[]{:S(2)}) collective-permute-start(f32[80,80]{0,1:T(8,128)S(1)} %add.73), channel_id=1, source_target_pairs={{0,16},{4,20},{8,24},{12,28},{16,0},{20,4},{24,8},{28,12},{1,17},{... | collective-permute-start | bytes 76808 | tf_op jit(solution)/shard_map/ppermute | solution.py:39

commit v4 on v3

--- a/solution.py
+++ b/solution.py
@@ -94,28 +94,31 @@
     ends = tile_count - 1
     from_left = lax.ppermute(level_mix, "tile", [(i, i + 1) for i in range(ends)])
     from_right = lax.ppermute(level_mix, "tile", [(i + 1, i) for i in range(ends)])
-    three = jnp.stack([from_left, level_mix, from_right])
-    if packed:
-        three = jnp.einsum(
-            "tkms,tsxy->tkmxy", three, hits, preferred_element_type=jnp.float32
-        ).astype(jnp.bfloat16)
-
     row_iota = jnp.arange(row_count, dtype=jnp.int32)
     taps_rows = taps_table(radius, row_iota[:, None] - row_iota[None, :])
     wide_iota = jnp.arange(3 * col_count, dtype=jnp.int32)
     col_iota = jnp.arange(col_count, dtype=jnp.int32)
     taps_cols = taps_table(radius, wide_iota[:, None] - col_count - col_iota[None, :])
     taps_cols = taps_cols.reshape(lev_dev, 3, col_count, col_count)
-    smooth_wide = jnp.einsum(
-        "tkmxy,kyz->tkmxz", three, taps_rows, preferred_element_type=jnp.float32
-    ).astype(jnp.bfloat16)
-    smooth_x = jnp.einsum(
-        "tkmey,ktex->kmxy", smooth_wide, taps_cols, preferred_element_type=jnp.float32
-    )
-    gradient = alpha + smooth_x
+
+    def smoothed(mix, cells, side):
+        if packed:
+            mix = jnp.einsum(
+                "kms,sxy->kmxy", mix, cells, preferred_element_type=jnp.float32
+            ).astype(jnp.bfloat16)
+        mix = jnp.einsum(
+            "kmxy,kyz->kmxz", mix, taps_rows, preferred_element_type=jnp.float32
+        ).astype(jnp.bfloat16)
+        return jnp.einsum(
+            "kmey,kex->kmxy", mix, taps_cols[:, side], preferred_element_type=jnp.float32
+        )
+
+    gradient = alpha + smoothed(level_mix, hits[1] if packed else None, 1)
+    gradient = gradient + smoothed(from_left, hits[0] if packed else None, 0)
+    gradient = gradient + smoothed(from_right, hits[2] if packed else None, 2)
     total_cells = float(lev_dev * group_count * col_count * tile_count * row_count)
     gram_local = (
-        jnp.einsum("kmxy,knxy->mn", gradient, gradient, precision=lax.Precision.HIGHEST) / total_cells
+        jnp.einsum("kmxy,knxy->mn", gradient, gradient, precision=lax.Precision.HIGH) / total_cells
     )
     gram_total = all_sum(gram_local, (("lev", group_count), ("tile", tile_count)))
     r_factor = jnp.linalg.cholesky(gram_total).T

time: 169 us -> 193 us (1.14)
  matrix products: 46.4 us -> 62.9 us
  blocking collectives: 12.8 us -> 0 us
  local copies, waits for them, and re-layouts: 10.2 us -> 20.2 us
  other arithmetic: 21.2 us -> 27.6 us
  waiting for transfers between devices: 55 us -> 58.3 us
    dot_general x2 -> x6, matrix products: 26.5 us -> 45.4 us  [the longest x3 22.7 us: smoothed(): jnp.einsum('kms,sxy->kmxy', mix, cells, preferred_element_type=jnp.float32)]
    all_to_all x1 -> x0, blocking collectives: 12.8 us -> none  [shards(): lax.all_to_all(member_forcing, 'lev', split_axis=1, concat_axis=0, tiled=...]
    ppermute x1, waiting for transfers between devices: 12 us -> 0.01 us  [shards(): lax.ppermute(level_mix, 'tile', [(i + 1, i) for i in range(ends)])]
    all_to_all x0 -> x1, waiting for transfers between devices: none -> 10.2 us  [shards(): lax.all_to_all(member_forcing, 'lev', split_axis=1, concat_axis=0, tiled=...]
    slice x2 -> x1, local copies, waits for them, and re-layouts: 0.02 us -> 10.1 us  [shards(): gradient = gradient + smoothed(from_left, hits[0] if packed else None, 0)]
    and x1, other arithmetic: 3.5 us -> 9.96 us  [one_hot(): hit = (cells[..., None] == grid) & keep[..., None]]
    ppermute x1, waiting for transfers between devices: 12.9 us -> 17 us  [shards(): lax.ppermute(level_mix, 'tile', [(i, i + 1) for i in range(ends)])]
    all_to_all x0 -> x1, starting transfers between devices: none -> 3.48 us  [shards(): lax.all_to_all(member_forcing, 'lev', split_axis=1, concat_axis=0, tiled=...]
  transfers between devices with their start and end apart: 9 -> 10, of which waited for: 9 -> 9; matrix products, arithmetic and copies ran while one was open for 1% -> 11% of each run, Pallas kernels for 0% -> 0%
where the time goes in v4:
time: 193 us; the launch traced here: 192 us
  matrix products  62.9 us (33%)
  waiting for transfers between devices  58.3 us (30%)
  other arithmetic  27.6 us (14%)
  starting transfers between devices  22.4 us (12%)
  local copies, waits for them, and re-layouts  20.2 us (10%)
    dot_general x3, matrix products, smoothed(): jnp.einsum('kms,sxy->kmxy', mix, cells, preferred_element_type=jnp.float32)  22.7 us
    dot_general x3, matrix products, smoothed(): jnp.einsum('kmey,kex->kmxy', mix, taps_cols[:, side], preferred_element_t...  22.7 us
    ppermute x1, waiting for transfers between devices, shards(): lax.ppermute(level_mix, 'tile', [(i, i + 1) for i in range(ends)])  17 us
    ppermute x5, waiting for transfers between devices, all_sum(): lax.ppermute(value, name, [(i, i ^ bit) for i in range(size)])  14.4 us
    dot_general x1, matrix products, shards(): jnp.einsum('kmxy,knxy->mn', gradient, gradient, precision=lax.Precision.H...  12.6 us
    all_to_all x1, waiting for transfers between devices, shards(): lax.all_to_all(local_mix.astype(jnp.bfloat16), 'lev', split_axis=0, conca...  11.3 us
    all_to_all x1, waiting for transfers between devices, shards(): lax.all_to_all(member_forcing, 'lev', split_axis=1, concat_axis=0, tiled=...  10.2 us
    slice x1, local copies, waits for them, and re-layouts, shards(): gradient = gradient + smoothed(from_left, hits[0] if packed else None, 0)  10.1 us
  transfers between devices with their start and end apart: 10, of which 9 were waited for; matrix products, arithmetic and copies ran while one was open for 11% of the time, Pallas kernels for 0%

profile of v4, /device:TPU:0, one launch (start us, length us, event | category | flops | bytes accessed | tf_op | source)
XLA Modules:
  0.0 192.4 jit_solution(798965240085385783)
XLA Ops:
  0.6 0.9 slice_bitcast_fusion.10
  1.5 0.8 slice_bitcast_fusion.12
  2.3 0.7 fusion.81
  3.0 0.7 compare_and_fusion
  3.7 0.8 copy.85
  4.5 2.8 %gather_fusion = f32[1024,4]{1,0:T(8,128)S(1)} fusion(f32[4,512]{0,1:T(8,128)S(1)} %copy.85, s32[1024]{0:T(1024)S(1)} %fusion.81), kind=kCustom, calls=%fused_computation | custom fusion | bytes 36864 | tf_op jit(solution)/shard_map/jit(_take)/gather | solution.py:58
  7.5 0.8 select_bitcast_fusion.1
  8.3 0.7 add_convert_fusion
  9.0 0.6 pad_maximum_fusion
  9.6 7.3 %all-to-all-start = ((f32[7,8,128]{2,0,1:T(8,128)}), f32[7,8,128]{2,0,1:T(8,128)S(1)}, u32[]{:S(2)}, u32[]{:S(2)}) async-start(f32[7,8,128]{2,0,1:T(8,128)} %pad_maximum_fusion), calls=%async_computation | async-start | bytes 65536 | tf_op jit(solution)/shard_map/all_to_all | solution.py:65
  16.9 1.3 iota_compare_fusion.1
  18.2 5.4 %all-to-all-done = f32[7,8,128]{2,0,1:T(8,128)S(1)} async-done(((f32[7,8,128]{2,0,1:T(8,128)}), f32[7,8,128]{2,0,1:T(8,128)S(1)}, u32[]{:S(2)}, u32[]{:S(2)}) %all-to-all-start) | async-done | bytes 28704 | tf_op jit(solution)/shard_map/all_to_all | solution.py:65
  23.6 4.0 %and_reduce_fusion = pred[3,1024]{1,0:T(4,128)(4,1)S(1)} fusion(s32[3,1024]{1,0:T(4,128)S(1)} %bitcast.145, pred[1024,1024]{1,0:T(8,128)(4,1)} %iota_compare_fusion.1), kind=kLoop, calls=%fused_computation.3 | loop fusion | flops 9434112 | bytes 1063936 | tf_op jit(solution)/shard_map/reduce_or | solution.py:24
  27.6 10.0 %fusion = pred[3,1024,4096]{1,2,0:T(32,128)(4,1)S(1)} fusion(s32[3,1024]{1,0:T(4,128)S(1)} %bitcast.146, pred[3,1024]{1,0:T(4,128)(4,1)S(1)} %not.7), kind=kLoop, calls=%fused_computation.2 | loop fusion | flops 25165824 | bytes 12598272 | tf_op jit(solution)/shard_map/and | solution.py:29
  37.6 10.1 %fusion.89 = (pred[1,1024,4096]{1,2,0:T(32,128)(4,1)}, pred[1,1024,4096]{1,2,0:T(32,128)(4,1)}, pred[1,1024,4096]{1,2,0:T(32,128)(4,1)S(1)}) fusion(pred[3,1024,4096]{1,2,0:T(32,128)(4,1)S(1)} %fusion), kind=kLoop, calls=%fused_computation.91 | loop fusion | bytes 25165824 | tf_op jit(solution)/shard_map/slice | solution.py:117
  47.8 1.3 fusion.3
  49.1 3.2 %fusion.41 = bf16[4,80,1024]{2,1,0:T(8,128)(2,1)S(1)} fusion(pred[1024,16,256,1]{0,2,1,3:T(32,128)(4,1)S(1)} %bitcast.138, bf16[4,80,16,256]{3,2,1,0:T(8,128)(2,1)S(1)} %copy-done, f32[4,1024]{1,0:T(4,128)S(1)} %fusion.3), kind=kOutput, calls=%fused_computation.33 | convolution fusion | flops 2685009920 | bytes 7487488 | tf_op jit(solution)/shard_map/lmxy,sxy->lms/dot_general | solution.py:77
  52.4 1.4 copy.91
  53.7 3.5 %all-to-all-start.1 = ((bf16[4,80,1024]{2,0,1:T(4,128)(2,1)}), bf16[4,80,1024]{2,0,1:T(4,128)(2,1)S(1)}, u32[]{:S(2)}, u32[]{:S(2)}) async-start(bf16[4,80,1024]{2,0,1:T(4,128)(2,1)} %copy.91), calls=%async_computation.1 | async-start | bytes 1310720 | tf_op jit(solution)/shard_map/all_to_all | solution.py:87
  57.2 10.2 %all-to-all-done.1 = bf16[4,80,1024]{2,0,1:T(4,128)(2,1)S(1)} async-done(((bf16[4,80,1024]{2,0,1:T(4,128)(2,1)}), bf16[4,80,1024]{2,0,1:T(4,128)(2,1)S(1)}, u32[]{:S(2)}, u32[]{:S(2)}) %all-to-all-start.1) | async-done | bytes 655392 | tf_op jit(solution)/shard_map/all_to_all | solution.py:87
  67.9 0.4 fusion.44
  68.3 1.3 copy.94
  69.6 3.7 %all-to-all-start.2 = ((bf16[16,20,1024]{2,1,0:T(8,128)(2,1)}), bf16[16,20,1024]{2,1,0:T(8,128)(2,1)S(1)}, u32[]{:S(2)}, u32[]{:S(2)}) async-start(bf16[16,20,1024]{2,1,0:T(8,128)(2,1)} %copy.94), calls=%async_computation.2 | async-start | bytes 1572864 | tf_op jit(solution)/shard_map/all_to_all | solution.py:91
  73.4 11.3 %all-to-all-done.2 = bf16[16,20,1024]{2,1,0:T(8,128)(2,1)S(1)} async-done(((bf16[16,20,1024]{2,1,0:T(8,128)(2,1)}), bf16[16,20,1024]{2,1,0:T(8,128)(2,1)S(1)}, u32[]{:S(2)}, u32[]{:S(2)}) %all-to-all-start.2) | async-done | bytes 655392 | tf_op jit(solution)/shard_map/all_to_all | solution.py:91
  84.7 0.5 copy.95
  85.4 2.4 %collective-permute-start = (bf16[4,80,1024]{2,1,0:T(8,128)(2,1)S(1)}, bf16[4,80,1024]{2,1,0:T(8,128)(2,1)S(1)}, u32[]{:S(2)}, u32[]{:S(2)}) collective-permute-start(bf16[4,80,1024]{2,1,0:T(8,128)(2,1)S(1)} %copy.99), channel_id=1, source_target_pairs={{0,4},{4,8},{8,12},{12,16},{16,20},{20,24},{24,28},{1,5},{5,9},{9,... | collective-permute-start | bytes 1966088 | tf_op jit(solution)/shard_map/ppermute | solution.py:95
  87.9 1.3 collective-permute-start.1
  89.2 9.4 %convolution_convert_fusion.2 = bf16[4,80,16,256]{3,1,2,0:T(8,128)(2,1)} fusion(pred[1024,16,256,1]{0,2,1,3:T(32,128)(4,1)} %bitcast.139, bf16[4,80,1024,1]{2,0,1,3:T(4,128)(2,1)S(1)} %bitcast.142), kind=kOutput, calls=%fused_computation.30 | convolution fusion | flops 2685665280 | bytes 7471104 | tf_op jit(solution)/shard_map/kms,sxy->kmxy/dot_general | solution.py:106
  98.6 17.0 %collective-permute-done = bf16[4,80,1024]{2,1,0:T(8,128)(2,1)S(1)} collective-permute-done((bf16[4,80,1024]{2,1,0:T(8,128)(2,1)S(1)}, bf16[4,80,1024]{2,1,0:T(8,128)(2,1)S(1)}, u32[]{:S(2)}, u32[]{:S(2)}) %collective-permute-start) | collective-permute-done | bytes 655392 | tf_op jit(solution)/shard_map/ppermute | solution.py:95
  115.6 4.2 %convolution_convert_fusion.1 = bf16[4,80,16,256]{3,1,2,0:T(8,128)(2,1)} fusion(pred[1024,16,256,1]{0,2,1,3:T(32,128)(4,1)S(1)} %bitcast.137, bf16[4,80,1024]{2,1,0:T(8,128)(2,1)S(1)} %collective-permute-done), kind=kOutput, calls=%fused_computation.29 | convolution fusion | flops 2685665280 | bytes 7471104 | tf_op jit(solution)/shard_map/kms,sxy->kmxy/dot_general | solution.py:106
  119.8 5.9 %fusion.15 = f32[4,16,80,256]{3,1,2,0:T(8,128)} fusion(bf16[4,80,16,256]{3,1,2,0:T(8,128)(2,1)} %convolution_convert_fusion.1, f32[4]{0:T(128)S(1)} %broadcast_add_fusion, f32[256,256]{1,0:T(8,128)S(1)} %abs_convert_fusion, f32[4]{0:T(128)S(1)} %convert_element_type.66, bf16[4,3,16,16]{2,3,0,1:T(8,128)(2,1)S(1)} %select_convert_fusion.1), kind=kOutput, calls=%fused_computation.22 | convolution fusion | flops 715653120 | bytes 8143872 | tf_op jit(solution)/shard_map/kmey,kex->kmxy/dot_general | solution.py:112
  125.7 9.1 %convolution_convert_fusion = bf16[4,80,16,256]{3,1,2,0:T(8,128)(2,1)} fusion(pred[1024,16,256,1]{0,2,1,3:T(32,128)(4,1)} %bitcast.136, bf16[4,80,1024]{2,1,0:T(8,128)(2,1)S(1)} %collective-permute-done.1), kind=kOutput, calls=%fused_computation.28 | convolution fusion | flops 2685665280 | bytes 7471104 | tf_op jit(solution)/shard_map/kms,sxy->kmxy/dot_general | solution.py:106
  134.8 5.9 %fusion.13 = f32[4,16,80,256]{3,1,2,0:T(8,128)} fusion(bf16[4,80,16,256]{3,1,2,0:T(8,128)(2,1)} %convolution_convert_fusion, f32[4]{0:T(128)S(1)} %broadcast_add_fusion, f32[256,256]{1,0:T(8,128)S(1)} %abs_convert_fusion, f32[4]{0:T(128)S(1)} %convert_element_type.66, bf16[4,3,16,16]{2,3,0,1:T(8,128)(2,1)S(1)} %select_convert_fusion.1), kind=kOutput, calls=%fused_computation.20 | convolution fusion | flops 715653120 | bytes 8143872 | tf_op jit(solution)/shard_map/kmey,kex->kmxy/dot_general | solution.py:112
  140.8 10.8 %bitcast_add_fusion = f32[4,80,16,256]{3,2,1,0:T(8,128)} fusion(f32[4,16,80,256]{3,1,2,0:T(8,128)} %fusion.13, f32[4,16,80,256]{3,1,2,0:T(8,128)} %fusion.15, f32[4,80,16,256]{3,2,1,0:T(8,128)} %param.17, bf16[4,80,16,256]{3,1,2,0:T(8,128)(2,1)} %convolution_convert_fusion.2, f32[4]{0:T(128)S(1)} %broadcast_add_fusion, f32[256,256]{1,0:T(8,128)S(1)} %abs_convert_fusion, ...), kind=kOutput, calls=%fused_computation.4 | convolution fusion | flops 719585280 | bytes 23872512 | tf_op jit(solution)/shard_map/kmey,kex->kmxy/dot_general | solution.py:112
  151.6 12.6 %fusion.48 = f32[80,80]{0,1:T(8,128)S(1)} fusion(f32[4,80,16,256]{3,2,1,0:T(8,128)} %bitcast_add_fusion), kind=kOutput, calls=%fused_computation.37 | convolution fusion | flops 629152000 | bytes 5268480 | tf_op jit(solution)/shard_map/kmxy,knxy->mn/dot_general | solution.py:121
  164.3 1.2 collective-permute-done.2
  165.5 0.5 collective-permute-start.3
  166.1 3.5 %collective-permute-done.3 = f32[80,80]{0,1:T(8,128)S(1)} collective-permute-done((f32[80,80]{0,1:T(8,128)S(1)}, f32[80,80]{0,1:T(8,128)S(1)}, u32[]{:S(2)}, u32[]{:S(2)}) %collective-permute-start.3) | collective-permute-done | bytes 25632 | tf_op jit(solution)/shard_map/ppermute | solution.py:39
  169.6 2.5 %collective-permute-start.4 = (f32[80,80]{0,1:T(8,128)S(1)}, f32[80,80]{0,1:T(8,128)S(1)}, u32[]{:S(2)}, u32[]{:S(2)}) collective-permute-start(f32[80,80]{0,1:T(8,128)S(1)} %add.78), channel_id=1, source_target_pairs={{0,4},{4,0},{8,12},{12,8},{16,20},{20,16},{24,28},{28,24},{1,5},{5... | collective-permute-start | bytes 76808 | tf_op jit(solution)/shard_map/ppermute | solution.py:39
  172.0 2.0 %collective-permute-done.4 = f32[80,80]{0,1:T(8,128)S(1)} collective-permute-done((f32[80,80]{0,1:T(8,128)S(1)}, f32[80,80]{0,1:T(8,128)S(1)}, u32[]{:S(2)}, u32[]{:S(2)}) %collective-permute-start.4) | collective-permute-done | bytes 25632 | tf_op jit(solution)/shard_map/ppermute | solution.py:39
  174.0 0.7 collective-permute-start.5
  174.7 3.3 %collective-permute-done.5 = f32[80,80]{0,1:T(8,128)S(1)} collective-permute-done((f32[80,80]{0,1:T(8,128)S(1)}, f32[80,80]{0,1:T(8,128)S(1)}, u32[]{:S(2)}, u32[]{:S(2)}) %collective-permute-start.5) | collective-permute-done | bytes 25632 | tf_op jit(solution)/shard_map/ppermute | solution.py:39
  178.0 0.5 collective-permute-start.6
  178.6 4.4 %collective-permute-done.6 = f32[80,80]{0,1:T(8,128)S(1)} collective-permute-done((f32[80,80]{0,1:T(8,128)S(1)}, f32[80,80]{0,1:T(8,128)S(1)}, u32[]{:S(2)}, u32[]{:S(2)}) %collective-permute-start.6) | collective-permute-done | bytes 25632 | tf_op jit(solution)/shard_map/ppermute | solution.py:39
  183.1 7.3 %cholesky.18 = f32[80,80]{1,0:T(8,128)S(1)} custom-call(f32[80,80]{1,0:T(8,128)S(1)} %fusion.79), custom_call_target="Cholesky" | custom-call | tf_op jit(solution)/shard_map/jit(cholesky)/cholesky | solution.py:124
  190.4 0.6 compare_reduce_fusion
  191.0 0.7 select_bitcast_fusion
  191.7 0.7 copy.109
  (40 shorter events, 1.3 us)
Async XLA Ops:
  0.6 48.5 %copy-start = (bf16[4,80,16,256]{3,2,1,0:T(8,128)(2,1)S(1)}, bf16[4,80,16,256]{3,2,1,0:T(8,128)(2,1)}, u32[]{:S(2)}) copy-start(bf16[4,80,16,256]{3,2,1,0:T(8,128)(2,1)} %param.14) | copy-start | bytes 7864324
  9.6 13.9 %all-to-all-start = ((f32[7,8,128]{2,0,1:T(8,128)}), f32[7,8,128]{2,0,1:T(8,128)S(1)}, u32[]{:S(2)}, u32[]{:S(2)}) async-start(f32[7,8,128]{2,0,1:T(8,128)} %pad_maximum_fusion), calls=%async_computation | async-start | bytes 65536 | tf_op jit(solution)/shard_map/all_to_all | solution.py:65
  47.8 4.6 %copy-start.3 = (pred[1,1024,4096]{1,2,0:T(32,128)(4,1)}, pred[1,1024,4096]{1,2,0:T(32,128)(4,1)S(1)}, u32[]{:S(2)}) copy-start(pred[1,1024,4096]{1,2,0:T(32,128)(4,1)S(1)} %get-tuple-element.14) | copy-start | bytes 12582916
  49.1 8.1 %copy-start.5 = (s32[4]{0:T(128)S(1)}, s32[4]{0:T(128)}, u32[]{:S(2)}) copy-start(s32[4]{0:T(128)} %param.16) | copy-start | bytes 52
  52.3 15.6 %copy-start.4 = (bf16[16,16]{1,0:T(8,128)(2,1)S(1)}, bf16[16,16]{1,0:T(8,128)(2,1)}, u32[]{:S(2)}) copy-start(bf16[16,16]{1,0:T(8,128)(2,1)} %param.15) | copy-start | bytes 1540
  53.7 13.7 %all-to-all-start.1 = ((bf16[4,80,1024]{2,0,1:T(4,128)(2,1)}), bf16[4,80,1024]{2,0,1:T(4,128)(2,1)S(1)}, u32[]{:S(2)}, u32[]{:S(2)}) async-start(bf16[4,80,1024]{2,0,1:T(4,128)(2,1)} %copy.91), calls=%async_computation.1 | async-start | bytes 1310720 | tf_op jit(solution)/shard_map/all_to_all | solution.py:87
  69.6 15.1 %all-to-all-start.2 = ((bf16[16,20,1024]{2,1,0:T(8,128)(2,1)}), bf16[16,20,1024]{2,1,0:T(8,128)(2,1)S(1)}, u32[]{:S(2)}, u32[]{:S(2)}) async-start(bf16[16,20,1024]{2,1,0:T(8,128)(2,1)} %copy.94), calls=%async_computation.2 | async-start | bytes 1572864 | tf_op jit(solution)/shard_map/all_to_all | solution.py:91
  85.4 30.2 %collective-permute-start = (bf16[4,80,1024]{2,1,0:T(8,128)(2,1)S(1)}, bf16[4,80,1024]{2,1,0:T(8,128)(2,1)S(1)}, u32[]{:S(2)}, u32[]{:S(2)}) collective-permute-start(bf16[4,80,1024]{2,1,0:T(8,128)(2,1)S(1)} %copy.99), channel_id=1, source_target_pairs={{0,4},{4,8},{8,12},{12,16},{16,20},{20,24},{24,28},{1,5},{5,9},{9,... | collective-permute-start | bytes 1966088 | tf_op jit(solution)/shard_map/ppermute | solution.py:95
  87.9 37.8 %collective-permute-start.1 = (bf16[4,80,1024]{2,1,0:T(8,128)(2,1)S(1)}, bf16[4,80,1024]{2,1,0:T(8,128)(2,1)S(1)}, u32[]{:S(2)}, u32[]{:S(2)}) collective-permute-start(bf16[4,80,1024]{2,1,0:T(8,128)(2,1)S(1)} %copy.99), channel_id=1, source_target_pairs={{4,0},{8,4},{12,8},{16,12},{20,16},{24,20},{28,24},{5,1},{9,5},{13... | collective-permute-start | bytes 1966088 | tf_op jit(solution)/shard_map/ppermute | solution.py:96
  89.2 26.4 %copy-start.2 = (pred[1,1024,4096]{1,2,0:T(32,128)(4,1)S(1)}, pred[1,1024,4096]{1,2,0:T(32,128)(4,1)}, u32[]{:S(2)}) copy-start(pred[1,1024,4096]{1,2,0:T(32,128)(4,1)} %get-tuple-element.12) | copy-start | bytes 12582916
  140.8 51.6 %copy-start.1 = (bf16[4,80,16,256]{3,2,1,0:T(8,128)(2,1)S(1)}, bf16[4,80,16,256]{3,2,1,0:T(8,128)(2,1)}, u32[]{:S(2)}) copy-start(bf16[4,80,16,256]{3,2,1,0:T(8,128)(2,1)} %param.14) | copy-start | bytes 7864324
  164.3 1.3 collective-permute-start.2
  165.5 4.0 %collective-permute-start.3 = (f32[80,80]{0,1:T(8,128)S(1)}, f32[80,80]{0,1:T(8,128)S(1)}, u32[]{:S(2)}, u32[]{:S(2)}) collective-permute-start(f32[80,80]{0,1:T(8,128)S(1)} %add.77), channel_id=1, source_target_pairs={{0,2},{1,3},{2,0},{3,1},{4,6},{5,7},{6,4},{7,5},{8,10},{9,11},{10,... | collective-permute-start | bytes 76808 | tf_op jit(solution)/shard_map/ppermute | solution.py:39
  169.6 4.5 %collective-permute-start.4 = (f32[80,80]{0,1:T(8,128)S(1)}, f32[80,80]{0,1:T(8,128)S(1)}, u32[]{:S(2)}, u32[]{:S(2)}) collective-permute-start(f32[80,80]{0,1:T(8,128)S(1)} %add.78), channel_id=1, source_target_pairs={{0,4},{4,0},{8,12},{12,8},{16,20},{20,16},{24,28},{28,24},{1,5},{5... | collective-permute-start | bytes 76808 | tf_op jit(solution)/shard_map/ppermute | solution.py:39
  174.0 4.0 %collective-permute-start.5 = (f32[80,80]{0,1:T(8,128)S(1)}, f32[80,80]{0,1:T(8,128)S(1)}, u32[]{:S(2)}, u32[]{:S(2)}) collective-permute-start(f32[80,80]{0,1:T(8,128)S(1)} %add.79), channel_id=1, source_target_pairs={{0,8},{4,12},{8,0},{12,4},{16,24},{20,28},{24,16},{28,20},{1,9},{5... | collective-permute-start | bytes 76808 | tf_op jit(solution)/shard_map/ppermute | solution.py:39
  178.0 4.9 %collective-permute-start.6 = (f32[80,80]{0,1:T(8,128)S(1)}, f32[80,80]{0,1:T(8,128)S(1)}, u32[]{:S(2)}, u32[]{:S(2)}) collective-permute-start(f32[80,80]{0,1:T(8,128)S(1)} %add.80), channel_id=1, source_target_pairs={{0,16},{4,20},{8,24},{12,28},{16,0},{20,4},{24,8},{28,12},{1,17},{... | collective-permute-start | bytes 76808 | tf_op jit(solution)/shard_map/ppermute | solution.py:39

commit v5 on v3

--- a/solution.py
+++ b/solution.py
@@ -31,13 +31,28 @@
 
 
 def all_sum(value, axes):
-    if any(size & (size - 1) for _, size in axes):
-        return lax.psum(value, tuple(name for name, _ in axes))
     for name, size in axes:
-        bit = 1
-        while bit < size:
-            value = value + lax.ppermute(value, name, [(i, i ^ bit) for i in range(size)])
-            bit *= 2
+        if size == 1:
+            continue
+        if size > 8:
+            bit = 1
+            while bit < size and not size & (size - 1):
+                value = value + lax.ppermute(value, name, [(i, i ^ bit) for i in range(size)])
+                bit *= 2
+            if size & (size - 1):
+                value = lax.psum(value, name)
+            continue
+        got = [value] + [
+            lax.ppermute(value, name, [(i, (i + shift) % size) for i in range(size)])
+            for shift in range(1, size)
+        ]
+        here = lax.axis_index(name)
+        order = (here - jnp.arange(size, dtype=jnp.int32)) % size
+        parts = list(jnp.take(jnp.stack(got), order, axis=0))
+        while len(parts) > 1:
+            paired = [parts[i] + parts[i + 1] for i in range(0, len(parts) - 1, 2)]
+            parts = paired + parts[len(parts) - len(parts) % 2:]
+        value = parts[0]
     return value
 
 

time: 169 us -> 173 us (1.024)
  blocking collectives: 12.8 us -> 0 us
  starting transfers between devices: 22.2 us -> 33.5 us
  local copies, waits for them, and re-layouts: 10.2 us -> 13.7 us
  waiting for transfers between devices: 55 us -> 57.3 us
    ppermute x1, waiting for transfers between devices: 12.9 us -> 26.2 us  [shards(): lax.ppermute(level_mix, 'tile', [(i, i + 1) for i in range(ends)])]
    all_to_all x1 -> x0, blocking collectives: 12.8 us -> none  [shards(): lax.all_to_all(member_forcing, 'lev', split_axis=1, concat_axis=0, tiled=...]
    ppermute x1, waiting for transfers between devices: 12 us -> 0.01 us  [shards(): lax.ppermute(level_mix, 'tile', [(i + 1, i) for i in range(ends)])]
    all_to_all x0 -> x1, waiting for transfers between devices: none -> 10.2 us  [shards(): lax.all_to_all(member_forcing, 'lev', split_axis=1, concat_axis=0, tiled=...]
    ppermute x5 -> x10, starting transfers between devices: 5.42 us -> 15.4 us  [all_sum(): lax.ppermute(value, name, [(i, (i + shift) % size) for i in range(size)])]
    ppermute x5 -> x10, waiting for transfers between devices: 13.2 us -> 4 us  [all_sum(): lax.ppermute(value, name, [(i, (i + shift) % size) for i in range(size)])]
    all_to_all x0 -> x1, starting transfers between devices: none -> 3.61 us  [shards(): lax.all_to_all(member_forcing, 'lev', split_axis=1, concat_axis=0, tiled=...]
    ppermute x1, starting transfers between devices: 4.59 us -> 2.42 us  [shards(): lax.ppermute(level_mix, 'tile', [(i, i + 1) for i in range(ends)])]
  transfers between devices with their start and end apart: 9 -> 15, of which waited for: 9 -> 9; matrix products, arithmetic and copies ran while one was open for 1% -> 1% of each run, Pallas kernels for 0% -> 0%
where the time goes in v5:
time: 173 us; the launch traced here: 172 us
  waiting for transfers between devices  57.3 us (33%)
  matrix products  45.4 us (26%)
  starting transfers between devices  33.5 us (19%)
  other arithmetic  21.3 us (12%)
  local copies, waits for them, and re-layouts  13.7 us (8%)
    ppermute x1, waiting for transfers between devices, shards(): lax.ppermute(level_mix, 'tile', [(i, i + 1) for i in range(ends)])  26.2 us
    dot_general x1, matrix products, shards(): jnp.einsum('tkms,tsxy->tkmxy', three, hits, preferred_element_type=jnp.fl...  15.9 us
    ppermute x10, starting transfers between devices, all_sum(): lax.ppermute(value, name, [(i, (i + shift) % size) for i in range(size)])  15.4 us
    dot_general x1, matrix products, shards(): jnp.einsum('kmxy,knxy->mn', gradient, gradient, precision=lax.Precision.H...  13.9 us
    all_to_all x1, waiting for transfers between devices, shards(): lax.all_to_all(local_mix.astype(jnp.bfloat16), 'lev', split_axis=0, conca...  11.5 us
    dot_general x1, matrix products, shards(): jnp.einsum('tkmey,ktex->kmxy', smooth_wide, taps_cols, preferred_element_...  10.6 us
    all_to_all x1, waiting for transfers between devices, shards(): lax.all_to_all(member_forcing, 'lev', split_axis=1, concat_axis=0, tiled=...  10.2 us
    another operation x3, other arithmetic, shards(): r_factor = jnp.linalg.cholesky(gram_total).T  7.98 us
  transfers between devices with their start and end apart: 15, of which 9 were waited for; matrix products, arithmetic and copies ran while one was open for 1% of the time, Pallas kernels for 0%

profile of v5, /device:TPU:0, one launch (start us, length us, event | category | flops | bytes accessed | tf_op | source)
XLA Modules:
  0.0 172.3 jit_solution(12247579578438746978)
XLA Ops:
  0.6 0.9 slice_bitcast_fusion.4
  1.5 0.8 slice_bitcast_fusion.6
  2.3 0.7 fusion.75
  3.0 0.7 compare_and_fusion
  3.7 0.8 copy.57
  4.5 2.8 %gather_fusion = f32[1024,4]{1,0:T(8,128)S(1)} fusion(f32[4,512]{0,1:T(8,128)S(1)} %copy.57, s32[1024]{0:T(1024)S(1)} %fusion.75), kind=kCustom, calls=%fused_computation | custom fusion | bytes 36864 | tf_op jit(solution)/shard_map/jit(_take)/gather | solution.py:73
  7.5 0.8 select_bitcast_fusion.1
  8.3 0.7 add_convert_fusion
  9.0 0.6 pad_maximum_fusion.1
  9.6 7.3 %all-to-all-start = ((f32[7,8,128]{2,0,1:T(8,128)}), f32[7,8,128]{2,0,1:T(8,128)S(1)}, u32[]{:S(2)}, u32[]{:S(2)}) async-start(f32[7,8,128]{2,0,1:T(8,128)} %pad_maximum_fusion.1), calls=%async_computation | async-start | bytes 65536 | tf_op jit(solution)/shard_map/all_to_all | solution.py:80
  16.9 1.3 iota_compare_fusion.1
  18.2 5.4 %all-to-all-done = f32[7,8,128]{2,0,1:T(8,128)S(1)} async-done(((f32[7,8,128]{2,0,1:T(8,128)}), f32[7,8,128]{2,0,1:T(8,128)S(1)}, u32[]{:S(2)}, u32[]{:S(2)}) %all-to-all-start) | async-done | bytes 28704 | tf_op jit(solution)/shard_map/all_to_all | solution.py:80
  23.6 4.0 %and_reduce_fusion = pred[3,1024]{1,0:T(4,128)(4,1)S(1)} fusion(s32[3,1024]{1,0:T(4,128)S(1)} %bitcast.148, pred[1024,1024]{1,0:T(8,128)(4,1)} %iota_compare_fusion.1), kind=kLoop, calls=%fused_computation.12 | loop fusion | flops 9434112 | bytes 1063936 | tf_op jit(solution)/shard_map/reduce_or | solution.py:24
  27.7 3.5 %fusion.7 = pred[1,1024,4096]{1,2,0:T(32,128)(4,1)S(1)} fusion(s32[1,1024]{1,0:T(1,128)S(1)} %slice.63, pred[1,1024]{1,0:T(4,128)(4,1)S(1)} %slice.64), kind=kLoop, calls=%fused_computation.11 | loop fusion | flops 8388608 | bytes 4199424 | tf_op jit(solution)/shard_map/and | solution.py:29
  31.2 1.3 fusion.22
  32.5 3.2 %fusion.42 = bf16[4,80,1024]{2,1,0:T(8,128)(2,1)S(1)} fusion(pred[1024,16,256,1]{0,2,1,3:T(32,128)(4,1)S(1)} %bitcast.143, bf16[4,80,16,256]{3,2,1,0:T(8,128)(2,1)S(1)} %copy-done, f32[4,1024]{1,0:T(4,128)S(1)} %fusion.22), kind=kOutput, calls=%fused_computation.36 | convolution fusion | flops 2685009920 | bytes 7487488 | tf_op jit(solution)/shard_map/lmxy,sxy->lms/dot_general | solution.py:92
  35.8 1.3 copy.63
  37.1 3.6 %all-to-all-start.1 = ((bf16[4,80,1024]{2,0,1:T(4,128)(2,1)}), bf16[4,80,1024]{2,0,1:T(4,128)(2,1)S(1)}, u32[]{:S(2)}, u32[]{:S(2)}) async-start(bf16[4,80,1024]{2,0,1:T(4,128)(2,1)} %copy.63), calls=%async_computation.1 | async-start | bytes 1310720 | tf_op jit(solution)/shard_map/all_to_all | solution.py:102
  40.7 10.2 %all-to-all-done.1 = bf16[4,80,1024]{2,0,1:T(4,128)(2,1)S(1)} async-done(((bf16[4,80,1024]{2,0,1:T(4,128)(2,1)}), bf16[4,80,1024]{2,0,1:T(4,128)(2,1)S(1)}, u32[]{:S(2)}, u32[]{:S(2)}) %all-to-all-start.1) | async-done | bytes 655392 | tf_op jit(solution)/shard_map/all_to_all | solution.py:102
  51.0 1.2 copy.64
  52.1 1.5 all_to_all.33
  54.0 1.3 copy.66
  55.3 3.5 %all-to-all-start.2 = ((bf16[16,20,1024]{2,1,0:T(8,128)(2,1)}), bf16[16,20,1024]{2,1,0:T(8,128)(2,1)S(1)}, u32[]{:S(2)}, u32[]{:S(2)}) async-start(bf16[16,20,1024]{2,1,0:T(8,128)(2,1)} %copy.66), calls=%async_computation.2 | async-start | bytes 1572864 | tf_op jit(solution)/shard_map/all_to_all | solution.py:106
  58.9 11.5 %all-to-all-done.2 = bf16[16,20,1024]{2,1,0:T(8,128)(2,1)S(1)} async-done(((bf16[16,20,1024]{2,1,0:T(8,128)(2,1)}), bf16[16,20,1024]{2,1,0:T(8,128)(2,1)S(1)}, u32[]{:S(2)}, u32[]{:S(2)}) %all-to-all-start.2) | async-done | bytes 655392 | tf_op jit(solution)/shard_map/all_to_all | solution.py:106
  71.1 2.4 %collective-permute-start = (bf16[4,80,1024]{2,1,0:T(8,128)(2,1)S(1)}, bf16[4,80,1024]{2,1,0:T(8,128)(2,1)S(1)}, u32[]{:S(2)}, u32[]{:S(2)}) collective-permute-start(bf16[4,80,1024]{2,1,0:T(8,128)(2,1)S(1)} %copy.68), channel_id=1, source_target_pairs={{0,4},{4,8},{8,12},{12,16},{16,20},{20,24},{24,28},{1,5},{5,9},{9,... | collective-permute-start | bytes 1966088 | tf_op jit(solution)/shard_map/ppermute | solution.py:110
  73.5 1.3 collective-permute-start.1
  75.1 26.2 %collective-permute-done = bf16[4,80,1024]{2,1,0:T(8,128)(2,1)S(1)} collective-permute-done((bf16[4,80,1024]{2,1,0:T(8,128)(2,1)S(1)}, bf16[4,80,1024]{2,1,0:T(8,128)(2,1)S(1)}, u32[]{:S(2)}, u32[]{:S(2)}) %collective-permute-start) | collective-permute-done | bytes 655392 | tf_op jit(solution)/shard_map/ppermute | solution.py:110
  101.3 15.9 %fusion.17 = bf16[3,4,80,16,256]{4,2,3,1,0:T(8,128)(2,1)} fusion(s32[16,256]{1,0:T(8,128)S(1)} %multiply_add_fusion, s32[3,1024]{1,0:T(4,128)S(1)} %bitcast.149, pred[3,1024]{1,0:T(4,128)(4,1)S(1)} %not.7, bf16[1,4,80,1024]{3,2,1,0:T(8,128)(2,1)S(1)} %bitcast.166, bf16[1,4,80,1024]{3,2,1,0:T(8,128)(2,1)S(1)} %copy.70, bf16[1,4,80,1024]{3,2,1,0:T(8,128)(2,1)S(1)} %bitcast.165), kind=kOutput, calls=%fused_computation.18 | convolution fusion | flops 8088059904 | bytes 9862144 | tf_op jit(solution)/shard_map/tkms,tsxy->tkmxy/dot_general | solution.py:114
  117.2 10.6 %bitcast_add_fusion = f32[4,80,16,256]{3,2,1,0:T(8,128)} fusion(f32[4,80,16,256]{3,2,1,0:T(8,128)} %param.17, bf16[3,4,80,16,256]{4,2,3,1,0:T(8,128)(2,1)} %fusion.17, f32[4]{0:T(128)S(1)} %broadcast_add_fusion, f32[256,256]{1,0:T(8,128)S(1)} %abs_convert_fusion, f32[4]{0:T(128)S(1)} %convert_element_type.57, f32[3,16,16]{1,2,0:T(8,128)S(1)} %abs_convert_fusion.1), kind=kOutput, calls=%fused_computation.19 | convolution fusion | flops 2145664000 | bytes 18615328 | tf_op jit(solution)/shard_map/tkmey,ktex->kmxy/dot_general | solution.py:127
  127.8 13.9 %fusion.49 = f32[80,80]{1,0:T(8,128)S(1)} fusion(f32[4,80,16,256]{3,2,1,0:T(8,128)} %bitcast_add_fusion), kind=kOutput, calls=%fused_computation.40 | convolution fusion | flops 1258297600 | bytes 5268480 | tf_op jit(solution)/shard_map/kmxy,knxy->mn/dot_general | solution.py:133
  141.9 0.7 collective-permute-start.3
  142.6 1.4 collective-permute-start.4
  144.0 1.3 collective-permute-done.2
  145.3 0.9 collective-permute-done.3
  146.2 0.6 gather_fusion.1
  146.9 2.5 %collective-permute-start.5 = (f32[80,80]{1,0:T(8,128)S(1)}, f32[80,80]{1,0:T(8,128)S(1)}, u32[]{:S(2)}, u32[]{:S(2)}) collective-permute-start(f32[80,80]{1,0:T(8,128)S(1)} %bitcast.155), channel_id=1, source_target_pairs={{0,4},{4,8},{8,12},{12,16},{16,20},{20,24},{24,28},{28,0},{1,5},{5... | collective-permute-start | bytes 76808 | tf_op jit(solution)/shard_map/ppermute | solution.py:46
  149.4 0.9 collective-permute-start.6
  150.3 2.2 %collective-permute-start.7 = (f32[80,80]{1,0:T(8,128)S(1)}, f32[80,80]{1,0:T(8,128)S(1)}, u32[]{:S(2)}, u32[]{:S(2)}) collective-permute-start(f32[80,80]{1,0:T(8,128)S(1)} %bitcast.157), channel_id=1, source_target_pairs={{0,12},{4,16},{8,20},{12,24},{16,28},{20,0},{24,4},{28,8},{1,13},{... | collective-permute-start | bytes 76808 | tf_op jit(solution)/shard_map/ppermute | solution.py:46
  152.5 3.1 %collective-permute-start.8 = (f32[80,80]{1,0:T(8,128)S(1)}, f32[80,80]{1,0:T(8,128)S(1)}, u32[]{:S(2)}, u32[]{:S(2)}) collective-permute-start(f32[80,80]{1,0:T(8,128)S(1)} %bitcast.158), channel_id=1, source_target_pairs={{0,16},{4,20},{8,24},{12,28},{16,0},{20,4},{24,8},{28,12},{1,17},{... | collective-permute-start | bytes 76808 | tf_op jit(solution)/shard_map/ppermute | solution.py:46
  155.6 2.4 %collective-permute-start.10 = (f32[80,80]{1,0:T(8,128)S(1)}, f32[80,80]{1,0:T(8,128)S(1)}, u32[]{:S(2)}, u32[]{:S(2)}) collective-permute-start(f32[80,80]{1,0:T(8,128)S(1)} %bitcast.160), channel_id=1, source_target_pairs={{0,24},{4,28},{8,0},{12,4},{16,8},{20,12},{24,16},{28,20},{1,25},{... | collective-permute-start | bytes 76808 | tf_op jit(solution)/shard_map/ppermute | solution.py:46
  157.9 2.2 %collective-permute-start.11 = (f32[80,80]{1,0:T(8,128)S(1)}, f32[80,80]{1,0:T(8,128)S(1)}, u32[]{:S(2)}, u32[]{:S(2)}) collective-permute-start(f32[80,80]{1,0:T(8,128)S(1)} %bitcast.161), channel_id=1, source_target_pairs={{0,28},{4,0},{8,4},{12,8},{16,12},{20,16},{24,20},{28,24},{1,29},{... | collective-permute-start | bytes 76808 | tf_op jit(solution)/shard_map/ppermute | solution.py:46
  160.3 0.6 collective-permute-done.9
  160.9 1.1 collective-permute-done.11
  162.0 0.6 gather_fusion.2
  163.0 7.3 %cholesky.18 = f32[80,80]{1,0:T(8,128)S(1)} custom-call(f32[80,80]{1,0:T(8,128)S(1)} %fusion.73), custom_call_target="Cholesky" | custom-call | tf_op jit(solution)/shard_map/jit(cholesky)/cholesky | solution.py:136
  170.3 0.6 compare_reduce_fusion
  170.9 0.7 select_bitcast_fusion
  171.6 0.7 copy.76
  (58 shorter events, 2.5 us)
Async XLA Ops:
  0.6 31.9 %copy-start = (bf16[4,80,16,256]{3,2,1,0:T(8,128)(2,1)S(1)}, bf16[4,80,16,256]{3,2,1,0:T(8,128)(2,1)}, u32[]{:S(2)}) copy-start(bf16[4,80,16,256]{3,2,1,0:T(8,128)(2,1)} %param.14) | copy-start | bytes 7864324
  9.6 13.9 %all-to-all-start = ((f32[7,8,128]{2,0,1:T(8,128)}), f32[7,8,128]{2,0,1:T(8,128)S(1)}, u32[]{:S(2)}, u32[]{:S(2)}) async-start(f32[7,8,128]{2,0,1:T(8,128)} %pad_maximum_fusion.1), calls=%async_computation | async-start | bytes 65536 | tf_op jit(solution)/shard_map/all_to_all | solution.py:80
  35.8 17.9 %copy-start.1 = (bf16[16,16]{1,0:T(8,128)(2,1)S(1)}, bf16[16,16]{1,0:T(8,128)(2,1)}, u32[]{:S(2)}) copy-start(bf16[16,16]{1,0:T(8,128)(2,1)} %param.15) | copy-start | bytes 1540
  37.1 21.7 %copy-start.2 = (s32[4]{0:T(128)S(1)}, s32[4]{0:T(128)}, u32[]{:S(2)}) copy-start(s32[4]{0:T(128)} %param.16) | copy-start | bytes 52
  37.1 13.8 %all-to-all-start.1 = ((bf16[4,80,1024]{2,0,1:T(4,128)(2,1)}), bf16[4,80,1024]{2,0,1:T(4,128)(2,1)S(1)}, u32[]{:S(2)}, u32[]{:S(2)}) async-start(bf16[4,80,1024]{2,0,1:T(4,128)(2,1)} %copy.63), calls=%async_computation.1 | async-start | bytes 1310720 | tf_op jit(solution)/shard_map/all_to_all | solution.py:102
  55.3 15.1 %all-to-all-start.2 = ((bf16[16,20,1024]{2,1,0:T(8,128)(2,1)}), bf16[16,20,1024]{2,1,0:T(8,128)(2,1)S(1)}, u32[]{:S(2)}, u32[]{:S(2)}) async-start(bf16[16,20,1024]{2,1,0:T(8,128)(2,1)} %copy.66), calls=%async_computation.2 | async-start | bytes 1572864 | tf_op jit(solution)/shard_map/all_to_all | solution.py:106
  71.1 30.2 %collective-permute-start = (bf16[4,80,1024]{2,1,0:T(8,128)(2,1)S(1)}, bf16[4,80,1024]{2,1,0:T(8,128)(2,1)S(1)}, u32[]{:S(2)}, u32[]{:S(2)}) collective-permute-start(bf16[4,80,1024]{2,1,0:T(8,128)(2,1)S(1)} %copy.68), channel_id=1, source_target_pairs={{0,4},{4,8},{8,12},{12,16},{16,20},{20,24},{24,28},{1,5},{5,9},{9,... | collective-permute-start | bytes 1966088 | tf_op jit(solution)/shard_map/ppermute | solution.py:110
  73.5 27.8 %collective-permute-start.1 = (bf16[4,80,1024]{2,1,0:T(8,128)(2,1)S(1)}, bf16[4,80,1024]{2,1,0:T(8,128)(2,1)S(1)}, u32[]{:S(2)}, u32[]{:S(2)}) collective-permute-start(bf16[4,80,1024]{2,1,0:T(8,128)(2,1)S(1)} %copy.68), channel_id=1, source_target_pairs={{4,0},{8,4},{12,8},{16,12},{20,16},{24,20},{28,24},{5,1},{9,5},{13... | collective-permute-start | bytes 1966088 | tf_op jit(solution)/shard_map/ppermute | solution.py:111
  141.8 3.5 %collective-permute-start.2 = (f32[80,80]{1,0:T(8,128)S(1)}, f32[80,80]{1,0:T(8,128)S(1)}, u32[]{:S(2)}, u32[]{:S(2)}) collective-permute-start(f32[80,80]{1,0:T(8,128)S(1)} %fusion.49), channel_id=1, source_target_pairs={{0,1},{1,2},{2,3},{3,0},{4,5},{5,6},{6,7},{7,4},{8,9},{9,10},{10,1... | collective-permute-start | bytes 76808 | tf_op jit(solution)/shard_map/ppermute | solution.py:46
  141.9 4.3 %collective-permute-start.3 = (f32[80,80]{1,0:T(8,128)S(1)}, f32[80,80]{1,0:T(8,128)S(1)}, u32[]{:S(2)}, u32[]{:S(2)}) collective-permute-start(f32[80,80]{1,0:T(8,128)S(1)} %fusion.49), channel_id=1, source_target_pairs={{0,2},{1,3},{2,0},{3,1},{4,6},{5,7},{6,4},{7,5},{8,10},{9,11},{10,... | collective-permute-start | bytes 76808 | tf_op jit(solution)/shard_map/ppermute | solution.py:46
  142.6 3.6 %collective-permute-start.4 = (f32[80,80]{1,0:T(8,128)S(1)}, f32[80,80]{1,0:T(8,128)S(1)}, u32[]{:S(2)}, u32[]{:S(2)}) collective-permute-start(f32[80,80]{1,0:T(8,128)S(1)} %fusion.49), channel_id=1, source_target_pairs={{0,3},{1,0},{2,1},{3,2},{4,7},{5,4},{6,5},{7,6},{8,11},{9,8},{10,9... | collective-permute-start | bytes 76808 | tf_op jit(solution)/shard_map/ppermute | solution.py:46
  146.9 8.7 %collective-permute-start.5 = (f32[80,80]{1,0:T(8,128)S(1)}, f32[80,80]{1,0:T(8,128)S(1)}, u32[]{:S(2)}, u32[]{:S(2)}) collective-permute-start(f32[80,80]{1,0:T(8,128)S(1)} %bitcast.155), channel_id=1, source_target_pairs={{0,4},{4,8},{8,12},{12,16},{16,20},{20,24},{24,28},{28,0},{1,5},{5... | collective-permute-start | bytes 76808 | tf_op jit(solution)/shard_map/ppermute | solution.py:46
  149.4 8.5 %collective-permute-start.6 = (f32[80,80]{1,0:T(8,128)S(1)}, f32[80,80]{1,0:T(8,128)S(1)}, u32[]{:S(2)}, u32[]{:S(2)}) collective-permute-start(f32[80,80]{1,0:T(8,128)S(1)} %bitcast.156), channel_id=1, source_target_pairs={{0,8},{4,12},{8,16},{12,20},{16,24},{20,28},{24,0},{28,4},{1,9},{5... | collective-permute-start | bytes 76808 | tf_op jit(solution)/shard_map/ppermute | solution.py:46
  150.3 9.9 %collective-permute-start.7 = (f32[80,80]{1,0:T(8,128)S(1)}, f32[80,80]{1,0:T(8,128)S(1)}, u32[]{:S(2)}, u32[]{:S(2)}) collective-permute-start(f32[80,80]{1,0:T(8,128)S(1)} %bitcast.157), channel_id=1, source_target_pairs={{0,12},{4,16},{8,20},{12,24},{16,28},{20,0},{24,4},{28,8},{1,13},{... | collective-permute-start | bytes 76808 | tf_op jit(solution)/shard_map/ppermute | solution.py:46
  152.5 7.8 %collective-permute-start.8 = (f32[80,80]{1,0:T(8,128)S(1)}, f32[80,80]{1,0:T(8,128)S(1)}, u32[]{:S(2)}, u32[]{:S(2)}) collective-permute-start(f32[80,80]{1,0:T(8,128)S(1)} %bitcast.158), channel_id=1, source_target_pairs={{0,16},{4,20},{8,24},{12,28},{16,0},{20,4},{24,8},{28,12},{1,17},{... | collective-permute-start | bytes 76808 | tf_op jit(solution)/shard_map/ppermute | solution.py:46
  155.6 5.3 %collective-permute-start.9 = (f32[80,80]{1,0:T(8,128)S(1)}, f32[80,80]{1,0:T(8,128)S(1)}, u32[]{:S(2)}, u32[]{:S(2)}) collective-permute-start(f32[80,80]{1,0:T(8,128)S(1)} %bitcast.159), channel_id=1, source_target_pairs={{0,20},{4,24},{8,28},{12,0},{16,4},{20,8},{24,12},{28,16},{1,21},{... | collective-permute-start | bytes 76808 | tf_op jit(solution)/shard_map/ppermute | solution.py:46
  155.6 5.3 %collective-permute-start.10 = (f32[80,80]{1,0:T(8,128)S(1)}, f32[80,80]{1,0:T(8,128)S(1)}, u32[]{:S(2)}, u32[]{:S(2)}) collective-permute-start(f32[80,80]{1,0:T(8,128)S(1)} %bitcast.160), channel_id=1, source_target_pairs={{0,24},{4,28},{8,0},{12,4},{16,8},{20,12},{24,16},{28,20},{1,25},{... | collective-permute-start | bytes 76808 | tf_op jit(solution)/shard_map/ppermute | solution.py:46
  157.9 4.0 %collective-permute-start.11 = (f32[80,80]{1,0:T(8,128)S(1)}, f32[80,80]{1,0:T(8,128)S(1)}, u32[]{:S(2)}, u32[]{:S(2)}) collective-permute-start(f32[80,80]{1,0:T(8,128)S(1)} %bitcast.161), channel_id=1, source_target_pairs={{0,28},{4,0},{8,4},{12,8},{16,12},{20,16},{24,20},{28,24},{1,29},{... | collective-permute-start | bytes 76808 | tf_op jit(solution)/shard_map/ppermute | solution.py:46

commit v6 on v3

--- a/solution.py
+++ b/solution.py
@@ -72,10 +72,13 @@
             "ls,st->lt", arrived[:lev_dev].reshape(lev_dev, -1), same,
             precision=lax.Precision.HIGHEST,
         )
-        keep = first_hits(near)
-        hits = one_hot(near, keep, cell_count).reshape(3, slots, col_count, row_count)
+        own_keep = first_hits(cell_index)
+
+        def own_hits():
+            return one_hot(cell_index, own_keep, cell_count).reshape(slots, col_count, row_count)
+
         picked = jnp.einsum(
-            "lmxy,sxy->lms", ensemble, hits[1], preferred_element_type=jnp.float32
+            "lmxy,sxy->lms", ensemble, own_hits(), preferred_element_type=jnp.float32
         )
         member_forcing = (picked * forcing[:, None]).astype(jnp.bfloat16)
     else:
@@ -94,25 +97,42 @@
     ends = tile_count - 1
     from_left = lax.ppermute(level_mix, "tile", [(i, i + 1) for i in range(ends)])
     from_right = lax.ppermute(level_mix, "tile", [(i + 1, i) for i in range(ends)])
-    three = jnp.stack([from_left, level_mix, from_right])
-    if packed:
-        three = jnp.einsum(
-            "tkms,tsxy->tkmxy", three, hits, preferred_element_type=jnp.float32
-        ).astype(jnp.bfloat16)
-
     row_iota = jnp.arange(row_count, dtype=jnp.int32)
     taps_rows = taps_table(radius, row_iota[:, None] - row_iota[None, :])
     wide_iota = jnp.arange(3 * col_count, dtype=jnp.int32)
     col_iota = jnp.arange(col_count, dtype=jnp.int32)
     taps_cols = taps_table(radius, wide_iota[:, None] - col_count - col_iota[None, :])
     taps_cols = taps_cols.reshape(lev_dev, 3, col_count, col_count)
-    smooth_wide = jnp.einsum(
-        "tkmxy,kyz->tkmxz", three, taps_rows, preferred_element_type=jnp.float32
+
+    own = level_mix
+    if packed:
+        own = jnp.einsum(
+            "kms,sxy->kmxy", own, own_hits(), preferred_element_type=jnp.float32
+        ).astype(jnp.bfloat16)
+    own = jnp.einsum(
+        "kmxy,kyz->kmxz", own, taps_rows, preferred_element_type=jnp.float32
+    ).astype(jnp.bfloat16)
+    own = jnp.einsum(
+        "kmey,kex->kmxy", own, taps_cols[:, 1], preferred_element_type=jnp.float32
+    )
+    gradient = alpha + own
+
+    sides = jnp.stack([from_left, from_right])
+    if packed:
+        side_cells = near[0::2]
+        side_hits = one_hot(side_cells, first_hits(side_cells), cell_count)
+        sides = jnp.einsum(
+            "tkms,tsxy->tkmxy", sides,
+            side_hits.reshape(2, slots, col_count, row_count),
+            preferred_element_type=jnp.float32,
+        ).astype(jnp.bfloat16)
+    sides = jnp.einsum(
+        "tkmxy,kyz->tkmxz", sides, taps_rows, preferred_element_type=jnp.float32
     ).astype(jnp.bfloat16)
     smooth_x = jnp.einsum(
-        "tkmey,ktex->kmxy", smooth_wide, taps_cols, preferred_element_type=jnp.float32
+        "tkmey,ktex->kmxy", sides, taps_cols[:, 0::2], preferred_element_type=jnp.float32
     )
-    gradient = alpha + smooth_x
+    gradient = gradient + smooth_x
     total_cells = float(lev_dev * group_count * col_count * tile_count * row_count)
     gram_local = (
         jnp.einsum("kmxy,knxy->mn", gradient, gradient, precision=lax.Precision.HIGHEST) / total_cells

time: 169 us -> 162 us (0.959)
  blocking collectives: 12.8 us -> 0 us
  matrix products: 46.4 us -> 55 us
  waiting for transfers between devices: 55 us -> 47.4 us
  starting transfers between devices: 22.2 us -> 26.4 us
  local copies, waits for them, and re-layouts: 10.2 us -> 12.2 us
  other arithmetic: 21.2 us -> 19.4 us
    all_to_all x1 -> x0, blocking collectives: 12.8 us -> none  [shards(): lax.all_to_all(member_forcing, 'lev', split_axis=1, concat_axis=0, tiled=...]
    ppermute x1, waiting for transfers between devices: 12 us -> 0.01 us  [shards(): lax.ppermute(level_mix, 'tile', [(i + 1, i) for i in range(ends)])]
    dot_general x3 -> x5, matrix products: 29.8 us -> 39.2 us  [the longest x1 11.7 us: shards(): jnp.einsum('tkms,tsxy->tkmxy', sides, side_hits.reshape(2, slots, col_cou...]
    all_to_all x0 -> x1, waiting for transfers between devices: none -> 9.45 us  [shards(): lax.all_to_all(member_forcing, 'lev', split_axis=1, concat_axis=0, tiled=...]
    and x1 -> x0, other arithmetic: 3.5 us -> none  [one_hot(): hit = (cells[..., None] == grid) & keep[..., None]]
    all_to_all x0 -> x1, starting transfers between devices: none -> 3.48 us  [shards(): lax.all_to_all(member_forcing, 'lev', split_axis=1, concat_axis=0, tiled=...]
    all_to_all x1, waiting for transfers between devices: 11.4 us -> 8.49 us  [shards(): lax.all_to_all(local_mix.astype(jnp.bfloat16), 'lev', split_axis=0, conca...]
    reduce_or x1 -> x2, other arithmetic: 4.01 us -> 3.64 us  [first_hits(): return jnp.logical_not(jnp.any(same & later, axis=-1))]
  transfers between devices with their start and end apart: 9 -> 10, of which waited for: 9 -> 9; matrix products, arithmetic and copies ran while one was open for 1% -> 12% of each run, Pallas kernels for 0% -> 0%
where the time goes in v6:
time: 162 us; the launch traced here: 161 us
  matrix products  55 us (34%)
  waiting for transfers between devices  47.4 us (29%)
  starting transfers between devices  26.4 us (16%)
  other arithmetic  19.4 us (12%)
  local copies, waits for them, and re-layouts  12.2 us (8%)
    dot_general x1, matrix products, shards(): jnp.einsum('kmxy,knxy->mn', gradient, gradient, precision=lax.Precision.H...  14.1 us
    ppermute x5, waiting for transfers between devices, all_sum(): lax.ppermute(value, name, [(i, i ^ bit) for i in range(size)])  13.3 us
    ppermute x1, waiting for transfers between devices, shards(): lax.ppermute(level_mix, 'tile', [(i, i + 1) for i in range(ends)])  12.2 us
    dot_general x1, matrix products, shards(): jnp.einsum('tkms,tsxy->tkmxy', sides, side_hits.reshape(2, slots, col_cou...  11.7 us
    dot_general x1, matrix products, shards(): jnp.einsum('tkmey,ktex->kmxy', sides, taps_cols[:, 0::2], preferred_eleme...  10.9 us
    all_to_all x1, waiting for transfers between devices, shards(): lax.all_to_all(member_forcing, 'lev', split_axis=1, concat_axis=0, tiled=...  9.45 us
    all_to_all x1, waiting for transfers between devices, shards(): lax.all_to_all(local_mix.astype(jnp.bfloat16), 'lev', split_axis=0, conca...  8.49 us
    another operation x3, other arithmetic, shards(): r_factor = jnp.linalg.cholesky(gram_total).T  7.98 us
  transfers between devices with their start and end apart: 10, of which 9 were waited for; matrix products, arithmetic and copies ran while one was open for 12% of the time, Pallas kernels for 0%

profile of v6, /device:TPU:0, one launch (start us, length us, event | category | flops | bytes accessed | tf_op | source)
XLA Modules:
  0.0 161.4 jit_solution(11600745948409858842)
XLA Ops:
  0.6 0.8 compare_and_fusion.4
  1.5 0.7 fusion.84
  2.2 0.8 slice_bitcast_fusion.9
  2.9 0.8 slice_bitcast_fusion.7
  3.7 0.8 copy.59
  4.6 2.8 %gather_fusion = f32[1024,4]{1,0:T(8,128)S(1)} fusion(f32[4,512]{0,1:T(8,128)S(1)} %copy.59, s32[1024]{0:T(1024)S(1)} %fusion.84), kind=kCustom, calls=%fused_computation | custom fusion | bytes 36864 | tf_op jit(solution)/shard_map/jit(_take)/gather | solution.py:58
  7.6 0.8 select_bitcast_fusion.1
  8.3 0.7 add_convert_fusion
  9.1 0.6 pad_maximum_fusion
  9.7 7.3 %all-to-all-start = ((f32[7,8,128]{2,0,1:T(8,128)}), f32[7,8,128]{2,0,1:T(8,128)S(1)}, u32[]{:S(2)}, u32[]{:S(2)}) async-start(f32[7,8,128]{2,0,1:T(8,128)} %pad_maximum_fusion), calls=%async_computation | async-start | bytes 65536 | tf_op jit(solution)/shard_map/all_to_all | solution.py:65
  16.9 0.8 abs_convert_fusion
  17.7 1.3 iota_compare_fusion
  19.0 0.7 broadcast_add_fusion
  19.7 4.0 %all-to-all-done = f32[7,8,128]{2,0,1:T(8,128)S(1)} async-done(((f32[7,8,128]{2,0,1:T(8,128)}), f32[7,8,128]{2,0,1:T(8,128)S(1)}, u32[]{:S(2)}, u32[]{:S(2)}) %all-to-all-start) | async-done | bytes 28704 | tf_op jit(solution)/shard_map/all_to_all | solution.py:65
  23.7 0.6 fusion.26
  24.3 1.3 fusion.17
  25.6 4.5 %fusion.62 = bf16[4,80,1024]{2,1,0:T(8,128)(2,1)S(1)} fusion(bf16[4,80,16,256]{3,2,1,0:T(8,128)(2,1)S(1)} %copy-done, s32[16,256]{1,0:T(8,128)S(1)} %multiply_add_fusion, s32[1024]{0:T(1024)S(1)} %slice_bitcast_fusion.5, pred[1024]{0:T(1024)(128)(4,1)S(1)} %not.14, f32[4,1024]{1,0:T(4,128)S(1)} %fusion.17), kind=kOutput, calls=%fused_computation.45 | convolution fusion | flops 2693398528 | bytes 3314688 | tf_op jit(solution)/shard_map/lmxy,sxy->lms/dot_general | solution.py:80
  30.1 1.4 copy.64
  31.4 3.5 %all-to-all-start.1 = ((bf16[4,80,1024]{2,0,1:T(4,128)(2,1)}), bf16[4,80,1024]{2,0,1:T(4,128)(2,1)S(1)}, u32[]{:S(2)}, u32[]{:S(2)}) async-start(bf16[4,80,1024]{2,0,1:T(4,128)(2,1)} %copy.64), calls=%async_computation.1 | async-start | bytes 1310720 | tf_op jit(solution)/shard_map/all_to_all | solution.py:90
  35.0 0.7 select_convert_fusion.5
  35.7 9.4 %all-to-all-done.1 = bf16[4,80,1024]{2,0,1:T(4,128)(2,1)S(1)} async-done(((bf16[4,80,1024]{2,0,1:T(4,128)(2,1)}), bf16[4,80,1024]{2,0,1:T(4,128)(2,1)S(1)}, u32[]{:S(2)}, u32[]{:S(2)}) %all-to-all-start.1) | async-done | bytes 655392 | tf_op jit(solution)/shard_map/all_to_all | solution.py:90
  45.2 1.2 copy.65
  46.3 1.5 all_to_all.33
  48.2 1.3 copy.67
  49.5 3.5 %all-to-all-start.2 = ((bf16[16,20,1024]{2,1,0:T(8,128)(2,1)}), bf16[16,20,1024]{2,1,0:T(8,128)(2,1)S(1)}, u32[]{:S(2)}, u32[]{:S(2)}) async-start(bf16[16,20,1024]{2,1,0:T(8,128)(2,1)} %copy.67), calls=%async_computation.2 | async-start | bytes 1572864 | tf_op jit(solution)/shard_map/all_to_all | solution.py:94
  53.1 3.1 %and_reduce_fusion = pred[2,1024]{1,0:T(4,128)(4,1)S(1)} fusion(s32[2,1024]{1,0:T(2,128)S(1)} %slice.62, pred[1024,1024]{1,0:T(8,128)(4,1)} %iota_compare_fusion), kind=kLoop, calls=%fused_computation.19 | loop fusion | flops 6289408 | bytes 1058816 | tf_op jit(solution)/shard_map/reduce_or | solution.py:24
  56.1 8.5 %all-to-all-done.2 = bf16[16,20,1024]{2,1,0:T(8,128)(2,1)S(1)} async-done(((bf16[16,20,1024]{2,1,0:T(8,128)(2,1)}), bf16[16,20,1024]{2,1,0:T(8,128)(2,1)S(1)}, u32[]{:S(2)}, u32[]{:S(2)}) %all-to-all-start.2) | async-done | bytes 655392 | tf_op jit(solution)/shard_map/all_to_all | solution.py:94
  65.3 1.3 collective-permute-start.1
  66.6 5.4 %collective-permute-start = (bf16[4,80,1024]{2,1,0:T(8,128)(2,1)S(1)}, bf16[4,80,1024]{2,1,0:T(8,128)(2,1)}, u32[]{:S(2)}, u32[]{:S(2)}) collective-permute-start(bf16[4,80,1024]{2,1,0:T(8,128)(2,1)S(1)} %copy.71), channel_id=1, source_target_pairs={{0,4},{4,8},{8,12},{12,16},{16,20},{20,24},{24,28},{1,5},{5,9},{9,... | collective-permute-start | bytes 1966088 | tf_op jit(solution)/shard_map/ppermute | solution.py:98
  72.1 6.3 %fusion.49 = bf16[4,80,16,256]{3,1,2,0:T(8,128)(2,1)} fusion(s32[16,256]{1,0:T(8,128)} %copy-done.3, s32[1024]{0:T(1024)S(1)} %slice_bitcast_fusion.5, pred[1024]{0:T(1024)(128)(4,1)} %copy-done.5, bf16[4,80,1024,1]{2,0,1,3:T(4,128)(2,1)S(1)} %bitcast.140), kind=kOutput, calls=%fused_computation.42 | convolution fusion | flops 2694053888 | bytes 3298304 | tf_op jit(solution)/shard_map/kms,sxy->kmxy/dot_general | solution.py:109
  78.3 5.9 %fusion.37 = f32[4,16,80,256]{3,1,2,0:T(8,128)} fusion(bf16[4,80,16,256]{3,1,2,0:T(8,128)(2,1)} %fusion.49, f32[4]{0:T(128)} %copy-done.6, f32[256,256]{1,0:T(8,128)S(1)} %copy-done.1, f32[4]{0:T(128)} %copy-done.8, bf16[4,3,16,16]{2,3,0,1:T(8,128)(2,1)} %select_convert_fusion.5), kind=kOutput, calls=%fused_computation.38 | convolution fusion | flops 715653120 | bytes 8143872 | tf_op jit(solution)/shard_map/kmey,kex->kmxy/dot_general | solution.py:115
  84.3 12.2 %collective-permute-done = bf16[4,80,1024]{2,1,0:T(8,128)(2,1)} collective-permute-done((bf16[4,80,1024]{2,1,0:T(8,128)(2,1)S(1)}, bf16[4,80,1024]{2,1,0:T(8,128)(2,1)}, u32[]{:S(2)}, u32[]{:S(2)}) %collective-permute-start) | collective-permute-done | bytes 655392 | tf_op jit(solution)/shard_map/ppermute | solution.py:98
  96.5 11.7 %fusion.27 = bf16[2,4,80,16,256]{4,2,3,1,0:T(8,128)(2,1)} fusion(s32[16,256]{1,0:T(8,128)} %copy-done.3, s32[2,1024]{1,0:T(2,128)S(1)} %slice.62, pred[2,1024]{1,0:T(4,128)(4,1)S(1)} %not.15, bf16[1,4,80,1024]{3,2,1,0:T(8,128)(2,1)} %bitcast.40, bf16[1,4,80,1024]{3,2,1,0:T(8,128)(2,1)} %bitcast.39), kind=kOutput, calls=%fused_computation.34 | convolution fusion | flops 5390729216 | bytes 6580224 | tf_op jit(solution)/shard_map/tkms,tsxy->tkmxy/dot_general | solution.py:124
  108.2 10.9 %bitcast_add_fusion = f32[4,80,16,256]{3,2,1,0:T(8,128)} fusion(f32[4,80,16,256]{3,2,1,0:T(8,128)} %param.17, f32[4,16,80,256]{3,1,2,0:T(8,128)} %fusion.37, bf16[2,4,80,16,256]{4,2,3,1,0:T(8,128)(2,1)} %fusion.27, f32[4]{0:T(128)S(1)} %copy-done.7, f32[256,256]{1,0:T(8,128)S(1)} %copy-done.1, f32[4]{0:T(128)S(1)} %copy-done.9, ...), kind=kOutput, calls=%fused_computation.23 | convolution fusion | flops 1432616960 | bytes 21267456 | tf_op jit(solution)/shard_map/tkmey,ktex->kmxy/dot_general | solution.py:132
  119.1 14.1 %fusion.73 = f32[80,80]{0,1:T(8,128)S(1)} fusion(f32[4,80,16,256]{3,2,1,0:T(8,128)} %bitcast_add_fusion), kind=kOutput, calls=%fused_computation.52 | convolution fusion | flops 1258297600 | bytes 5268480 | tf_op jit(solution)/shard_map/kmxy,knxy->mn/dot_general | solution.py:138
  133.2 1.2 collective-permute-done.2
  134.4 0.6 collective-permute-start.3
  135.0 3.4 %collective-permute-done.3 = f32[80,80]{0,1:T(8,128)S(1)} collective-permute-done((f32[80,80]{0,1:T(8,128)S(1)}, f32[80,80]{0,1:T(8,128)S(1)}, u32[]{:S(2)}, u32[]{:S(2)}) %collective-permute-start.3) | collective-permute-done | bytes 25632 | tf_op jit(solution)/shard_map/ppermute | solution.py:39
  138.4 2.6 %collective-permute-start.4 = (f32[80,80]{0,1:T(8,128)S(1)}, f32[80,80]{0,1:T(8,128)S(1)}, u32[]{:S(2)}, u32[]{:S(2)}) collective-permute-start(f32[80,80]{0,1:T(8,128)S(1)} %add.79), channel_id=1, source_target_pairs={{0,4},{4,0},{8,12},{12,8},{16,20},{20,16},{24,28},{28,24},{1,5},{5... | collective-permute-start | bytes 76808 | tf_op jit(solution)/shard_map/ppermute | solution.py:39
  141.0 2.0 %collective-permute-done.4 = f32[80,80]{0,1:T(8,128)S(1)} collective-permute-done((f32[80,80]{0,1:T(8,128)S(1)}, f32[80,80]{0,1:T(8,128)S(1)}, u32[]{:S(2)}, u32[]{:S(2)}) %collective-permute-start.4) | collective-permute-done | bytes 25632 | tf_op jit(solution)/shard_map/ppermute | solution.py:39
  143.0 1.0 collective-permute-start.5
  144.1 3.0 %collective-permute-done.5 = f32[80,80]{0,1:T(8,128)S(1)} collective-permute-done((f32[80,80]{0,1:T(8,128)S(1)}, f32[80,80]{0,1:T(8,128)S(1)}, u32[]{:S(2)}, u32[]{:S(2)}) %collective-permute-start.5) | collective-permute-done | bytes 25632 | tf_op jit(solution)/shard_map/ppermute | solution.py:39
  147.0 1.2 collective-permute-start.6
  148.2 3.7 %collective-permute-done.6 = f32[80,80]{0,1:T(8,128)S(1)} collective-permute-done((f32[80,80]{0,1:T(8,128)S(1)}, f32[80,80]{0,1:T(8,128)S(1)}, u32[]{:S(2)}, u32[]{:S(2)}) %collective-permute-start.6) | collective-permute-done | bytes 25632 | tf_op jit(solution)/shard_map/ppermute | solution.py:39
  152.0 7.3 %cholesky.18 = f32[80,80]{1,0:T(8,128)S(1)} custom-call(f32[80,80]{1,0:T(8,128)S(1)} %fusion.81), custom_call_target="Cholesky" | custom-call | tf_op jit(solution)/shard_map/jit(cholesky)/cholesky | solution.py:141
  159.4 0.6 compare_reduce_fusion
  160.0 0.7 select_bitcast_fusion
  160.7 0.7 copy.79
  (50 shorter events, 1.7 us)
Async XLA Ops:
  0.6 25.0 %copy-start = (bf16[4,80,16,256]{3,2,1,0:T(8,128)(2,1)S(1)}, bf16[4,80,16,256]{3,2,1,0:T(8,128)(2,1)}, u32[]{:S(2)}) copy-start(bf16[4,80,16,256]{3,2,1,0:T(8,128)(2,1)} %param.14) | copy-start | bytes 7864324
  9.7 13.9 %all-to-all-start = ((f32[7,8,128]{2,0,1:T(8,128)}), f32[7,8,128]{2,0,1:T(8,128)S(1)}, u32[]{:S(2)}, u32[]{:S(2)}) async-start(f32[7,8,128]{2,0,1:T(8,128)} %pad_maximum_fusion), calls=%async_computation | async-start | bytes 65536 | tf_op jit(solution)/shard_map/all_to_all | solution.py:65
  19.6 15.4 %copy-start.6 = (f32[4]{0:T(128)}, f32[4]{0:T(128)S(1)}, u32[]{:S(2)}) copy-start(f32[4]{0:T(128)S(1)} %broadcast_add_fusion) | copy-start | bytes 52
  19.6 10.4 %copy-start.3 = (s32[16,256]{1,0:T(8,128)}, s32[16,256]{1,0:T(8,128)S(1)}, u32[]{:S(2)}) copy-start(s32[16,256]{1,0:T(8,128)S(1)} %multiply_add_fusion) | copy-start | bytes 49156
  24.2 5.8 %copy-start.5 = (pred[1024]{0:T(1024)(128)(4,1)}, pred[1024]{0:T(1024)(128)(4,1)S(1)}, u32[]{:S(2)}) copy-start(pred[1024]{0:T(1024)(128)(4,1)S(1)} %not.14) | copy-start | bytes 3076
  25.6 9.4 %copy-start.10 = (s32[4]{0:T(128)S(1)}, s32[4]{0:T(128)}, u32[]{:S(2)}) copy-start(s32[4]{0:T(128)} %param.16) | copy-start | bytes 52
  30.1 17.7 %copy-start.4 = (bf16[16,16]{1,0:T(8,128)(2,1)S(1)}, bf16[16,16]{1,0:T(8,128)(2,1)}, u32[]{:S(2)}) copy-start(bf16[16,16]{1,0:T(8,128)(2,1)} %param.15) | copy-start | bytes 1540
  31.4 13.7 %all-to-all-start.1 = ((bf16[4,80,1024]{2,0,1:T(4,128)(2,1)}), bf16[4,80,1024]{2,0,1:T(4,128)(2,1)S(1)}, u32[]{:S(2)}, u32[]{:S(2)}) async-start(bf16[4,80,1024]{2,0,1:T(4,128)(2,1)} %copy.64), calls=%async_computation.1 | async-start | bytes 1310720 | tf_op jit(solution)/shard_map/all_to_all | solution.py:90
  35.0 14.5 %copy-start.8 = (f32[4]{0:T(128)}, f32[4]{0:T(128)S(1)}, u32[]{:S(2)}) copy-start(f32[4]{0:T(128)S(1)} %convert_element_type.65) | copy-start | bytes 52
  49.5 15.1 %all-to-all-start.2 = ((bf16[16,20,1024]{2,1,0:T(8,128)(2,1)}), bf16[16,20,1024]{2,1,0:T(8,128)(2,1)S(1)}, u32[]{:S(2)}, u32[]{:S(2)}) async-start(bf16[16,20,1024]{2,1,0:T(8,128)(2,1)} %copy.67), calls=%async_computation.2 | async-start | bytes 1572864 | tf_op jit(solution)/shard_map/all_to_all | solution.py:94
  65.3 18.9 %collective-permute-start.1 = (bf16[4,80,1024]{2,1,0:T(8,128)(2,1)S(1)}, bf16[4,80,1024]{2,1,0:T(8,128)(2,1)}, u32[]{:S(2)}, u32[]{:S(2)}) collective-permute-start(bf16[4,80,1024]{2,1,0:T(8,128)(2,1)S(1)} %copy.71), channel_id=1, source_target_pairs={{4,0},{8,4},{12,8},{16,12},{20,16},{24,20},{28,24},{5,1},{9,5},{13... | collective-permute-start | bytes 1966088 | tf_op jit(solution)/shard_map/ppermute | solution.py:99
  66.6 29.8 %collective-permute-start = (bf16[4,80,1024]{2,1,0:T(8,128)(2,1)S(1)}, bf16[4,80,1024]{2,1,0:T(8,128)(2,1)}, u32[]{:S(2)}, u32[]{:S(2)}) collective-permute-start(bf16[4,80,1024]{2,1,0:T(8,128)(2,1)S(1)} %copy.71), channel_id=1, source_target_pairs={{0,4},{4,8},{8,12},{12,16},{16,20},{20,24},{24,28},{1,5},{5,9},{9,... | collective-permute-start | bytes 1966088 | tf_op jit(solution)/shard_map/ppermute | solution.py:98
  72.1 6.3 %copy-start.1 = (f32[256,256]{1,0:T(8,128)S(1)}, f32[256,256]{1,0:T(8,128)}, u32[]{:S(2)}) copy-start(f32[256,256]{1,0:T(8,128)} %abs_convert_fusion) | copy-start | bytes 786436
  96.5 11.7 %copy-start.2 = (bf16[4,3,16,16]{2,3,0,1:T(8,128)(2,1)S(1)}, bf16[4,3,16,16]{2,3,0,1:T(8,128)(2,1)}, u32[]{:S(2)}) copy-start(bf16[4,3,16,16]{2,3,0,1:T(8,128)(2,1)} %select_convert_fusion.5) | copy-start | bytes 18436
  96.5 11.7 %copy-start.7 = (f32[4]{0:T(128)S(1)}, f32[4]{0:T(128)}, u32[]{:S(2)}) copy-start(f32[4]{0:T(128)} %copy-done.6) | copy-start | bytes 52
  96.5 11.7 %copy-start.9 = (f32[4]{0:T(128)S(1)}, f32[4]{0:T(128)}, u32[]{:S(2)}) copy-start(f32[4]{0:T(128)} %copy-done.8) | copy-start | bytes 52
  133.1 1.3 collective-permute-start.2
  134.4 4.0 %collective-permute-start.3 = (f32[80,80]{0,1:T(8,128)S(1)}, f32[80,80]{0,1:T(8,128)S(1)}, u32[]{:S(2)}, u32[]{:S(2)}) collective-permute-start(f32[80,80]{0,1:T(8,128)S(1)} %add.78), channel_id=1, source_target_pairs={{0,2},{1,3},{2,0},{3,1},{4,6},{5,7},{6,4},{7,5},{8,10},{9,11},{10,... | collective-permute-start | bytes 76808 | tf_op jit(solution)/shard_map/ppermute | solution.py:39
  138.4 4.6 %collective-permute-start.4 = (f32[80,80]{0,1:T(8,128)S(1)}, f32[80,80]{0,1:T(8,128)S(1)}, u32[]{:S(2)}, u32[]{:S(2)}) collective-permute-start(f32[80,80]{0,1:T(8,128)S(1)} %add.79), channel_id=1, source_target_pairs={{0,4},{4,0},{8,12},{12,8},{16,20},{20,16},{24,28},{28,24},{1,5},{5... | collective-permute-start | bytes 76808 | tf_op jit(solution)/shard_map/ppermute | solution.py:39
  143.0 4.0 %collective-permute-start.5 = (f32[80,80]{0,1:T(8,128)S(1)}, f32[80,80]{0,1:T(8,128)S(1)}, u32[]{:S(2)}, u32[]{:S(2)}) collective-permute-start(f32[80,80]{0,1:T(8,128)S(1)} %add.80), channel_id=1, source_target_pairs={{0,8},{4,12},{8,0},{12,4},{16,24},{20,28},{24,16},{28,20},{1,9},{5... | collective-permute-start | bytes 76808 | tf_op jit(solution)/shard_map/ppermute | solution.py:39
  147.0 4.9 %collective-permute-start.6 = (f32[80,80]{0,1:T(8,128)S(1)}, f32[80,80]{0,1:T(8,128)S(1)}, u32[]{:S(2)}, u32[]{:S(2)}) collective-permute-start(f32[80,80]{0,1:T(8,128)S(1)} %add.81), channel_id=1, source_target_pairs={{0,16},{4,20},{8,24},{12,28},{16,0},{20,4},{24,8},{28,12},{1,17},{... | collective-permute-start | bytes 76808 | tf_op jit(solution)/shard_map/ppermute | solution.py:39

commit v7 on v6

--- a/solution.py
+++ b/solution.py
@@ -39,6 +39,16 @@
             value = value + lax.ppermute(value, name, [(i, i ^ bit) for i in range(size)])
             bit *= 2
     return value
+
+
+def gram_of(panel):
+    high = panel.astype(jnp.bfloat16)
+    low = (panel - high.astype(jnp.float32)).astype(jnp.bfloat16)
+    members = panel.shape[1]
+    parts = jnp.concatenate([high, low], axis=1)
+    blocks = jnp.einsum("kpxy,kqxy->pq", parts, parts, preferred_element_type=jnp.float32)
+    top, bottom = blocks[:members], blocks[members:]
+    return (top[:, :members] + top[:, members:]) + (bottom[:, :members] + bottom[:, members:])
 
 
 def shards(
@@ -135,7 +145,7 @@
     gradient = gradient + smooth_x
     total_cells = float(lev_dev * group_count * col_count * tile_count * row_count)
     gram_local = (
-        jnp.einsum("kmxy,knxy->mn", gradient, gradient, precision=lax.Precision.HIGHEST) / total_cells
+        gram_of(gradient) / total_cells
     )
     gram_total = all_sum(gram_local, (("lev", group_count), ("tile", tile_count)))
     r_factor = jnp.linalg.cholesky(gram_total).T

time: 162 us -> 157 us (0.969)
  matrix products: 55 us -> 46.9 us
  other arithmetic: 19.4 us -> 22.6 us
    dot_general x1, matrix products: 14.1 us -> 4.17 us  [gram_of(): jnp.einsum('kpxy,kqxy->pq', parts, parts, preferred_element_type=jnp.floa...]
    concatenate x0 -> x1, other arithmetic: none -> 2.98 us  [gram_of(): parts = jnp.concatenate([high, low], axis=1)]
    dot_general x1, matrix products: 10.9 us -> 12.7 us  [shards(): jnp.einsum('tkmey,ktex->kmxy', sides, taps_cols[:, 0::2], preferred_eleme...]
where the time goes in v7:
time: 157 us; the launch traced here: 156 us
  waiting for transfers between devices  47.3 us (30%)
  matrix products  46.9 us (30%)
  starting transfers between devices  26.5 us (17%)
  other arithmetic  22.6 us (14%)
  local copies, waits for them, and re-layouts  12.2 us (8%)
    ppermute x5, waiting for transfers between devices, all_sum(): lax.ppermute(value, name, [(i, i ^ bit) for i in range(size)])  13.2 us
    dot_general x1, matrix products, shards(): jnp.einsum('tkmey,ktex->kmxy', sides, taps_cols[:, 0::2], preferred_eleme...  12.7 us
    ppermute x1, waiting for transfers between devices, shards(): lax.ppermute(level_mix, 'tile', [(i, i + 1) for i in range(ends)])  12.2 us
    dot_general x1, matrix products, shards(): jnp.einsum('tkms,tsxy->tkmxy', sides, side_hits.reshape(2, slots, col_cou...  11.7 us
    all_to_all x1, waiting for transfers between devices, shards(): lax.all_to_all(member_forcing, 'lev', split_axis=1, concat_axis=0, tiled=...  9.44 us
    all_to_all x1, waiting for transfers between devices, shards(): lax.all_to_all(local_mix.astype(jnp.bfloat16), 'lev', split_axis=0, conca...  8.49 us
    another operation x3, other arithmetic, shards(): r_factor = jnp.linalg.cholesky(gram_total).T  7.98 us
    all_to_all x1, starting transfers between devices, shards(): lax.all_to_all(outgoing, 'tile', split_axis=1, concat_axis=1, tiled=True)  7.25 us
  transfers between devices with their start and end apart: 10, of which 9 were waited for; matrix products, arithmetic and copies ran while one was open for 12% of the time, Pallas kernels for 0%

profile of v7, /device:TPU:0, one launch (start us, length us, event | category | flops | bytes accessed | tf_op | source)
XLA Modules:
  0.0 156.5 jit_solution(2600244698093263810)
XLA Ops:
  0.6 0.8 compare_and_fusion.4
  1.5 0.7 fusion.83
  2.2 0.8 slice_bitcast_fusion.9
  2.9 0.8 slice_bitcast_fusion.7
  3.7 0.8 copy.68
  4.6 2.8 %gather_fusion = f32[1024,4]{1,0:T(8,128)S(1)} fusion(f32[4,512]{0,1:T(8,128)S(1)} %copy.68, s32[1024]{0:T(1024)S(1)} %fusion.83), kind=kCustom, calls=%fused_computation | custom fusion | bytes 36864 | tf_op jit(solution)/shard_map/jit(_take)/gather | solution.py:68
  7.6 0.8 select_bitcast_fusion.1
  8.3 0.7 add_convert_fusion
  9.1 0.6 pad_maximum_fusion.1
  9.7 7.3 %all-to-all-start = ((f32[7,8,128]{2,0,1:T(8,128)}), f32[7,8,128]{2,0,1:T(8,128)S(1)}, u32[]{:S(2)}, u32[]{:S(2)}) async-start(f32[7,8,128]{2,0,1:T(8,128)} %pad_maximum_fusion.1), calls=%async_computation | async-start | bytes 65536 | tf_op jit(solution)/shard_map/all_to_all | solution.py:75
  17.0 0.8 abs_convert_fusion
  17.7 1.3 iota_compare_fusion
  19.0 0.7 broadcast_add_fusion
  19.7 4.0 %all-to-all-done = f32[7,8,128]{2,0,1:T(8,128)S(1)} async-done(((f32[7,8,128]{2,0,1:T(8,128)}), f32[7,8,128]{2,0,1:T(8,128)S(1)}, u32[]{:S(2)}, u32[]{:S(2)}) %all-to-all-start) | async-done | bytes 28704 | tf_op jit(solution)/shard_map/all_to_all | solution.py:75
  24.3 1.3 fusion.17
  25.6 4.5 %fusion.62 = bf16[4,80,1024]{2,1,0:T(8,128)(2,1)S(1)} fusion(bf16[4,80,16,256]{3,2,1,0:T(8,128)(2,1)S(1)} %copy-done, s32[16,256]{1,0:T(8,128)S(1)} %multiply_add_fusion, s32[1024]{0:T(1024)S(1)} %slice_bitcast_fusion.5, pred[1024]{0:T(1024)(128)(4,1)S(1)} %not.14, f32[4,1024]{1,0:T(4,128)S(1)} %fusion.17), kind=kOutput, calls=%fused_computation.47 | convolution fusion | flops 2693398528 | bytes 3314688 | tf_op jit(solution)/shard_map/lmxy,sxy->lms/dot_general | solution.py:90
  30.1 1.4 copy.73
  31.5 3.5 %all-to-all-start.1 = ((bf16[4,80,1024]{2,0,1:T(4,128)(2,1)}), bf16[4,80,1024]{2,0,1:T(4,128)(2,1)S(1)}, u32[]{:S(2)}, u32[]{:S(2)}) async-start(bf16[4,80,1024]{2,0,1:T(4,128)(2,1)} %copy.73), calls=%async_computation.1 | async-start | bytes 1310720 | tf_op jit(solution)/shard_map/all_to_all | solution.py:100
  35.0 0.7 select_convert_fusion.5
  35.7 9.4 %all-to-all-done.1 = bf16[4,80,1024]{2,0,1:T(4,128)(2,1)S(1)} async-done(((bf16[4,80,1024]{2,0,1:T(4,128)(2,1)}), bf16[4,80,1024]{2,0,1:T(4,128)(2,1)S(1)}, u32[]{:S(2)}, u32[]{:S(2)}) %all-to-all-start.1) | async-done | bytes 655392 | tf_op jit(solution)/shard_map/all_to_all | solution.py:100
  45.2 1.2 copy.74
  46.3 1.5 all_to_all.33
  48.2 1.3 copy.76
  49.5 3.5 %all-to-all-start.2 = ((bf16[16,20,1024]{2,1,0:T(8,128)(2,1)}), bf16[16,20,1024]{2,1,0:T(8,128)(2,1)S(1)}, u32[]{:S(2)}, u32[]{:S(2)}) async-start(bf16[16,20,1024]{2,1,0:T(8,128)(2,1)} %copy.76), calls=%async_computation.2 | async-start | bytes 1572864 | tf_op jit(solution)/shard_map/all_to_all | solution.py:104
  53.1 3.1 %and_reduce_fusion = pred[2,1024]{1,0:T(4,128)(4,1)S(1)} fusion(s32[2,1024]{1,0:T(2,128)S(1)} %slice.80, pred[1024,1024]{1,0:T(8,128)(4,1)} %iota_compare_fusion), kind=kLoop, calls=%fused_computation.19 | loop fusion | flops 6289408 | bytes 1058816 | tf_op jit(solution)/shard_map/reduce_or | solution.py:24
  56.1 8.5 %all-to-all-done.2 = bf16[16,20,1024]{2,1,0:T(8,128)(2,1)S(1)} async-done(((bf16[16,20,1024]{2,1,0:T(8,128)(2,1)}), bf16[16,20,1024]{2,1,0:T(8,128)(2,1)S(1)}, u32[]{:S(2)}, u32[]{:S(2)}) %all-to-all-start.2) | async-done | bytes 655392 | tf_op jit(solution)/shard_map/all_to_all | solution.py:104
  65.3 1.3 collective-permute-start.1
  66.6 5.4 %collective-permute-start = (bf16[4,80,1024]{2,1,0:T(8,128)(2,1)S(1)}, bf16[4,80,1024]{2,1,0:T(8,128)(2,1)}, u32[]{:S(2)}, u32[]{:S(2)}) collective-permute-start(bf16[4,80,1024]{2,1,0:T(8,128)(2,1)S(1)} %copy.80), channel_id=1, source_target_pairs={{0,4},{4,8},{8,12},{12,16},{16,20},{20,24},{24,28},{1,5},{5,9},{9,... | collective-permute-start | bytes 1966088 | tf_op jit(solution)/shard_map/ppermute | solution.py:108
  72.1 6.3 %fusion.49 = bf16[4,80,16,256]{3,1,2,0:T(8,128)(2,1)} fusion(s32[16,256]{1,0:T(8,128)} %copy-done.3, s32[1024]{0:T(1024)S(1)} %slice_bitcast_fusion.5, pred[1024]{0:T(1024)(128)(4,1)} %copy-done.5, bf16[4,80,1024,1]{2,0,1,3:T(4,128)(2,1)S(1)} %bitcast.146), kind=kOutput, calls=%fused_computation.44 | convolution fusion | flops 2694053888 | bytes 3298304 | tf_op jit(solution)/shard_map/kms,sxy->kmxy/dot_general | solution.py:119
  78.3 5.9 %fusion.37 = f32[4,16,80,256]{3,1,2,0:T(8,128)} fusion(bf16[4,80,16,256]{3,1,2,0:T(8,128)(2,1)} %fusion.49, f32[4]{0:T(128)} %copy-done.6, f32[256,256]{1,0:T(8,128)S(1)} %copy-done.1, f32[4]{0:T(128)} %copy-done.8, bf16[4,3,16,16]{2,3,0,1:T(8,128)(2,1)} %select_convert_fusion.5), kind=kOutput, calls=%fused_computation.40 | convolution fusion | flops 715653120 | bytes 8143872 | tf_op jit(solution)/shard_map/kmey,kex->kmxy/dot_general | solution.py:125
  84.3 12.2 %collective-permute-done = bf16[4,80,1024]{2,1,0:T(8,128)(2,1)} collective-permute-done((bf16[4,80,1024]{2,1,0:T(8,128)(2,1)S(1)}, bf16[4,80,1024]{2,1,0:T(8,128)(2,1)}, u32[]{:S(2)}, u32[]{:S(2)}) %collective-permute-start) | collective-permute-done | bytes 655392 | tf_op jit(solution)/shard_map/ppermute | solution.py:108
  96.5 11.7 %fusion.27 = bf16[2,4,80,16,256]{4,2,3,1,0:T(8,128)(2,1)} fusion(s32[16,256]{1,0:T(8,128)} %copy-done.3, s32[2,1024]{1,0:T(2,128)S(1)} %slice.80, pred[2,1024]{1,0:T(4,128)(4,1)S(1)} %not.15, bf16[1,4,80,1024]{3,2,1,0:T(8,128)(2,1)} %bitcast.40, bf16[1,4,80,1024]{3,2,1,0:T(8,128)(2,1)} %bitcast.39), kind=kOutput, calls=%fused_computation.36 | convolution fusion | flops 5390729216 | bytes 6580224 | tf_op jit(solution)/shard_map/tkms,tsxy->tkmxy/dot_general | solution.py:134
  108.2 12.7 %subtract_convert_fusion = (bf16[4,80,16,256]{3,2,1,0:T(8,128)(2,1)}, bf16[4,80,16,256]{3,2,1,0:T(8,128)(2,1)}, f32[4,80,16,256]{3,2,1,0:T(8,128)}) fusion(bf16[2,4,80,16,256]{4,2,3,1,0:T(8,128)(2,1)} %fusion.27, f32[4]{0:T(128)S(1)} %copy-done.7, f32[256,256]{1,0:T(8,128)S(1)} %copy-done.1, f32[4]{0:T(128)S(1)} %copy-done.9, ...), kind=kOutput, calls=%fused_computation.32 | convolution fusion | flops 1437859840 | bytes 26510336 | tf_op jit(solution)/shard_map/tkmey,ktex->kmxy/dot_general | solution.py:142
  120.8 3.0 %pad_maximum_fusion = bf16[4,160,16,256]{3,2,1,0:T(8,128)(2,1)S(1)} fusion(bf16[4,80,16,256]{3,2,1,0:T(8,128)(2,1)} %get-tuple-element.10, bf16[4,80,16,256]{3,2,1,0:T(8,128)(2,1)} %get-tuple-element.11), kind=kLoop, calls=%fused_computation.23 | loop fusion | flops 2621440 | bytes 10485760 | tf_op jit(solution)/shard_map/concatenate | solution.py:48
  123.8 4.2 %fusion.70 = f32[160,160]{0,1:T(8,128)S(1)} fusion(bf16[4,160,16,256]{3,2,1,0:T(8,128)(2,1)S(1)} %pad_maximum_fusion), kind=kOutput, calls=%fused_computation.53 | convolution fusion | flops 838860800 | bytes 5345280 | tf_op jit(solution)/shard_map/kpxy,kqxy->pq/dot_general | solution.py:49
  128.2 1.2 collective-permute-done.2
  129.4 0.7 collective-permute-start.3
  130.1 3.4 %collective-permute-done.3 = f32[80,80]{0,1:T(8,128)S(1)} collective-permute-done((f32[80,80]{0,1:T(8,128)S(1)}, f32[80,80]{0,1:T(8,128)S(1)}, u32[]{:S(2)}, u32[]{:S(2)}) %collective-permute-start.3) | collective-permute-done | bytes 25632 | tf_op jit(solution)/shard_map/ppermute | solution.py:39
  133.5 2.6 %collective-permute-start.4 = (f32[80,80]{0,1:T(8,128)S(1)}, f32[80,80]{0,1:T(8,128)S(1)}, u32[]{:S(2)}, u32[]{:S(2)}) collective-permute-start(f32[80,80]{0,1:T(8,128)S(1)} %add.91), channel_id=1, source_target_pairs={{0,4},{4,0},{8,12},{12,8},{16,20},{20,16},{24,28},{28,24},{1,5},{5... | collective-permute-start | bytes 76808 | tf_op jit(solution)/shard_map/ppermute | solution.py:39
  136.1 2.0 %collective-permute-done.4 = f32[80,80]{0,1:T(8,128)S(1)} collective-permute-done((f32[80,80]{0,1:T(8,128)S(1)}, f32[80,80]{0,1:T(8,128)S(1)}, u32[]{:S(2)}, u32[]{:S(2)}) %collective-permute-start.4) | collective-permute-done | bytes 25632 | tf_op jit(solution)/shard_map/ppermute | solution.py:39
  138.1 1.1 collective-permute-start.5
  139.1 2.9 %collective-permute-done.5 = f32[80,80]{0,1:T(8,128)S(1)} collective-permute-done((f32[80,80]{0,1:T(8,128)S(1)}, f32[80,80]{0,1:T(8,128)S(1)}, u32[]{:S(2)}, u32[]{:S(2)}) %collective-permute-start.5) | collective-permute-done | bytes 25632 | tf_op jit(solution)/shard_map/ppermute | solution.py:39
  142.1 1.2 collective-permute-start.6
  143.3 3.7 %collective-permute-done.6 = f32[80,80]{0,1:T(8,128)S(1)} collective-permute-done((f32[80,80]{0,1:T(8,128)S(1)}, f32[80,80]{0,1:T(8,128)S(1)}, u32[]{:S(2)}, u32[]{:S(2)}) %collective-permute-start.6) | collective-permute-done | bytes 25632 | tf_op jit(solution)/shard_map/ppermute | solution.py:39
  147.1 7.3 %cholesky.18 = f32[80,80]{1,0:T(8,128)S(1)} custom-call(f32[80,80]{1,0:T(8,128)S(1)} %fusion.80), custom_call_target="Cholesky" | custom-call | tf_op jit(solution)/shard_map/jit(cholesky)/cholesky | solution.py:151
  154.4 0.6 compare_reduce_fusion
  155.1 0.7 select_bitcast_fusion
  155.7 0.7 copy.91
  (52 shorter events, 2.4 us)
Async XLA Ops:
  0.6 25.0 %copy-start = (bf16[4,80,16,256]{3,2,1,0:T(8,128)(2,1)S(1)}, bf16[4,80,16,256]{3,2,1,0:T(8,128)(2,1)}, u32[]{:S(2)}) copy-start(bf16[4,80,16,256]{3,2,1,0:T(8,128)(2,1)} %param.14) | copy-start | bytes 7864324
  9.7 13.9 %all-to-all-start = ((f32[7,8,128]{2,0,1:T(8,128)}), f32[7,8,128]{2,0,1:T(8,128)S(1)}, u32[]{:S(2)}, u32[]{:S(2)}) async-start(f32[7,8,128]{2,0,1:T(8,128)} %pad_maximum_fusion.1), calls=%async_computation | async-start | bytes 65536 | tf_op jit(solution)/shard_map/all_to_all | solution.py:75
  19.7 15.4 %copy-start.6 = (f32[4]{0:T(128)}, f32[4]{0:T(128)S(1)}, u32[]{:S(2)}) copy-start(f32[4]{0:T(128)S(1)} %broadcast_add_fusion) | copy-start | bytes 52
  19.7 10.4 %copy-start.3 = (s32[16,256]{1,0:T(8,128)}, s32[16,256]{1,0:T(8,128)S(1)}, u32[]{:S(2)}) copy-start(s32[16,256]{1,0:T(8,128)S(1)} %multiply_add_fusion) | copy-start | bytes 49156
  24.3 5.8 %copy-start.5 = (pred[1024]{0:T(1024)(128)(4,1)}, pred[1024]{0:T(1024)(128)(4,1)S(1)}, u32[]{:S(2)}) copy-start(pred[1024]{0:T(1024)(128)(4,1)S(1)} %not.14) | copy-start | bytes 3076
  25.6 9.4 %copy-start.10 = (s32[4]{0:T(128)S(1)}, s32[4]{0:T(128)}, u32[]{:S(2)}) copy-start(s32[4]{0:T(128)} %param.16) | copy-start | bytes 52
  30.1 17.7 %copy-start.4 = (bf16[16,16]{1,0:T(8,128)(2,1)S(1)}, bf16[16,16]{1,0:T(8,128)(2,1)}, u32[]{:S(2)}) copy-start(bf16[16,16]{1,0:T(8,128)(2,1)} %param.15) | copy-start | bytes 1540
  31.5 13.7 %all-to-all-start.1 = ((bf16[4,80,1024]{2,0,1:T(4,128)(2,1)}), bf16[4,80,1024]{2,0,1:T(4,128)(2,1)S(1)}, u32[]{:S(2)}, u32[]{:S(2)}) async-start(bf16[4,80,1024]{2,0,1:T(4,128)(2,1)} %copy.73), calls=%async_computation.1 | async-start | bytes 1310720 | tf_op jit(solution)/shard_map/all_to_all | solution.py:100
  35.0 14.5 %copy-start.8 = (f32[4]{0:T(128)}, f32[4]{0:T(128)S(1)}, u32[]{:S(2)}) copy-start(f32[4]{0:T(128)S(1)} %convert_element_type.74) | copy-start | bytes 52
  49.5 15.1 %all-to-all-start.2 = ((bf16[16,20,1024]{2,1,0:T(8,128)(2,1)}), bf16[16,20,1024]{2,1,0:T(8,128)(2,1)S(1)}, u32[]{:S(2)}, u32[]{:S(2)}) async-start(bf16[16,20,1024]{2,1,0:T(8,128)(2,1)} %copy.76), calls=%async_computation.2 | async-start | bytes 1572864 | tf_op jit(solution)/shard_map/all_to_all | solution.py:104
  65.3 18.9 %collective-permute-start.1 = (bf16[4,80,1024]{2,1,0:T(8,128)(2,1)S(1)}, bf16[4,80,1024]{2,1,0:T(8,128)(2,1)}, u32[]{:S(2)}, u32[]{:S(2)}) collective-permute-start(bf16[4,80,1024]{2,1,0:T(8,128)(2,1)S(1)} %copy.80), channel_id=1, source_target_pairs={{4,0},{8,4},{12,8},{16,12},{20,16},{24,20},{28,24},{5,1},{9,5},{13... | collective-permute-start | bytes 1966088 | tf_op jit(solution)/shard_map/ppermute | solution.py:109
  66.6 29.8 %collective-permute-start = (bf16[4,80,1024]{2,1,0:T(8,128)(2,1)S(1)}, bf16[4,80,1024]{2,1,0:T(8,128)(2,1)}, u32[]{:S(2)}, u32[]{:S(2)}) collective-permute-start(bf16[4,80,1024]{2,1,0:T(8,128)(2,1)S(1)} %copy.80), channel_id=1, source_target_pairs={{0,4},{4,8},{8,12},{12,16},{16,20},{20,24},{24,28},{1,5},{5,9},{9,... | collective-permute-start | bytes 1966088 | tf_op jit(solution)/shard_map/ppermute | solution.py:108
  72.1 6.3 %copy-start.1 = (f32[256,256]{1,0:T(8,128)S(1)}, f32[256,256]{1,0:T(8,128)}, u32[]{:S(2)}) copy-start(f32[256,256]{1,0:T(8,128)} %abs_convert_fusion) | copy-start | bytes 786436
  96.5 11.7 %copy-start.2 = (bf16[4,3,16,16]{2,3,0,1:T(8,128)(2,1)S(1)}, bf16[4,3,16,16]{2,3,0,1:T(8,128)(2,1)}, u32[]{:S(2)}) copy-start(bf16[4,3,16,16]{2,3,0,1:T(8,128)(2,1)} %select_convert_fusion.5) | copy-start | bytes 18436
  96.5 11.7 %copy-start.7 = (f32[4]{0:T(128)S(1)}, f32[4]{0:T(128)}, u32[]{:S(2)}) copy-start(f32[4]{0:T(128)} %copy-done.6) | copy-start | bytes 52
  96.5 11.7 %copy-start.9 = (f32[4]{0:T(128)S(1)}, f32[4]{0:T(128)}, u32[]{:S(2)}) copy-start(f32[4]{0:T(128)} %copy-done.8) | copy-start | bytes 52
  128.1 1.3 collective-permute-start.2
  129.4 4.1 %collective-permute-start.3 = (f32[80,80]{0,1:T(8,128)S(1)}, f32[80,80]{0,1:T(8,128)S(1)}, u32[]{:S(2)}, u32[]{:S(2)}) collective-permute-start(f32[80,80]{0,1:T(8,128)S(1)} %fusion.95), channel_id=1, source_target_pairs={{0,2},{1,3},{2,0},{3,1},{4,6},{5,7},{6,4},{7,5},{8,10},{9,11},{10,... | collective-permute-start | bytes 76808 | tf_op jit(solution)/shard_map/ppermute | solution.py:39
  133.5 4.6 %collective-permute-start.4 = (f32[80,80]{0,1:T(8,128)S(1)}, f32[80,80]{0,1:T(8,128)S(1)}, u32[]{:S(2)}, u32[]{:S(2)}) collective-permute-start(f32[80,80]{0,1:T(8,128)S(1)} %add.91), channel_id=1, source_target_pairs={{0,4},{4,0},{8,12},{12,8},{16,20},{20,16},{24,28},{28,24},{1,5},{5... | collective-permute-start | bytes 76808 | tf_op jit(solution)/shard_map/ppermute | solution.py:39
  138.1 4.0 %collective-permute-start.5 = (f32[80,80]{0,1:T(8,128)S(1)}, f32[80,80]{0,1:T(8,128)S(1)}, u32[]{:S(2)}, u32[]{:S(2)}) collective-permute-start(f32[80,80]{0,1:T(8,128)S(1)} %add.92), channel_id=1, source_target_pairs={{0,8},{4,12},{8,0},{12,4},{16,24},{20,28},{24,16},{28,20},{1,9},{5... | collective-permute-start | bytes 76808 | tf_op jit(solution)/shard_map/ppermute | solution.py:39
  142.1 4.9 %collective-permute-start.6 = (f32[80,80]{0,1:T(8,128)S(1)}, f32[80,80]{0,1:T(8,128)S(1)}, u32[]{:S(2)}, u32[]{:S(2)}) collective-permute-start(f32[80,80]{0,1:T(8,128)S(1)} %add.93), channel_id=1, source_target_pairs={{0,16},{4,20},{8,24},{12,28},{16,0},{20,4},{24,8},{28,12},{1,17},{... | collective-permute-start | bytes 76808 | tf_op jit(solution)/shard_map/ppermute | solution.py:39

commit v8 on v7

--- a/solution.py
+++ b/solution.py
@@ -39,6 +39,21 @@
             value = value + lax.ppermute(value, name, [(i, i ^ bit) for i in range(size)])
             bit *= 2
     return value
+
+
+def spread(mix, cells, keep, taps_rows, col_count, row_count):
+    rows = cells % row_count
+    cols = cells // row_count
+    row_hit = (rows[:, None] == jnp.arange(row_count, dtype=jnp.int32)[None, :]) & keep[:, None]
+    slot_taps = jnp.einsum(
+        "sy,kyz->ksz", row_hit.astype(jnp.bfloat16), taps_rows,
+        preferred_element_type=jnp.float32,
+    ).astype(jnp.bfloat16)
+    col_hit = cols[:, None] == jnp.arange(col_count, dtype=jnp.int32)[None, :]
+    weights = jnp.where(col_hit[None, :, :, None], slot_taps[:, :, None, :], 0).astype(jnp.bfloat16)
+    return jnp.einsum(
+        "kms,ksxz->kmxz", mix, weights, preferred_element_type=jnp.float32
+    ).astype(jnp.bfloat16)
 
 
 def gram_of(panel):
@@ -114,14 +129,12 @@
     taps_cols = taps_table(radius, wide_iota[:, None] - col_count - col_iota[None, :])
     taps_cols = taps_cols.reshape(lev_dev, 3, col_count, col_count)
 
-    own = level_mix
     if packed:
+        own = spread(level_mix, cell_index, own_keep, taps_rows, col_count, row_count)
+    else:
         own = jnp.einsum(
-            "kms,sxy->kmxy", own, own_hits(), preferred_element_type=jnp.float32
+            "kmxy,kyz->kmxz", level_mix, taps_rows, preferred_element_type=jnp.float32
         ).astype(jnp.bfloat16)
-    own = jnp.einsum(
-        "kmxy,kyz->kmxz", own, taps_rows, preferred_element_type=jnp.float32
-    ).astype(jnp.bfloat16)
     own = jnp.einsum(
         "kmey,kex->kmxy", own, taps_cols[:, 1], preferred_element_type=jnp.float32
     )
@@ -130,15 +143,13 @@
     sides = jnp.stack([from_left, from_right])
     if packed:
         side_cells = near[0::2]
-        side_hits = one_hot(side_cells, first_hits(side_cells), cell_count)
+        sides = jax.vmap(spread, in_axes=(0, 0, 0, None, None, None))(
+            sides, side_cells, first_hits(side_cells), taps_rows, col_count, row_count
+        )
+    else:
         sides = jnp.einsum(
-            "tkms,tsxy->tkmxy", sides,
-            side_hits.reshape(2, slots, col_count, row_count),
-            preferred_element_type=jnp.float32,
+            "tkmxy,kyz->tkmxz", sides, taps_rows, preferred_element_type=jnp.float32
         ).astype(jnp.bfloat16)
-    sides = jnp.einsum(
-        "tkmxy,kyz->tkmxz", sides, taps_rows, preferred_element_type=jnp.float32
-    ).astype(jnp.bfloat16)
     smooth_x = jnp.einsum(
         "tkmey,ktex->kmxy", sides, taps_cols[:, 0::2], preferred_element_type=jnp.float32
     )

time: 157 us -> 155 us (0.987)
  waiting for transfers between devices: 47.3 us -> 34.1 us
  local copies, waits for them, and re-layouts: 12.2 us -> 22.4 us
  other arithmetic: 22.6 us -> 20.3 us
  matrix products: 46.9 us -> 49.1 us
    dot_general x2 -> x4, matrix products: 17.9 us -> 32.8 us  [the longest x2 25 us: spread(): jnp.einsum('kms,ksxz->kmxz', mix, weights, preferred_element_type=jnp.flo...]
    dot_general x1, matrix products: 12.7 us -> 1.64 us  [shards(): jnp.einsum('tkmey,ktex->kmxy', sides, taps_cols[:, 0::2], preferred_eleme...]
    convert_element_type x0 -> x2, local copies, waits for them, and re-layouts: none -> 10.2 us  [spread(): slot_taps = jnp.einsum('sy,kyz->ksz', row_hit.astype(jnp.bfloat16), taps_...]
    all_to_all x1, waiting for transfers between devices: 8.49 us -> 0.01 us  [shards(): lax.all_to_all(local_mix.astype(jnp.bfloat16), 'lev', split_axis=0, conca...]
    all_to_all x1, waiting for transfers between devices: 9.44 us -> 2.97 us  [shards(): lax.all_to_all(member_forcing, 'lev', split_axis=1, concat_axis=0, tiled=...]
    ppermute x1, waiting for transfers between devices: 0.01 us -> 2.8 us  [shards(): lax.ppermute(level_mix, 'tile', [(i + 1, i) for i in range(ends)])]
    concatenate x1, other arithmetic: 2.98 us -> 0.45 us  [gram_of(): parts = jnp.concatenate([high, low], axis=1)]
    dot_general x1, matrix products: 5.95 us -> 4.32 us  [shards(): jnp.einsum('kmey,kex->kmxy', own, taps_cols[:, 1], preferred_element_type...]
  transfers between devices with their start and end apart: 10 -> 10, of which waited for: 9 -> 9; matrix products, arithmetic and copies ran while one was open for 12% -> 23% of each run, Pallas kernels for 0% -> 0%
where the time goes in v8:
time: 155 us; the launch traced here: 154 us
  matrix products  49.1 us (32%)
  waiting for transfers between devices  34.1 us (22%)
  starting transfers between devices  26.8 us (17%)
  local copies, waits for them, and re-layouts  22.4 us (14%)
  other arithmetic  20.3 us (13%)
    dot_general x2, matrix products, spread(): jnp.einsum('kms,ksxz->kmxz', mix, weights, preferred_element_type=jnp.flo...  25 us
    ppermute x1, waiting for transfers between devices, shards(): lax.ppermute(level_mix, 'tile', [(i, i + 1) for i in range(ends)])  12.9 us
    ppermute x5, waiting for transfers between devices, all_sum(): lax.ppermute(value, name, [(i, i ^ bit) for i in range(size)])  12.2 us
    convert_element_type x2, local copies, waits for them, and re-layouts, spread(): slot_taps = jnp.einsum('sy,kyz->ksz', row_hit.astype(jnp.bfloat16), taps_...  10.2 us
    another operation x3, other arithmetic, shards(): r_factor = jnp.linalg.cholesky(gram_total).T  7.98 us
    dot_general x2, matrix products, spread(): jnp.einsum('sy,kyz->ksz', row_hit.astype(jnp.bfloat16), taps_rows, prefer...  7.77 us
    all_to_all x1, starting transfers between devices, shards(): lax.all_to_all(outgoing, 'tile', split_axis=1, concat_axis=1, tiled=True)  7.25 us
    ppermute x5, starting transfers between devices, all_sum(): lax.ppermute(value, name, [(i, i ^ bit) for i in range(size)])  6.53 us
  transfers between devices with their start and end apart: 10, of which 9 were waited for; matrix products, arithmetic and copies ran while one was open for 23% of the time, Pallas kernels for 0%

profile of v8, /device:TPU:0, one launch (start us, length us, event | category | flops | bytes accessed | tf_op | source)
XLA Modules:
  0.0 153.6 jit_solution(16063443798432347680)
XLA Ops:
  0.6 0.8 compare_and_fusion.1
  1.5 0.7 fusion.75
  2.2 0.8 slice_bitcast_fusion.9
  2.9 0.8 slice_bitcast_fusion.7
  3.7 0.8 copy.71
  4.6 2.8 %gather_fusion = f32[1024,4]{1,0:T(8,128)S(1)} fusion(f32[4,512]{0,1:T(8,128)S(1)} %copy.71, s32[1024]{0:T(1024)S(1)} %fusion.75), kind=kCustom, calls=%fused_computation | custom fusion | bytes 36864 | tf_op jit(solution)/shard_map/jit(_take)/gather | solution.py:83
  7.6 0.8 select_bitcast_fusion.1
  8.3 0.7 add_convert_fusion
  9.7 7.3 %all-to-all-start = ((f32[7,8,128]{2,0,1:T(8,128)}), f32[7,8,128]{2,0,1:T(8,128)S(1)}, u32[]{:S(2)}, u32[]{:S(2)}) async-start(f32[7,8,128]{2,0,1:T(8,128)} %pad_maximum_fusion.1), calls=%async_computation | async-start | bytes 65536 | tf_op jit(solution)/shard_map/all_to_all | solution.py:90
  16.9 0.7 broadcast_add_fusion
  17.6 0.7 convert_element_type.81
  18.3 0.7 abs_convert_fusion
  19.0 1.3 iota_compare_fusion
  20.4 3.2 %all-to-all-done = f32[7,8,128]{2,0,1:T(8,128)S(1)} async-done(((f32[7,8,128]{2,0,1:T(8,128)}), f32[7,8,128]{2,0,1:T(8,128)S(1)}, u32[]{:S(2)}, u32[]{:S(2)}) %all-to-all-start) | async-done | bytes 28704 | tf_op jit(solution)/shard_map/all_to_all | solution.py:90
  24.3 1.3 fusion.17
  25.7 4.4 %fusion.50 = bf16[4,80,1024]{2,1,0:T(8,128)(2,1)S(1)} fusion(bf16[4,80,16,256]{3,2,1,0:T(8,128)(2,1)S(1)} %copy-done, s32[16,256]{1,0:T(8,128)S(1)} %multiply_add_fusion, s32[1024]{0:T(1024)S(1)} %slice_bitcast_fusion.5, pred[1024]{0:T(1024)(128)(4,1)S(1)} %not.14, f32[4,1024]{1,0:T(4,128)S(1)} %fusion.17), kind=kOutput, calls=%fused_computation.46 | convolution fusion | flops 2693398528 | bytes 3314688 | tf_op jit(solution)/shard_map/lmxy,sxy->lms/dot_general | solution.py:105
  30.1 1.4 copy.76
  31.5 3.5 %all-to-all-start.1 = ((bf16[4,80,1024]{2,0,1:T(4,128)(2,1)}), bf16[4,80,1024]{2,0,1:T(4,128)(2,1)S(1)}, u32[]{:S(2)}, u32[]{:S(2)}) async-start(bf16[4,80,1024]{2,0,1:T(4,128)(2,1)} %copy.76), calls=%async_computation.1 | async-start | bytes 1310720 | tf_op jit(solution)/shard_map/all_to_all | solution.py:115
  35.0 3.1 %and_reduce_fusion = pred[2,1024]{1,0:T(4,128)(4,1)S(1)} fusion(s32[2,1024]{1,0:T(2,128)S(1)} %slice.80, pred[1024,1024]{1,0:T(8,128)(4,1)} %iota_compare_fusion), kind=kLoop, calls=%fused_computation.18 | loop fusion | flops 6289408 | bytes 1058816 | tf_op jit(solution)/shard_map/reduce_or | solution.py:24
  38.1 4.1 %convert_bitcast_fusion = bf16[2,4,1024,256]{2,3,1,0:T(8,128)(2,1)} fusion(s32[2,1024]{1,0:T(2,128)S(1)} %get-tuple-element.14, pred[2,1024]{1,0:T(4,128)(4,1)S(1)} %not.15, f32[4]{0:T(128)S(1)} %broadcast_add_fusion, f32[256,256]{0,1:T(8,128)} %abs_convert_fusion, f32[4]{0:T(128)S(1)} %convert_element_type.81), kind=kOutput, calls=%fused_computation.30 | convolution fusion | flops 1078198272 | bytes 4466720 | tf_op jit(solution)/shard_map/vmap(sy,kyz->ksz)/dot_general | solution.py:48
  42.2 3.0 %all-to-all-done.1 = bf16[4,80,1024]{2,0,1:T(4,128)(2,1)S(1)} async-done(((bf16[4,80,1024]{2,0,1:T(4,128)(2,1)}), bf16[4,80,1024]{2,0,1:T(4,128)(2,1)S(1)}, u32[]{:S(2)}, u32[]{:S(2)}) %all-to-all-start.1) | async-done | bytes 655392 | tf_op jit(solution)/shard_map/all_to_all | solution.py:115
  45.2 1.2 copy.77
  46.4 1.5 all_to_all.33
  48.3 1.3 copy.79
  49.5 3.7 %all-to-all-start.2 = ((bf16[16,20,1024]{2,1,0:T(8,128)(2,1)}), bf16[16,20,1024]{2,1,0:T(8,128)(2,1)S(1)}, u32[]{:S(2)}, u32[]{:S(2)}) async-start(bf16[16,20,1024]{2,1,0:T(8,128)(2,1)} %copy.79), calls=%async_computation.2 | async-start | bytes 1572864 | tf_op jit(solution)/shard_map/all_to_all | solution.py:119
  53.2 3.6 %convert_bitcast_fusion.1 = bf16[4,1024,256]{1,2,0:T(8,128)(2,1)} fusion(s32[1024]{0:T(1024)S(1)} %get-tuple-element.12, pred[1024]{0:T(1024)(128)(4,1)S(1)} %not.14, f32[4]{0:T(128)S(1)} %broadcast_add_fusion, f32[256,256]{0,1:T(8,128)} %abs_convert_fusion, f32[4]{0:T(128)S(1)} %convert_element_type.81), kind=kOutput, calls=%fused_computation.38 | convolution fusion | flops 539754496 | bytes 2364448 | tf_op jit(solution)/shard_map/sy,kyz->ksz/dot_general | solution.py:48
  56.8 4.0 %copy.81 = bf16[4,1024,256]{2,1,0:T(8,128)(2,1)} copy(bf16[4,1024,256]{1,2,0:T(8,128)(2,1)} %convert_bitcast_fusion.1) | data formatting | bytes 4194304 | tf_op jit(solution)/shard_map/convert_element_type | solution.py:51
  60.8 6.2 %copy.86 = bf16[2,4,1024,256]{3,2,1,0:T(8,128)(2,1)} copy(bf16[2,4,1024,256]{2,3,1,0:T(8,128)(2,1)} %convert_bitcast_fusion) | data formatting | bytes 8388608 | tf_op jit(solution)/shard_map/vmap()/convert_element_type | solution.py:51
  67.8 1.3 collective-permute-start.1
  69.1 4.6 %collective-permute-start = (bf16[4,80,1024]{2,1,0:T(8,128)(2,1)S(1)}, bf16[4,80,1024]{2,1,0:T(8,128)(2,1)S(1)}, u32[]{:S(2)}, u32[]{:S(2)}) collective-permute-start(bf16[4,80,1024]{2,1,0:T(8,128)(2,1)S(1)} %copy.84), channel_id=1, source_target_pairs={{0,4},{4,8},{8,12},{12,16},{16,20},{20,24},{24,28},{1,5},{5,9},{9,... | collective-permute-start | bytes 1966088 | tf_op jit(solution)/shard_map/ppermute | solution.py:123
  73.7 10.1 %fusion.37 = bf16[4,80,16,256]{3,1,2,0:T(8,128)(2,1)} fusion(pred[1024,16]{0,1:T(8,128)(4,1)S(1)} %iota_compare_fusion.4, bf16[4,1024,256]{2,1,0:T(8,128)(2,1)} %copy.81, bf16[4,80,1024,1]{2,0,1,3:T(4,128)(2,1)S(1)} %bitcast.142), kind=kOutput, calls=%fused_computation.43 | convolution fusion | flops 2702442496 | bytes 5390336 | tf_op jit(solution)/shard_map/kms,ksxz->kmxz/dot_general | solution.py:54
  83.8 2.8 %collective-permute-done.1 = bf16[4,80,1024]{2,1,0:T(8,128)(2,1)S(1)} collective-permute-done((bf16[4,80,1024]{2,1,0:T(8,128)(2,1)S(1)}, bf16[4,80,1024]{2,1,0:T(8,128)(2,1)S(1)}, u32[]{:S(2)}, u32[]{:S(2)}) %collective-permute-start.1) | collective-permute-done | bytes 655392 | tf_op jit(solution)/shard_map/ppermute | solution.py:124
  86.6 12.9 %collective-permute-done = bf16[4,80,1024]{2,1,0:T(8,128)(2,1)S(1)} collective-permute-done((bf16[4,80,1024]{2,1,0:T(8,128)(2,1)S(1)}, bf16[4,80,1024]{2,1,0:T(8,128)(2,1)S(1)}, u32[]{:S(2)}, u32[]{:S(2)}) %collective-permute-start) | collective-permute-done | bytes 655392 | tf_op jit(solution)/shard_map/ppermute | solution.py:123
  99.6 14.9 %fusion.24 = bf16[2,4,80,16,256]{4,2,3,1,0:T(8,128)(2,1)S(1)} fusion(pred[2,1024,16]{1,2,0:T(8,128)(4,1)S(1)} %iota_compare_fusion.3, bf16[2,4,1024,256]{3,2,1,0:T(8,128)(2,1)S(1)} %copy-done.1, bf16[2,4,80,1024,1]{3,2,4,1,0:T(8,128)(2,1)S(1)} %maximum_bitcast_fusion.5), kind=kOutput, calls=%fused_computation.33 | convolution fusion | flops 5404884992 | bytes 10780672 | tf_op jit(solution)/shard_map/vmap(kms,ksxz->kmxz)/dot_general | solution.py:54
  114.6 1.6 %fusion.21 = f32[4,16,80,256,1]{3,1,4,2,0:T(8,128)S(1)} fusion(bf16[2,4,80,16,256]{4,2,3,1,0:T(8,128)(2,1)S(1)} %fusion.24, bf16[4,3,16,16]{2,3,0,1:T(8,128)(2,1)S(1)} %select_convert_fusion.3), kind=kOutput, calls=%fused_computation.27 | convolution fusion | flops 83886080 | bytes 10518528 | tf_op jit(solution)/shard_map/tkmey,ktex->kmxy/dot_general | solution.py:153
  116.3 4.3 %subtract_convert_fusion = (bf16[4,80,16,256]{3,2,1,0:T(8,128)(2,1)S(1)}, bf16[4,80,16,256]{3,2,1,0:T(8,128)(2,1)S(1)}, f32[4,80,16,256]{3,2,1,0:T(8,128)}) fusion(f32[4,16,80,256,1]{3,1,4,2,0:T(8,128)S(1)} %fusion.21, f32[4,80,16,256]{3,2,1,0:T(8,128)S(1)} %bitcast.138, bf16[4,80,16,256]{3,1,2,0:T(8,128)(2,1)S(1)} %copy-done.2, ...), kind=kOutput, calls=%fused_computation.29 | convolution fusion | flops 49807360 | bytes 23609344 | tf_op jit(solution)/shard_map/kmey,kex->kmxy/dot_general | solution.py:138
  121.1 4.2 %fusion.58 = f32[160,160]{0,1:T(8,128)S(1)} fusion(bf16[4,160,16,256]{3,2,1,0:T(8,128)(2,1)S(1)} %pad_maximum_fusion), kind=kOutput, calls=%fused_computation.52 | convolution fusion | flops 838860800 | bytes 5345280 | tf_op jit(solution)/shard_map/kpxy,kqxy->pq/dot_general | solution.py:64
  125.4 1.2 collective-permute-done.2
  126.7 1.7 %collective-permute-start.3 = (f32[80,80]{0,1:T(8,128)S(1)}, f32[80,80]{0,1:T(8,128)S(1)}, u32[]{:S(2)}, u32[]{:S(2)}) collective-permute-start(f32[80,80]{0,1:T(8,128)S(1)} %fusion.85), channel_id=1, source_target_pairs={{0,2},{1,3},{2,0},{3,1},{4,6},{5,7},{6,4},{7,5},{8,10},{9,11},{10,... | collective-permute-start | bytes 76808 | tf_op jit(solution)/shard_map/ppermute | solution.py:39
  128.5 2.3 %collective-permute-done.3 = f32[80,80]{0,1:T(8,128)S(1)} collective-permute-done((f32[80,80]{0,1:T(8,128)S(1)}, f32[80,80]{0,1:T(8,128)S(1)}, u32[]{:S(2)}, u32[]{:S(2)}) %collective-permute-start.3) | collective-permute-done | bytes 25632 | tf_op jit(solution)/shard_map/ppermute | solution.py:39
  130.8 2.5 %collective-permute-start.4 = (f32[80,80]{0,1:T(8,128)S(1)}, f32[80,80]{0,1:T(8,128)S(1)}, u32[]{:S(2)}, u32[]{:S(2)}) collective-permute-start(f32[80,80]{0,1:T(8,128)S(1)} %add.114), channel_id=1, source_target_pairs={{0,4},{4,0},{8,12},{12,8},{16,20},{20,16},{24,28},{28,24},{1,5},{5... | collective-permute-start | bytes 76808 | tf_op jit(solution)/shard_map/ppermute | solution.py:39
  133.3 2.0 %collective-permute-done.4 = f32[80,80]{0,1:T(8,128)S(1)} collective-permute-done((f32[80,80]{0,1:T(8,128)S(1)}, f32[80,80]{0,1:T(8,128)S(1)}, u32[]{:S(2)}, u32[]{:S(2)}) %collective-permute-start.4) | collective-permute-done | bytes 25632 | tf_op jit(solution)/shard_map/ppermute | solution.py:39
  135.3 1.1 collective-permute-start.5
  136.3 3.0 %collective-permute-done.5 = f32[80,80]{0,1:T(8,128)S(1)} collective-permute-done((f32[80,80]{0,1:T(8,128)S(1)}, f32[80,80]{0,1:T(8,128)S(1)}, u32[]{:S(2)}, u32[]{:S(2)}) %collective-permute-start.5) | collective-permute-done | bytes 25632 | tf_op jit(solution)/shard_map/ppermute | solution.py:39
  139.3 1.2 collective-permute-start.6
  140.5 3.7 %collective-permute-done.6 = f32[80,80]{0,1:T(8,128)S(1)} collective-permute-done((f32[80,80]{0,1:T(8,128)S(1)}, f32[80,80]{0,1:T(8,128)S(1)}, u32[]{:S(2)}, u32[]{:S(2)}) %collective-permute-start.6) | collective-permute-done | bytes 25632 | tf_op jit(solution)/shard_map/ppermute | solution.py:39
  144.3 7.3 %cholesky.18 = f32[80,80]{1,0:T(8,128)S(1)} custom-call(f32[80,80]{1,0:T(8,128)S(1)} %fusion.72), custom_call_target="Cholesky" | custom-call | tf_op jit(solution)/shard_map/jit(cholesky)/cholesky | solution.py:162
  152.9 0.7 copy.96
  (52 shorter events, 5.2 us)
Async XLA Ops:
  0.6 25.1 %copy-start = (bf16[4,80,16,256]{3,2,1,0:T(8,128)(2,1)S(1)}, bf16[4,80,16,256]{3,2,1,0:T(8,128)(2,1)}, u32[]{:S(2)}) copy-start(bf16[4,80,16,256]{3,2,1,0:T(8,128)(2,1)} %param.14) | copy-start | bytes 7864324
  9.7 13.9 %all-to-all-start = ((f32[7,8,128]{2,0,1:T(8,128)}), f32[7,8,128]{2,0,1:T(8,128)S(1)}, u32[]{:S(2)}, u32[]{:S(2)}) async-start(f32[7,8,128]{2,0,1:T(8,128)} %pad_maximum_fusion.1), calls=%async_computation | async-start | bytes 65536 | tf_op jit(solution)/shard_map/all_to_all | solution.py:90
  31.5 13.7 %all-to-all-start.1 = ((bf16[4,80,1024]{2,0,1:T(4,128)(2,1)}), bf16[4,80,1024]{2,0,1:T(4,128)(2,1)S(1)}, u32[]{:S(2)}, u32[]{:S(2)}) async-start(bf16[4,80,1024]{2,0,1:T(4,128)(2,1)} %copy.76), calls=%async_computation.1 | async-start | bytes 1310720 | tf_op jit(solution)/shard_map/all_to_all | solution.py:115
  38.1 9.8 %copy-start.3 = (bf16[16,16]{1,0:T(8,128)(2,1)S(1)}, bf16[16,16]{1,0:T(8,128)(2,1)}, u32[]{:S(2)}) copy-start(bf16[16,16]{1,0:T(8,128)(2,1)} %param.15) | copy-start | bytes 1540
  49.5 17.5 %all-to-all-start.2 = ((bf16[16,20,1024]{2,1,0:T(8,128)(2,1)}), bf16[16,20,1024]{2,1,0:T(8,128)(2,1)S(1)}, u32[]{:S(2)}, u32[]{:S(2)}) async-start(bf16[16,20,1024]{2,1,0:T(8,128)(2,1)} %copy.79), calls=%async_computation.2 | async-start | bytes 1572864 | tf_op jit(solution)/shard_map/all_to_all | solution.py:119
  67.8 18.8 %collective-permute-start.1 = (bf16[4,80,1024]{2,1,0:T(8,128)(2,1)S(1)}, bf16[4,80,1024]{2,1,0:T(8,128)(2,1)S(1)}, u32[]{:S(2)}, u32[]{:S(2)}) collective-permute-start(bf16[4,80,1024]{2,1,0:T(8,128)(2,1)S(1)} %copy.84), channel_id=1, source_target_pairs={{4,0},{8,4},{12,8},{16,12},{20,16},{24,20},{28,24},{5,1},{9,5},{13... | collective-permute-start | bytes 1966088 | tf_op jit(solution)/shard_map/ppermute | solution.py:124
  69.1 30.4 %collective-permute-start = (bf16[4,80,1024]{2,1,0:T(8,128)(2,1)S(1)}, bf16[4,80,1024]{2,1,0:T(8,128)(2,1)S(1)}, u32[]{:S(2)}, u32[]{:S(2)}) collective-permute-start(bf16[4,80,1024]{2,1,0:T(8,128)(2,1)S(1)} %copy.84), channel_id=1, source_target_pairs={{0,4},{4,8},{8,12},{12,16},{16,20},{20,24},{24,28},{1,5},{5,9},{9,... | collective-permute-start | bytes 1966088 | tf_op jit(solution)/shard_map/ppermute | solution.py:123
  73.7 25.9 %copy-start.1 = (bf16[2,4,1024,256]{3,2,1,0:T(8,128)(2,1)S(1)}, bf16[2,4,1024,256]{3,2,1,0:T(8,128)(2,1)}, u32[]{:S(2)}) copy-start(bf16[2,4,1024,256]{3,2,1,0:T(8,128)(2,1)} %copy.86) | copy-start | bytes 12582916
  99.5 16.7 %slice-start = ((s8[5242880]{0:T(1024)(128)(4,1)}), s8[4194304]{0:T(1024)(128)(4,1)S(1)}, s32[]{:S(2)}) async-start(s8[5242880]{0:T(1024)(128)(4,1)} %bitcast.137), calls=%async_computation.3 | async-start | bytes 8388608
  99.6 16.6 %slice-start.1 = ((s8[5242880]{0:T(1024)(128)(4,1)}), s8[1048576]{0:T(1024)(128)(4,1)S(1)}, s32[]{:S(2)}) async-start(s8[5242880]{0:T(1024)(128)(4,1)} %bitcast.137), calls=%async_computation.4 | async-start | bytes 2097152
  114.6 1.7 %copy-start.2 = (bf16[4,80,16,256]{3,1,2,0:T(8,128)(2,1)S(1)}, bf16[4,80,16,256]{3,1,2,0:T(8,128)(2,1)}, u32[]{:S(2)}) copy-start(bf16[4,80,16,256]{3,1,2,0:T(8,128)(2,1)} %fusion.37) | copy-start | bytes 7864324
  125.4 1.3 collective-permute-start.2
  126.7 4.1 %collective-permute-start.3 = (f32[80,80]{0,1:T(8,128)S(1)}, f32[80,80]{0,1:T(8,128)S(1)}, u32[]{:S(2)}, u32[]{:S(2)}) collective-permute-start(f32[80,80]{0,1:T(8,128)S(1)} %fusion.85), channel_id=1, source_target_pairs={{0,2},{1,3},{2,0},{3,1},{4,6},{5,7},{6,4},{7,5},{8,10},{9,11},{10,... | collective-permute-start | bytes 76808 | tf_op jit(solution)/shard_map/ppermute | solution.py:39
  130.8 4.5 %collective-permute-start.4 = (f32[80,80]{0,1:T(8,128)S(1)}, f32[80,80]{0,1:T(8,128)S(1)}, u32[]{:S(2)}, u32[]{:S(2)}) collective-permute-start(f32[80,80]{0,1:T(8,128)S(1)} %add.114), channel_id=1, source_target_pairs={{0,4},{4,0},{8,12},{12,8},{16,20},{20,16},{24,28},{28,24},{1,5},{5... | collective-permute-start | bytes 76808 | tf_op jit(solution)/shard_map/ppermute | solution.py:39
  135.3 4.0 %collective-permute-start.5 = (f32[80,80]{0,1:T(8,128)S(1)}, f32[80,80]{0,1:T(8,128)S(1)}, u32[]{:S(2)}, u32[]{:S(2)}) collective-permute-start(f32[80,80]{0,1:T(8,128)S(1)} %add.115), channel_id=1, source_target_pairs={{0,8},{4,12},{8,0},{12,4},{16,24},{20,28},{24,16},{28,20},{1,9},{5... | collective-permute-start | bytes 76808 | tf_op jit(solution)/shard_map/ppermute | solution.py:39
  139.3 4.9 %collective-permute-start.6 = (f32[80,80]{0,1:T(8,128)S(1)}, f32[80,80]{0,1:T(8,128)S(1)}, u32[]{:S(2)}, u32[]{:S(2)}) collective-permute-start(f32[80,80]{0,1:T(8,128)S(1)} %add.116), channel_id=1, source_target_pairs={{0,16},{4,20},{8,24},{12,28},{16,0},{20,4},{24,8},{28,12},{1,17},{... | collective-permute-start | bytes 76808 | tf_op jit(solution)/shard_map/ppermute | solution.py:39

commit v9 on v8

--- a/solution.py
+++ b/solution.py
@@ -41,18 +41,15 @@
     return value
 
 
-def spread(mix, cells, keep, taps_rows, col_count, row_count):
+def spread(mix, cells, keep, radius, col_count, row_count):
     rows = cells % row_count
     cols = cells // row_count
-    row_hit = (rows[:, None] == jnp.arange(row_count, dtype=jnp.int32)[None, :]) & keep[:, None]
-    slot_taps = jnp.einsum(
-        "sy,kyz->ksz", row_hit.astype(jnp.bfloat16), taps_rows,
-        preferred_element_type=jnp.float32,
-    ).astype(jnp.bfloat16)
-    col_hit = cols[:, None] == jnp.arange(col_count, dtype=jnp.int32)[None, :]
-    weights = jnp.where(col_hit[None, :, :, None], slot_taps[:, :, None, :], 0).astype(jnp.bfloat16)
+    offsets = rows[:, None] - jnp.arange(row_count, dtype=jnp.int32)[None, :]
+    slot_taps = taps_table(radius, offsets) * keep[None, :, None].astype(jnp.bfloat16)
+    col_hit = cols[None, :] == jnp.arange(col_count, dtype=jnp.int32)[:, None]
+    placed = jnp.where(col_hit[None, None], mix[:, :, None, :], 0).astype(jnp.bfloat16)
     return jnp.einsum(
-        "kms,ksxz->kmxz", mix, weights, preferred_element_type=jnp.float32
+        "kmxs,ksz->kmxz", placed, slot_taps, preferred_element_type=jnp.float32
     ).astype(jnp.bfloat16)
 
 
@@ -130,7 +127,7 @@
     taps_cols = taps_cols.reshape(lev_dev, 3, col_count, col_count)
 
     if packed:
-        own = spread(level_mix, cell_index, own_keep, taps_rows, col_count, row_count)
+        own = spread(level_mix, cell_index, own_keep, radius, col_count, row_count)
     else:
         own = jnp.einsum(
             "kmxy,kyz->kmxz", level_mix, taps_rows, preferred_element_type=jnp.float32
@@ -144,7 +141,7 @@
     if packed:
         side_cells = near[0::2]
         sides = jax.vmap(spread, in_axes=(0, 0, 0, None, None, None))(
-            sides, side_cells, first_hits(side_cells), taps_rows, col_count, row_count
+            sides, side_cells, first_hits(side_cells), radius, col_count, row_count
         )
     else:
         sides = jnp.einsum(

time: 155 us -> 154 us (level)
  matrix products: 49.1 us -> 31.8 us
  waiting for transfers between devices: 34.1 us -> 50.2 us
  other arithmetic: 20.3 us -> 27 us
  local copies, waits for them, and re-layouts: 22.4 us -> 17.5 us
    dot_general x4 -> x0, matrix products: 32.8 us -> none  [the longest x2 25 us: spread(): jnp.einsum('kms,ksxz->kmxz', mix, weights, preferred_element_type=jnp.flo...]
    dot_general x1, matrix products: 1.64 us -> 13.9 us  [shards(): jnp.einsum('tkmey,ktex->kmxy', sides, taps_cols[:, 0::2], preferred_eleme...]
    convert_element_type x2 -> x0, local copies, waits for them, and re-layouts: 10.2 us -> none  [spread(): slot_taps = jnp.einsum('sy,kyz->ksz', row_hit.astype(jnp.bfloat16), taps_...]
    all_to_all x1, waiting for transfers between devices: 0.01 us -> 9.86 us  [shards(): lax.all_to_all(local_mix.astype(jnp.bfloat16), 'lev', split_axis=0, conca...]
    dot_general x1, matrix products: 4.32 us -> 7.58 us  [shards(): jnp.einsum('kmey,kex->kmxy', own, taps_cols[:, 1], preferred_element_type...]
    all_to_all x1, waiting for transfers between devices: 2.97 us -> 5.92 us  [shards(): lax.all_to_all(member_forcing, 'lev', split_axis=1, concat_axis=0, tiled=...]
    concatenate x1, other arithmetic: 0.45 us -> 2.98 us  [gram_of(): parts = jnp.concatenate([high, low], axis=1)]
    another operation x0 -> x1, local copies, waits for them, and re-layouts: none -> 2.51 us  [shards(): sides = jnp.stack([from_left, from_right])]
  transfers between devices with their start and end apart: 10 -> 10, of which waited for: 9 -> 10; matrix products, arithmetic and copies ran while one was open for 23% -> 11% of each run, Pallas kernels for 0% -> 0%
where the time goes in v9:
time: 154 us
  waiting for transfers between devices  50.2 us (33%)
  matrix products  31.8 us (21%)
  other arithmetic  27 us (18%)
  starting transfers between devices  26.3 us (17%)
  local copies, waits for them, and re-layouts  17.5 us (11%)
    dot_general x1, matrix products, shards(): jnp.einsum('tkmey,ktex->kmxy', sides, taps_cols[:, 0::2], preferred_eleme...  13.9 us
    ppermute x5, waiting for transfers between devices, all_sum(): lax.ppermute(value, name, [(i, i ^ bit) for i in range(size)])  13.4 us
    ppermute x1, waiting for transfers between devices, shards(): lax.ppermute(level_mix, 'tile', [(i, i + 1) for i in range(ends)])  13.1 us
    all_to_all x1, waiting for transfers between devices, shards(): lax.all_to_all(local_mix.astype(jnp.bfloat16), 'lev', split_axis=0, conca...  9.86 us
    another operation x3, other arithmetic, shards(): r_factor = jnp.linalg.cholesky(gram_total).T  7.98 us
    dot_general x1, matrix products, shards(): jnp.einsum('kmey,kex->kmxy', own, taps_cols[:, 1], preferred_element_type...  7.58 us
    all_to_all x1, starting transfers between devices, shards(): lax.all_to_all(outgoing, 'tile', split_axis=1, concat_axis=1, tiled=True)  7.25 us
    all_to_all x1, waiting for transfers between devices, shards(): lax.all_to_all(member_forcing, 'lev', split_axis=1, concat_axis=0, tiled=...  5.92 us
  transfers between devices with their start and end apart: 10, of which 10 were waited for; matrix products, arithmetic and copies ran while one was open for 11% of the time, Pallas kernels for 0%

profile of v9, /device:TPU:0, one launch (start us, length us, event | category | flops | bytes accessed | tf_op | source)
XLA Modules:
  0.0 153.6 jit_solution(9181340885904384289)
XLA Ops:
  0.6 0.8 compare_and_fusion.1
  1.5 0.7 fusion.96
  2.2 0.8 slice_bitcast_fusion.9
  2.9 0.8 slice_bitcast_fusion.7
  3.7 0.8 copy.68
  4.6 2.8 %gather_fusion = f32[1024,4]{1,0:T(8,128)S(1)} fusion(f32[4,512]{0,1:T(8,128)S(1)} %copy.68, s32[1024]{0:T(1024)S(1)} %fusion.96), kind=kCustom, calls=%fused_computation | custom fusion | bytes 36864 | tf_op jit(solution)/shard_map/jit(_take)/gather | solution.py:80
  7.6 0.8 select_bitcast_fusion.1
  8.3 0.7 add_convert_fusion
  9.7 7.3 %all-to-all-start = ((f32[7,8,128]{2,0,1:T(8,128)}), f32[7,8,128]{2,0,1:T(8,128)S(1)}, u32[]{:S(2)}, u32[]{:S(2)}) async-start(f32[7,8,128]{2,0,1:T(8,128)} %pad_maximum_fusion.2), calls=%async_computation | async-start | bytes 65536 | tf_op jit(solution)/shard_map/all_to_all | solution.py:87
  16.9 0.7 broadcast_add_fusion
  18.3 1.3 iota_compare_fusion
  19.7 4.0 %all-to-all-done = f32[7,8,128]{2,0,1:T(8,128)S(1)} async-done(((f32[7,8,128]{2,0,1:T(8,128)}), f32[7,8,128]{2,0,1:T(8,128)S(1)}, u32[]{:S(2)}, u32[]{:S(2)}) %all-to-all-start) | async-done | bytes 28704 | tf_op jit(solution)/shard_map/all_to_all | solution.py:87
  24.4 1.3 fusion.15
  25.7 4.4 %fusion.80 = bf16[4,80,1024]{2,1,0:T(8,128)(2,1)S(1)} fusion(bf16[4,80,16,256]{3,2,1,0:T(8,128)(2,1)S(1)} %copy-done, s32[16,256]{1,0:T(8,128)S(1)} %multiply_add_fusion, s32[1024]{0:T(1024)S(1)} %slice_bitcast_fusion.5, pred[1024]{0:T(1024)(128)(4,1)S(1)} %get-tuple-element.21, f32[4,1024]{1,0:T(4,128)S(1)} %fusion.15), kind=kOutput, calls=%fused_computation.55 | convolution fusion | flops 2693398528 | bytes 3314688 | tf_op jit(solution)/shard_map/lmxy,sxy->lms/dot_general | solution.py:102
  30.2 1.4 copy.73
  31.6 3.5 %all-to-all-start.1 = ((bf16[4,80,1024]{2,0,1:T(4,128)(2,1)}), bf16[4,80,1024]{2,0,1:T(4,128)(2,1)S(1)}, u32[]{:S(2)}, u32[]{:S(2)}) async-start(bf16[4,80,1024]{2,0,1:T(4,128)(2,1)} %copy.73), calls=%async_computation.1 | async-start | bytes 1310720 | tf_op jit(solution)/shard_map/all_to_all | solution.py:112
  35.1 1.2 abs_convert_fusion.1
  36.3 3.1 %and_reduce_fusion = pred[2,1024]{1,0:T(4,128)(4,1)S(1)} fusion(s32[2,1024]{1,0:T(2,128)S(1)} %slice.80, pred[1024,1024]{1,0:T(8,128)(4,1)} %iota_compare_fusion), kind=kLoop, calls=%fused_computation.17 | loop fusion | flops 6289408 | bytes 1058816 | tf_op jit(solution)/shard_map/reduce_or | solution.py:24
  39.4 5.9 %all-to-all-done.1 = bf16[4,80,1024]{2,0,1:T(4,128)(2,1)S(1)} async-done(((bf16[4,80,1024]{2,0,1:T(4,128)(2,1)}), bf16[4,80,1024]{2,0,1:T(4,128)(2,1)S(1)}, u32[]{:S(2)}, u32[]{:S(2)}) %all-to-all-start.1) | async-done | bytes 655392 | tf_op jit(solution)/shard_map/all_to_all | solution.py:112
  45.3 1.2 copy.74
  46.4 1.5 all_to_all.31
  48.3 1.3 copy.76
  49.6 3.5 %all-to-all-start.2 = ((bf16[16,20,1024]{2,1,0:T(8,128)(2,1)}), bf16[16,20,1024]{2,1,0:T(8,128)(2,1)S(1)}, u32[]{:S(2)}, u32[]{:S(2)}) async-start(bf16[16,20,1024]{2,1,0:T(8,128)(2,1)} %copy.76), calls=%async_computation.2 | async-start | bytes 1572864 | tf_op jit(solution)/shard_map/all_to_all | solution.py:116
  53.1 1.7 %abs_convert_fusion = f32[2,1024,256]{2,1,0:T(8,128)} fusion(s32[2,1024]{1,0:T(2,128)S(1)} %get-tuple-element.14), kind=kLoop, calls=%fused_computation.46 | loop fusion | flops 1572864 | bytes 2105344 | tf_op jit(solution)/shard_map/vmap()/convert_element_type | solution.py:11
  54.9 9.9 %all-to-all-done.2 = bf16[16,20,1024]{2,1,0:T(8,128)(2,1)S(1)} async-done(((bf16[16,20,1024]{2,1,0:T(8,128)(2,1)}), bf16[16,20,1024]{2,1,0:T(8,128)(2,1)S(1)}, u32[]{:S(2)}, u32[]{:S(2)}) %all-to-all-start.2) | async-done | bytes 655392 | tf_op jit(solution)/shard_map/all_to_all | solution.py:116
  64.7 1.4 copy.77
  66.1 2.1 %copy.78 = bf16[4,80,1024]{2,1,0:T(8,128)(2,1)} copy(bf16[4,80,1024]{2,0,1:T(4,128)(2,1)} %bitcast.30) | data formatting | bytes 1310720 | tf_op jit(solution)/shard_map/jit(_where)/broadcast_in_dim | solution.py:50
  68.2 1.3 collective-permute-start.1
  69.5 5.6 %collective-permute-start = (bf16[4,80,1024]{2,0,1:T(4,128)(2,1)}, bf16[4,80,1024]{2,0,1:T(4,128)(2,1)}, u32[]{:S(2)}, u32[]{:S(2)}) collective-permute-start(bf16[4,80,1024]{2,0,1:T(4,128)(2,1)} %bitcast.30), channel_id=1, source_target_pairs={{0,4},{4,8},{8,12},{12,16},{16,20},{20,24},{24,28},{1,5},{5,9},{9,... | collective-permute-start | bytes 1966088 | tf_op jit(solution)/shard_map/ppermute | solution.py:120
  75.1 7.6 %fusion.48 = f32[4,16,80,256]{3,1,2,0:T(8,128)} fusion(pred[16,1024]{1,0:T(8,128)(4,1)S(1)} %iota_compare_fusion.2, bf16[4,80,1024]{2,1,0:T(8,128)(2,1)} %copy.78, f32[4]{0:T(128)S(1)} %broadcast_add_fusion, f32[1024,256]{1,0:T(8,128)} %abs_convert_fusion.1, f32[4]{0:T(128)S(1)} %convert_element_type.92, bf16[1024]{0:T(1024)(128)(2,1)S(1)} %get-tuple-element.20, ...), kind=kOutput, calls=%fused_computation.41 | convolution fusion | flops 2739142656 | bytes 6982656 | tf_op jit(solution)/shard_map/kmey,kex->kmxy/dot_general | solution.py:135
  82.7 3.9 %collective-permute-done.1 = bf16[4,80,1024]{2,0,1:T(4,128)(2,1)S(1)} collective-permute-done((bf16[4,80,1024]{2,0,1:T(4,128)(2,1)}, bf16[4,80,1024]{2,0,1:T(4,128)(2,1)S(1)}, u32[]{:S(2)}, u32[]{:S(2)}) %collective-permute-start.1) | collective-permute-done | bytes 655392 | tf_op jit(solution)/shard_map/ppermute | solution.py:121
  86.6 13.1 %collective-permute-done = bf16[4,80,1024]{2,0,1:T(4,128)(2,1)} collective-permute-done((bf16[4,80,1024]{2,0,1:T(4,128)(2,1)}, bf16[4,80,1024]{2,0,1:T(4,128)(2,1)}, u32[]{:S(2)}, u32[]{:S(2)}) %collective-permute-start) | collective-permute-done | bytes 655392 | tf_op jit(solution)/shard_map/ppermute | solution.py:120
  99.6 2.1 %pad_maximum_fusion.1 = bf16[2,4,80,1024]{3,1,2,0:T(4,128)(2,1)S(1)} fusion(bf16[1,4,80,1024]{3,1,2,0:T(4,128)(2,1)S(1)} %bitcast.129, bf16[1,4,80,1024]{3,1,2,0:T(4,128)(2,1)} %bitcast.36), kind=kLoop, calls=%fused_computation.57 | loop fusion | flops 655360 | bytes 2621440 | tf_op jit(solution)/shard_map/stack | solution.py:140
  101.7 2.5 %copy.79 = bf16[2,4,80,1024]{3,0,2,1:T(2,128)(2,1)} copy(bf16[2,4,80,1024]{3,1,2,0:T(4,128)(2,1)S(1)} %pad_maximum_fusion.1) | data formatting | bytes 2621440 | tf_op jit(solution)/shard_map/stack | solution.py:140
  104.2 13.9 %subtract_convert_fusion = (bf16[4,80,16,256]{3,2,1,0:T(8,128)(2,1)}, bf16[4,80,16,256]{3,2,1,0:T(8,128)(2,1)}, f32[4,80,16,256]{3,2,1,0:T(8,128)}) fusion(f32[4]{0:T(128)S(1)} %broadcast_add_fusion, pred[2,16,1024]{2,1,0:T(8,128)(4,1)S(1)} %iota_compare_fusion.1, bf16[2,4,80,1024]{3,0,2,1:T(2,128)(2,1)} %copy.79, f32[2,1024,256]{2,1,0:T(8,128)} %abs_convert_fusion, ...), kind=kOutput, calls=%fused_computation.26 | convolution fusion | flops 5486149632 | bytes 24450048 | tf_op jit(solution)/shard_map/tkmey,ktex->kmxy/dot_general | solution.py:150
  118.1 3.0 %pad_maximum_fusion = bf16[4,160,16,256]{3,2,1,0:T(8,128)(2,1)S(1)} fusion(bf16[4,80,16,256]{3,2,1,0:T(8,128)(2,1)} %get-tuple-element.10, bf16[4,80,16,256]{3,2,1,0:T(8,128)(2,1)} %get-tuple-element.11), kind=kLoop, calls=%fused_computation.21 | loop fusion | flops 2621440 | bytes 10485760 | tf_op jit(solution)/shard_map/concatenate | solution.py:60
  121.1 4.2 %fusion.86 = f32[160,160]{0,1:T(8,128)S(1)} fusion(bf16[4,160,16,256]{3,2,1,0:T(8,128)(2,1)S(1)} %pad_maximum_fusion), kind=kOutput, calls=%fused_computation.59 | convolution fusion | flops 838860800 | bytes 5345280 | tf_op jit(solution)/shard_map/kpxy,kqxy->pq/dot_general | solution.py:61
  125.4 1.2 collective-permute-done.2
  126.7 0.7 collective-permute-start.3
  127.4 3.4 %collective-permute-done.3 = f32[80,80]{0,1:T(8,128)S(1)} collective-permute-done((f32[80,80]{0,1:T(8,128)S(1)}, f32[80,80]{0,1:T(8,128)S(1)}, u32[]{:S(2)}, u32[]{:S(2)}) %collective-permute-start.3) | collective-permute-done | bytes 25632 | tf_op jit(solution)/shard_map/ppermute | solution.py:39
  130.8 2.5 %collective-permute-start.4 = (f32[80,80]{0,1:T(8,128)S(1)}, f32[80,80]{0,1:T(8,128)S(1)}, u32[]{:S(2)}, u32[]{:S(2)}) collective-permute-start(f32[80,80]{0,1:T(8,128)S(1)} %add.116), channel_id=1, source_target_pairs={{0,4},{4,0},{8,12},{12,8},{16,20},{20,16},{24,28},{28,24},{1,5},{5... | collective-permute-start | bytes 76808 | tf_op jit(solution)/shard_map/ppermute | solution.py:39
  133.3 2.0 %collective-permute-done.4 = f32[80,80]{0,1:T(8,128)S(1)} collective-permute-done((f32[80,80]{0,1:T(8,128)S(1)}, f32[80,80]{0,1:T(8,128)S(1)}, u32[]{:S(2)}, u32[]{:S(2)}) %collective-permute-start.4) | collective-permute-done | bytes 25632 | tf_op jit(solution)/shard_map/ppermute | solution.py:39
  135.3 0.9 collective-permute-start.5
  136.2 3.1 %collective-permute-done.5 = f32[80,80]{0,1:T(8,128)S(1)} collective-permute-done((f32[80,80]{0,1:T(8,128)S(1)}, f32[80,80]{0,1:T(8,128)S(1)}, u32[]{:S(2)}, u32[]{:S(2)}) %collective-permute-start.5) | collective-permute-done | bytes 25632 | tf_op jit(solution)/shard_map/ppermute | solution.py:39
  139.3 1.1 collective-permute-start.6
  140.3 3.8 %collective-permute-done.6 = f32[80,80]{0,1:T(8,128)S(1)} collective-permute-done((f32[80,80]{0,1:T(8,128)S(1)}, f32[80,80]{0,1:T(8,128)S(1)}, u32[]{:S(2)}, u32[]{:S(2)}) %collective-permute-start.6) | collective-permute-done | bytes 25632 | tf_op jit(solution)/shard_map/ppermute | solution.py:39
  144.3 7.3 %cholesky.18 = f32[80,80]{1,0:T(8,128)S(1)} custom-call(f32[80,80]{1,0:T(8,128)S(1)} %fusion.93), custom_call_target="Cholesky" | custom-call | tf_op jit(solution)/shard_map/jit(cholesky)/cholesky | solution.py:159
  152.9 0.7 copy.88
  (39 shorter events, 4.4 us)
Async XLA Ops:
  0.6 25.1 %copy-start = (bf16[4,80,16,256]{3,2,1,0:T(8,128)(2,1)S(1)}, bf16[4,80,16,256]{3,2,1,0:T(8,128)(2,1)}, u32[]{:S(2)}) copy-start(bf16[4,80,16,256]{3,2,1,0:T(8,128)(2,1)} %param.14) | copy-start | bytes 7864324
  9.7 13.9 %all-to-all-start = ((f32[7,8,128]{2,0,1:T(8,128)}), f32[7,8,128]{2,0,1:T(8,128)S(1)}, u32[]{:S(2)}, u32[]{:S(2)}) async-start(f32[7,8,128]{2,0,1:T(8,128)} %pad_maximum_fusion.2), calls=%async_computation | async-start | bytes 65536 | tf_op jit(solution)/shard_map/all_to_all | solution.py:87
  30.2 17.8 %copy-start.1 = (bf16[16,16]{1,0:T(8,128)(2,1)S(1)}, bf16[16,16]{1,0:T(8,128)(2,1)}, u32[]{:S(2)}) copy-start(bf16[16,16]{1,0:T(8,128)(2,1)} %param.15) | copy-start | bytes 1540
  31.6 13.7 %all-to-all-start.1 = ((bf16[4,80,1024]{2,0,1:T(4,128)(2,1)}), bf16[4,80,1024]{2,0,1:T(4,128)(2,1)S(1)}, u32[]{:S(2)}, u32[]{:S(2)}) async-start(bf16[4,80,1024]{2,0,1:T(4,128)(2,1)} %copy.73), calls=%async_computation.1 | async-start | bytes 1310720 | tf_op jit(solution)/shard_map/all_to_all | solution.py:112
  49.6 15.1 %all-to-all-start.2 = ((bf16[16,20,1024]{2,1,0:T(8,128)(2,1)}), bf16[16,20,1024]{2,1,0:T(8,128)(2,1)S(1)}, u32[]{:S(2)}, u32[]{:S(2)}) async-start(bf16[16,20,1024]{2,1,0:T(8,128)(2,1)} %copy.76), calls=%async_computation.2 | async-start | bytes 1572864 | tf_op jit(solution)/shard_map/all_to_all | solution.py:116
  68.2 18.4 %collective-permute-start.1 = (bf16[4,80,1024]{2,0,1:T(4,128)(2,1)}, bf16[4,80,1024]{2,0,1:T(4,128)(2,1)S(1)}, u32[]{:S(2)}, u32[]{:S(2)}) collective-permute-start(bf16[4,80,1024]{2,0,1:T(4,128)(2,1)} %bitcast.30), channel_id=1, source_target_pairs={{4,0},{8,4},{12,8},{16,12},{20,16},{24,20},{28,24},{5,1},{9,5},{13... | collective-permute-start | bytes 1966088 | tf_op jit(solution)/shard_map/ppermute | solution.py:121
  69.5 30.1 %collective-permute-start = (bf16[4,80,1024]{2,0,1:T(4,128)(2,1)}, bf16[4,80,1024]{2,0,1:T(4,128)(2,1)}, u32[]{:S(2)}, u32[]{:S(2)}) collective-permute-start(bf16[4,80,1024]{2,0,1:T(4,128)(2,1)} %bitcast.30), channel_id=1, source_target_pairs={{0,4},{4,8},{8,12},{12,16},{16,20},{20,24},{24,28},{1,5},{5,9},{9,... | collective-permute-start | bytes 1966088 | tf_op jit(solution)/shard_map/ppermute | solution.py:120
  125.3 1.3 collective-permute-start.2
  126.7 4.1 %collective-permute-start.3 = (f32[80,80]{0,1:T(8,128)S(1)}, f32[80,80]{0,1:T(8,128)S(1)}, u32[]{:S(2)}, u32[]{:S(2)}) collective-permute-start(f32[80,80]{0,1:T(8,128)S(1)} %fusion.113), channel_id=1, source_target_pairs={{0,2},{1,3},{2,0},{3,1},{4,6},{5,7},{6,4},{7,5},{8,10},{9,11},{10,... | collective-permute-start | bytes 76808 | tf_op jit(solution)/shard_map/ppermute | solution.py:39
  130.8 4.5 %collective-permute-start.4 = (f32[80,80]{0,1:T(8,128)S(1)}, f32[80,80]{0,1:T(8,128)S(1)}, u32[]{:S(2)}, u32[]{:S(2)}) collective-permute-start(f32[80,80]{0,1:T(8,128)S(1)} %add.116), channel_id=1, source_target_pairs={{0,4},{4,0},{8,12},{12,8},{16,20},{20,16},{24,28},{28,24},{1,5},{5... | collective-permute-start | bytes 76808 | tf_op jit(solution)/shard_map/ppermute | solution.py:39
  135.3 4.0 %collective-permute-start.5 = (f32[80,80]{0,1:T(8,128)S(1)}, f32[80,80]{0,1:T(8,128)S(1)}, u32[]{:S(2)}, u32[]{:S(2)}) collective-permute-start(f32[80,80]{0,1:T(8,128)S(1)} %add.117), channel_id=1, source_target_pairs={{0,8},{4,12},{8,0},{12,4},{16,24},{20,28},{24,16},{28,20},{1,9},{5... | collective-permute-start | bytes 76808 | tf_op jit(solution)/shard_map/ppermute | solution.py:39
  139.3 4.9 %collective-permute-start.6 = (f32[80,80]{0,1:T(8,128)S(1)}, f32[80,80]{0,1:T(8,128)S(1)}, u32[]{:S(2)}, u32[]{:S(2)}) collective-permute-start(f32[80,80]{0,1:T(8,128)S(1)} %add.118), channel_id=1, source_target_pairs={{0,16},{4,20},{8,24},{12,28},{16,0},{20,4},{24,8},{28,12},{1,17},{... | collective-permute-start | bytes 76808 | tf_op jit(solution)/shard_map/ppermute | solution.py:39

commit v10 on v9

--- a/solution.py
+++ b/solution.py
@@ -47,10 +47,11 @@
     offsets = rows[:, None] - jnp.arange(row_count, dtype=jnp.int32)[None, :]
     slot_taps = taps_table(radius, offsets) * keep[None, :, None].astype(jnp.bfloat16)
     col_hit = cols[None, :] == jnp.arange(col_count, dtype=jnp.int32)[:, None]
-    placed = jnp.where(col_hit[None, None], mix[:, :, None, :], 0).astype(jnp.bfloat16)
-    return jnp.einsum(
-        "kmxs,ksz->kmxz", placed, slot_taps, preferred_element_type=jnp.float32
+    placed = jnp.where(col_hit[None, None, None], mix[:, :, :, None, :], 0).astype(jnp.bfloat16)
+    out = jnp.einsum(
+        "gkmxs,ksz->kgmxz", placed, slot_taps, preferred_element_type=jnp.float32
     ).astype(jnp.bfloat16)
+    return out.reshape((out.shape[0], -1) + out.shape[3:])
 
 
 def gram_of(panel):
@@ -73,11 +74,18 @@
     cell_count = col_count * row_count
     slots = tile_count * capacity
     packed = slots < cell_count
+    share = members // group_count
     assert HALO <= col_count
 
     slot_index = lax.broadcasted_iota(jnp.int32, (tile_count, capacity), 1)
     live_mask = (slot_index < counts[0][:, None]).astype(jnp.float32)
-    values = jnp.take(obs_adjoint, foot_obs[0], axis=1)
+    obs_hit = foot_obs[0][:, :, None] == lax.broadcasted_iota(
+        jnp.int32, (1, 1, obs_adjoint.shape[1]), 2
+    )
+    values = jnp.einsum(
+        "lo,dco->ldc", obs_adjoint, obs_hit.astype(jnp.float32),
+        precision=lax.Precision.HIGHEST,
+    )
     payload = values * (foot_weight[0] * live_mask)[None]
     own_cells = foot_cell[0]
     prev_cells = jnp.concatenate([own_cells[:1], own_cells[:-1]], axis=0)
@@ -100,22 +108,30 @@
             return one_hot(cell_index, own_keep, cell_count).reshape(slots, col_count, row_count)
 
         picked = jnp.einsum(
-            "lmxy,sxy->lms", ensemble, own_hits(), preferred_element_type=jnp.float32
+            "lgmxy,sxy->glms", ensemble.reshape(lev_dev, group_count, share, col_count, row_count),
+            own_hits(), preferred_element_type=jnp.float32,
         )
-        member_forcing = (picked * forcing[:, None]).astype(jnp.bfloat16)
+        member_forcing = (picked * forcing[None, :, None]).astype(jnp.bfloat16)
     else:
         forcing = jnp.zeros((lev_dev, cell_count), jnp.float32)
         forcing = forcing.at[:, cell_index].add(arrived[:lev_dev].reshape(lev_dev, -1))
         forcing = forcing.reshape(lev_dev, col_count, row_count)
         member_forcing = (ensemble * forcing[:, None]).astype(jnp.bfloat16)
+        member_forcing = jnp.swapaxes(
+            member_forcing.reshape((lev_dev, group_count, share) + member_forcing.shape[2:]), 0, 1
+        )
 
-    regrouped = lax.all_to_all(member_forcing, "lev", split_axis=1, concat_axis=0, tiled=True)
+    regrouped = lax.all_to_all(member_forcing, "lev", split_axis=0, concat_axis=0, tiled=True)
+    regrouped = regrouped.reshape((group_count * lev_dev,) + regrouped.shape[2:])
     local_mix = jnp.einsum(
         "lk,lm...->km...", vert_root, regrouped, preferred_element_type=jnp.float32
-    )
-    level_mix = lax.all_to_all(
-        local_mix.astype(jnp.bfloat16), "lev", split_axis=0, concat_axis=1, tiled=True
-    )
+    ).astype(jnp.bfloat16)
+    local_mix = local_mix.reshape((group_count, lev_dev) + local_mix.shape[1:])
+    level_mix = lax.all_to_all(local_mix, "lev", split_axis=0, concat_axis=0, tiled=True)
+    if not packed:
+        level_mix = jnp.swapaxes(level_mix, 0, 1).reshape(
+            (lev_dev, members) + level_mix.shape[3:]
+        )
     ends = tile_count - 1
     from_left = lax.ppermute(level_mix, "tile", [(i, i + 1) for i in range(ends)])
     from_right = lax.ppermute(level_mix, "tile", [(i + 1, i) for i in range(ends)])

time: 154 us -> 141 us (0.916)
  local copies, waits for them, and re-layouts: 17.5 us -> 9.83 us
  other arithmetic: 27 us -> 21.7 us
  waiting for transfers between devices: 50.2 us -> 51.8 us
    dot_general x1 -> x4, matrix products: 4.43 us -> 19.5 us  [the longest x2 12.8 us: spread(): jnp.einsum('gkmxs,ksz->kgmxz', placed, slot_taps, preferred_element_type=...]
    dot_general x1, matrix products: 13.9 us -> 0.89 us  [shards(): jnp.einsum('tkmey,ktex->kmxy', sides, taps_cols[:, 0::2], preferred_eleme...]
    reshape x0 -> x3, local copies, waits for them, and re-layouts: none -> 4.19 us  [the longest x2 2.7 us: shards(): local_mix = local_mix.reshape((group_count, lev_dev) + local_mix.shape[1:])]
    dot_general x1, matrix products: 7.58 us -> 3.61 us  [shards(): jnp.einsum('kmey,kex->kmxy', own, taps_cols[:, 1], preferred_element_type...]
    ppermute x1, waiting for transfers between devices: 3.93 us -> 7.3 us  [shards(): lax.ppermute(level_mix, 'tile', [(i + 1, i) for i in range(ends)])]
    gather x2 -> x0, local copies, waits for them, and re-layouts: 3 us -> none  [shards(): values = jnp.take(obs_adjoint, foot_obs[0], axis=1)]
    all_to_all x3 -> x2, local copies, waits for them, and re-layouts: 4.03 us -> 1.38 us  [the longest x1 1.17 us: shards(): lax.all_to_all(member_forcing, 'lev', split_axis=0, concat_axis=0, tiled=...]
    concatenate x1, other arithmetic: 2.98 us -> 0.45 us  [gram_of(): parts = jnp.concatenate([high, low], axis=1)]
  transfers between devices with their start and end apart: 10 -> 10, of which waited for: 10 -> 10; matrix products, arithmetic and copies ran while one was open for 11% -> 10% of each run, Pallas kernels for 0% -> 0%
where the time goes in v10:
time: 141 us
  waiting for transfers between devices  51.8 us (37%)
  matrix products  30.7 us (22%)
  starting transfers between devices  25.6 us (18%)
  other arithmetic  21.7 us (15%)
  local copies, waits for them, and re-layouts  9.83 us (7%)
    ppermute x5, waiting for transfers between devices, all_sum(): lax.ppermute(value, name, [(i, i ^ bit) for i in range(size)])  13.4 us
    ppermute x1, waiting for transfers between devices, shards(): lax.ppermute(level_mix, 'tile', [(i, i + 1) for i in range(ends)])  12.9 us
    dot_general x2, matrix products, spread(): jnp.einsum('gkmxs,ksz->kgmxz', placed, slot_taps, preferred_element_type=...  12.8 us
    all_to_all x1, waiting for transfers between devices, shards(): lax.all_to_all(local_mix, 'lev', split_axis=0, concat_axis=0, tiled=True)  8.29 us
    another operation x3, other arithmetic, shards(): r_factor = jnp.linalg.cholesky(gram_total).T  7.98 us
    ppermute x1, waiting for transfers between devices, shards(): lax.ppermute(level_mix, 'tile', [(i + 1, i) for i in range(ends)])  7.3 us
    all_to_all x1, starting transfers between devices, shards(): lax.all_to_all(outgoing, 'tile', split_axis=1, concat_axis=1, tiled=True)  7.25 us
    all_to_all x1, waiting for transfers between devices, shards(): lax.all_to_all(member_forcing, 'lev', split_axis=0, concat_axis=0, tiled=...  5.92 us
  transfers between devices with their start and end apart: 10, of which 10 were waited for; matrix products, arithmetic and copies ran while one was open for 10% of the time, Pallas kernels for 0%

profile of v10, /device:TPU:0, one launch (start us, length us, event | category | flops | bytes accessed | tf_op | source)
XLA Modules:
  0.0 140.6 jit_solution(9663642828420344955)
XLA Ops:
  0.6 0.9 slice_bitcast_fusion.8
  1.5 0.8 slice_bitcast_fusion.6
  2.3 0.8 select_bitcast_fusion.1
  3.0 0.7 add_convert_fusion
  3.7 1.8 %fusion.63 = f32[4,8,128]{2,0,1:T(4,128)S(1)} fusion(s32[8,128]{1,0:T(8,128)} %bitcast.118, f32[4,512]{1,0:T(4,128)} %param.9, f32[8,128]{1,0:T(8,128)S(1)} %select_bitcast_fusion.1), kind=kOutput, calls=%fused_computation.61 | convolution fusion | flops 25694208 | bytes 32768 | tf_op jit(solution)/shard_map/lo,dco->ldc/dot_general | solution.py:85
  5.5 0.6 pad_maximum_fusion.2
  6.2 7.3 %all-to-all-start = ((f32[7,8,128]{2,0,1:T(8,128)}), f32[7,8,128]{2,0,1:T(8,128)S(1)}, u32[]{:S(2)}, u32[]{:S(2)}) async-start(f32[7,8,128]{2,0,1:T(8,128)} %pad_maximum_fusion.2), calls=%async_computation | async-start | bytes 65536 | tf_op jit(solution)/shard_map/all_to_all | solution.py:95
  13.4 0.7 broadcast_add_fusion
  14.1 0.7 convert_element_type.93
  14.8 1.3 iota_compare_fusion
  16.1 4.0 %all-to-all-done = f32[7,8,128]{2,0,1:T(8,128)S(1)} async-done(((f32[7,8,128]{2,0,1:T(8,128)}), f32[7,8,128]{2,0,1:T(8,128)S(1)}, u32[]{:S(2)}, u32[]{:S(2)}) %all-to-all-start) | async-done | bytes 28704 | tf_op jit(solution)/shard_map/all_to_all | solution.py:95
  20.9 1.3 fusion.15
  22.2 5.0 %fusion.53 = bf16[4,4,20,1024]{3,2,0,1:T(8,128)(2,1)S(1)} fusion(bf16[4,4,20,16,256]{4,3,2,1,0:T(8,128)(2,1)S(1)} %bitcast.103, s32[16,256]{1,0:T(8,128)S(1)} %multiply_add_fusion, s32[1024]{0:T(1024)S(1)} %bitcast.116, pred[1024]{0:T(1024)(128)(4,1)S(1)} %get-tuple-element.23, f32[4,1024]{1,0:T(4,128)S(1)} %fusion.15), kind=kOutput, calls=%fused_computation.55 | convolution fusion | flops 2693398528 | bytes 3314688 | tf_op jit(solution)/shard_map/lgmxy,sxy->glms/dot_general | solution.py:110
  27.2 1.4 copy.62
  28.5 3.5 %all-to-all-start.1 = ((bf16[4,4,20,1024]{3,1,2,0:T(4,128)(2,1)}), bf16[4,4,20,1024]{3,1,2,0:T(4,128)(2,1)S(1)}, u32[]{:S(2)}, u32[]{:S(2)}) async-start(bf16[4,4,20,1024]{3,1,2,0:T(4,128)(2,1)} %copy.62), calls=%async_computation.1 | async-start | bytes 1310720 | tf_op jit(solution)/shard_map/all_to_all | solution.py:124
  32.0 1.2 abs_convert_fusion.1
  33.3 3.1 %and_reduce_fusion = pred[2,1024]{1,0:T(4,128)(4,1)S(1)} fusion(s32[2,1024]{1,0:T(2,128)S(1)} %slice.80, pred[1024,1024]{1,0:T(8,128)(4,1)} %iota_compare_fusion), kind=kLoop, calls=%fused_computation.16 | loop fusion | flops 6289408 | bytes 1058816 | tf_op jit(solution)/shard_map/reduce_or | solution.py:24
  36.3 5.9 %all-to-all-done.1 = bf16[4,4,20,1024]{3,1,2,0:T(4,128)(2,1)S(1)} async-done(((bf16[4,4,20,1024]{3,1,2,0:T(4,128)(2,1)}), bf16[4,4,20,1024]{3,1,2,0:T(4,128)(2,1)S(1)}, u32[]{:S(2)}, u32[]{:S(2)}) %all-to-all-start.1) | async-done | bytes 655392 | tf_op jit(solution)/shard_map/all_to_all | solution.py:124
  42.2 1.2 copy.63
  43.4 1.5 %reshape.262 = bf16[16,20,1024]{2,0,1:T(8,128)(2,1)S(1)} reshape(bf16[4,4,20,1024]{3,1,0,2:T(4,128)(2,1)} %copy.63) | data formatting | bytes 1310720 | tf_op jit(solution)/shard_map/reshape | solution.py:125
  44.9 1.2 fusion.58
  46.1 1.6 %reshape.263 = bf16[4,4,20,1024]{3,1,0,2:T(4,128)(2,1)S(1)} reshape(bf16[16,20,1024]{2,0,1:T(8,128)(2,1)} %fusion.58) | data formatting | bytes 1310720 | tf_op jit(solution)/shard_map/reshape | solution.py:129
  47.7 1.1 copy.65
  48.9 3.7 %all-to-all-start.2 = ((bf16[4,4,20,1024]{3,1,2,0:T(4,128)(2,1)}), bf16[4,4,20,1024]{3,1,2,0:T(4,128)(2,1)S(1)}, u32[]{:S(2)}, u32[]{:S(2)}) async-start(bf16[4,4,20,1024]{3,1,2,0:T(4,128)(2,1)} %copy.65), calls=%async_computation.2 | async-start | bytes 1310720 | tf_op jit(solution)/shard_map/all_to_all | solution.py:130
  52.5 1.7 %abs_convert_fusion = f32[2,1024,256]{2,1,0:T(8,128)} fusion(s32[2,1024]{1,0:T(2,128)S(1)} %get-tuple-element.15), kind=kLoop, calls=%fused_computation.44 | loop fusion | flops 1572864 | bytes 2105344 | tf_op jit(solution)/shard_map/vmap()/convert_element_type | solution.py:11
  54.3 8.3 %all-to-all-done.2 = bf16[4,4,20,1024]{3,1,2,0:T(4,128)(2,1)S(1)} async-done(((bf16[4,4,20,1024]{3,1,2,0:T(4,128)(2,1)}), bf16[4,4,20,1024]{3,1,2,0:T(4,128)(2,1)S(1)}, u32[]{:S(2)}, u32[]{:S(2)}) %all-to-all-start.2) | async-done | bytes 655392 | tf_op jit(solution)/shard_map/all_to_all | solution.py:130
  62.6 1.3 collective-permute-start.1
  63.9 4.6 %collective-permute-start = (bf16[4,4,20,1024]{3,1,2,0:T(4,128)(2,1)S(1)}, bf16[4,4,20,1024]{3,1,2,0:T(4,128)(2,1)S(1)}, u32[]{:S(2)}, u32[]{:S(2)}) collective-permute-start(bf16[4,4,20,1024]{3,1,2,0:T(4,128)(2,1)S(1)} %all-to-all-done.2), channel_id=1, source_target_pairs={{0,4},{4,8},{8,12},{12,16},{16,20},{20,24},{24,28},{1,5},{5,9},{9,... | collective-permute-start | bytes 1966088 | tf_op jit(solution)/shard_map/ppermute | solution.py:136
  68.7 4.7 %fusion.48 = bf16[4,4,20,16,256]{4,3,2,1,0:T(8,128)(2,1)S(1)} fusion(f32[4]{0:T(128)S(1)} %broadcast_add_fusion, f32[1024,256]{1,0:T(8,128)} %abs_convert_fusion.1, f32[4]{0:T(128)S(1)} %convert_element_type.93, pred[16,1024]{1,0:T(8,128)(4,1)S(1)} %iota_compare_fusion.8, bf16[4,4,20,1024]{3,2,0,1:T(8,128)(2,1)S(1)} %copy.66, ...), kind=kOutput, calls=%fused_computation.53 | convolution fusion | flops 2697199616 | bytes 4343840 | tf_op jit(solution)/shard_map/gkmxs,ksz->kgmxz/dot_general | solution.py:51
  73.4 7.3 %collective-permute-done.1 = bf16[4,4,20,1024]{3,1,2,0:T(4,128)(2,1)S(1)} collective-permute-done((bf16[4,4,20,1024]{3,1,2,0:T(4,128)(2,1)S(1)}, bf16[4,4,20,1024]{3,1,2,0:T(4,128)(2,1)S(1)}, u32[]{:S(2)}, u32[]{:S(2)}) %collective-permute-start.1) | collective-permute-done | bytes 655392 | tf_op jit(solution)/shard_map/ppermute | solution.py:137
  80.7 12.9 %collective-permute-done = bf16[4,4,20,1024]{3,1,2,0:T(4,128)(2,1)S(1)} collective-permute-done((bf16[4,4,20,1024]{3,1,2,0:T(4,128)(2,1)S(1)}, bf16[4,4,20,1024]{3,1,2,0:T(4,128)(2,1)S(1)}, u32[]{:S(2)}, u32[]{:S(2)}) %collective-permute-start) | collective-permute-done | bytes 655392 | tf_op jit(solution)/shard_map/ppermute | solution.py:136
  93.7 0.9 pad_maximum_fusion.1
  95.0 8.0 %fusion.32 = bf16[2,4,4,20,16,256]{5,4,3,2,1,0:T(8,128)(2,1)S(1)} fusion(f32[4]{0:T(128)S(1)} %broadcast_add_fusion, f32[2,1024,256]{2,1,0:T(8,128)} %abs_convert_fusion, f32[4]{0:T(128)S(1)} %convert_element_type.93, pred[2,16,1024]{2,1,0:T(8,128)(4,1)S(1)} %iota_compare_fusion.7, bf16[2,4,4,20,1024]{4,3,1,2,0:T(8,128)(2,1)S(1)} %copy.67, ...), kind=kOutput, calls=%fused_computation.40 | convolution fusion | flops 5394399232 | bytes 8687648 | tf_op jit(solution)/shard_map/vmap(gkmxs,ksz->kgmxz)/dot_general | solution.py:51
  103.1 0.9 fusion.19
  104.0 3.6 %subtract_convert_fusion = (bf16[4,80,16,256]{3,2,1,0:T(8,128)(2,1)S(1)}, bf16[4,80,16,256]{3,2,1,0:T(8,128)(2,1)S(1)}, f32[4,80,16,256]{3,2,1,0:T(8,128)}) fusion(f32[4,16,80,256,1]{3,1,4,2,0:T(8,128)S(1)} %fusion.19, f32[4,80,16,256]{3,2,1,0:T(8,128)S(1)} %bitcast.106, bf16[4,80,16,256]{3,2,1,0:T(8,128)(2,1)S(1)} %bitcast.107, ...), kind=kOutput, calls=%fused_computation.27 | convolution fusion | flops 49807360 | bytes 23609344 | tf_op jit(solution)/shard_map/kmey,kex->kmxy/dot_general | solution.py:151
  108.1 4.2 %fusion.59 = f32[160,160]{0,1:T(8,128)S(1)} fusion(bf16[4,160,16,256]{3,2,1,0:T(8,128)(2,1)S(1)} %pad_maximum_fusion), kind=kOutput, calls=%fused_computation.59 | convolution fusion | flops 838860800 | bytes 5345280 | tf_op jit(solution)/shard_map/kpxy,kqxy->pq/dot_general | solution.py:62
  112.4 1.2 collective-permute-done.2
  114.3 3.5 %collective-permute-done.3 = f32[80,80]{0,1:T(8,128)S(1)} collective-permute-done((f32[80,80]{0,1:T(8,128)S(1)}, f32[80,80]{0,1:T(8,128)S(1)}, u32[]{:S(2)}, u32[]{:S(2)}) %collective-permute-start.3) | collective-permute-done | bytes 25632 | tf_op jit(solution)/shard_map/ppermute | solution.py:39
  117.8 2.5 %collective-permute-start.4 = (f32[80,80]{0,1:T(8,128)S(1)}, f32[80,80]{0,1:T(8,128)S(1)}, u32[]{:S(2)}, u32[]{:S(2)}) collective-permute-start(f32[80,80]{0,1:T(8,128)S(1)} %add.91), channel_id=1, source_target_pairs={{0,4},{4,0},{8,12},{12,8},{16,20},{20,16},{24,28},{28,24},{1,5},{5... | collective-permute-start | bytes 76808 | tf_op jit(solution)/shard_map/ppermute | solution.py:39
  120.3 2.0 %collective-permute-done.4 = f32[80,80]{0,1:T(8,128)S(1)} collective-permute-done((f32[80,80]{0,1:T(8,128)S(1)}, f32[80,80]{0,1:T(8,128)S(1)}, u32[]{:S(2)}, u32[]{:S(2)}) %collective-permute-start.4) | collective-permute-done | bytes 25632 | tf_op jit(solution)/shard_map/ppermute | solution.py:39
  122.2 1.0 collective-permute-start.5
  123.3 3.0 %collective-permute-done.5 = f32[80,80]{0,1:T(8,128)S(1)} collective-permute-done((f32[80,80]{0,1:T(8,128)S(1)}, f32[80,80]{0,1:T(8,128)S(1)}, u32[]{:S(2)}, u32[]{:S(2)}) %collective-permute-start.5) | collective-permute-done | bytes 25632 | tf_op jit(solution)/shard_map/ppermute | solution.py:39
  126.3 1.2 collective-permute-start.6
  127.4 3.7 %collective-permute-done.6 = f32[80,80]{0,1:T(8,128)S(1)} collective-permute-done((f32[80,80]{0,1:T(8,128)S(1)}, f32[80,80]{0,1:T(8,128)S(1)}, u32[]{:S(2)}, u32[]{:S(2)}) %collective-permute-start.6) | collective-permute-done | bytes 25632 | tf_op jit(solution)/shard_map/ppermute | solution.py:39
  131.3 7.3 %cholesky.18 = f32[80,80]{1,0:T(8,128)S(1)} custom-call(f32[80,80]{1,0:T(8,128)S(1)} %fusion.68), custom_call_target="Cholesky" | custom-call | tf_op jit(solution)/shard_map/jit(cholesky)/cholesky | solution.py:175
  138.6 0.6 compare_reduce_fusion
  139.2 0.7 select_bitcast_fusion
  139.9 0.7 copy.77
  (38 shorter events, 3.0 us)
Async XLA Ops:
  0.6 21.6 %copy-start = (bf16[4,80,16,256]{3,2,1,0:T(8,128)(2,1)S(1)}, bf16[4,80,16,256]{3,2,1,0:T(8,128)(2,1)}, u32[]{:S(2)}) copy-start(bf16[4,80,16,256]{3,2,1,0:T(8,128)(2,1)} %param.14) | copy-start | bytes 7864324
  6.2 13.9 %all-to-all-start = ((f32[7,8,128]{2,0,1:T(8,128)}), f32[7,8,128]{2,0,1:T(8,128)S(1)}, u32[]{:S(2)}, u32[]{:S(2)}) async-start(f32[7,8,128]{2,0,1:T(8,128)} %pad_maximum_fusion.2), calls=%async_computation | async-start | bytes 65536 | tf_op jit(solution)/shard_map/all_to_all | solution.py:95
  27.2 17.8 %copy-start.1 = (bf16[16,16]{1,0:T(8,128)(2,1)S(1)}, bf16[16,16]{1,0:T(8,128)(2,1)}, u32[]{:S(2)}) copy-start(bf16[16,16]{1,0:T(8,128)(2,1)} %param.15) | copy-start | bytes 1540
  28.5 13.7 %all-to-all-start.1 = ((bf16[4,4,20,1024]{3,1,2,0:T(4,128)(2,1)}), bf16[4,4,20,1024]{3,1,2,0:T(4,128)(2,1)S(1)}, u32[]{:S(2)}, u32[]{:S(2)}) async-start(bf16[4,4,20,1024]{3,1,2,0:T(4,128)(2,1)} %copy.62), calls=%async_computation.1 | async-start | bytes 1310720 | tf_op jit(solution)/shard_map/all_to_all | solution.py:124
  48.9 13.7 %all-to-all-start.2 = ((bf16[4,4,20,1024]{3,1,2,0:T(4,128)(2,1)}), bf16[4,4,20,1024]{3,1,2,0:T(4,128)(2,1)S(1)}, u32[]{:S(2)}, u32[]{:S(2)}) async-start(bf16[4,4,20,1024]{3,1,2,0:T(4,128)(2,1)} %copy.65), calls=%async_computation.2 | async-start | bytes 1310720 | tf_op jit(solution)/shard_map/all_to_all | solution.py:130
  62.6 18.2 %collective-permute-start.1 = (bf16[4,4,20,1024]{3,1,2,0:T(4,128)(2,1)S(1)}, bf16[4,4,20,1024]{3,1,2,0:T(4,128)(2,1)S(1)}, u32[]{:S(2)}, u32[]{:S(2)}) collective-permute-start(bf16[4,4,20,1024]{3,1,2,0:T(4,128)(2,1)S(1)} %all-to-all-done.2), channel_id=1, source_target_pairs={{4,0},{8,4},{12,8},{16,12},{20,16},{24,20},{28,24},{5,1},{9,5},{13... | collective-permute-start | bytes 1966088 | tf_op jit(solution)/shard_map/ppermute | solution.py:137
  63.9 29.8 %collective-permute-start = (bf16[4,4,20,1024]{3,1,2,0:T(4,128)(2,1)S(1)}, bf16[4,4,20,1024]{3,1,2,0:T(4,128)(2,1)S(1)}, u32[]{:S(2)}, u32[]{:S(2)}) collective-permute-start(bf16[4,4,20,1024]{3,1,2,0:T(4,128)(2,1)S(1)} %all-to-all-done.2), channel_id=1, source_target_pairs={{0,4},{4,8},{8,12},{12,16},{16,20},{20,24},{24,28},{1,5},{5,9},{9,... | collective-permute-start | bytes 1966088 | tf_op jit(solution)/shard_map/ppermute | solution.py:136
  94.6 9.4 %slice-start = ((s8[5242880]{0:T(1024)(128)(4,1)}), s8[4194304]{0:T(1024)(128)(4,1)S(1)}, s32[]{:S(2)}) async-start(s8[5242880]{0:T(1024)(128)(4,1)} %bitcast.105), calls=%async_computation.3 | async-start | bytes 8388608
  95.0 8.9 %slice-start.1 = ((s8[5242880]{0:T(1024)(128)(4,1)}), s8[1048576]{0:T(1024)(128)(4,1)S(1)}, s32[]{:S(2)}) async-start(s8[5242880]{0:T(1024)(128)(4,1)} %bitcast.105), calls=%async_computation.4 | async-start | bytes 2097152
  112.3 1.3 collective-permute-start.2
  113.7 4.1 %collective-permute-start.3 = (f32[80,80]{0,1:T(8,128)S(1)}, f32[80,80]{0,1:T(8,128)S(1)}, u32[]{:S(2)}, u32[]{:S(2)}) collective-permute-start(f32[80,80]{0,1:T(8,128)S(1)} %fusion.81), channel_id=1, source_target_pairs={{0,2},{1,3},{2,0},{3,1},{4,6},{5,7},{6,4},{7,5},{8,10},{9,11},{10,... | collective-permute-start | bytes 76808 | tf_op jit(solution)/shard_map/ppermute | solution.py:39
  117.8 4.5 %collective-permute-start.4 = (f32[80,80]{0,1:T(8,128)S(1)}, f32[80,80]{0,1:T(8,128)S(1)}, u32[]{:S(2)}, u32[]{:S(2)}) collective-permute-start(f32[80,80]{0,1:T(8,128)S(1)} %add.91), channel_id=1, source_target_pairs={{0,4},{4,0},{8,12},{12,8},{16,20},{20,16},{24,28},{28,24},{1,5},{5... | collective-permute-start | bytes 76808 | tf_op jit(solution)/shard_map/ppermute | solution.py:39
  122.2 4.0 %collective-permute-start.5 = (f32[80,80]{0,1:T(8,128)S(1)}, f32[80,80]{0,1:T(8,128)S(1)}, u32[]{:S(2)}, u32[]{:S(2)}) collective-permute-start(f32[80,80]{0,1:T(8,128)S(1)} %add.92), channel_id=1, source_target_pairs={{0,8},{4,12},{8,0},{12,4},{16,24},{20,28},{24,16},{28,20},{1,9},{5... | collective-permute-start | bytes 76808 | tf_op jit(solution)/shard_map/ppermute | solution.py:39
  126.3 4.9 %collective-permute-start.6 = (f32[80,80]{0,1:T(8,128)S(1)}, f32[80,80]{0,1:T(8,128)S(1)}, u32[]{:S(2)}, u32[]{:S(2)}) collective-permute-start(f32[80,80]{0,1:T(8,128)S(1)} %add.93), channel_id=1, source_target_pairs={{0,16},{4,20},{8,24},{12,28},{16,0},{20,4},{24,8},{28,12},{1,17},{... | collective-permute-start | bytes 76808 | tf_op jit(solution)/shard_map/ppermute | solution.py:39

commit v11 on v10

--- a/solution.py
+++ b/solution.py
@@ -52,6 +52,22 @@
         "gkmxs,ksz->kgmxz", placed, slot_taps, preferred_element_type=jnp.float32
     ).astype(jnp.bfloat16)
     return out.reshape((out.shape[0], -1) + out.shape[3:])
+
+
+def halo_of(local_mix, tile_count, group_count, step):
+    here = lax.axis_index("lev")
+    got = []
+    for shift in range(group_count):
+        chunk = lax.dynamic_index_in_dim(local_mix, (here + shift) % group_count, 0, keepdims=False)
+        pairs = [
+            (t * group_count + g, (t + step) * group_count + (g + shift) % group_count)
+            for t in range(tile_count)
+            if 0 <= t + step < tile_count
+            for g in range(group_count)
+        ]
+        got.append(lax.ppermute(chunk, ("tile", "lev"), pairs))
+    order = (here - jnp.arange(group_count, dtype=jnp.int32)) % group_count
+    return jnp.take(jnp.stack(got), order, axis=0)
 
 
 def gram_of(panel):
@@ -133,8 +149,12 @@
             (lev_dev, members) + level_mix.shape[3:]
         )
     ends = tile_count - 1
-    from_left = lax.ppermute(level_mix, "tile", [(i, i + 1) for i in range(ends)])
-    from_right = lax.ppermute(level_mix, "tile", [(i + 1, i) for i in range(ends)])
+    if packed:
+        from_left = halo_of(local_mix, tile_count, group_count, 1)
+        from_right = halo_of(local_mix, tile_count, group_count, -1)
+    else:
+        from_left = lax.ppermute(level_mix, "tile", [(i, i + 1) for i in range(ends)])
+        from_right = lax.ppermute(level_mix, "tile", [(i + 1, i) for i in range(ends)])
     row_iota = jnp.arange(row_count, dtype=jnp.int32)
     taps_rows = taps_table(radius, row_iota[:, None] - row_iota[None, :])
     wide_iota = jnp.arange(3 * col_count, dtype=jnp.int32)

time: 141 us -> 149 us (1.057)
  waiting for transfers between devices: 51.8 us -> 19.5 us
  starting transfers between devices: 25.6 us -> 49.7 us
  other arithmetic: 21.7 us -> 27.8 us
  local copies, waits for them, and re-layouts: 9.83 us -> 15.9 us
  matrix products: 30.7 us -> 34.1 us
    ppermute x2 -> x8, starting transfers between devices: 5.87 us -> 26.3 us  [halo_of(): got.append(lax.ppermute(chunk, ('tile', 'lev'), pairs))]
    ppermute x2 -> x8, waiting for transfers between devices: 20.2 us -> 0.02 us  [halo_of(): got.append(lax.ppermute(chunk, ('tile', 'lev'), pairs))]
    all_to_all x1, waiting for transfers between devices: 8.29 us -> 0.01 us  [shards(): lax.all_to_all(local_mix, 'lev', split_axis=0, concat_axis=0, tiled=True)]
    gather x0 -> x2, local copies, waits for them, and re-layouts: none -> 3.83 us  [halo_of(): return jnp.take(jnp.stack(got), order, axis=0)]
    another operation x0 -> x2, other arithmetic: none -> 3.49 us  [halo_of(): return jnp.take(jnp.stack(got), order, axis=0)]
    ppermute x5, starting transfers between devices: 5.36 us -> 8.25 us  [all_sum(): lax.ppermute(value, name, [(i, i ^ bit) for i in range(size)])]
    dot_general x1, matrix products: 3.61 us -> 5.99 us  [shards(): jnp.einsum('kmey,kex->kmxy', own, taps_cols[:, 1], preferred_element_type...]
    dot_general x1, matrix products: 0.89 us -> 3.25 us  [shards(): jnp.einsum('tkmey,ktex->kmxy', sides, taps_cols[:, 0::2], preferred_eleme...]
  transfers between devices with their start and end apart: 10 -> 16, of which waited for: 10 -> 7; matrix products, arithmetic and copies ran while one was open for 10% -> 21% of each run, Pallas kernels for 0% -> 0%
where the time goes in v11:
time: 149 us; the launch traced here: 148 us
  starting transfers between devices  49.7 us (33%)
  matrix products  34.1 us (23%)
  other arithmetic  27.8 us (19%)
  waiting for transfers between devices  19.5 us (13%)
  local copies, waits for them, and re-layouts  15.9 us (11%)
    ppermute x8, starting transfers between devices, halo_of(): got.append(lax.ppermute(chunk, ('tile', 'lev'), pairs))  26.3 us
    ppermute x5, waiting for transfers between devices, all_sum(): lax.ppermute(value, name, [(i, i ^ bit) for i in range(size)])  12 us
    dot_general x2, matrix products, spread(): jnp.einsum('gkmxs,ksz->kgmxz', placed, slot_taps, preferred_element_type=...  11.4 us
    ppermute x5, starting transfers between devices, all_sum(): lax.ppermute(value, name, [(i, i ^ bit) for i in range(size)])  8.25 us
    another operation x3, other arithmetic, shards(): r_factor = jnp.linalg.cholesky(gram_total).T  7.98 us
    all_to_all x1, starting transfers between devices, shards(): lax.all_to_all(outgoing, 'tile', split_axis=1, concat_axis=1, tiled=True)  7.25 us
    dot_general x1, matrix products, shards(): jnp.einsum('kmey,kex->kmxy', own, taps_cols[:, 1], preferred_element_type...  5.99 us
    dot_general x1, matrix products, shards(): jnp.einsum('lgmxy,sxy->glms', ensemble.reshape(lev_dev, group_count, shar...  4.95 us
  transfers between devices with their start and end apart: 16, of which 7 were waited for; matrix products, arithmetic and copies ran while one was open for 21% of the time, Pallas kernels for 0%

profile of v11, /device:TPU:0, one launch (start us, length us, event | category | flops | bytes accessed | tf_op | source)
XLA Modules:
  0.0 148.1 jit_solution(11654038539039343138)
XLA Ops:
  3.7 1.8 %fusion.63 = f32[4,8,128]{2,0,1:T(4,128)S(1)} fusion(s32[8,128]{1,0:T(8,128)} %bitcast.137, f32[4,512]{1,0:T(4,128)} %param.11, f32[8,128]{1,0:T(8,128)S(1)} %select_bitcast_fusion.3), kind=kOutput, calls=%fused_computation.63 | convolution fusion | flops 25694208 | bytes 32768 | tf_op jit(solution)/shard_map/lo,dco->ldc/dot_general | solution.py:101
  6.2 7.3 %all-to-all-start = ((f32[7,8,128]{2,0,1:T(8,128)}), f32[7,8,128]{2,0,1:T(8,128)S(1)}, u32[]{:S(2)}, u32[]{:S(2)}) async-start(f32[7,8,128]{2,0,1:T(8,128)} %pad_maximum_fusion.4), calls=%async_computation | async-start | bytes 65536 | tf_op jit(solution)/shard_map/all_to_all | solution.py:111
  14.8 1.3 iota_compare_fusion
  16.7 3.4 %all-to-all-done = f32[7,8,128]{2,0,1:T(8,128)S(1)} async-done(((f32[7,8,128]{2,0,1:T(8,128)}), f32[7,8,128]{2,0,1:T(8,128)S(1)}, u32[]{:S(2)}, u32[]{:S(2)}) %all-to-all-start) | async-done | bytes 28704 | tf_op jit(solution)/shard_map/all_to_all | solution.py:111
  20.8 1.3 fusion.15
  22.2 4.9 %fusion.53 = bf16[4,4,20,1024]{3,2,0,1:T(8,128)(2,1)S(1)} fusion(bf16[4,4,20,16,256]{4,3,2,1,0:T(8,128)(2,1)S(1)} %bitcast.121, s32[16,256]{1,0:T(8,128)S(1)} %multiply_add_fusion, s32[1024]{0:T(1024)S(1)} %bitcast.135, pred[1024]{0:T(1024)(128)(4,1)S(1)} %get-tuple-element.28, f32[4,1024]{1,0:T(4,128)S(1)} %fusion.15), kind=kOutput, calls=%fused_computation.57 | convolution fusion | flops 2693398528 | bytes 3314688 | tf_op jit(solution)/shard_map/lgmxy,sxy->glms/dot_general | solution.py:126
  27.1 1.4 copy.61
  28.5 3.8 %all-to-all-start.1 = ((bf16[4,4,20,1024]{3,1,2,0:T(4,128)(2,1)}), bf16[4,4,20,1024]{3,1,2,0:T(4,128)(2,1)S(1)}, u32[]{:S(2)}, u32[]{:S(2)}) async-start(bf16[4,4,20,1024]{3,1,2,0:T(4,128)(2,1)} %copy.61), calls=%async_computation.1 | async-start | bytes 1310720 | tf_op jit(solution)/shard_map/all_to_all | solution.py:140
  32.3 1.2 abs_convert_fusion.1
  33.5 1.7 %abs_convert_fusion = f32[2,1024,256]{2,1,0:T(8,128)} fusion(s32[2,1024]{1,0:T(2,128)S(1)} %get-tuple-element.20), kind=kLoop, calls=%fused_computation.46 | loop fusion | flops 1572864 | bytes 2105344 | tf_op jit(solution)/shard_map/vmap()/convert_element_type | solution.py:11
  35.3 3.1 %and_reduce_fusion = pred[2,1024]{1,0:T(4,128)(4,1)S(1)} fusion(s32[2,1024]{1,0:T(2,128)S(1)} %slice.80, pred[1024,1024]{1,0:T(8,128)(4,1)} %iota_compare_fusion), kind=kLoop, calls=%fused_computation.18 | loop fusion | flops 6289408 | bytes 1058816 | tf_op jit(solution)/shard_map/reduce_or | solution.py:24
  38.3 4.0 %all-to-all-done.1 = bf16[4,4,20,1024]{3,1,2,0:T(4,128)(2,1)S(1)} async-done(((bf16[4,4,20,1024]{3,1,2,0:T(4,128)(2,1)}), bf16[4,4,20,1024]{3,1,2,0:T(4,128)(2,1)S(1)}, u32[]{:S(2)}, u32[]{:S(2)}) %all-to-all-start.1) | async-done | bytes 655392 | tf_op jit(solution)/shard_map/all_to_all | solution.py:140
  42.3 1.2 copy.62
  43.5 1.5 %reshape.267 = bf16[16,20,1024]{2,0,1:T(8,128)(2,1)S(1)} reshape(bf16[4,4,20,1024]{3,1,0,2:T(4,128)(2,1)} %copy.62) | data formatting | bytes 1310720 | tf_op jit(solution)/shard_map/reshape | solution.py:141
  45.0 1.2 fusion.58
  46.2 1.6 %reshape.268 = bf16[4,4,20,1024]{3,1,0,2:T(4,128)(2,1)S(1)} reshape(bf16[16,20,1024]{2,0,1:T(8,128)(2,1)} %fusion.58) | data formatting | bytes 1310720 | tf_op jit(solution)/shard_map/reshape | solution.py:145
  47.8 1.0 dynamic-slice_bitcast_fusion.3
  48.8 1.3 collective-permute-start.4
  50.1 1.3 collective-permute-start.7
  51.4 1.3 collective-permute-start.6
  52.7 6.5 %collective-permute-start = (bf16[4,20,1024]{2,0,1:T(4,128)(2,1)}, bf16[4,20,1024]{2,0,1:T(4,128)(2,1)}, u32[]{:S(2)}, u32[]{:S(2)}) collective-permute-start(bf16[4,20,1024]{2,0,1:T(4,128)(2,1)} %get-tuple-element.13), channel_id=1, source_target_pairs={{0,4},{1,5},{2,6},{3,7},{4,8},{5,9},{6,10},{7,11},{8,12},{9,13},{1... | collective-permute-start | bytes 491528 | tf_op jit(solution)/shard_map/ppermute | solution.py:68
  59.2 4.3 %collective-permute-start.3 = (bf16[4,20,1024]{2,0,1:T(4,128)(2,1)}, bf16[4,20,1024]{2,0,1:T(4,128)(2,1)}, u32[]{:S(2)}, u32[]{:S(2)}) collective-permute-start(bf16[4,20,1024]{2,0,1:T(4,128)(2,1)} %get-tuple-element.14), channel_id=1, source_target_pairs={{0,7},{1,4},{2,5},{3,6},{4,11},{5,8},{6,9},{7,10},{8,15},{9,12},{1... | collective-permute-start | bytes 491528 | tf_op jit(solution)/shard_map/ppermute | solution.py:68
  63.5 4.4 %collective-permute-start.2 = (bf16[4,20,1024]{2,0,1:T(4,128)(2,1)}, bf16[4,20,1024]{2,0,1:T(4,128)(2,1)}, u32[]{:S(2)}, u32[]{:S(2)}) collective-permute-start(bf16[4,20,1024]{2,0,1:T(4,128)(2,1)} %get-tuple-element.15), channel_id=1, source_target_pairs={{0,6},{1,7},{2,4},{3,5},{4,10},{5,11},{6,8},{7,9},{8,14},{9,15},{1... | collective-permute-start | bytes 491528 | tf_op jit(solution)/shard_map/ppermute | solution.py:68
  67.8 1.3 collective-permute-start.5
  69.2 6.0 %collective-permute-start.1 = (bf16[4,20,1024]{2,0,1:T(4,128)(2,1)S(1)}, bf16[4,20,1024]{2,0,1:T(4,128)(2,1)}, u32[]{:S(2)}, u32[]{:S(2)}) collective-permute-start(bf16[4,20,1024]{2,0,1:T(4,128)(2,1)S(1)} %get-tuple-element.16), channel_id=1, source_target_pairs={{0,5},{1,6},{2,7},{3,4},{4,9},{5,10},{6,11},{7,8},{8,13},{9,14},{1... | collective-permute-start | bytes 491528 | tf_op jit(solution)/shard_map/ppermute | solution.py:68
  75.2 1.1 copy.64
  76.3 4.2 %all-to-all-start.2 = ((bf16[4,4,20,1024]{3,1,2,0:T(4,128)(2,1)}), bf16[4,4,20,1024]{3,1,2,0:T(4,128)(2,1)}, u32[]{:S(2)}, u32[]{:S(2)}) async-start(bf16[4,4,20,1024]{3,1,2,0:T(4,128)(2,1)} %copy.64), calls=%async_computation.2 | async-start | bytes 1310720 | tf_op jit(solution)/shard_map/all_to_all | solution.py:146
  80.5 1.7 %pad_maximum_fusion.3 = bf16[4,4,20,1024]{3,1,2,0:T(4,128)(2,1)S(1)} fusion(bf16[1,4,20,1024]{3,1,2,0:T(4,128)(2,1)} %bitcast.127, bf16[1,4,20,1024]{3,1,2,0:T(4,128)(2,1)} %bitcast.128, bf16[1,4,20,1024]{3,1,2,0:T(4,128)(2,1)} %bitcast.41, bf16[1,4,20,1024]{3,1,2,0:T(4,128)(2,1)} %bitcast.126), kind=kLoop, calls=%fused_computation.68 | loop fusion | flops 983040 | bytes 1310720 | tf_op jit(solution)/shard_map/stack | solution.py:70
  82.2 1.9 %gather_fusion.1 = bf16[4,4,20,1024]{3,1,2,0:T(4,128)(2,1)} fusion(bf16[4,4,20,1024]{3,1,2,0:T(4,128)(2,1)S(1)} %pad_maximum_fusion.3, s32[1024]{0:T(1024)S(1)} %pad_clamp_fusion), kind=kCustom, calls=%fused_computation.1.clone | custom fusion | bytes 1310736 | tf_op jit(solution)/shard_map/jit(_take)/gather | solution.py:70
  84.2 1.7 %pad_maximum_fusion.2 = bf16[4,4,20,1024]{3,1,2,0:T(4,128)(2,1)S(1)} fusion(bf16[1,4,20,1024]{3,1,2,0:T(4,128)(2,1)} %bitcast.38, bf16[1,4,20,1024]{3,1,2,0:T(4,128)(2,1)} %bitcast.36, bf16[1,4,20,1024]{3,1,2,0:T(4,128)(2,1)} %bitcast.34, bf16[1,4,20,1024]{3,1,2,0:T(4,128)(2,1)} %bitcast.32), kind=kLoop, calls=%fused_computation.67 | loop fusion | flops 983040 | bytes 1310720 | tf_op jit(solution)/shard_map/stack | solution.py:70
  85.9 1.9 %gather_fusion = bf16[4,4,20,1024]{3,1,2,0:T(4,128)(2,1)} fusion(bf16[4,4,20,1024]{3,1,2,0:T(4,128)(2,1)S(1)} %pad_maximum_fusion.2, s32[1024]{0:T(1024)S(1)} %pad_clamp_fusion), kind=kCustom, calls=%fused_computation.clone | custom fusion | bytes 1310736 | tf_op jit(solution)/shard_map/jit(_take)/gather | solution.py:70
  87.8 2.1 %select_bitcast_fusion.1 = (bf16[1,4,4,20,1024]{4,2,3,1,0:T(4,128)(2,1)S(1)}, bf16[1,4,4,20,1024]{4,2,3,1,0:T(4,128)(2,1)S(1)}) fusion(bf16[4,4,20,1024]{3,1,2,0:T(4,128)(2,1)} %gather_fusion, pred[4]{0:T(512)(128)(4,1)} %compare_and_fusion.1, bf16[4,4,20,1024]{3,1,2,0:T(4,128)(2,1)} %gather_fusion.1), kind=kLoop, calls=%fused_computation.70 | loop fusion | flops 655360 | bytes 2621444 | tf_op jit(solution)/shard_map/stack | solution.py:176
  89.9 0.9 pad_maximum_fusion.1
  91.3 6.3 %fusion.32 = bf16[2,4,4,20,16,256]{5,4,3,2,1,0:T(8,128)(2,1)S(1)} fusion(f32[4]{0:T(128)S(1)} %copy-done.7, f32[2,1024,256]{2,1,0:T(8,128)S(1)} %copy-done.1, f32[4]{0:T(128)S(1)} %copy-done.9, pred[2,16,1024]{2,1,0:T(8,128)(4,1)S(1)} %iota_compare_fusion.7, bf16[2,4,4,20,1024]{4,3,1,2,0:T(8,128)(2,1)S(1)} %copy.66, bf16[2,1024]{1,0:T(2,128)(2,1)S(1)} %not_convert_fusion), kind=kOutput, calls=%fused_computation.42 | convolution fusion | flops 5394399232 | bytes 8687648 | tf_op jit(solution)/shard_map/vmap(gkmxs,ksz->kgmxz)/dot_general | solution.py:51
  97.7 3.3 %fusion.19 = f32[4,16,80,256,1]{3,1,4,2,0:T(8,128)} fusion(bf16[2,4,80,16,256]{4,3,2,1,0:T(8,128)(2,1)S(1)} %bitcast.124, bf16[4,3,16,16]{2,3,0,1:T(8,128)(2,1)S(1)} %select_convert_fusion.2), kind=kOutput, calls=%fused_computation.27 | convolution fusion | flops 83886080 | bytes 10518528 | tf_op jit(solution)/shard_map/tkmey,ktex->kmxy/dot_general | solution.py:186
  100.9 1.4 copy.65
  102.4 5.1 %fusion.48 = bf16[4,4,20,16,256]{4,3,2,1,0:T(8,128)(2,1)S(1)} fusion(f32[4]{0:T(128)S(1)} %copy-done.7, f32[1024,256]{1,0:T(8,128)} %abs_convert_fusion.1, f32[4]{0:T(128)S(1)} %copy-done.9, pred[16,1024]{1,0:T(8,128)(4,1)S(1)} %iota_compare_fusion.8, bf16[4,4,20,1024]{3,2,0,1:T(8,128)(2,1)S(1)} %copy.65, bf16[1024]{0:T(1024)(128)(2,1)S(1)} %get-tuple-element.27), kind=kOutput, calls=%fused_computation.55 | convolution fusion | flops 2697199616 | bytes 4343840 | tf_op jit(solution)/shard_map/gkmxs,ksz->kgmxz/dot_general | solution.py:51
  107.5 6.0 %subtract_convert_fusion = (bf16[4,80,16,256]{3,2,1,0:T(8,128)(2,1)S(1)}, bf16[4,80,16,256]{3,2,1,0:T(8,128)(2,1)S(1)}, f32[4,80,16,256]{3,2,1,0:T(8,128)}) fusion(f32[4,16,80,256,1]{3,1,4,2,0:T(8,128)S(1)} %bitcast.123, f32[4,80,16,256]{3,2,1,0:T(8,128)} %param.19, bf16[4,80,16,256]{3,2,1,0:T(8,128)(2,1)S(1)} %bitcast.125, ...), kind=kOutput, calls=%fused_computation.29 | convolution fusion | flops 49807360 | bytes 23609344 | tf_op jit(solution)/shard_map/kmey,kex->kmxy/dot_general | solution.py:171
  113.9 4.2 %fusion.59 = f32[160,160]{0,1:T(8,128)S(1)} fusion(bf16[4,160,16,256]{3,2,1,0:T(8,128)(2,1)S(1)} %pad_maximum_fusion), kind=kOutput, calls=%fused_computation.61 | convolution fusion | flops 838860800 | bytes 5345280 | tf_op jit(solution)/shard_map/kpxy,kqxy->pq/dot_general | solution.py:78
  118.7 0.9 collective-permute-done.8
  119.7 1.9 %collective-permute-start.9 = (f32[80,80]{0,1:T(8,128)S(1)}, f32[80,80]{0,1:T(8,128)S(1)}, u32[]{:S(2)}, u32[]{:S(2)}) collective-permute-start(f32[80,80]{0,1:T(8,128)S(1)} %fusion.82), channel_id=1, source_target_pairs={{0,2},{1,3},{2,0},{3,1},{4,6},{5,7},{6,4},{7,5},{8,10},{9,11},{10,... | collective-permute-start | bytes 76808 | tf_op jit(solution)/shard_map/ppermute | solution.py:39
  121.6 2.1 %collective-permute-done.9 = f32[80,80]{0,1:T(8,128)S(1)} collective-permute-done((f32[80,80]{0,1:T(8,128)S(1)}, f32[80,80]{0,1:T(8,128)S(1)}, u32[]{:S(2)}, u32[]{:S(2)}) %collective-permute-start.9) | collective-permute-done | bytes 25632 | tf_op jit(solution)/shard_map/ppermute | solution.py:39
  123.8 3.5 %collective-permute-start.10 = (f32[80,80]{0,1:T(8,128)S(1)}, f32[80,80]{0,1:T(8,128)S(1)}, u32[]{:S(2)}, u32[]{:S(2)}) collective-permute-start(f32[80,80]{0,1:T(8,128)S(1)} %add.160), channel_id=1, source_target_pairs={{0,4},{4,0},{8,12},{12,8},{16,20},{20,16},{24,28},{28,24},{1,5},{5... | collective-permute-start | bytes 76808 | tf_op jit(solution)/shard_map/ppermute | solution.py:39
  127.3 2.0 %collective-permute-done.10 = f32[80,80]{0,1:T(8,128)S(1)} collective-permute-done((f32[80,80]{0,1:T(8,128)S(1)}, f32[80,80]{0,1:T(8,128)S(1)}, u32[]{:S(2)}, u32[]{:S(2)}) %collective-permute-start.10) | collective-permute-done | bytes 25632 | tf_op jit(solution)/shard_map/ppermute | solution.py:39
  130.0 3.3 %collective-permute-done.11 = f32[80,80]{0,1:T(8,128)S(1)} collective-permute-done((f32[80,80]{0,1:T(8,128)S(1)}, f32[80,80]{0,1:T(8,128)S(1)}, u32[]{:S(2)}, u32[]{:S(2)}) %collective-permute-start.11) | collective-permute-done | bytes 25632 | tf_op jit(solution)/shard_map/ppermute | solution.py:39
  133.3 1.6 %collective-permute-start.12 = (f32[80,80]{0,1:T(8,128)S(1)}, f32[80,80]{0,1:T(8,128)S(1)}, u32[]{:S(2)}, u32[]{:S(2)}) collective-permute-start(f32[80,80]{0,1:T(8,128)S(1)} %add.162), channel_id=1, source_target_pairs={{0,16},{4,20},{8,24},{12,28},{16,0},{20,4},{24,8},{28,12},{1,17},{... | collective-permute-start | bytes 76808 | tf_op jit(solution)/shard_map/ppermute | solution.py:39
  134.8 3.8 %collective-permute-done.12 = f32[80,80]{0,1:T(8,128)S(1)} collective-permute-done((f32[80,80]{0,1:T(8,128)S(1)}, f32[80,80]{0,1:T(8,128)S(1)}, u32[]{:S(2)}, u32[]{:S(2)}) %collective-permute-start.12) | collective-permute-done | bytes 25632 | tf_op jit(solution)/shard_map/ppermute | solution.py:39
  138.7 7.3 %cholesky.18 = f32[80,80]{1,0:T(8,128)S(1)} custom-call(f32[80,80]{1,0:T(8,128)S(1)} %fusion.68), custom_call_target="Cholesky" | custom-call | tf_op jit(solution)/shard_map/jit(cholesky)/cholesky | solution.py:195
  (75 shorter events, 10.9 us)
Async XLA Ops:
  0.6 21.6 %copy-start = (bf16[4,80,16,256]{3,2,1,0:T(8,128)(2,1)S(1)}, bf16[4,80,16,256]{3,2,1,0:T(8,128)(2,1)}, u32[]{:S(2)}) copy-start(bf16[4,80,16,256]{3,2,1,0:T(8,128)(2,1)} %param.16) | copy-start | bytes 7864324
  6.2 13.9 %all-to-all-start = ((f32[7,8,128]{2,0,1:T(8,128)}), f32[7,8,128]{2,0,1:T(8,128)S(1)}, u32[]{:S(2)}, u32[]{:S(2)}) async-start(f32[7,8,128]{2,0,1:T(8,128)} %pad_maximum_fusion.4), calls=%async_computation | async-start | bytes 65536 | tf_op jit(solution)/shard_map/all_to_all | solution.py:111
  14.1 6.7 %copy-start.6 = (f32[4]{0:T(128)}, f32[4]{0:T(128)S(1)}, u32[]{:S(2)}) copy-start(f32[4]{0:T(128)S(1)} %broadcast_add_fusion) | copy-start | bytes 52
  14.7 6.0 %copy-start.8 = (f32[4]{0:T(128)}, f32[4]{0:T(128)S(1)}, u32[]{:S(2)}) copy-start(f32[4]{0:T(128)S(1)} %convert_element_type.93) | copy-start | bytes 52
  28.5 16.5 %copy-start.5 = (bf16[16,16]{1,0:T(8,128)(2,1)S(1)}, bf16[16,16]{1,0:T(8,128)(2,1)}, u32[]{:S(2)}) copy-start(bf16[16,16]{1,0:T(8,128)(2,1)} %param.17) | copy-start | bytes 1540
  28.5 13.8 %all-to-all-start.1 = ((bf16[4,4,20,1024]{3,1,2,0:T(4,128)(2,1)}), bf16[4,4,20,1024]{3,1,2,0:T(4,128)(2,1)S(1)}, u32[]{:S(2)}, u32[]{:S(2)}) async-start(bf16[4,4,20,1024]{3,1,2,0:T(4,128)(2,1)} %copy.61), calls=%async_computation.1 | async-start | bytes 1310720 | tf_op jit(solution)/shard_map/all_to_all | solution.py:140
  48.8 14.7 %collective-permute-start.4 = (bf16[4,20,1024]{2,0,1:T(4,128)(2,1)}, bf16[4,20,1024]{2,0,1:T(4,128)(2,1)S(1)}, u32[]{:S(2)}, u32[]{:S(2)}) collective-permute-start(bf16[4,20,1024]{2,0,1:T(4,128)(2,1)} %get-tuple-element.13), channel_id=1, source_target_pairs={{4,0},{5,1},{6,2},{7,3},{8,4},{9,5},{10,6},{11,7},{12,8},{13,9},{1... | collective-permute-start | bytes 491528 | tf_op jit(solution)/shard_map/ppermute | solution.py:68
  50.1 17.7 %collective-permute-start.7 = (bf16[4,20,1024]{2,0,1:T(4,128)(2,1)}, bf16[4,20,1024]{2,0,1:T(4,128)(2,1)S(1)}, u32[]{:S(2)}, u32[]{:S(2)}) collective-permute-start(bf16[4,20,1024]{2,0,1:T(4,128)(2,1)} %get-tuple-element.14), channel_id=1, source_target_pairs={{4,3},{5,0},{6,1},{7,2},{8,7},{9,4},{10,5},{11,6},{12,11},{13,8},{... | collective-permute-start | bytes 491528 | tf_op jit(solution)/shard_map/ppermute | solution.py:68
  51.4 17.7 %collective-permute-start.6 = (bf16[4,20,1024]{2,0,1:T(4,128)(2,1)}, bf16[4,20,1024]{2,0,1:T(4,128)(2,1)S(1)}, u32[]{:S(2)}, u32[]{:S(2)}) collective-permute-start(bf16[4,20,1024]{2,0,1:T(4,128)(2,1)} %get-tuple-element.15), channel_id=1, source_target_pairs={{4,2},{5,3},{6,0},{7,1},{8,6},{9,7},{10,4},{11,5},{12,10},{13,11},... | collective-permute-start | bytes 491528 | tf_op jit(solution)/shard_map/ppermute | solution.py:68
  52.7 31.4 %collective-permute-start = (bf16[4,20,1024]{2,0,1:T(4,128)(2,1)}, bf16[4,20,1024]{2,0,1:T(4,128)(2,1)}, u32[]{:S(2)}, u32[]{:S(2)}) collective-permute-start(bf16[4,20,1024]{2,0,1:T(4,128)(2,1)} %get-tuple-element.13), channel_id=1, source_target_pairs={{0,4},{1,5},{2,6},{3,7},{4,8},{5,9},{6,10},{7,11},{8,12},{9,13},{1... | collective-permute-start | bytes 491528 | tf_op jit(solution)/shard_map/ppermute | solution.py:68
  59.2 25.0 %collective-permute-start.3 = (bf16[4,20,1024]{2,0,1:T(4,128)(2,1)}, bf16[4,20,1024]{2,0,1:T(4,128)(2,1)}, u32[]{:S(2)}, u32[]{:S(2)}) collective-permute-start(bf16[4,20,1024]{2,0,1:T(4,128)(2,1)} %get-tuple-element.14), channel_id=1, source_target_pairs={{0,7},{1,4},{2,5},{3,6},{4,11},{5,8},{6,9},{7,10},{8,15},{9,12},{1... | collective-permute-start | bytes 491528 | tf_op jit(solution)/shard_map/ppermute | solution.py:68
  63.5 11.7 %copy-start.2 = (bf16[4,20,1024]{2,0,1:T(4,128)(2,1)}, bf16[4,20,1024]{2,0,1:T(4,128)(2,1)S(1)}, u32[]{:S(2)}) copy-start(bf16[4,20,1024]{2,0,1:T(4,128)(2,1)S(1)} %collective-permute-done.4) | copy-start | bytes 491524
  63.5 20.7 %collective-permute-start.2 = (bf16[4,20,1024]{2,0,1:T(4,128)(2,1)}, bf16[4,20,1024]{2,0,1:T(4,128)(2,1)}, u32[]{:S(2)}, u32[]{:S(2)}) collective-permute-start(bf16[4,20,1024]{2,0,1:T(4,128)(2,1)} %get-tuple-element.15), channel_id=1, source_target_pairs={{0,6},{1,7},{2,4},{3,5},{4,10},{5,11},{6,8},{7,9},{8,14},{9,15},{1... | collective-permute-start | bytes 491528 | tf_op jit(solution)/shard_map/ppermute | solution.py:68
  67.8 7.3 %copy-start.3 = (bf16[4,20,1024]{2,0,1:T(4,128)(2,1)}, bf16[4,20,1024]{2,0,1:T(4,128)(2,1)S(1)}, u32[]{:S(2)}) copy-start(bf16[4,20,1024]{2,0,1:T(4,128)(2,1)S(1)} %collective-permute-done.7) | copy-start | bytes 491524
  67.8 12.6 %collective-permute-start.5 = (bf16[4,20,1024]{2,0,1:T(4,128)(2,1)S(1)}, bf16[4,20,1024]{2,0,1:T(4,128)(2,1)}, u32[]{:S(2)}, u32[]{:S(2)}) collective-permute-start(bf16[4,20,1024]{2,0,1:T(4,128)(2,1)S(1)} %get-tuple-element.16), channel_id=1, source_target_pairs={{4,1},{5,2},{6,3},{7,0},{8,5},{9,6},{10,7},{11,4},{12,9},{13,10},{... | collective-permute-start | bytes 491528 | tf_op jit(solution)/shard_map/ppermute | solution.py:68
  69.1 6.0 %copy-start.4 = (bf16[4,20,1024]{2,0,1:T(4,128)(2,1)}, bf16[4,20,1024]{2,0,1:T(4,128)(2,1)S(1)}, u32[]{:S(2)}) copy-start(bf16[4,20,1024]{2,0,1:T(4,128)(2,1)S(1)} %collective-permute-done.6) | copy-start | bytes 491524
  69.2 15.0 %collective-permute-start.1 = (bf16[4,20,1024]{2,0,1:T(4,128)(2,1)S(1)}, bf16[4,20,1024]{2,0,1:T(4,128)(2,1)}, u32[]{:S(2)}, u32[]{:S(2)}) collective-permute-start(bf16[4,20,1024]{2,0,1:T(4,128)(2,1)S(1)} %get-tuple-element.16), channel_id=1, source_target_pairs={{0,5},{1,6},{2,7},{3,4},{4,9},{5,10},{6,11},{7,8},{8,13},{9,14},{1... | collective-permute-start | bytes 491528 | tf_op jit(solution)/shard_map/ppermute | solution.py:68
  76.3 24.6 %all-to-all-start.2 = ((bf16[4,4,20,1024]{3,1,2,0:T(4,128)(2,1)}), bf16[4,4,20,1024]{3,1,2,0:T(4,128)(2,1)}, u32[]{:S(2)}, u32[]{:S(2)}) async-start(bf16[4,4,20,1024]{3,1,2,0:T(4,128)(2,1)} %copy.64), calls=%async_computation.2 | async-start | bytes 1310720 | tf_op jit(solution)/shard_map/all_to_all | solution.py:146
  87.8 3.4 %copy-start.1 = (f32[2,1024,256]{2,1,0:T(8,128)S(1)}, f32[2,1024,256]{2,1,0:T(8,128)}, u32[]{:S(2)}) copy-start(f32[2,1024,256]{2,1,0:T(8,128)} %abs_convert_fusion) | copy-start | bytes 6291460
  87.8 3.4 %copy-start.7 = (f32[4]{0:T(128)S(1)}, f32[4]{0:T(128)}, u32[]{:S(2)}) copy-start(f32[4]{0:T(128)} %copy-done.6) | copy-start | bytes 52
  87.8 3.5 %copy-start.9 = (f32[4]{0:T(128)S(1)}, f32[4]{0:T(128)}, u32[]{:S(2)}) copy-start(f32[4]{0:T(128)} %copy-done.8) | copy-start | bytes 52
  100.9 6.5 %slice-start = ((s8[5242880]{0:T(1024)(128)(4,1)}), s8[4194304]{0:T(1024)(128)(4,1)S(1)}, s32[]{:S(2)}) async-start(s8[5242880]{0:T(1024)(128)(4,1)} %bitcast.122), calls=%async_computation.3 | async-start | bytes 8388608
  102.4 5.1 %slice-start.1 = ((s8[5242880]{0:T(1024)(128)(4,1)}), s8[1048576]{0:T(1024)(128)(4,1)S(1)}, s32[]{:S(2)}) async-start(s8[5242880]{0:T(1024)(128)(4,1)} %bitcast.122), calls=%async_computation.4 | async-start | bytes 2097152
  118.2 1.4 collective-permute-start.8
  119.7 4.1 %collective-permute-start.9 = (f32[80,80]{0,1:T(8,128)S(1)}, f32[80,80]{0,1:T(8,128)S(1)}, u32[]{:S(2)}, u32[]{:S(2)}) collective-permute-start(f32[80,80]{0,1:T(8,128)S(1)} %fusion.82), channel_id=1, source_target_pairs={{0,2},{1,3},{2,0},{3,1},{4,6},{5,7},{6,4},{7,5},{8,10},{9,11},{10,... | collective-permute-start | bytes 76808 | tf_op jit(solution)/shard_map/ppermute | solution.py:39
  123.8 5.5 %collective-permute-start.10 = (f32[80,80]{0,1:T(8,128)S(1)}, f32[80,80]{0,1:T(8,128)S(1)}, u32[]{:S(2)}, u32[]{:S(2)}) collective-permute-start(f32[80,80]{0,1:T(8,128)S(1)} %add.160), channel_id=1, source_target_pairs={{0,4},{4,0},{8,12},{12,8},{16,20},{20,16},{24,28},{28,24},{1,5},{5... | collective-permute-start | bytes 76808 | tf_op jit(solution)/shard_map/ppermute | solution.py:39
  129.2 4.0 %collective-permute-start.11 = (f32[80,80]{0,1:T(8,128)S(1)}, f32[80,80]{0,1:T(8,128)S(1)}, u32[]{:S(2)}, u32[]{:S(2)}) collective-permute-start(f32[80,80]{0,1:T(8,128)S(1)} %add.161), channel_id=1, source_target_pairs={{0,8},{4,12},{8,0},{12,4},{16,24},{20,28},{24,16},{28,20},{1,9},{5... | collective-permute-start | bytes 76808 | tf_op jit(solution)/shard_map/ppermute | solution.py:39
  133.3 5.3 %collective-permute-start.12 = (f32[80,80]{0,1:T(8,128)S(1)}, f32[80,80]{0,1:T(8,128)S(1)}, u32[]{:S(2)}, u32[]{:S(2)}) collective-permute-start(f32[80,80]{0,1:T(8,128)S(1)} %add.162), channel_id=1, source_target_pairs={{0,16},{4,20},{8,24},{12,28},{16,0},{20,4},{24,8},{28,12},{1,17},{... | collective-permute-start | bytes 76808 | tf_op jit(solution)/shard_map/ppermute | solution.py:39

commit v12 on v10

--- a/solution.py
+++ b/solution.py
@@ -49,7 +49,7 @@
     col_hit = cols[None, :] == jnp.arange(col_count, dtype=jnp.int32)[:, None]
     placed = jnp.where(col_hit[None, None, None], mix[:, :, :, None, :], 0).astype(jnp.bfloat16)
     out = jnp.einsum(
-        "gkmxs,ksz->kgmxz", placed, slot_taps, preferred_element_type=jnp.float32
+        "gmkxs,ksz->kgmxz", placed, slot_taps, preferred_element_type=jnp.float32
     ).astype(jnp.bfloat16)
     return out.reshape((out.shape[0], -1) + out.shape[3:])
 
@@ -108,28 +108,27 @@
             return one_hot(cell_index, own_keep, cell_count).reshape(slots, col_count, row_count)
 
         picked = jnp.einsum(
-            "lgmxy,sxy->glms", ensemble.reshape(lev_dev, group_count, share, col_count, row_count),
+            "lgmxy,sxy->gmls", ensemble.reshape(lev_dev, group_count, share, col_count, row_count),
             own_hits(), preferred_element_type=jnp.float32,
         )
-        member_forcing = (picked * forcing[None, :, None]).astype(jnp.bfloat16)
+        member_forcing = (picked * forcing[None, None]).astype(jnp.bfloat16)
     else:
         forcing = jnp.zeros((lev_dev, cell_count), jnp.float32)
         forcing = forcing.at[:, cell_index].add(arrived[:lev_dev].reshape(lev_dev, -1))
         forcing = forcing.reshape(lev_dev, col_count, row_count)
         member_forcing = (ensemble * forcing[:, None]).astype(jnp.bfloat16)
-        member_forcing = jnp.swapaxes(
-            member_forcing.reshape((lev_dev, group_count, share) + member_forcing.shape[2:]), 0, 1
+        member_forcing = jnp.moveaxis(
+            member_forcing.reshape((lev_dev, group_count, share) + member_forcing.shape[2:]), 0, 2
         )
 
     regrouped = lax.all_to_all(member_forcing, "lev", split_axis=0, concat_axis=0, tiled=True)
-    regrouped = regrouped.reshape((group_count * lev_dev,) + regrouped.shape[2:])
+    mixing = vert_root.reshape(group_count, lev_dev, group_count, lev_dev)
     local_mix = jnp.einsum(
-        "lk,lm...->km...", vert_root, regrouped, preferred_element_type=jnp.float32
+        "hml...,hlgk->gmk...", regrouped, mixing, preferred_element_type=jnp.float32
     ).astype(jnp.bfloat16)
-    local_mix = local_mix.reshape((group_count, lev_dev) + local_mix.shape[1:])
     level_mix = lax.all_to_all(local_mix, "lev", split_axis=0, concat_axis=0, tiled=True)
     if not packed:
-        level_mix = jnp.swapaxes(level_mix, 0, 1).reshape(
+        level_mix = jnp.moveaxis(level_mix, 2, 0).reshape(
             (lev_dev, members) + level_mix.shape[3:]
         )
     ends = tile_count - 1

time: 141 us -> 136 us (0.965)
  local copies, waits for them, and re-layouts: 9.83 us -> 6.54 us
    reshape x3 -> x2, local copies, waits for them, and re-layouts: 4.19 us -> 0.99 us  [shards(): mixing = vert_root.reshape(group_count, lev_dev, group_count, lev_dev)]
  transfers between devices with their start and end apart: 10 -> 10, of which waited for: 10 -> 10; matrix products, arithmetic and copies ran while one was open for 10% -> 11% of each run, Pallas kernels for 0% -> 0%
where the time goes in v12:
time: 136 us
  waiting for transfers between devices  50.6 us (37%)
  matrix products  30.2 us (22%)
  starting transfers between devices  25.7 us (19%)
  other arithmetic  21.7 us (16%)
  local copies, waits for them, and re-layouts  6.54 us (5%)
    ppermute x5, waiting for transfers between devices, all_sum(): lax.ppermute(value, name, [(i, i ^ bit) for i in range(size)])  13.2 us
    ppermute x1, waiting for transfers between devices, shards(): lax.ppermute(level_mix, 'tile', [(i, i + 1) for i in range(ends)])  12.9 us
    dot_general x2, matrix products, spread(): jnp.einsum('gmkxs,ksz->kgmxz', placed, slot_taps, preferred_element_type=...  12.8 us
    all_to_all x1, waiting for transfers between devices, shards(): lax.all_to_all(local_mix, 'lev', split_axis=0, concat_axis=0, tiled=True)  8.47 us
    another operation x3, other arithmetic, shards(): r_factor = jnp.linalg.cholesky(gram_total).T  7.98 us
    all_to_all x1, starting transfers between devices, shards(): lax.all_to_all(outgoing, 'tile', split_axis=1, concat_axis=1, tiled=True)  7.25 us
    ppermute x1, waiting for transfers between devices, shards(): lax.ppermute(level_mix, 'tile', [(i + 1, i) for i in range(ends)])  7.1 us
    all_to_all x1, waiting for transfers between devices, shards(): lax.all_to_all(member_forcing, 'lev', split_axis=0, concat_axis=0, tiled=...  5.91 us
  transfers between devices with their start and end apart: 10, of which 10 were waited for; matrix products, arithmetic and copies ran while one was open for 11% of the time, Pallas kernels for 0%

profile of v12, /device:TPU:0, one launch (start us, length us, event | category | flops | bytes accessed | tf_op | source)
XLA Modules:
  0.0 135.8 jit_solution(1206367989616212201)
XLA Ops:
  0.6 0.9 slice_bitcast_fusion.8
  1.5 0.8 slice_bitcast_fusion.6
  2.3 0.8 select_bitcast_fusion.1
  3.0 0.7 add_convert_fusion
  3.7 1.8 %fusion.64 = f32[4,8,128]{2,0,1:T(4,128)S(1)} fusion(s32[8,128]{1,0:T(8,128)} %bitcast.124, f32[4,512]{1,0:T(4,128)} %param.9, f32[8,128]{1,0:T(8,128)S(1)} %select_bitcast_fusion.1), kind=kOutput, calls=%fused_computation.62 | convolution fusion | flops 25694208 | bytes 32768 | tf_op jit(solution)/shard_map/lo,dco->ldc/dot_general | solution.py:85
  5.5 0.6 pad_maximum_fusion.2
  6.2 7.3 %all-to-all-start = ((f32[7,8,128]{2,0,1:T(8,128)}), f32[7,8,128]{2,0,1:T(8,128)S(1)}, u32[]{:S(2)}, u32[]{:S(2)}) async-start(f32[7,8,128]{2,0,1:T(8,128)} %pad_maximum_fusion.2), calls=%async_computation | async-start | bytes 65536 | tf_op jit(solution)/shard_map/all_to_all | solution.py:95
  13.4 0.7 broadcast_add_fusion
  14.1 0.7 convert_element_type.93
  14.8 1.3 iota_compare_fusion
  16.1 0.8 reshape.259
  17.1 3.0 %all-to-all-done = f32[7,8,128]{2,0,1:T(8,128)S(1)} async-done(((f32[7,8,128]{2,0,1:T(8,128)}), f32[7,8,128]{2,0,1:T(8,128)S(1)}, u32[]{:S(2)}, u32[]{:S(2)}) %all-to-all-start) | async-done | bytes 28704 | tf_op jit(solution)/shard_map/all_to_all | solution.py:95
  20.1 0.6 fusion.30
  20.9 1.3 fusion.15
  22.2 5.0 %fusion.53 = bf16[4,20,4,1024]{3,1,0,2:T(8,128)(2,1)S(1)} fusion(bf16[4,4,20,16,256]{4,3,2,1,0:T(8,128)(2,1)S(1)} %bitcast.109, s32[16,256]{1,0:T(8,128)S(1)} %multiply_add_fusion, s32[1024]{0:T(1024)S(1)} %bitcast.122, pred[1024]{0:T(1024)(128)(4,1)S(1)} %get-tuple-element.21, f32[4,1024]{1,0:T(4,128)S(1)} %fusion.15), kind=kOutput, calls=%fused_computation.55 | convolution fusion | flops 2693398528 | bytes 3314688 | tf_op jit(solution)/shard_map/lgmxy,sxy->gmls/dot_general | solution.py:110
  27.2 1.4 %copy.43 = bf16[4,20,4,1024]{3,2,1,0:T(4,128)(2,1)} copy(bf16[4,20,4,1024]{3,1,0,2:T(8,128)(2,1)S(1)} %fusion.53) | data formatting | bytes 1310720 | tf_op jit(solution)/shard_map/convert_element_type | solution.py:114
  28.5 3.5 %all-to-all-start.1 = ((bf16[4,20,4,1024]{3,2,1,0:T(4,128)(2,1)}), bf16[4,20,4,1024]{3,2,1,0:T(4,128)(2,1)S(1)}, u32[]{:S(2)}, u32[]{:S(2)}) async-start(bf16[4,20,4,1024]{3,2,1,0:T(4,128)(2,1)} %copy.43), calls=%async_computation.1 | async-start | bytes 1310720 | tf_op jit(solution)/shard_map/all_to_all | solution.py:124
  32.0 1.2 abs_convert_fusion.1
  33.2 3.1 %and_reduce_fusion = pred[2,1024]{1,0:T(4,128)(4,1)S(1)} fusion(s32[2,1024]{1,0:T(2,128)S(1)} %slice.80, pred[1024,1024]{1,0:T(8,128)(4,1)} %iota_compare_fusion), kind=kLoop, calls=%fused_computation.16 | loop fusion | flops 6289408 | bytes 1058816 | tf_op jit(solution)/shard_map/reduce_or | solution.py:24
  36.3 5.9 %all-to-all-done.1 = bf16[4,20,4,1024]{3,2,1,0:T(4,128)(2,1)S(1)} async-done(((bf16[4,20,4,1024]{3,2,1,0:T(4,128)(2,1)}), bf16[4,20,4,1024]{3,2,1,0:T(4,128)(2,1)S(1)}, u32[]{:S(2)}, u32[]{:S(2)}) %all-to-all-start.1) | async-done | bytes 655392 | tf_op jit(solution)/shard_map/all_to_all | solution.py:124
  42.2 0.7 fusion.59
  42.9 1.1 copy.46
  44.0 3.5 %all-to-all-start.2 = ((bf16[4,20,4,1024]{3,2,1,0:T(4,128)(2,1)}), bf16[4,20,4,1024]{3,2,1,0:T(4,128)(2,1)S(1)}, u32[]{:S(2)}, u32[]{:S(2)}) async-start(bf16[4,20,4,1024]{3,2,1,0:T(4,128)(2,1)} %copy.46), calls=%async_computation.2 | async-start | bytes 1310720 | tf_op jit(solution)/shard_map/all_to_all | solution.py:129
  47.5 1.7 %abs_convert_fusion = f32[2,1024,256]{2,1,0:T(8,128)} fusion(s32[2,1024]{1,0:T(2,128)S(1)} %get-tuple-element.13), kind=kLoop, calls=%fused_computation.44 | loop fusion | flops 1572864 | bytes 2105344 | tf_op jit(solution)/shard_map/vmap()/convert_element_type | solution.py:11
  49.3 8.5 %all-to-all-done.2 = bf16[4,20,4,1024]{3,2,1,0:T(4,128)(2,1)S(1)} async-done(((bf16[4,20,4,1024]{3,2,1,0:T(4,128)(2,1)}), bf16[4,20,4,1024]{3,2,1,0:T(4,128)(2,1)S(1)}, u32[]{:S(2)}, u32[]{:S(2)}) %all-to-all-start.2) | async-done | bytes 655392 | tf_op jit(solution)/shard_map/all_to_all | solution.py:129
  57.7 1.3 collective-permute-start.1
  59.0 4.8 %collective-permute-start = (bf16[4,20,4,1024]{3,2,1,0:T(4,128)(2,1)S(1)}, bf16[4,20,4,1024]{3,2,1,0:T(4,128)(2,1)S(1)}, u32[]{:S(2)}, u32[]{:S(2)}) collective-permute-start(bf16[4,20,4,1024]{3,2,1,0:T(4,128)(2,1)S(1)} %all-to-all-done.2), channel_id=1, source_target_pairs={{0,4},{4,8},{8,12},{12,16},{16,20},{20,24},{24,28},{1,5},{5,9},{9,... | collective-permute-start | bytes 1966088 | tf_op jit(solution)/shard_map/ppermute | solution.py:135
  64.0 4.8 %fusion.48 = bf16[4,4,20,16,256]{4,3,2,1,0:T(8,128)(2,1)S(1)} fusion(f32[4]{0:T(128)S(1)} %broadcast_add_fusion, f32[1024,256]{1,0:T(8,128)} %abs_convert_fusion.1, f32[4]{0:T(128)S(1)} %convert_element_type.93, pred[16,1024]{1,0:T(8,128)(4,1)S(1)} %iota_compare_fusion.8, bf16[4,20,4,1024]{3,1,0,2:T(8,128)(2,1)S(1)} %copy.47, ...), kind=kOutput, calls=%fused_computation.53 | convolution fusion | flops 2697199616 | bytes 4343840 | tf_op jit(solution)/shard_map/gmkxs,ksz->kgmxz/dot_general | solution.py:51
  68.8 7.1 %collective-permute-done.1 = bf16[4,20,4,1024]{3,2,1,0:T(4,128)(2,1)S(1)} collective-permute-done((bf16[4,20,4,1024]{3,2,1,0:T(4,128)(2,1)S(1)}, bf16[4,20,4,1024]{3,2,1,0:T(4,128)(2,1)S(1)}, u32[]{:S(2)}, u32[]{:S(2)}) %collective-permute-start.1) | collective-permute-done | bytes 655392 | tf_op jit(solution)/shard_map/ppermute | solution.py:136
  75.9 12.9 %collective-permute-done = bf16[4,20,4,1024]{3,2,1,0:T(4,128)(2,1)S(1)} collective-permute-done((bf16[4,20,4,1024]{3,2,1,0:T(4,128)(2,1)S(1)}, bf16[4,20,4,1024]{3,2,1,0:T(4,128)(2,1)S(1)}, u32[]{:S(2)}, u32[]{:S(2)}) %collective-permute-start) | collective-permute-done | bytes 655392 | tf_op jit(solution)/shard_map/ppermute | solution.py:135
  88.8 0.9 pad_maximum_fusion.1
  90.2 8.0 %fusion.32 = bf16[2,4,4,20,16,256]{5,4,3,2,1,0:T(8,128)(2,1)S(1)} fusion(f32[4]{0:T(128)S(1)} %broadcast_add_fusion, f32[2,1024,256]{2,1,0:T(8,128)} %abs_convert_fusion, f32[4]{0:T(128)S(1)} %convert_element_type.93, pred[2,16,1024]{2,1,0:T(8,128)(4,1)S(1)} %iota_compare_fusion.7, bf16[2,4,20,4,1024]{4,2,1,3,0:T(8,128)(2,1)S(1)} %copy.48, ...), kind=kOutput, calls=%fused_computation.40 | convolution fusion | flops 5394399232 | bytes 8687648 | tf_op jit(solution)/shard_map/vmap(gmkxs,ksz->kgmxz)/dot_general | solution.py:51
  98.2 0.9 fusion.19
  99.2 3.6 %subtract_convert_fusion = (bf16[4,80,16,256]{3,2,1,0:T(8,128)(2,1)S(1)}, bf16[4,80,16,256]{3,2,1,0:T(8,128)(2,1)S(1)}, f32[4,80,16,256]{3,2,1,0:T(8,128)}) fusion(f32[4,16,80,256,1]{3,1,4,2,0:T(8,128)S(1)} %fusion.19, f32[4,80,16,256]{3,2,1,0:T(8,128)S(1)} %bitcast.112, bf16[4,80,16,256]{3,2,1,0:T(8,128)(2,1)S(1)} %bitcast.113, ...), kind=kOutput, calls=%fused_computation.27 | convolution fusion | flops 49807360 | bytes 23609344 | tf_op jit(solution)/shard_map/kmey,kex->kmxy/dot_general | solution.py:150
  103.2 4.2 %fusion.60 = f32[160,160]{0,1:T(8,128)S(1)} fusion(bf16[4,160,16,256]{3,2,1,0:T(8,128)(2,1)S(1)} %pad_maximum_fusion), kind=kOutput, calls=%fused_computation.60 | convolution fusion | flops 838860800 | bytes 5345280 | tf_op jit(solution)/shard_map/kpxy,kqxy->pq/dot_general | solution.py:62
  107.6 1.2 collective-permute-done.2
  108.9 0.7 collective-permute-start.3
  109.6 3.4 %collective-permute-done.3 = f32[80,80]{0,1:T(8,128)S(1)} collective-permute-done((f32[80,80]{0,1:T(8,128)S(1)}, f32[80,80]{0,1:T(8,128)S(1)}, u32[]{:S(2)}, u32[]{:S(2)}) %collective-permute-start.3) | collective-permute-done | bytes 25632 | tf_op jit(solution)/shard_map/ppermute | solution.py:39
  113.0 2.5 %collective-permute-start.4 = (f32[80,80]{0,1:T(8,128)S(1)}, f32[80,80]{0,1:T(8,128)S(1)}, u32[]{:S(2)}, u32[]{:S(2)}) collective-permute-start(f32[80,80]{0,1:T(8,128)S(1)} %add.91), channel_id=1, source_target_pairs={{0,4},{4,0},{8,12},{12,8},{16,20},{20,16},{24,28},{28,24},{1,5},{5... | collective-permute-start | bytes 76808 | tf_op jit(solution)/shard_map/ppermute | solution.py:39
  115.4 2.0 %collective-permute-done.4 = f32[80,80]{0,1:T(8,128)S(1)} collective-permute-done((f32[80,80]{0,1:T(8,128)S(1)}, f32[80,80]{0,1:T(8,128)S(1)}, u32[]{:S(2)}, u32[]{:S(2)}) %collective-permute-start.4) | collective-permute-done | bytes 25632 | tf_op jit(solution)/shard_map/ppermute | solution.py:39
  117.4 1.0 collective-permute-start.5
  118.5 3.0 %collective-permute-done.5 = f32[80,80]{0,1:T(8,128)S(1)} collective-permute-done((f32[80,80]{0,1:T(8,128)S(1)}, f32[80,80]{0,1:T(8,128)S(1)}, u32[]{:S(2)}, u32[]{:S(2)}) %collective-permute-start.5) | collective-permute-done | bytes 25632 | tf_op jit(solution)/shard_map/ppermute | solution.py:39
  121.4 1.2 collective-permute-start.6
  122.6 3.7 %collective-permute-done.6 = f32[80,80]{0,1:T(8,128)S(1)} collective-permute-done((f32[80,80]{0,1:T(8,128)S(1)}, f32[80,80]{0,1:T(8,128)S(1)}, u32[]{:S(2)}, u32[]{:S(2)}) %collective-permute-start.6) | collective-permute-done | bytes 25632 | tf_op jit(solution)/shard_map/ppermute | solution.py:39
  126.4 7.3 %cholesky.18 = f32[80,80]{1,0:T(8,128)S(1)} custom-call(f32[80,80]{1,0:T(8,128)S(1)} %fusion.70), custom_call_target="Cholesky" | custom-call | tf_op jit(solution)/shard_map/jit(cholesky)/cholesky | solution.py:174
  133.8 0.6 compare_reduce_fusion
  134.4 0.7 select_bitcast_fusion
  135.1 0.7 copy.58
  (35 shorter events, 2.0 us)
Async XLA Ops:
  0.6 21.6 %copy-start = (bf16[4,80,16,256]{3,2,1,0:T(8,128)(2,1)S(1)}, bf16[4,80,16,256]{3,2,1,0:T(8,128)(2,1)}, u32[]{:S(2)}) copy-start(bf16[4,80,16,256]{3,2,1,0:T(8,128)(2,1)} %param.14) | copy-start | bytes 7864324
  6.2 13.9 %all-to-all-start = ((f32[7,8,128]{2,0,1:T(8,128)}), f32[7,8,128]{2,0,1:T(8,128)S(1)}, u32[]{:S(2)}, u32[]{:S(2)}) async-start(f32[7,8,128]{2,0,1:T(8,128)} %pad_maximum_fusion.2), calls=%async_computation | async-start | bytes 65536 | tf_op jit(solution)/shard_map/all_to_all | solution.py:95
  28.5 13.7 %all-to-all-start.1 = ((bf16[4,20,4,1024]{3,2,1,0:T(4,128)(2,1)}), bf16[4,20,4,1024]{3,2,1,0:T(4,128)(2,1)S(1)}, u32[]{:S(2)}, u32[]{:S(2)}) async-start(bf16[4,20,4,1024]{3,2,1,0:T(4,128)(2,1)} %copy.43), calls=%async_computation.1 | async-start | bytes 1310720 | tf_op jit(solution)/shard_map/all_to_all | solution.py:124
  44.0 13.7 %all-to-all-start.2 = ((bf16[4,20,4,1024]{3,2,1,0:T(4,128)(2,1)}), bf16[4,20,4,1024]{3,2,1,0:T(4,128)(2,1)S(1)}, u32[]{:S(2)}, u32[]{:S(2)}) async-start(bf16[4,20,4,1024]{3,2,1,0:T(4,128)(2,1)} %copy.46), calls=%async_computation.2 | async-start | bytes 1310720 | tf_op jit(solution)/shard_map/all_to_all | solution.py:129
  57.7 18.2 %collective-permute-start.1 = (bf16[4,20,4,1024]{3,2,1,0:T(4,128)(2,1)S(1)}, bf16[4,20,4,1024]{3,2,1,0:T(4,128)(2,1)S(1)}, u32[]{:S(2)}, u32[]{:S(2)}) collective-permute-start(bf16[4,20,4,1024]{3,2,1,0:T(4,128)(2,1)S(1)} %all-to-all-done.2), channel_id=1, source_target_pairs={{4,0},{8,4},{12,8},{16,12},{20,16},{24,20},{28,24},{5,1},{9,5},{13... | collective-permute-start | bytes 1966088 | tf_op jit(solution)/shard_map/ppermute | solution.py:136
  59.0 29.8 %collective-permute-start = (bf16[4,20,4,1024]{3,2,1,0:T(4,128)(2,1)S(1)}, bf16[4,20,4,1024]{3,2,1,0:T(4,128)(2,1)S(1)}, u32[]{:S(2)}, u32[]{:S(2)}) collective-permute-start(bf16[4,20,4,1024]{3,2,1,0:T(4,128)(2,1)S(1)} %all-to-all-done.2), channel_id=1, source_target_pairs={{0,4},{4,8},{8,12},{12,16},{16,20},{20,24},{24,28},{1,5},{5,9},{9,... | collective-permute-start | bytes 1966088 | tf_op jit(solution)/shard_map/ppermute | solution.py:135
  89.8 9.4 %slice-start = ((s8[5242880]{0:T(1024)(128)(4,1)}), s8[4194304]{0:T(1024)(128)(4,1)S(1)}, s32[]{:S(2)}) async-start(s8[5242880]{0:T(1024)(128)(4,1)} %bitcast.111), calls=%async_computation.3 | async-start | bytes 8388608
  90.2 8.9 %slice-start.1 = ((s8[5242880]{0:T(1024)(128)(4,1)}), s8[1048576]{0:T(1024)(128)(4,1)S(1)}, s32[]{:S(2)}) async-start(s8[5242880]{0:T(1024)(128)(4,1)} %bitcast.111), calls=%async_computation.4 | async-start | bytes 2097152
  107.5 1.3 collective-permute-start.2
  108.9 4.1 %collective-permute-start.3 = (f32[80,80]{0,1:T(8,128)S(1)}, f32[80,80]{0,1:T(8,128)S(1)}, u32[]{:S(2)}, u32[]{:S(2)}) collective-permute-start(f32[80,80]{0,1:T(8,128)S(1)} %fusion.82), channel_id=1, source_target_pairs={{0,2},{1,3},{2,0},{3,1},{4,6},{5,7},{6,4},{7,5},{8,10},{9,11},{10,... | collective-permute-start | bytes 76808 | tf_op jit(solution)/shard_map/ppermute | solution.py:39
  113.0 4.5 %collective-permute-start.4 = (f32[80,80]{0,1:T(8,128)S(1)}, f32[80,80]{0,1:T(8,128)S(1)}, u32[]{:S(2)}, u32[]{:S(2)}) collective-permute-start(f32[80,80]{0,1:T(8,128)S(1)} %add.91), channel_id=1, source_target_pairs={{0,4},{4,0},{8,12},{12,8},{16,20},{20,16},{24,28},{28,24},{1,5},{5... | collective-permute-start | bytes 76808 | tf_op jit(solution)/shard_map/ppermute | solution.py:39
  117.4 4.0 %collective-permute-start.5 = (f32[80,80]{0,1:T(8,128)S(1)}, f32[80,80]{0,1:T(8,128)S(1)}, u32[]{:S(2)}, u32[]{:S(2)}) collective-permute-start(f32[80,80]{0,1:T(8,128)S(1)} %add.92), channel_id=1, source_target_pairs={{0,8},{4,12},{8,0},{12,4},{16,24},{20,28},{24,16},{28,20},{1,9},{5... | collective-permute-start | bytes 76808 | tf_op jit(solution)/shard_map/ppermute | solution.py:39
  121.4 4.9 %collective-permute-start.6 = (f32[80,80]{0,1:T(8,128)S(1)}, f32[80,80]{0,1:T(8,128)S(1)}, u32[]{:S(2)}, u32[]{:S(2)}) collective-permute-start(f32[80,80]{0,1:T(8,128)S(1)} %add.93), channel_id=1, source_target_pairs={{0,16},{4,20},{8,24},{12,28},{16,0},{20,4},{24,8},{28,12},{1,17},{... | collective-permute-start | bytes 76808 | tf_op jit(solution)/shard_map/ppermute | solution.py:39

commit v13 on v12

--- a/solution.py
+++ b/solution.py
@@ -152,18 +152,20 @@
     )
     gradient = alpha + own
 
-    sides = jnp.stack([from_left, from_right])
     if packed:
-        side_cells = near[0::2]
-        sides = jax.vmap(spread, in_axes=(0, 0, 0, None, None, None))(
-            sides, side_cells, first_hits(side_cells), radius, col_count, row_count
+        left = spread(from_left, near[0], first_hits(near[0]), radius, col_count, row_count)
+        right = spread(from_right, near[2], first_hits(near[2]), radius, col_count, row_count)
+    else:
+        left, right = (
+            jnp.einsum(
+                "kmxy,kyz->kmxz", side, taps_rows, preferred_element_type=jnp.float32
+            ).astype(jnp.bfloat16)
+            for side in (from_left, from_right)
         )
-    else:
-        sides = jnp.einsum(
-            "tkmxy,kyz->tkmxz", sides, taps_rows, preferred_element_type=jnp.float32
-        ).astype(jnp.bfloat16)
     smooth_x = jnp.einsum(
-        "tkmey,ktex->kmxy", sides, taps_cols[:, 0::2], preferred_element_type=jnp.float32
+        "kmey,kex->kmxy", left, taps_cols[:, 0], preferred_element_type=jnp.float32
+    ) + jnp.einsum(
+        "kmey,kex->kmxy", right, taps_cols[:, 2], preferred_element_type=jnp.float32
     )
     gradient = gradient + smooth_x
     total_cells = float(lev_dev * group_count * col_count * tile_count * row_count)

time: 136 us -> 135 us (level)
  waiting for transfers between devices: 50.6 us -> 55.7 us
  other arithmetic: 21.7 us -> 18.4 us
  starting transfers between devices: 25.7 us -> 22.5 us
    ppermute x1, waiting for transfers between devices: 12.9 us -> 20.5 us  [shards(): lax.ppermute(level_mix, 'tile', [(i, i + 1) for i in range(ends)])]
    ppermute x1, waiting for transfers between devices: 7.1 us -> 0.01 us  [shards(): lax.ppermute(level_mix, 'tile', [(i + 1, i) for i in range(ends)])]
    dot_general x1 -> x2, matrix products: 0.9 us -> 4.45 us  [the longest x1 3.63 us: shards(): jnp.einsum('kmey,kex->kmxy', right, taps_cols[:, 2], preferred_element_ty...]
    all_to_all x1, waiting for transfers between devices: 5.91 us -> 8.96 us  [shards(): lax.all_to_all(member_forcing, 'lev', split_axis=0, concat_axis=0, tiled=...]
    dot_general x1, matrix products: 3.61 us -> 0.81 us  [shards(): jnp.einsum('kmey,kex->kmxy', own, taps_cols[:, 1], preferred_element_type...]
    ppermute x1, starting transfers between devices: 4.77 us -> 2.58 us  [shards(): lax.ppermute(level_mix, 'tile', [(i, i + 1) for i in range(ends)])]
    reduce_or x2 -> x3, other arithmetic: 3.64 us -> 1.75 us  [first_hits(): return jnp.logical_not(jnp.any(same & later, axis=-1))]
    dot_general x2 -> x3, matrix products: 12.8 us -> 12 us  [spread(): jnp.einsum('gmkxs,ksz->kgmxz', placed, slot_taps, preferred_element_type=...]
  transfers between devices with their start and end apart: 10 -> 10, of which waited for: 10 -> 9; matrix products, arithmetic and copies ran while one was open for 11% -> 12% of each run, Pallas kernels for 0% -> 0%
where the time goes in v13:
time: 135 us; the launch traced here: 134 us
  waiting for transfers between devices  55.7 us (41%)
  matrix products  30.2 us (22%)
  starting transfers between devices  22.5 us (17%)
  other arithmetic  18.4 us (14%)
  local copies, waits for them, and re-layouts  6.64 us (5%)
    ppermute x1, waiting for transfers between devices, shards(): lax.ppermute(level_mix, 'tile', [(i, i + 1) for i in range(ends)])  20.5 us
    ppermute x5, waiting for transfers between devices, all_sum(): lax.ppermute(value, name, [(i, i ^ bit) for i in range(size)])  14.3 us
    dot_general x3, matrix products, spread(): jnp.einsum('gmkxs,ksz->kgmxz', placed, slot_taps, preferred_element_type=...  12 us
    all_to_all x1, waiting for transfers between devices, shards(): lax.all_to_all(member_forcing, 'lev', split_axis=0, concat_axis=0, tiled=...  8.96 us
    another operation x3, other arithmetic, shards(): r_factor = jnp.linalg.cholesky(gram_total).T  7.98 us
    all_to_all x1, waiting for transfers between devices, shards(): lax.all_to_all(local_mix, 'lev', split_axis=0, concat_axis=0, tiled=True)  7.77 us
    all_to_all x1, starting transfers between devices, shards(): lax.all_to_all(outgoing, 'tile', split_axis=1, concat_axis=1, tiled=True)  7.25 us
    dot_general x1, matrix products, shards(): jnp.einsum('lgmxy,sxy->gmls', ensemble.reshape(lev_dev, group_count, shar...  4.95 us
  transfers between devices with their start and end apart: 10, of which 9 were waited for; matrix products, arithmetic and copies ran while one was open for 12% of the time, Pallas kernels for 0%

profile of v13, /device:TPU:0, one launch (start us, length us, event | category | flops | bytes accessed | tf_op | source)
XLA Modules:
  0.0 134.4 jit_solution(6330706700297901719)
XLA Ops:
  0.6 0.9 slice_bitcast_fusion.11
  1.5 0.8 slice_bitcast_fusion.9
  2.3 0.8 select_bitcast_fusion.1
  3.0 0.7 add_convert_fusion
  3.7 1.8 %fusion.82 = f32[4,8,128]{2,0,1:T(4,128)S(1)} fusion(s32[8,128]{1,0:T(8,128)} %bitcast.140, f32[4,512]{1,0:T(4,128)} %param.9, f32[8,128]{1,0:T(8,128)S(1)} %select_bitcast_fusion.1), kind=kOutput, calls=%fused_computation.73 | convolution fusion | flops 25694208 | bytes 32768 | tf_op jit(solution)/shard_map/lo,dco->ldc/dot_general | solution.py:85
  5.5 0.6 pad_maximum_fusion.1
  6.2 7.3 %all-to-all-start = ((f32[7,8,128]{2,0,1:T(8,128)}), f32[7,8,128]{2,0,1:T(8,128)S(1)}, u32[]{:S(2)}, u32[]{:S(2)}) async-start(f32[7,8,128]{2,0,1:T(8,128)} %pad_maximum_fusion.1), calls=%async_computation | async-start | bytes 65536 | tf_op jit(solution)/shard_map/all_to_all | solution.py:95
  13.4 0.7 broadcast_add_fusion
  14.1 0.7 convert_element_type.115
  14.9 0.8 reshape.434
  15.9 4.3 %all-to-all-done = f32[7,8,128]{2,0,1:T(8,128)S(1)} async-done(((f32[7,8,128]{2,0,1:T(8,128)}), f32[7,8,128]{2,0,1:T(8,128)S(1)}, u32[]{:S(2)}, u32[]{:S(2)}) %all-to-all-start) | async-done | bytes 28704 | tf_op jit(solution)/shard_map/all_to_all | solution.py:95
  20.1 0.6 fusion.30
  20.7 0.6 fusion.29
  21.3 0.6 fusion.28
  22.0 1.3 fusion.16
  23.4 4.9 %fusion.71 = bf16[4,20,4,1024]{3,1,0,2:T(8,128)(2,1)S(1)} fusion(bf16[4,4,20,16,256]{4,3,2,1,0:T(8,128)(2,1)S(1)} %bitcast.122, s32[16,256]{1,0:T(8,128)S(1)} %multiply_add_fusion, s32[1024]{0:T(1024)S(1)} %bitcast.134, pred[1024]{0:T(1024)(128)(4,1)S(1)} %get-tuple-element.24, f32[4,1024]{1,0:T(4,128)S(1)} %fusion.16), kind=kOutput, calls=%fused_computation.67 | convolution fusion | flops 2693398528 | bytes 3314688 | tf_op jit(solution)/shard_map/lgmxy,sxy->gmls/dot_general | solution.py:110
  28.3 1.3 %copy.41 = bf16[4,20,4,1024]{3,2,1,0:T(4,128)(2,1)} copy(bf16[4,20,4,1024]{3,1,0,2:T(8,128)(2,1)S(1)} %fusion.71) | data formatting | bytes 1310720 | tf_op jit(solution)/shard_map/convert_element_type | solution.py:114
  29.7 3.5 %all-to-all-start.1 = ((bf16[4,20,4,1024]{3,2,1,0:T(4,128)(2,1)}), bf16[4,20,4,1024]{3,2,1,0:T(4,128)(2,1)S(1)}, u32[]{:S(2)}, u32[]{:S(2)}) async-start(bf16[4,20,4,1024]{3,2,1,0:T(4,128)(2,1)} %copy.41), calls=%async_computation.1 | async-start | bytes 1310720 | tf_op jit(solution)/shard_map/all_to_all | solution.py:124
  33.2 1.2 abs_convert_fusion.2
  34.4 9.0 %all-to-all-done.1 = bf16[4,20,4,1024]{3,2,1,0:T(4,128)(2,1)S(1)} async-done(((bf16[4,20,4,1024]{3,2,1,0:T(4,128)(2,1)}), bf16[4,20,4,1024]{3,2,1,0:T(4,128)(2,1)S(1)}, u32[]{:S(2)}, u32[]{:S(2)}) %all-to-all-start.1) | async-done | bytes 655392 | tf_op jit(solution)/shard_map/all_to_all | solution.py:124
  43.4 0.7 fusion.77
  44.1 1.1 copy.44
  45.2 3.5 %all-to-all-start.2 = ((bf16[4,20,4,1024]{3,2,1,0:T(4,128)(2,1)}), bf16[4,20,4,1024]{3,2,1,0:T(4,128)(2,1)S(1)}, u32[]{:S(2)}, u32[]{:S(2)}) async-start(bf16[4,20,4,1024]{3,2,1,0:T(4,128)(2,1)} %copy.44), calls=%async_computation.2 | async-start | bytes 1310720 | tf_op jit(solution)/shard_map/all_to_all | solution.py:129
  48.6 1.2 abs_convert_fusion.1
  49.9 1.2 abs_convert_fusion
  51.1 7.8 %all-to-all-done.2 = bf16[4,20,4,1024]{3,2,1,0:T(4,128)(2,1)S(1)} async-done(((bf16[4,20,4,1024]{3,2,1,0:T(4,128)(2,1)}), bf16[4,20,4,1024]{3,2,1,0:T(4,128)(2,1)S(1)}, u32[]{:S(2)}, u32[]{:S(2)}) %all-to-all-start.2) | async-done | bytes 655392 | tf_op jit(solution)/shard_map/all_to_all | solution.py:129
  58.9 2.6 %collective-permute-start = (bf16[4,20,4,1024]{3,2,1,0:T(4,128)(2,1)S(1)}, bf16[4,20,4,1024]{3,2,1,0:T(4,128)(2,1)S(1)}, u32[]{:S(2)}, u32[]{:S(2)}) collective-permute-start(bf16[4,20,4,1024]{3,2,1,0:T(4,128)(2,1)S(1)} %all-to-all-done.2), channel_id=1, source_target_pairs={{0,4},{4,8},{8,12},{12,16},{16,20},{20,24},{24,28},{1,5},{5,9},{9,... | collective-permute-start | bytes 1966088 | tf_op jit(solution)/shard_map/ppermute | solution.py:135
  61.7 4.7 %fusion.56 = bf16[4,4,20,16,256]{4,3,2,1,0:T(8,128)(2,1)S(1)} fusion(f32[4]{0:T(128)S(1)} %broadcast_add_fusion, f32[1024,256]{1,0:T(8,128)} %abs_convert_fusion.2, f32[4]{0:T(128)S(1)} %convert_element_type.115, pred[16,1024]{1,0:T(8,128)(4,1)S(1)} %iota_compare_fusion.9, bf16[4,20,4,1024]{3,1,0,2:T(8,128)(2,1)S(1)} %copy.45, ...), kind=kOutput, calls=%fused_computation.63 | convolution fusion | flops 2697199616 | bytes 4343840 | tf_op jit(solution)/shard_map/gmkxs,ksz->kgmxz/dot_general | solution.py:51
  66.4 1.3 collective-permute-start.1
  67.7 0.8 fusion.92
  68.6 20.5 %collective-permute-done = bf16[4,20,4,1024]{3,2,1,0:T(4,128)(2,1)S(1)} collective-permute-done((bf16[4,20,4,1024]{3,2,1,0:T(4,128)(2,1)S(1)}, bf16[4,20,4,1024]{3,2,1,0:T(4,128)(2,1)S(1)}, u32[]{:S(2)}, u32[]{:S(2)}) %collective-permute-start) | collective-permute-done | bytes 655392 | tf_op jit(solution)/shard_map/ppermute | solution.py:135
  89.3 3.5 %fusion.61 = bf16[4,4,20,16,256]{4,3,2,1,0:T(8,128)(2,1)S(1)} fusion(f32[1024,256]{1,0:T(8,128)S(1)} %copy-done.2, f32[4]{0:T(128)S(1)} %broadcast_add_fusion, f32[4]{0:T(128)S(1)} %convert_element_type.115, pred[16,1024]{1,0:T(8,128)(4,1)S(1)} %iota_compare_fusion.8, bf16[4,20,4,1024]{3,1,0,2:T(8,128)(2,1)S(1)} %copy.46, ...), kind=kOutput, calls=%fused_computation.64 | convolution fusion | flops 2697199616 | bytes 4343840 | tf_op jit(solution)/shard_map/gmkxs,ksz->kgmxz/dot_general | solution.py:51
  92.8 0.8 fusion.91
  94.0 3.7 %fusion.66 = bf16[4,4,20,16,256]{4,3,2,1,0:T(8,128)(2,1)S(1)} fusion(f32[1024,256]{1,0:T(8,128)S(1)} %copy-done.1, f32[4]{0:T(128)S(1)} %broadcast_add_fusion, f32[4]{0:T(128)S(1)} %convert_element_type.115, pred[16,1024]{1,0:T(8,128)(4,1)S(1)} %iota_compare_fusion.7, bf16[4,20,4,1024]{3,1,0,2:T(8,128)(2,1)S(1)} %copy.47, ...), kind=kOutput, calls=%fused_computation.65 | convolution fusion | flops 2697199616 | bytes 4343840 | tf_op jit(solution)/shard_map/gmkxs,ksz->kgmxz/dot_general | solution.py:51
  97.8 3.6 %subtract_convert_fusion = (bf16[4,80,16,256]{3,2,1,0:T(8,128)(2,1)S(1)}, bf16[4,80,16,256]{3,2,1,0:T(8,128)(2,1)S(1)}, f32[4,80,16,256]{3,2,1,0:T(8,128)}) fusion(f32[4,16,80,256]{3,1,2,0:T(8,128)S(1)} %fusion.91, bf16[4,80,16,256]{3,2,1,0:T(8,128)(2,1)S(1)} %bitcast.127, bf16[4,3,16,16]{2,3,0,1:T(8,128)(2,1)S(1)} %select_convert_fusion.3, ...), kind=kOutput, calls=%fused_computation.24 | convolution fusion | flops 51118080 | bytes 28852224 | tf_op jit(solution)/shard_map/kmey,kex->kmxy/dot_general | solution.py:167
  101.9 4.2 %fusion.78 = f32[160,160]{0,1:T(8,128)S(1)} fusion(bf16[4,160,16,256]{3,2,1,0:T(8,128)(2,1)S(1)} %pad_maximum_fusion), kind=kOutput, calls=%fused_computation.71 | convolution fusion | flops 838860800 | bytes 5345280 | tf_op jit(solution)/shard_map/kpxy,kqxy->pq/dot_general | solution.py:62
  106.2 1.2 collective-permute-done.2
  107.5 0.7 collective-permute-start.3
  108.2 3.4 %collective-permute-done.3 = f32[80,80]{0,1:T(8,128)S(1)} collective-permute-done((f32[80,80]{0,1:T(8,128)S(1)}, f32[80,80]{0,1:T(8,128)S(1)}, u32[]{:S(2)}, u32[]{:S(2)}) %collective-permute-start.3) | collective-permute-done | bytes 25632 | tf_op jit(solution)/shard_map/ppermute | solution.py:39
  111.6 2.5 %collective-permute-start.4 = (f32[80,80]{0,1:T(8,128)S(1)}, f32[80,80]{0,1:T(8,128)S(1)}, u32[]{:S(2)}, u32[]{:S(2)}) collective-permute-start(f32[80,80]{0,1:T(8,128)S(1)} %add.121), channel_id=1, source_target_pairs={{0,4},{4,0},{8,12},{12,8},{16,20},{20,16},{24,28},{28,24},{1,5},{5... | collective-permute-start | bytes 76808 | tf_op jit(solution)/shard_map/ppermute | solution.py:39
  114.1 2.0 %collective-permute-done.4 = f32[80,80]{0,1:T(8,128)S(1)} collective-permute-done((f32[80,80]{0,1:T(8,128)S(1)}, f32[80,80]{0,1:T(8,128)S(1)}, u32[]{:S(2)}, u32[]{:S(2)}) %collective-permute-start.4) | collective-permute-done | bytes 25632 | tf_op jit(solution)/shard_map/ppermute | solution.py:39
  116.1 0.7 collective-permute-start.5
  116.8 3.3 %collective-permute-done.5 = f32[80,80]{0,1:T(8,128)S(1)} collective-permute-done((f32[80,80]{0,1:T(8,128)S(1)}, f32[80,80]{0,1:T(8,128)S(1)}, u32[]{:S(2)}, u32[]{:S(2)}) %collective-permute-start.5) | collective-permute-done | bytes 25632 | tf_op jit(solution)/shard_map/ppermute | solution.py:39
  120.6 4.4 %collective-permute-done.6 = f32[80,80]{0,1:T(8,128)S(1)} collective-permute-done((f32[80,80]{0,1:T(8,128)S(1)}, f32[80,80]{0,1:T(8,128)S(1)}, u32[]{:S(2)}, u32[]{:S(2)}) %collective-permute-start.6) | collective-permute-done | bytes 25632 | tf_op jit(solution)/shard_map/ppermute | solution.py:39
  125.1 7.3 %cholesky.18 = f32[80,80]{1,0:T(8,128)S(1)} custom-call(f32[80,80]{1,0:T(8,128)S(1)} %fusion.90), custom_call_target="Cholesky" | custom-call | tf_op jit(solution)/shard_map/jit(cholesky)/cholesky | solution.py:176
  132.4 0.6 compare_reduce_fusion
  133.1 0.7 select_bitcast_fusion
  133.7 0.7 copy.55
  (44 shorter events, 2.6 us)
Async XLA Ops:
  0.6 22.7 %copy-start = (bf16[4,80,16,256]{3,2,1,0:T(8,128)(2,1)S(1)}, bf16[4,80,16,256]{3,2,1,0:T(8,128)(2,1)}, u32[]{:S(2)}) copy-start(bf16[4,80,16,256]{3,2,1,0:T(8,128)(2,1)} %param.14) | copy-start | bytes 7864324
  6.2 13.9 %all-to-all-start = ((f32[7,8,128]{2,0,1:T(8,128)}), f32[7,8,128]{2,0,1:T(8,128)S(1)}, u32[]{:S(2)}, u32[]{:S(2)}) async-start(f32[7,8,128]{2,0,1:T(8,128)} %pad_maximum_fusion.1), calls=%async_computation | async-start | bytes 65536 | tf_op jit(solution)/shard_map/all_to_all | solution.py:95
  29.7 13.7 %all-to-all-start.1 = ((bf16[4,20,4,1024]{3,2,1,0:T(4,128)(2,1)}), bf16[4,20,4,1024]{3,2,1,0:T(4,128)(2,1)S(1)}, u32[]{:S(2)}, u32[]{:S(2)}) async-start(bf16[4,20,4,1024]{3,2,1,0:T(4,128)(2,1)} %copy.41), calls=%async_computation.1 | async-start | bytes 1310720 | tf_op jit(solution)/shard_map/all_to_all | solution.py:124
  45.2 13.7 %all-to-all-start.2 = ((bf16[4,20,4,1024]{3,2,1,0:T(4,128)(2,1)}), bf16[4,20,4,1024]{3,2,1,0:T(4,128)(2,1)S(1)}, u32[]{:S(2)}, u32[]{:S(2)}) async-start(bf16[4,20,4,1024]{3,2,1,0:T(4,128)(2,1)} %copy.44), calls=%async_computation.2 | async-start | bytes 1310720 | tf_op jit(solution)/shard_map/all_to_all | solution.py:129
  58.9 30.2 %collective-permute-start = (bf16[4,20,4,1024]{3,2,1,0:T(4,128)(2,1)S(1)}, bf16[4,20,4,1024]{3,2,1,0:T(4,128)(2,1)S(1)}, u32[]{:S(2)}, u32[]{:S(2)}) collective-permute-start(bf16[4,20,4,1024]{3,2,1,0:T(4,128)(2,1)S(1)} %all-to-all-done.2), channel_id=1, source_target_pairs={{0,4},{4,8},{8,12},{12,16},{16,20},{20,24},{24,28},{1,5},{5,9},{9,... | collective-permute-start | bytes 1966088 | tf_op jit(solution)/shard_map/ppermute | solution.py:135
  66.4 27.2 %collective-permute-start.1 = (bf16[4,20,4,1024]{3,2,1,0:T(4,128)(2,1)S(1)}, bf16[4,20,4,1024]{3,2,1,0:T(4,128)(2,1)S(1)}, u32[]{:S(2)}, u32[]{:S(2)}) collective-permute-start(bf16[4,20,4,1024]{3,2,1,0:T(4,128)(2,1)S(1)} %all-to-all-done.2), channel_id=1, source_target_pairs={{4,0},{8,4},{12,8},{16,12},{20,16},{24,20},{28,24},{5,1},{9,5},{13... | collective-permute-start | bytes 1966088 | tf_op jit(solution)/shard_map/ppermute | solution.py:136
  67.7 21.5 %copy-start.2 = (f32[1024,256]{1,0:T(8,128)S(1)}, f32[1024,256]{1,0:T(8,128)}, u32[]{:S(2)}) copy-start(f32[1024,256]{1,0:T(8,128)} %abs_convert_fusion.1) | copy-start | bytes 3145732
  92.8 1.2 copy-start.1
  92.8 4.9 %slice-start = ((s8[5242880]{0:T(1024)(128)(4,1)}), s8[4194304]{0:T(1024)(128)(4,1)S(1)}, s32[]{:S(2)}) async-start(s8[5242880]{0:T(1024)(128)(4,1)} %bitcast.125), calls=%async_computation.3 | async-start | bytes 8388608
  94.0 3.7 %slice-start.1 = ((s8[5242880]{0:T(1024)(128)(4,1)}), s8[1048576]{0:T(1024)(128)(4,1)S(1)}, s32[]{:S(2)}) async-start(s8[5242880]{0:T(1024)(128)(4,1)} %bitcast.125), calls=%async_computation.4 | async-start | bytes 2097152
  106.1 1.3 collective-permute-start.2
  107.5 4.1 %collective-permute-start.3 = (f32[80,80]{0,1:T(8,128)S(1)}, f32[80,80]{0,1:T(8,128)S(1)}, u32[]{:S(2)}, u32[]{:S(2)}) collective-permute-start(f32[80,80]{0,1:T(8,128)S(1)} %fusion.111), channel_id=1, source_target_pairs={{0,2},{1,3},{2,0},{3,1},{4,6},{5,7},{6,4},{7,5},{8,10},{9,11},{10,... | collective-permute-start | bytes 76808 | tf_op jit(solution)/shard_map/ppermute | solution.py:39
  111.6 4.5 %collective-permute-start.4 = (f32[80,80]{0,1:T(8,128)S(1)}, f32[80,80]{0,1:T(8,128)S(1)}, u32[]{:S(2)}, u32[]{:S(2)}) collective-permute-start(f32[80,80]{0,1:T(8,128)S(1)} %add.121), channel_id=1, source_target_pairs={{0,4},{4,0},{8,12},{12,8},{16,20},{20,16},{24,28},{28,24},{1,5},{5... | collective-permute-start | bytes 76808 | tf_op jit(solution)/shard_map/ppermute | solution.py:39
  116.1 4.0 %collective-permute-start.5 = (f32[80,80]{0,1:T(8,128)S(1)}, f32[80,80]{0,1:T(8,128)S(1)}, u32[]{:S(2)}, u32[]{:S(2)}) collective-permute-start(f32[80,80]{0,1:T(8,128)S(1)} %add.122), channel_id=1, source_target_pairs={{0,8},{4,12},{8,0},{12,4},{16,24},{20,28},{24,16},{28,20},{1,9},{5... | collective-permute-start | bytes 76808 | tf_op jit(solution)/shard_map/ppermute | solution.py:39
  120.1 4.9 %collective-permute-start.6 = (f32[80,80]{0,1:T(8,128)S(1)}, f32[80,80]{0,1:T(8,128)S(1)}, u32[]{:S(2)}, u32[]{:S(2)}) collective-permute-start(f32[80,80]{0,1:T(8,128)S(1)} %add.123), channel_id=1, source_target_pairs={{0,16},{4,20},{8,24},{12,28},{16,0},{20,4},{24,8},{28,12},{1,17},{... | collective-permute-start | bytes 76808 | tf_op jit(solution)/shard_map/ppermute | solution.py:39

commit v14 on v13

--- a/solution.py
+++ b/solution.py
@@ -87,10 +87,13 @@
         precision=lax.Precision.HIGHEST,
     )
     payload = values * (foot_weight[0] * live_mask)[None]
-    own_cells = foot_cell[0]
-    prev_cells = jnp.concatenate([own_cells[:1], own_cells[:-1]], axis=0)
-    next_cells = jnp.concatenate([own_cells[1:], own_cells[-1:]], axis=0)
-    cell_rows = jnp.stack([prev_cells, own_cells, next_cells]).astype(jnp.float32)
+    dest = jnp.arange(tile_count, dtype=jnp.int32)
+    beside = jnp.clip(dest[None, :] + jnp.arange(-1, 2, dtype=jnp.int32)[:, None], 0, tile_count - 1)
+    near_rows = (beside[:, :, None] == dest[None, None, :]).astype(jnp.float32)
+    cell_rows = jnp.einsum(
+        "jde,ec->jdc", near_rows, foot_cell[0].astype(jnp.float32),
+        precision=lax.Precision.HIGHEST,
+    )
     outgoing = jnp.concatenate([payload, cell_rows], axis=0)
     arrived = lax.all_to_all(outgoing, "tile", split_axis=1, concat_axis=1, tiled=True)
     near = arrived[lev_dev:].astype(jnp.int32).reshape(3, slots)

time: 135 us -> 134 us (level)
  local copies, waits for them, and re-layouts: 6.64 us -> 5.04 us
    slice x2 -> x0, local copies, waits for them, and re-layouts: 1.62 us -> none  [shards(): prev_cells = jnp.concatenate([own_cells[:1], own_cells[:-1]], axis=0)]
where the time goes in v14:
time: 134 us; the launch traced here: 133 us
  waiting for transfers between devices  55.8 us (42%)
  matrix products  31.2 us (23%)
  starting transfers between devices  22.6 us (17%)
  other arithmetic  17.7 us (13%)
  local copies, waits for them, and re-layouts  5.04 us (4%)
    ppermute x1, waiting for transfers between devices, shards(): lax.ppermute(level_mix, 'tile', [(i, i + 1) for i in range(ends)])  20.5 us
    ppermute x5, waiting for transfers between devices, all_sum(): lax.ppermute(value, name, [(i, i ^ bit) for i in range(size)])  14.3 us
    dot_general x3, matrix products, spread(): jnp.einsum('gmkxs,ksz->kgmxz', placed, slot_taps, preferred_element_type=...  12 us
    all_to_all x1, waiting for transfers between devices, shards(): lax.all_to_all(member_forcing, 'lev', split_axis=0, concat_axis=0, tiled=...  8.97 us
    another operation x3, other arithmetic, shards(): r_factor = jnp.linalg.cholesky(gram_total).T  7.98 us
    all_to_all x1, waiting for transfers between devices, shards(): lax.all_to_all(local_mix, 'lev', split_axis=0, concat_axis=0, tiled=True)  7.77 us
    all_to_all x1, starting transfers between devices, shards(): lax.all_to_all(outgoing, 'tile', split_axis=1, concat_axis=1, tiled=True)  7.25 us
    dot_general x1, matrix products, shards(): jnp.einsum('lgmxy,sxy->gmls', ensemble.reshape(lev_dev, group_count, shar...  4.95 us
  transfers between devices with their start and end apart: 10, of which 9 were waited for; matrix products, arithmetic and copies ran while one was open for 12% of the time, Pallas kernels for 0%

profile of v14, /device:TPU:0, one launch (start us, length us, event | category | flops | bytes accessed | tf_op | source)
XLA Modules:
  0.0 133.2 jit_solution(17902615399084960886)
XLA Ops:
  0.7 1.0 fusion.94
  1.8 0.8 select_bitcast_fusion.1
  2.5 1.8 %fusion.82 = f32[4,8,128]{2,0,1:T(4,128)S(1)} fusion(s32[8,128]{1,0:T(8,128)} %bitcast.130, f32[4,512]{1,0:T(4,128)} %param.9, f32[8,128]{1,0:T(8,128)S(1)} %select_bitcast_fusion.1), kind=kOutput, calls=%fused_computation.73 | convolution fusion | flops 25694208 | bytes 32768 | tf_op jit(solution)/shard_map/lo,dco->ldc/dot_general | solution.py:85
  4.3 0.6 pad_maximum_fusion.1
  5.0 7.3 %all-to-all-start = ((f32[7,8,128]{2,0,1:T(8,128)}), f32[7,8,128]{2,0,1:T(8,128)S(1)}, u32[]{:S(2)}, u32[]{:S(2)}) async-start(f32[7,8,128]{2,0,1:T(8,128)} %pad_maximum_fusion.1), calls=%async_computation | async-start | bytes 65536 | tf_op jit(solution)/shard_map/all_to_all | solution.py:98
  12.2 0.7 broadcast_add_fusion
  12.9 0.7 convert_element_type.119
  13.7 0.8 reshape.456
  14.6 4.3 %all-to-all-done = f32[7,8,128]{2,0,1:T(8,128)S(1)} async-done(((f32[7,8,128]{2,0,1:T(8,128)}), f32[7,8,128]{2,0,1:T(8,128)S(1)}, u32[]{:S(2)}, u32[]{:S(2)}) %all-to-all-start) | async-done | bytes 28704 | tf_op jit(solution)/shard_map/all_to_all | solution.py:98
  18.9 0.6 fusion.30
  19.5 0.6 fusion.29
  20.1 0.6 fusion.28
  20.8 1.3 %fusion.16 = f32[4,1024]{1,0:T(4,128)S(1)} fusion(s32[1024]{0:T(1024)S(1)} %bitcast.123, f32[7,8,128]{2,0,1:T(8,128)S(1)} %all-to-all-done), kind=kOutput, calls=%fused_computation.16 | convolution fusion | flops 51380224 | bytes 40960 | tf_op jit(solution)/shard_map/ls,st->lt/dot_general | solution.py:104
  22.1 4.9 %fusion.71 = bf16[4,20,4,1024]{3,1,0,2:T(8,128)(2,1)S(1)} fusion(bf16[4,4,20,16,256]{4,3,2,1,0:T(8,128)(2,1)S(1)} %bitcast.115, s32[16,256]{1,0:T(8,128)S(1)} %multiply_add_fusion, s32[1024]{0:T(1024)S(1)} %bitcast.124, pred[1024]{0:T(1024)(128)(4,1)S(1)} %get-tuple-element.20, f32[4,1024]{1,0:T(4,128)S(1)} %fusion.16), kind=kOutput, calls=%fused_computation.67 | convolution fusion | flops 2693398528 | bytes 3314688 | tf_op jit(solution)/shard_map/lgmxy,sxy->gmls/dot_general | solution.py:113
  27.1 1.3 %copy.41 = bf16[4,20,4,1024]{3,2,1,0:T(4,128)(2,1)} copy(bf16[4,20,4,1024]{3,1,0,2:T(8,128)(2,1)S(1)} %fusion.71) | data formatting | bytes 1310720 | tf_op jit(solution)/shard_map/convert_element_type | solution.py:117
  28.4 3.5 %all-to-all-start.1 = ((bf16[4,20,4,1024]{3,2,1,0:T(4,128)(2,1)}), bf16[4,20,4,1024]{3,2,1,0:T(4,128)(2,1)S(1)}, u32[]{:S(2)}, u32[]{:S(2)}) async-start(bf16[4,20,4,1024]{3,2,1,0:T(4,128)(2,1)} %copy.41), calls=%async_computation.1 | async-start | bytes 1310720 | tf_op jit(solution)/shard_map/all_to_all | solution.py:127
  32.0 1.2 abs_convert_fusion.2
  33.2 9.0 %all-to-all-done.1 = bf16[4,20,4,1024]{3,2,1,0:T(4,128)(2,1)S(1)} async-done(((bf16[4,20,4,1024]{3,2,1,0:T(4,128)(2,1)}), bf16[4,20,4,1024]{3,2,1,0:T(4,128)(2,1)S(1)}, u32[]{:S(2)}, u32[]{:S(2)}) %all-to-all-start.1) | async-done | bytes 655392 | tf_op jit(solution)/shard_map/all_to_all | solution.py:127
  42.1 0.7 fusion.77
  42.9 1.1 copy.44
  44.0 3.5 %all-to-all-start.2 = ((bf16[4,20,4,1024]{3,2,1,0:T(4,128)(2,1)}), bf16[4,20,4,1024]{3,2,1,0:T(4,128)(2,1)S(1)}, u32[]{:S(2)}, u32[]{:S(2)}) async-start(bf16[4,20,4,1024]{3,2,1,0:T(4,128)(2,1)} %copy.44), calls=%async_computation.2 | async-start | bytes 1310720 | tf_op jit(solution)/shard_map/all_to_all | solution.py:132
  47.4 1.2 abs_convert_fusion.1
  48.7 1.2 abs_convert_fusion
  49.9 7.8 %all-to-all-done.2 = bf16[4,20,4,1024]{3,2,1,0:T(4,128)(2,1)S(1)} async-done(((bf16[4,20,4,1024]{3,2,1,0:T(4,128)(2,1)}), bf16[4,20,4,1024]{3,2,1,0:T(4,128)(2,1)S(1)}, u32[]{:S(2)}, u32[]{:S(2)}) %all-to-all-start.2) | async-done | bytes 655392 | tf_op jit(solution)/shard_map/all_to_all | solution.py:132
  57.7 2.6 %collective-permute-start = (bf16[4,20,4,1024]{3,2,1,0:T(4,128)(2,1)S(1)}, bf16[4,20,4,1024]{3,2,1,0:T(4,128)(2,1)S(1)}, u32[]{:S(2)}, u32[]{:S(2)}) collective-permute-start(bf16[4,20,4,1024]{3,2,1,0:T(4,128)(2,1)S(1)} %all-to-all-done.2), channel_id=1, source_target_pairs={{0,4},{4,8},{8,12},{12,16},{16,20},{20,24},{24,28},{1,5},{5,9},{9,... | collective-permute-start | bytes 1966088 | tf_op jit(solution)/shard_map/ppermute | solution.py:138
  60.5 4.7 %fusion.56 = bf16[4,4,20,16,256]{4,3,2,1,0:T(8,128)(2,1)S(1)} fusion(f32[4]{0:T(128)S(1)} %broadcast_add_fusion, f32[1024,256]{1,0:T(8,128)} %abs_convert_fusion.2, f32[4]{0:T(128)S(1)} %convert_element_type.119, pred[16,1024]{1,0:T(8,128)(4,1)S(1)} %iota_compare_fusion.9, bf16[4,20,4,1024]{3,1,0,2:T(8,128)(2,1)S(1)} %copy.45, ...), kind=kOutput, calls=%fused_computation.63 | convolution fusion | flops 2697199616 | bytes 4343840 | tf_op jit(solution)/shard_map/gmkxs,ksz->kgmxz/dot_general | solution.py:51
  65.2 1.3 collective-permute-start.1
  66.5 0.8 fusion.92
  67.4 20.5 %collective-permute-done = bf16[4,20,4,1024]{3,2,1,0:T(4,128)(2,1)S(1)} collective-permute-done((bf16[4,20,4,1024]{3,2,1,0:T(4,128)(2,1)S(1)}, bf16[4,20,4,1024]{3,2,1,0:T(4,128)(2,1)S(1)}, u32[]{:S(2)}, u32[]{:S(2)}) %collective-permute-start) | collective-permute-done | bytes 655392 | tf_op jit(solution)/shard_map/ppermute | solution.py:138
  88.1 3.5 %fusion.61 = bf16[4,4,20,16,256]{4,3,2,1,0:T(8,128)(2,1)S(1)} fusion(f32[1024,256]{1,0:T(8,128)S(1)} %copy-done.2, f32[4]{0:T(128)S(1)} %broadcast_add_fusion, f32[4]{0:T(128)S(1)} %convert_element_type.119, pred[16,1024]{1,0:T(8,128)(4,1)S(1)} %iota_compare_fusion.8, bf16[4,20,4,1024]{3,1,0,2:T(8,128)(2,1)S(1)} %copy.46, ...), kind=kOutput, calls=%fused_computation.64 | convolution fusion | flops 2697199616 | bytes 4343840 | tf_op jit(solution)/shard_map/gmkxs,ksz->kgmxz/dot_general | solution.py:51
  91.6 0.8 fusion.91
  92.8 3.7 %fusion.66 = bf16[4,4,20,16,256]{4,3,2,1,0:T(8,128)(2,1)S(1)} fusion(f32[1024,256]{1,0:T(8,128)S(1)} %copy-done.1, f32[4]{0:T(128)S(1)} %broadcast_add_fusion, f32[4]{0:T(128)S(1)} %convert_element_type.119, pred[16,1024]{1,0:T(8,128)(4,1)S(1)} %iota_compare_fusion.7, bf16[4,20,4,1024]{3,1,0,2:T(8,128)(2,1)S(1)} %copy.47, ...), kind=kOutput, calls=%fused_computation.65 | convolution fusion | flops 2697199616 | bytes 4343840 | tf_op jit(solution)/shard_map/gmkxs,ksz->kgmxz/dot_general | solution.py:51
  96.6 3.6 %subtract_convert_fusion = (bf16[4,80,16,256]{3,2,1,0:T(8,128)(2,1)S(1)}, bf16[4,80,16,256]{3,2,1,0:T(8,128)(2,1)S(1)}, f32[4,80,16,256]{3,2,1,0:T(8,128)}) fusion(f32[4,16,80,256]{3,1,2,0:T(8,128)S(1)} %fusion.91, bf16[4,80,16,256]{3,2,1,0:T(8,128)(2,1)S(1)} %bitcast.120, bf16[4,3,16,16]{2,3,0,1:T(8,128)(2,1)S(1)} %select_convert_fusion.3, ...), kind=kOutput, calls=%fused_computation.24 | convolution fusion | flops 51118080 | bytes 28852224 | tf_op jit(solution)/shard_map/kmey,kex->kmxy/dot_general | solution.py:170
  100.2 0.5 pad_maximum_fusion
  100.7 4.2 %fusion.78 = f32[160,160]{0,1:T(8,128)S(1)} fusion(bf16[4,160,16,256]{3,2,1,0:T(8,128)(2,1)S(1)} %pad_maximum_fusion), kind=kOutput, calls=%fused_computation.71 | convolution fusion | flops 838860800 | bytes 5345280 | tf_op jit(solution)/shard_map/kpxy,kqxy->pq/dot_general | solution.py:62
  105.0 1.2 collective-permute-done.2
  106.3 0.7 collective-permute-start.3
  107.0 3.4 %collective-permute-done.3 = f32[80,80]{0,1:T(8,128)S(1)} collective-permute-done((f32[80,80]{0,1:T(8,128)S(1)}, f32[80,80]{0,1:T(8,128)S(1)}, u32[]{:S(2)}, u32[]{:S(2)}) %collective-permute-start.3) | collective-permute-done | bytes 25632 | tf_op jit(solution)/shard_map/ppermute | solution.py:39
  110.4 2.5 %collective-permute-start.4 = (f32[80,80]{0,1:T(8,128)S(1)}, f32[80,80]{0,1:T(8,128)S(1)}, u32[]{:S(2)}, u32[]{:S(2)}) collective-permute-start(f32[80,80]{0,1:T(8,128)S(1)} %add.149), channel_id=1, source_target_pairs={{0,4},{4,0},{8,12},{12,8},{16,20},{20,16},{24,28},{28,24},{1,5},{5... | collective-permute-start | bytes 76808 | tf_op jit(solution)/shard_map/ppermute | solution.py:39
  112.9 2.0 %collective-permute-done.4 = f32[80,80]{0,1:T(8,128)S(1)} collective-permute-done((f32[80,80]{0,1:T(8,128)S(1)}, f32[80,80]{0,1:T(8,128)S(1)}, u32[]{:S(2)}, u32[]{:S(2)}) %collective-permute-start.4) | collective-permute-done | bytes 25632 | tf_op jit(solution)/shard_map/ppermute | solution.py:39
  114.9 0.7 collective-permute-start.5
  115.6 3.3 %collective-permute-done.5 = f32[80,80]{0,1:T(8,128)S(1)} collective-permute-done((f32[80,80]{0,1:T(8,128)S(1)}, f32[80,80]{0,1:T(8,128)S(1)}, u32[]{:S(2)}, u32[]{:S(2)}) %collective-permute-start.5) | collective-permute-done | bytes 25632 | tf_op jit(solution)/shard_map/ppermute | solution.py:39
  118.9 0.5 collective-permute-start.6
  119.4 4.4 %collective-permute-done.6 = f32[80,80]{0,1:T(8,128)S(1)} collective-permute-done((f32[80,80]{0,1:T(8,128)S(1)}, f32[80,80]{0,1:T(8,128)S(1)}, u32[]{:S(2)}, u32[]{:S(2)}) %collective-permute-start.6) | collective-permute-done | bytes 25632 | tf_op jit(solution)/shard_map/ppermute | solution.py:39
  123.9 7.3 %cholesky.18 = f32[80,80]{1,0:T(8,128)S(1)} custom-call(f32[80,80]{1,0:T(8,128)S(1)} %fusion.90), custom_call_target="Cholesky" | custom-call | tf_op jit(solution)/shard_map/jit(cholesky)/cholesky | solution.py:179
  131.2 0.6 compare_reduce_fusion
  131.9 0.7 select_bitcast_fusion
  132.5 0.7 copy.55
  (44 shorter events, 1.7 us)
Async XLA Ops:
  0.6 21.5 %copy-start = (bf16[4,80,16,256]{3,2,1,0:T(8,128)(2,1)S(1)}, bf16[4,80,16,256]{3,2,1,0:T(8,128)(2,1)}, u32[]{:S(2)}) copy-start(bf16[4,80,16,256]{3,2,1,0:T(8,128)(2,1)} %param.14) | copy-start | bytes 7864324
  5.0 13.9 %all-to-all-start = ((f32[7,8,128]{2,0,1:T(8,128)}), f32[7,8,128]{2,0,1:T(8,128)S(1)}, u32[]{:S(2)}, u32[]{:S(2)}) async-start(f32[7,8,128]{2,0,1:T(8,128)} %pad_maximum_fusion.1), calls=%async_computation | async-start | bytes 65536 | tf_op jit(solution)/shard_map/all_to_all | solution.py:98
  28.4 13.7 %all-to-all-start.1 = ((bf16[4,20,4,1024]{3,2,1,0:T(4,128)(2,1)}), bf16[4,20,4,1024]{3,2,1,0:T(4,128)(2,1)S(1)}, u32[]{:S(2)}, u32[]{:S(2)}) async-start(bf16[4,20,4,1024]{3,2,1,0:T(4,128)(2,1)} %copy.41), calls=%async_computation.1 | async-start | bytes 1310720 | tf_op jit(solution)/shard_map/all_to_all | solution.py:127
  44.0 13.7 %all-to-all-start.2 = ((bf16[4,20,4,1024]{3,2,1,0:T(4,128)(2,1)}), bf16[4,20,4,1024]{3,2,1,0:T(4,128)(2,1)S(1)}, u32[]{:S(2)}, u32[]{:S(2)}) async-start(bf16[4,20,4,1024]{3,2,1,0:T(4,128)(2,1)} %copy.44), calls=%async_computation.2 | async-start | bytes 1310720 | tf_op jit(solution)/shard_map/all_to_all | solution.py:132
  57.7 30.2 %collective-permute-start = (bf16[4,20,4,1024]{3,2,1,0:T(4,128)(2,1)S(1)}, bf16[4,20,4,1024]{3,2,1,0:T(4,128)(2,1)S(1)}, u32[]{:S(2)}, u32[]{:S(2)}) collective-permute-start(bf16[4,20,4,1024]{3,2,1,0:T(4,128)(2,1)S(1)} %all-to-all-done.2), channel_id=1, source_target_pairs={{0,4},{4,8},{8,12},{12,16},{16,20},{20,24},{24,28},{1,5},{5,9},{9,... | collective-permute-start | bytes 1966088 | tf_op jit(solution)/shard_map/ppermute | solution.py:138
  65.2 27.2 %collective-permute-start.1 = (bf16[4,20,4,1024]{3,2,1,0:T(4,128)(2,1)S(1)}, bf16[4,20,4,1024]{3,2,1,0:T(4,128)(2,1)S(1)}, u32[]{:S(2)}, u32[]{:S(2)}) collective-permute-start(bf16[4,20,4,1024]{3,2,1,0:T(4,128)(2,1)S(1)} %all-to-all-done.2), channel_id=1, source_target_pairs={{4,0},{8,4},{12,8},{16,12},{20,16},{24,20},{28,24},{5,1},{9,5},{13... | collective-permute-start | bytes 1966088 | tf_op jit(solution)/shard_map/ppermute | solution.py:139
  66.5 21.5 %copy-start.2 = (f32[1024,256]{1,0:T(8,128)S(1)}, f32[1024,256]{1,0:T(8,128)}, u32[]{:S(2)}) copy-start(f32[1024,256]{1,0:T(8,128)} %abs_convert_fusion.1) | copy-start | bytes 3145732
  91.6 1.2 copy-start.1
  91.6 4.9 %slice-start = ((s8[5242880]{0:T(1024)(128)(4,1)}), s8[4194304]{0:T(1024)(128)(4,1)S(1)}, s32[]{:S(2)}) async-start(s8[5242880]{0:T(1024)(128)(4,1)} %bitcast.118), calls=%async_computation.3 | async-start | bytes 8388608
  92.8 3.7 %slice-start.1 = ((s8[5242880]{0:T(1024)(128)(4,1)}), s8[1048576]{0:T(1024)(128)(4,1)S(1)}, s32[]{:S(2)}) async-start(s8[5242880]{0:T(1024)(128)(4,1)} %bitcast.118), calls=%async_computation.4 | async-start | bytes 2097152
  104.9 1.3 collective-permute-start.2
  106.3 4.1 %collective-permute-start.3 = (f32[80,80]{0,1:T(8,128)S(1)}, f32[80,80]{0,1:T(8,128)S(1)}, u32[]{:S(2)}, u32[]{:S(2)}) collective-permute-start(f32[80,80]{0,1:T(8,128)S(1)} %fusion.115), channel_id=1, source_target_pairs={{0,2},{1,3},{2,0},{3,1},{4,6},{5,7},{6,4},{7,5},{8,10},{9,11},{10,... | collective-permute-start | bytes 76808 | tf_op jit(solution)/shard_map/ppermute | solution.py:39
  110.4 4.5 %collective-permute-start.4 = (f32[80,80]{0,1:T(8,128)S(1)}, f32[80,80]{0,1:T(8,128)S(1)}, u32[]{:S(2)}, u32[]{:S(2)}) collective-permute-start(f32[80,80]{0,1:T(8,128)S(1)} %add.149), channel_id=1, source_target_pairs={{0,4},{4,0},{8,12},{12,8},{16,20},{20,16},{24,28},{28,24},{1,5},{5... | collective-permute-start | bytes 76808 | tf_op jit(solution)/shard_map/ppermute | solution.py:39
  114.9 4.0 %collective-permute-start.5 = (f32[80,80]{0,1:T(8,128)S(1)}, f32[80,80]{0,1:T(8,128)S(1)}, u32[]{:S(2)}, u32[]{:S(2)}) collective-permute-start(f32[80,80]{0,1:T(8,128)S(1)} %add.150), channel_id=1, source_target_pairs={{0,8},{4,12},{8,0},{12,4},{16,24},{20,28},{24,16},{28,20},{1,9},{5... | collective-permute-start | bytes 76808 | tf_op jit(solution)/shard_map/ppermute | solution.py:39
  118.9 4.9 %collective-permute-start.6 = (f32[80,80]{0,1:T(8,128)S(1)}, f32[80,80]{0,1:T(8,128)S(1)}, u32[]{:S(2)}, u32[]{:S(2)}) collective-permute-start(f32[80,80]{0,1:T(8,128)S(1)} %add.151), channel_id=1, source_target_pairs={{0,16},{4,20},{8,24},{12,28},{16,0},{20,4},{24,8},{28,12},{1,17},{... | collective-permute-start | bytes 76808 | tf_op jit(solution)/shard_map/ppermute | solution.py:39

commit v15 on v14

--- a/solution.py
+++ b/solution.py
@@ -94,8 +94,9 @@
         "jde,ec->jdc", near_rows, foot_cell[0].astype(jnp.float32),
         precision=lax.Precision.HIGHEST,
     )
-    outgoing = jnp.concatenate([payload, cell_rows], axis=0)
-    arrived = lax.all_to_all(outgoing, "tile", split_axis=1, concat_axis=1, tiled=True)
+    outgoing = jnp.swapaxes(jnp.concatenate([payload, cell_rows], axis=0), 0, 1)
+    arrived = lax.all_to_all(outgoing, "tile", split_axis=0, concat_axis=0, tiled=True)
+    arrived = jnp.swapaxes(arrived, 0, 1)
     near = arrived[lev_dev:].astype(jnp.int32).reshape(3, slots)
     cell_index = near[1]
 

time: 134 us -> 134 us (level)
  no operation moved by 1% of the time
where the time goes in v15:
time: 134 us; the launch traced here: 133 us
  waiting for transfers between devices  55.8 us (42%)
  matrix products  31.2 us (23%)
  starting transfers between devices  22.5 us (17%)
  other arithmetic  17.7 us (13%)
  local copies, waits for them, and re-layouts  5.04 us (4%)
    ppermute x1, waiting for transfers between devices, shards(): lax.ppermute(level_mix, 'tile', [(i, i + 1) for i in range(ends)])  20.5 us
    ppermute x5, waiting for transfers between devices, all_sum(): lax.ppermute(value, name, [(i, i ^ bit) for i in range(size)])  14.3 us
    dot_general x3, matrix products, spread(): jnp.einsum('gmkxs,ksz->kgmxz', placed, slot_taps, preferred_element_type=...  12 us
    all_to_all x1, waiting for transfers between devices, shards(): lax.all_to_all(member_forcing, 'lev', split_axis=0, concat_axis=0, tiled=...  8.97 us
    another operation x3, other arithmetic, shards(): r_factor = jnp.linalg.cholesky(gram_total).T  7.98 us
    all_to_all x1, waiting for transfers between devices, shards(): lax.all_to_all(local_mix, 'lev', split_axis=0, concat_axis=0, tiled=True)  7.77 us
    all_to_all x1, starting transfers between devices, shards(): lax.all_to_all(outgoing, 'tile', split_axis=0, concat_axis=0, tiled=True)  7.25 us
    dot_general x1, matrix products, shards(): jnp.einsum('lgmxy,sxy->gmls', ensemble.reshape(lev_dev, group_count, shar...  4.94 us
  transfers between devices with their start and end apart: 10, of which 9 were waited for; matrix products, arithmetic and copies ran while one was open for 12% of the time, Pallas kernels for 0%

profile of v15, /device:TPU:0, one launch (start us, length us, event | category | flops | bytes accessed | tf_op | source)
XLA Modules:
  0.0 133.3 jit_solution(2129322279317937735)
XLA Ops:
  0.7 1.0 fusion.94
  1.8 0.8 select_bitcast_fusion.1
  2.5 1.8 %fusion.82 = f32[4,8,128]{2,0,1:T(4,128)S(1)} fusion(s32[8,128]{1,0:T(8,128)} %bitcast.135, f32[4,512]{1,0:T(4,128)} %param.9, f32[8,128]{1,0:T(8,128)S(1)} %select_bitcast_fusion.1), kind=kOutput, calls=%fused_computation.73 | convolution fusion | flops 25694208 | bytes 32768 | tf_op jit(solution)/shard_map/lo,dco->ldc/dot_general | solution.py:85
  4.3 0.6 maximum_bitcast_fusion
  5.0 7.3 %all-to-all-start = ((f32[8,7,128]{2,1,0:T(8,128)}), f32[8,7,128]{2,1,0:T(8,128)S(1)}, u32[]{:S(2)}, u32[]{:S(2)}) async-start(f32[8,7,128]{2,1,0:T(8,128)} %maximum_bitcast_fusion), calls=%async_computation | async-start | bytes 65536 | tf_op jit(solution)/shard_map/all_to_all | solution.py:98
  12.2 0.7 broadcast_add_fusion
  12.9 0.7 convert_element_type.119
  13.7 0.8 reshape.456
  14.6 4.3 %all-to-all-done = f32[8,7,128]{2,1,0:T(8,128)S(1)} async-done(((f32[8,7,128]{2,1,0:T(8,128)}), f32[8,7,128]{2,1,0:T(8,128)S(1)}, u32[]{:S(2)}, u32[]{:S(2)}) %all-to-all-start) | async-done | bytes 28704 | tf_op jit(solution)/shard_map/all_to_all | solution.py:98
  18.9 1.3 %fusion.16 = f32[4,1024]{1,0:T(4,128)S(1)} fusion(s32[1024]{0:T(1024)S(1)} %bitcast.126, f32[7,8,128]{2,0,1:T(8,128)S(1)} %bitcast.125), kind=kOutput, calls=%fused_computation.16 | convolution fusion | flops 51380224 | bytes 40960 | tf_op jit(solution)/shard_map/ls,st->lt/dot_general | solution.py:105
  20.3 0.6 fusion.28
  20.9 0.6 fusion.30
  21.5 0.6 fusion.29
  22.2 4.9 %fusion.71 = bf16[4,20,4,1024]{3,1,0,2:T(8,128)(2,1)S(1)} fusion(bf16[4,4,20,16,256]{4,3,2,1,0:T(8,128)(2,1)S(1)} %bitcast.118, s32[16,256]{1,0:T(8,128)S(1)} %multiply_add_fusion, s32[1024]{0:T(1024)S(1)} %bitcast.129, pred[1024]{0:T(1024)(128)(4,1)S(1)} %get-tuple-element.20, f32[4,1024]{1,0:T(4,128)S(1)} %fusion.16), kind=kOutput, calls=%fused_computation.67 | convolution fusion | flops 2693398528 | bytes 3314688 | tf_op jit(solution)/shard_map/lgmxy,sxy->gmls/dot_general | solution.py:114
  27.1 1.3 %copy.41 = bf16[4,20,4,1024]{3,2,1,0:T(4,128)(2,1)} copy(bf16[4,20,4,1024]{3,1,0,2:T(8,128)(2,1)S(1)} %fusion.71) | data formatting | bytes 1310720 | tf_op jit(solution)/shard_map/convert_element_type | solution.py:118
  28.4 3.5 %all-to-all-start.1 = ((bf16[4,20,4,1024]{3,2,1,0:T(4,128)(2,1)}), bf16[4,20,4,1024]{3,2,1,0:T(4,128)(2,1)S(1)}, u32[]{:S(2)}, u32[]{:S(2)}) async-start(bf16[4,20,4,1024]{3,2,1,0:T(4,128)(2,1)} %copy.41), calls=%async_computation.1 | async-start | bytes 1310720 | tf_op jit(solution)/shard_map/all_to_all | solution.py:128
  32.0 1.2 abs_convert_fusion.2
  33.2 9.0 %all-to-all-done.1 = bf16[4,20,4,1024]{3,2,1,0:T(4,128)(2,1)S(1)} async-done(((bf16[4,20,4,1024]{3,2,1,0:T(4,128)(2,1)}), bf16[4,20,4,1024]{3,2,1,0:T(4,128)(2,1)S(1)}, u32[]{:S(2)}, u32[]{:S(2)}) %all-to-all-start.1) | async-done | bytes 655392 | tf_op jit(solution)/shard_map/all_to_all | solution.py:128
  42.1 0.7 fusion.77
  42.9 1.1 copy.44
  44.0 3.5 %all-to-all-start.2 = ((bf16[4,20,4,1024]{3,2,1,0:T(4,128)(2,1)}), bf16[4,20,4,1024]{3,2,1,0:T(4,128)(2,1)S(1)}, u32[]{:S(2)}, u32[]{:S(2)}) async-start(bf16[4,20,4,1024]{3,2,1,0:T(4,128)(2,1)} %copy.44), calls=%async_computation.2 | async-start | bytes 1310720 | tf_op jit(solution)/shard_map/all_to_all | solution.py:133
  47.4 1.2 abs_convert_fusion.1
  48.7 1.2 abs_convert_fusion
  49.9 7.8 %all-to-all-done.2 = bf16[4,20,4,1024]{3,2,1,0:T(4,128)(2,1)S(1)} async-done(((bf16[4,20,4,1024]{3,2,1,0:T(4,128)(2,1)}), bf16[4,20,4,1024]{3,2,1,0:T(4,128)(2,1)S(1)}, u32[]{:S(2)}, u32[]{:S(2)}) %all-to-all-start.2) | async-done | bytes 655392 | tf_op jit(solution)/shard_map/all_to_all | solution.py:133
  57.7 2.6 %collective-permute-start = (bf16[4,20,4,1024]{3,2,1,0:T(4,128)(2,1)S(1)}, bf16[4,20,4,1024]{3,2,1,0:T(4,128)(2,1)S(1)}, u32[]{:S(2)}, u32[]{:S(2)}) collective-permute-start(bf16[4,20,4,1024]{3,2,1,0:T(4,128)(2,1)S(1)} %all-to-all-done.2), channel_id=1, source_target_pairs={{0,4},{4,8},{8,12},{12,16},{16,20},{20,24},{24,28},{1,5},{5,9},{9,... | collective-permute-start | bytes 1966088 | tf_op jit(solution)/shard_map/ppermute | solution.py:139
  60.5 4.7 %fusion.56 = bf16[4,4,20,16,256]{4,3,2,1,0:T(8,128)(2,1)S(1)} fusion(f32[4]{0:T(128)S(1)} %broadcast_add_fusion, f32[1024,256]{1,0:T(8,128)} %abs_convert_fusion.2, f32[4]{0:T(128)S(1)} %convert_element_type.119, pred[16,1024]{1,0:T(8,128)(4,1)S(1)} %iota_compare_fusion.9, bf16[4,20,4,1024]{3,1,0,2:T(8,128)(2,1)S(1)} %copy.45, ...), kind=kOutput, calls=%fused_computation.63 | convolution fusion | flops 2697199616 | bytes 4343840 | tf_op jit(solution)/shard_map/gmkxs,ksz->kgmxz/dot_general | solution.py:51
  65.2 1.3 collective-permute-start.1
  66.6 0.8 fusion.92
  67.4 20.5 %collective-permute-done = bf16[4,20,4,1024]{3,2,1,0:T(4,128)(2,1)S(1)} collective-permute-done((bf16[4,20,4,1024]{3,2,1,0:T(4,128)(2,1)S(1)}, bf16[4,20,4,1024]{3,2,1,0:T(4,128)(2,1)S(1)}, u32[]{:S(2)}, u32[]{:S(2)}) %collective-permute-start) | collective-permute-done | bytes 655392 | tf_op jit(solution)/shard_map/ppermute | solution.py:139
  88.1 3.5 %fusion.61 = bf16[4,4,20,16,256]{4,3,2,1,0:T(8,128)(2,1)S(1)} fusion(f32[1024,256]{1,0:T(8,128)S(1)} %copy-done.2, f32[4]{0:T(128)S(1)} %broadcast_add_fusion, f32[4]{0:T(128)S(1)} %convert_element_type.119, pred[16,1024]{1,0:T(8,128)(4,1)S(1)} %iota_compare_fusion.8, bf16[4,20,4,1024]{3,1,0,2:T(8,128)(2,1)S(1)} %copy.46, ...), kind=kOutput, calls=%fused_computation.64 | convolution fusion | flops 2697199616 | bytes 4343840 | tf_op jit(solution)/shard_map/gmkxs,ksz->kgmxz/dot_general | solution.py:51
  91.7 0.8 fusion.91
  92.9 3.7 %fusion.66 = bf16[4,4,20,16,256]{4,3,2,1,0:T(8,128)(2,1)S(1)} fusion(f32[1024,256]{1,0:T(8,128)S(1)} %copy-done.1, f32[4]{0:T(128)S(1)} %broadcast_add_fusion, f32[4]{0:T(128)S(1)} %convert_element_type.119, pred[16,1024]{1,0:T(8,128)(4,1)S(1)} %iota_compare_fusion.7, bf16[4,20,4,1024]{3,1,0,2:T(8,128)(2,1)S(1)} %copy.47, ...), kind=kOutput, calls=%fused_computation.65 | convolution fusion | flops 2697199616 | bytes 4343840 | tf_op jit(solution)/shard_map/gmkxs,ksz->kgmxz/dot_general | solution.py:51
  96.6 3.6 %subtract_convert_fusion = (bf16[4,80,16,256]{3,2,1,0:T(8,128)(2,1)S(1)}, bf16[4,80,16,256]{3,2,1,0:T(8,128)(2,1)S(1)}, f32[4,80,16,256]{3,2,1,0:T(8,128)}) fusion(f32[4,16,80,256]{3,1,2,0:T(8,128)S(1)} %fusion.91, bf16[4,80,16,256]{3,2,1,0:T(8,128)(2,1)S(1)} %bitcast.123, bf16[4,3,16,16]{2,3,0,1:T(8,128)(2,1)S(1)} %select_convert_fusion.3, ...), kind=kOutput, calls=%fused_computation.24 | convolution fusion | flops 51118080 | bytes 28852224 | tf_op jit(solution)/shard_map/kmey,kex->kmxy/dot_general | solution.py:171
  100.2 0.5 pad_maximum_fusion
  100.7 4.2 %fusion.78 = f32[160,160]{0,1:T(8,128)S(1)} fusion(bf16[4,160,16,256]{3,2,1,0:T(8,128)(2,1)S(1)} %pad_maximum_fusion), kind=kOutput, calls=%fused_computation.71 | convolution fusion | flops 838860800 | bytes 5345280 | tf_op jit(solution)/shard_map/kpxy,kqxy->pq/dot_general | solution.py:62
  105.0 1.2 collective-permute-done.2
  106.3 0.7 collective-permute-start.3
  107.0 3.4 %collective-permute-done.3 = f32[80,80]{0,1:T(8,128)S(1)} collective-permute-done((f32[80,80]{0,1:T(8,128)S(1)}, f32[80,80]{0,1:T(8,128)S(1)}, u32[]{:S(2)}, u32[]{:S(2)}) %collective-permute-start.3) | collective-permute-done | bytes 25632 | tf_op jit(solution)/shard_map/ppermute | solution.py:39
  110.4 2.5 %collective-permute-start.4 = (f32[80,80]{0,1:T(8,128)S(1)}, f32[80,80]{0,1:T(8,128)S(1)}, u32[]{:S(2)}, u32[]{:S(2)}) collective-permute-start(f32[80,80]{0,1:T(8,128)S(1)} %add.149), channel_id=1, source_target_pairs={{0,4},{4,0},{8,12},{12,8},{16,20},{20,16},{24,28},{28,24},{1,5},{5... | collective-permute-start | bytes 76808 | tf_op jit(solution)/shard_map/ppermute | solution.py:39
  112.9 2.0 %collective-permute-done.4 = f32[80,80]{0,1:T(8,128)S(1)} collective-permute-done((f32[80,80]{0,1:T(8,128)S(1)}, f32[80,80]{0,1:T(8,128)S(1)}, u32[]{:S(2)}, u32[]{:S(2)}) %collective-permute-start.4) | collective-permute-done | bytes 25632 | tf_op jit(solution)/shard_map/ppermute | solution.py:39
  114.9 0.7 collective-permute-start.5
  115.6 3.3 %collective-permute-done.5 = f32[80,80]{0,1:T(8,128)S(1)} collective-permute-done((f32[80,80]{0,1:T(8,128)S(1)}, f32[80,80]{0,1:T(8,128)S(1)}, u32[]{:S(2)}, u32[]{:S(2)}) %collective-permute-start.5) | collective-permute-done | bytes 25632 | tf_op jit(solution)/shard_map/ppermute | solution.py:39
  118.9 0.5 collective-permute-start.6
  119.4 4.4 %collective-permute-done.6 = f32[80,80]{0,1:T(8,128)S(1)} collective-permute-done((f32[80,80]{0,1:T(8,128)S(1)}, f32[80,80]{0,1:T(8,128)S(1)}, u32[]{:S(2)}, u32[]{:S(2)}) %collective-permute-start.6) | collective-permute-done | bytes 25632 | tf_op jit(solution)/shard_map/ppermute | solution.py:39
  123.9 7.3 %cholesky.18 = f32[80,80]{1,0:T(8,128)S(1)} custom-call(f32[80,80]{1,0:T(8,128)S(1)} %fusion.90), custom_call_target="Cholesky" | custom-call | tf_op jit(solution)/shard_map/jit(cholesky)/cholesky | solution.py:180
  131.2 0.6 compare_reduce_fusion
  131.9 0.7 select_bitcast_fusion
  132.5 0.7 copy.55
  (44 shorter events, 1.7 us)
Async XLA Ops:
  0.6 21.5 %copy-start = (bf16[4,80,16,256]{3,2,1,0:T(8,128)(2,1)S(1)}, bf16[4,80,16,256]{3,2,1,0:T(8,128)(2,1)}, u32[]{:S(2)}) copy-start(bf16[4,80,16,256]{3,2,1,0:T(8,128)(2,1)} %param.14) | copy-start | bytes 7864324
  5.0 13.9 %all-to-all-start = ((f32[8,7,128]{2,1,0:T(8,128)}), f32[8,7,128]{2,1,0:T(8,128)S(1)}, u32[]{:S(2)}, u32[]{:S(2)}) async-start(f32[8,7,128]{2,1,0:T(8,128)} %maximum_bitcast_fusion), calls=%async_computation | async-start | bytes 65536 | tf_op jit(solution)/shard_map/all_to_all | solution.py:98
  28.4 13.7 %all-to-all-start.1 = ((bf16[4,20,4,1024]{3,2,1,0:T(4,128)(2,1)}), bf16[4,20,4,1024]{3,2,1,0:T(4,128)(2,1)S(1)}, u32[]{:S(2)}, u32[]{:S(2)}) async-start(bf16[4,20,4,1024]{3,2,1,0:T(4,128)(2,1)} %copy.41), calls=%async_computation.1 | async-start | bytes 1310720 | tf_op jit(solution)/shard_map/all_to_all | solution.py:128
  44.0 13.7 %all-to-all-start.2 = ((bf16[4,20,4,1024]{3,2,1,0:T(4,128)(2,1)}), bf16[4,20,4,1024]{3,2,1,0:T(4,128)(2,1)S(1)}, u32[]{:S(2)}, u32[]{:S(2)}) async-start(bf16[4,20,4,1024]{3,2,1,0:T(4,128)(2,1)} %copy.44), calls=%async_computation.2 | async-start | bytes 1310720 | tf_op jit(solution)/shard_map/all_to_all | solution.py:133
  57.7 30.2 %collective-permute-start = (bf16[4,20,4,1024]{3,2,1,0:T(4,128)(2,1)S(1)}, bf16[4,20,4,1024]{3,2,1,0:T(4,128)(2,1)S(1)}, u32[]{:S(2)}, u32[]{:S(2)}) collective-permute-start(bf16[4,20,4,1024]{3,2,1,0:T(4,128)(2,1)S(1)} %all-to-all-done.2), channel_id=1, source_target_pairs={{0,4},{4,8},{8,12},{12,16},{16,20},{20,24},{24,28},{1,5},{5,9},{9,... | collective-permute-start | bytes 1966088 | tf_op jit(solution)/shard_map/ppermute | solution.py:139
  65.2 27.2 %collective-permute-start.1 = (bf16[4,20,4,1024]{3,2,1,0:T(4,128)(2,1)S(1)}, bf16[4,20,4,1024]{3,2,1,0:T(4,128)(2,1)S(1)}, u32[]{:S(2)}, u32[]{:S(2)}) collective-permute-start(bf16[4,20,4,1024]{3,2,1,0:T(4,128)(2,1)S(1)} %all-to-all-done.2), channel_id=1, source_target_pairs={{4,0},{8,4},{12,8},{16,12},{20,16},{24,20},{28,24},{5,1},{9,5},{13... | collective-permute-start | bytes 1966088 | tf_op jit(solution)/shard_map/ppermute | solution.py:140
  66.5 21.5 %copy-start.2 = (f32[1024,256]{1,0:T(8,128)S(1)}, f32[1024,256]{1,0:T(8,128)}, u32[]{:S(2)}) copy-start(f32[1024,256]{1,0:T(8,128)} %abs_convert_fusion.1) | copy-start | bytes 3145732
  91.6 1.2 copy-start.1
  91.6 4.9 %slice-start = ((s8[5242880]{0:T(1024)(128)(4,1)}), s8[4194304]{0:T(1024)(128)(4,1)S(1)}, s32[]{:S(2)}) async-start(s8[5242880]{0:T(1024)(128)(4,1)} %bitcast.121), calls=%async_computation.3 | async-start | bytes 8388608
  92.9 3.7 %slice-start.1 = ((s8[5242880]{0:T(1024)(128)(4,1)}), s8[1048576]{0:T(1024)(128)(4,1)S(1)}, s32[]{:S(2)}) async-start(s8[5242880]{0:T(1024)(128)(4,1)} %bitcast.121), calls=%async_computation.4 | async-start | bytes 2097152
  104.9 1.3 collective-permute-start.2
  106.3 4.1 %collective-permute-start.3 = (f32[80,80]{0,1:T(8,128)S(1)}, f32[80,80]{0,1:T(8,128)S(1)}, u32[]{:S(2)}, u32[]{:S(2)}) collective-permute-start(f32[80,80]{0,1:T(8,128)S(1)} %fusion.115), channel_id=1, source_target_pairs={{0,2},{1,3},{2,0},{3,1},{4,6},{5,7},{6,4},{7,5},{8,10},{9,11},{10,... | collective-permute-start | bytes 76808 | tf_op jit(solution)/shard_map/ppermute | solution.py:39
  110.4 4.5 %collective-permute-start.4 = (f32[80,80]{0,1:T(8,128)S(1)}, f32[80,80]{0,1:T(8,128)S(1)}, u32[]{:S(2)}, u32[]{:S(2)}) collective-permute-start(f32[80,80]{0,1:T(8,128)S(1)} %add.149), channel_id=1, source_target_pairs={{0,4},{4,0},{8,12},{12,8},{16,20},{20,16},{24,28},{28,24},{1,5},{5... | collective-permute-start | bytes 76808 | tf_op jit(solution)/shard_map/ppermute | solution.py:39
  114.9 4.0 %collective-permute-start.5 = (f32[80,80]{0,1:T(8,128)S(1)}, f32[80,80]{0,1:T(8,128)S(1)}, u32[]{:S(2)}, u32[]{:S(2)}) collective-permute-start(f32[80,80]{0,1:T(8,128)S(1)} %add.150), channel_id=1, source_target_pairs={{0,8},{4,12},{8,0},{12,4},{16,24},{20,28},{24,16},{28,20},{1,9},{5... | collective-permute-start | bytes 76808 | tf_op jit(solution)/shard_map/ppermute | solution.py:39
  118.9 4.9 %collective-permute-start.6 = (f32[80,80]{0,1:T(8,128)S(1)}, f32[80,80]{0,1:T(8,128)S(1)}, u32[]{:S(2)}, u32[]{:S(2)}) collective-permute-start(f32[80,80]{0,1:T(8,128)S(1)} %add.151), channel_id=1, source_target_pairs={{0,16},{4,20},{8,24},{12,28},{16,0},{20,4},{24,8},{28,12},{1,17},{... | collective-permute-start | bytes 76808 | tf_op jit(solution)/shard_map/ppermute | solution.py:39

commit v16 on v14

--- a/solution.py
+++ b/solution.py
@@ -58,8 +58,8 @@
     high = panel.astype(jnp.bfloat16)
     low = (panel - high.astype(jnp.float32)).astype(jnp.bfloat16)
     members = panel.shape[1]
-    parts = jnp.concatenate([high, low], axis=1)
-    blocks = jnp.einsum("kpxy,kqxy->pq", parts, parts, preferred_element_type=jnp.float32)
+    parts = jnp.concatenate([jnp.swapaxes(high, 0, 1), jnp.swapaxes(low, 0, 1)], axis=0)
+    blocks = jnp.einsum("pkxy,qkxy->pq", parts, parts, preferred_element_type=jnp.float32)
     top, bottom = blocks[:members], blocks[members:]
     return (top[:, :members] + top[:, members:]) + (bottom[:, :members] + bottom[:, members:])
 

time: 134 us -> 134 us (level)
  matrix products: 31.2 us -> 28.9 us
  local copies, waits for them, and re-layouts: 5.04 us -> 6.47 us
    dot_general x1, matrix products: 3.63 us -> 1.27 us  [shards(): jnp.einsum('kmey,kex->kmxy', right, taps_cols[:, 2], preferred_element_ty...]
    unnamed x11 -> x13, local copies, waits for them, and re-layouts: 0.9 us -> 2.33 us
where the time goes in v16:
time: 134 us; the launch traced here: 133 us
  waiting for transfers between devices  55.9 us (42%)
  matrix products  28.9 us (22%)
  starting transfers between devices  22.6 us (17%)
  other arithmetic  18.6 us (14%)
  local copies, waits for them, and re-layouts  6.47 us (5%)
    ppermute x1, waiting for transfers between devices, shards(): lax.ppermute(level_mix, 'tile', [(i, i + 1) for i in range(ends)])  20.7 us
    ppermute x5, waiting for transfers between devices, all_sum(): lax.ppermute(value, name, [(i, i ^ bit) for i in range(size)])  14.3 us
    dot_general x3, matrix products, spread(): jnp.einsum('gmkxs,ksz->kgmxz', placed, slot_taps, preferred_element_type=...  12 us
    all_to_all x1, waiting for transfers between devices, shards(): lax.all_to_all(member_forcing, 'lev', split_axis=0, concat_axis=0, tiled=...  8.91 us
    another operation x3, other arithmetic, shards(): r_factor = jnp.linalg.cholesky(gram_total).T  7.98 us
    all_to_all x1, waiting for transfers between devices, shards(): lax.all_to_all(local_mix, 'lev', split_axis=0, concat_axis=0, tiled=True)  7.76 us
    all_to_all x1, starting transfers between devices, shards(): lax.all_to_all(outgoing, 'tile', split_axis=1, concat_axis=1, tiled=True)  7.25 us
    dot_general x1, matrix products, shards(): jnp.einsum('lgmxy,sxy->gmls', ensemble.reshape(lev_dev, group_count, shar...  4.95 us
  transfers between devices with their start and end apart: 10, of which 9 were waited for; matrix products, arithmetic and copies ran while one was open for 12% of the time, Pallas kernels for 0%

profile of v16, /device:TPU:0, one launch (start us, length us, event | category | flops | bytes accessed | tf_op | source)
XLA Modules:
  0.0 133.5 jit_solution(9093173310367693542)
XLA Ops:
  0.7 1.0 fusion.95
  1.8 0.8 select_bitcast_fusion.1
  2.5 1.8 %fusion.83 = f32[4,8,128]{2,0,1:T(4,128)S(1)} fusion(s32[8,128]{1,0:T(8,128)} %bitcast.132, f32[4,512]{1,0:T(4,128)} %param.9, f32[8,128]{1,0:T(8,128)S(1)} %select_bitcast_fusion.1), kind=kOutput, calls=%fused_computation.75 | convolution fusion | flops 25694208 | bytes 32768 | tf_op jit(solution)/shard_map/lo,dco->ldc/dot_general | solution.py:85
  4.3 0.6 pad_maximum_fusion.1
  5.0 7.3 %all-to-all-start = ((f32[7,8,128]{2,0,1:T(8,128)}), f32[7,8,128]{2,0,1:T(8,128)S(1)}, u32[]{:S(2)}, u32[]{:S(2)}) async-start(f32[7,8,128]{2,0,1:T(8,128)} %pad_maximum_fusion.1), calls=%async_computation | async-start | bytes 65536 | tf_op jit(solution)/shard_map/all_to_all | solution.py:98
  12.2 0.7 broadcast_add_fusion
  12.9 0.7 convert_element_type.119
  13.7 0.8 reshape.456
  14.6 4.3 %all-to-all-done = f32[7,8,128]{2,0,1:T(8,128)S(1)} async-done(((f32[7,8,128]{2,0,1:T(8,128)}), f32[7,8,128]{2,0,1:T(8,128)S(1)}, u32[]{:S(2)}, u32[]{:S(2)}) %all-to-all-start) | async-done | bytes 28704 | tf_op jit(solution)/shard_map/all_to_all | solution.py:98
  18.9 0.6 fusion.28
  19.5 0.6 fusion.29
  20.1 0.6 fusion.30
  20.7 1.3 %fusion.16 = f32[4,1024]{1,0:T(4,128)S(1)} fusion(s32[1024]{0:T(1024)S(1)} %bitcast.125, f32[7,8,128]{2,0,1:T(8,128)S(1)} %all-to-all-done), kind=kOutput, calls=%fused_computation.16 | convolution fusion | flops 51380224 | bytes 40960 | tf_op jit(solution)/shard_map/ls,st->lt/dot_general | solution.py:104
  22.1 5.0 %fusion.72 = bf16[4,20,4,1024]{3,1,0,2:T(8,128)(2,1)S(1)} fusion(bf16[4,4,20,16,256]{4,3,2,1,0:T(8,128)(2,1)S(1)} %bitcast.117, s32[16,256]{1,0:T(8,128)S(1)} %multiply_add_fusion, s32[1024]{0:T(1024)S(1)} %bitcast.126, pred[1024]{0:T(1024)(128)(4,1)S(1)} %get-tuple-element.20, f32[4,1024]{1,0:T(4,128)S(1)} %fusion.16), kind=kOutput, calls=%fused_computation.68 | convolution fusion | flops 2693398528 | bytes 3314688 | tf_op jit(solution)/shard_map/lgmxy,sxy->gmls/dot_general | solution.py:113
  27.0 1.4 %copy.41 = bf16[4,20,4,1024]{3,2,1,0:T(4,128)(2,1)} copy(bf16[4,20,4,1024]{3,1,0,2:T(8,128)(2,1)S(1)} %fusion.72) | data formatting | bytes 1310720 | tf_op jit(solution)/shard_map/convert_element_type | solution.py:117
  28.4 3.5 %all-to-all-start.1 = ((bf16[4,20,4,1024]{3,2,1,0:T(4,128)(2,1)}), bf16[4,20,4,1024]{3,2,1,0:T(4,128)(2,1)S(1)}, u32[]{:S(2)}, u32[]{:S(2)}) async-start(bf16[4,20,4,1024]{3,2,1,0:T(4,128)(2,1)} %copy.41), calls=%async_computation.1 | async-start | bytes 1310720 | tf_op jit(solution)/shard_map/all_to_all | solution.py:127
  32.0 1.2 abs_convert_fusion.2
  33.2 8.9 %all-to-all-done.1 = bf16[4,20,4,1024]{3,2,1,0:T(4,128)(2,1)S(1)} async-done(((bf16[4,20,4,1024]{3,2,1,0:T(4,128)(2,1)}), bf16[4,20,4,1024]{3,2,1,0:T(4,128)(2,1)S(1)}, u32[]{:S(2)}, u32[]{:S(2)}) %all-to-all-start.1) | async-done | bytes 655392 | tf_op jit(solution)/shard_map/all_to_all | solution.py:127
  42.1 0.7 fusion.78
  42.8 1.1 copy.44
  43.9 3.5 %all-to-all-start.2 = ((bf16[4,20,4,1024]{3,2,1,0:T(4,128)(2,1)}), bf16[4,20,4,1024]{3,2,1,0:T(4,128)(2,1)S(1)}, u32[]{:S(2)}, u32[]{:S(2)}) async-start(bf16[4,20,4,1024]{3,2,1,0:T(4,128)(2,1)} %copy.44), calls=%async_computation.2 | async-start | bytes 1310720 | tf_op jit(solution)/shard_map/all_to_all | solution.py:132
  47.4 1.2 abs_convert_fusion.1
  48.6 1.2 abs_convert_fusion
  49.9 7.8 %all-to-all-done.2 = bf16[4,20,4,1024]{3,2,1,0:T(4,128)(2,1)S(1)} async-done(((bf16[4,20,4,1024]{3,2,1,0:T(4,128)(2,1)}), bf16[4,20,4,1024]{3,2,1,0:T(4,128)(2,1)S(1)}, u32[]{:S(2)}, u32[]{:S(2)}) %all-to-all-start.2) | async-done | bytes 655392 | tf_op jit(solution)/shard_map/all_to_all | solution.py:132
  57.8 2.6 %collective-permute-start = (bf16[4,20,4,1024]{3,2,1,0:T(4,128)(2,1)S(1)}, bf16[4,20,4,1024]{3,2,1,0:T(4,128)(2,1)S(1)}, u32[]{:S(2)}, u32[]{:S(2)}) collective-permute-start(bf16[4,20,4,1024]{3,2,1,0:T(4,128)(2,1)S(1)} %all-to-all-done.2), channel_id=1, source_target_pairs={{0,4},{4,8},{8,12},{12,16},{16,20},{20,24},{24,28},{1,5},{5,9},{9,... | collective-permute-start | bytes 1966088 | tf_op jit(solution)/shard_map/ppermute | solution.py:138
  60.4 4.7 %fusion.57 = bf16[4,4,20,16,256]{4,3,2,1,0:T(8,128)(2,1)S(1)} fusion(f32[4]{0:T(128)S(1)} %broadcast_add_fusion, f32[1024,256]{1,0:T(8,128)} %abs_convert_fusion.2, f32[4]{0:T(128)S(1)} %convert_element_type.119, pred[16,1024]{1,0:T(8,128)(4,1)S(1)} %iota_compare_fusion.9, bf16[4,20,4,1024]{3,1,0,2:T(8,128)(2,1)S(1)} %copy.45, ...), kind=kOutput, calls=%fused_computation.64 | convolution fusion | flops 2697199616 | bytes 4343840 | tf_op jit(solution)/shard_map/gmkxs,ksz->kgmxz/dot_general | solution.py:51
  65.2 1.3 collective-permute-start.1
  66.5 0.8 fusion.93
  67.3 20.7 %collective-permute-done = bf16[4,20,4,1024]{3,2,1,0:T(4,128)(2,1)S(1)} collective-permute-done((bf16[4,20,4,1024]{3,2,1,0:T(4,128)(2,1)S(1)}, bf16[4,20,4,1024]{3,2,1,0:T(4,128)(2,1)S(1)}, u32[]{:S(2)}, u32[]{:S(2)}) %collective-permute-start) | collective-permute-done | bytes 655392 | tf_op jit(solution)/shard_map/ppermute | solution.py:138
  88.3 3.5 %fusion.62 = bf16[4,4,20,16,256]{4,3,2,1,0:T(8,128)(2,1)S(1)} fusion(f32[1024,256]{1,0:T(8,128)S(1)} %copy-done.3, f32[4]{0:T(128)S(1)} %broadcast_add_fusion, f32[4]{0:T(128)S(1)} %convert_element_type.119, pred[16,1024]{1,0:T(8,128)(4,1)S(1)} %iota_compare_fusion.8, bf16[4,20,4,1024]{3,1,0,2:T(8,128)(2,1)S(1)} %copy.46, ...), kind=kOutput, calls=%fused_computation.65 | convolution fusion | flops 2697199616 | bytes 4343840 | tf_op jit(solution)/shard_map/gmkxs,ksz->kgmxz/dot_general | solution.py:51
  91.8 0.8 fusion.92
  93.0 3.7 %fusion.67 = bf16[4,4,20,16,256]{4,3,2,1,0:T(8,128)(2,1)S(1)} fusion(f32[1024,256]{1,0:T(8,128)S(1)} %copy-done.2, f32[4]{0:T(128)S(1)} %broadcast_add_fusion, f32[4]{0:T(128)S(1)} %convert_element_type.119, pred[16,1024]{1,0:T(8,128)(4,1)S(1)} %iota_compare_fusion.7, bf16[4,20,4,1024]{3,1,0,2:T(8,128)(2,1)S(1)} %copy.47, ...), kind=kOutput, calls=%fused_computation.66 | convolution fusion | flops 2697199616 | bytes 4343840 | tf_op jit(solution)/shard_map/gmkxs,ksz->kgmxz/dot_general | solution.py:51
  96.8 1.3 bitcast_add_fusion
  98.1 0.9 convert_bitcast_fusion
  99.0 1.4 %copy-done.1 = f32[4,80,16,256]{3,2,1,0:T(8,128)} copy-done((f32[4,80,16,256]{3,2,1,0:T(8,128)}, f32[4,80,16,256]{3,2,1,0:T(8,128)S(1)}, u32[]{:S(2)}) %copy-start.1) | copy-done | bytes 5242904
  100.9 4.2 %fusion.79 = f32[160,160]{0,1:T(8,128)S(1)} fusion(bf16[160,4,16,256]{3,2,0,1:T(8,128)(2,1)S(1)} %pad_maximum_fusion), kind=kOutput, calls=%fused_computation.73 | convolution fusion | flops 838860800 | bytes 5345280 | tf_op jit(solution)/shard_map/pkxy,qkxy->pq/dot_general | solution.py:62
  105.2 1.2 collective-permute-done.2
  106.5 0.7 collective-permute-start.3
  107.2 3.4 %collective-permute-done.3 = f32[80,80]{0,1:T(8,128)S(1)} collective-permute-done((f32[80,80]{0,1:T(8,128)S(1)}, f32[80,80]{0,1:T(8,128)S(1)}, u32[]{:S(2)}, u32[]{:S(2)}) %collective-permute-start.3) | collective-permute-done | bytes 25632 | tf_op jit(solution)/shard_map/ppermute | solution.py:39
  110.6 2.5 %collective-permute-start.4 = (f32[80,80]{0,1:T(8,128)S(1)}, f32[80,80]{0,1:T(8,128)S(1)}, u32[]{:S(2)}, u32[]{:S(2)}) collective-permute-start(f32[80,80]{0,1:T(8,128)S(1)} %add.149), channel_id=1, source_target_pairs={{0,4},{4,0},{8,12},{12,8},{16,20},{20,16},{24,28},{28,24},{1,5},{5... | collective-permute-start | bytes 76808 | tf_op jit(solution)/shard_map/ppermute | solution.py:39
  113.1 2.0 %collective-permute-done.4 = f32[80,80]{0,1:T(8,128)S(1)} collective-permute-done((f32[80,80]{0,1:T(8,128)S(1)}, f32[80,80]{0,1:T(8,128)S(1)}, u32[]{:S(2)}, u32[]{:S(2)}) %collective-permute-start.4) | collective-permute-done | bytes 25632 | tf_op jit(solution)/shard_map/ppermute | solution.py:39
  115.1 0.7 collective-permute-start.5
  115.8 3.3 %collective-permute-done.5 = f32[80,80]{0,1:T(8,128)S(1)} collective-permute-done((f32[80,80]{0,1:T(8,128)S(1)}, f32[80,80]{0,1:T(8,128)S(1)}, u32[]{:S(2)}, u32[]{:S(2)}) %collective-permute-start.5) | collective-permute-done | bytes 25632 | tf_op jit(solution)/shard_map/ppermute | solution.py:39
  119.6 4.4 %collective-permute-done.6 = f32[80,80]{0,1:T(8,128)S(1)} collective-permute-done((f32[80,80]{0,1:T(8,128)S(1)}, f32[80,80]{0,1:T(8,128)S(1)}, u32[]{:S(2)}, u32[]{:S(2)}) %collective-permute-start.6) | collective-permute-done | bytes 25632 | tf_op jit(solution)/shard_map/ppermute | solution.py:39
  124.1 7.3 %cholesky.18 = f32[80,80]{1,0:T(8,128)S(1)} custom-call(f32[80,80]{1,0:T(8,128)S(1)} %fusion.91), custom_call_target="Cholesky" | custom-call | tf_op jit(solution)/shard_map/jit(cholesky)/cholesky | solution.py:179
  131.4 0.6 compare_reduce_fusion
  132.1 0.7 select_bitcast_fusion
  132.7 0.7 copy.55
  (47 shorter events, 2.7 us)
Async XLA Ops:
  0.6 21.4 %copy-start = (bf16[4,80,16,256]{3,2,1,0:T(8,128)(2,1)S(1)}, bf16[4,80,16,256]{3,2,1,0:T(8,128)(2,1)}, u32[]{:S(2)}) copy-start(bf16[4,80,16,256]{3,2,1,0:T(8,128)(2,1)} %param.14) | copy-start | bytes 7864324
  5.0 13.9 %all-to-all-start = ((f32[7,8,128]{2,0,1:T(8,128)}), f32[7,8,128]{2,0,1:T(8,128)S(1)}, u32[]{:S(2)}, u32[]{:S(2)}) async-start(f32[7,8,128]{2,0,1:T(8,128)} %pad_maximum_fusion.1), calls=%async_computation | async-start | bytes 65536 | tf_op jit(solution)/shard_map/all_to_all | solution.py:98
  28.4 13.7 %all-to-all-start.1 = ((bf16[4,20,4,1024]{3,2,1,0:T(4,128)(2,1)}), bf16[4,20,4,1024]{3,2,1,0:T(4,128)(2,1)S(1)}, u32[]{:S(2)}, u32[]{:S(2)}) async-start(bf16[4,20,4,1024]{3,2,1,0:T(4,128)(2,1)} %copy.41), calls=%async_computation.1 | async-start | bytes 1310720 | tf_op jit(solution)/shard_map/all_to_all | solution.py:127
  43.9 13.7 %all-to-all-start.2 = ((bf16[4,20,4,1024]{3,2,1,0:T(4,128)(2,1)}), bf16[4,20,4,1024]{3,2,1,0:T(4,128)(2,1)S(1)}, u32[]{:S(2)}, u32[]{:S(2)}) async-start(bf16[4,20,4,1024]{3,2,1,0:T(4,128)(2,1)} %copy.44), calls=%async_computation.2 | async-start | bytes 1310720 | tf_op jit(solution)/shard_map/all_to_all | solution.py:132
  57.8 30.2 %collective-permute-start = (bf16[4,20,4,1024]{3,2,1,0:T(4,128)(2,1)S(1)}, bf16[4,20,4,1024]{3,2,1,0:T(4,128)(2,1)S(1)}, u32[]{:S(2)}, u32[]{:S(2)}) collective-permute-start(bf16[4,20,4,1024]{3,2,1,0:T(4,128)(2,1)S(1)} %all-to-all-done.2), channel_id=1, source_target_pairs={{0,4},{4,8},{8,12},{12,16},{16,20},{20,24},{24,28},{1,5},{5,9},{9,... | collective-permute-start | bytes 1966088 | tf_op jit(solution)/shard_map/ppermute | solution.py:138
  65.2 27.5 %collective-permute-start.1 = (bf16[4,20,4,1024]{3,2,1,0:T(4,128)(2,1)S(1)}, bf16[4,20,4,1024]{3,2,1,0:T(4,128)(2,1)S(1)}, u32[]{:S(2)}, u32[]{:S(2)}) collective-permute-start(bf16[4,20,4,1024]{3,2,1,0:T(4,128)(2,1)S(1)} %all-to-all-done.2), channel_id=1, source_target_pairs={{4,0},{8,4},{12,8},{16,12},{20,16},{24,20},{28,24},{5,1},{9,5},{13... | collective-permute-start | bytes 1966088 | tf_op jit(solution)/shard_map/ppermute | solution.py:139
  66.5 21.8 %copy-start.3 = (f32[1024,256]{1,0:T(8,128)S(1)}, f32[1024,256]{1,0:T(8,128)}, u32[]{:S(2)}) copy-start(f32[1024,256]{1,0:T(8,128)} %abs_convert_fusion.1) | copy-start | bytes 3145732
  91.8 1.2 copy-start.2
  91.8 4.9 %slice-start = ((s8[5242880]{0:T(1024)(128)(4,1)}), s8[4194304]{0:T(1024)(128)(4,1)S(1)}, s32[]{:S(2)}) async-start(s8[5242880]{0:T(1024)(128)(4,1)} %bitcast.120), calls=%async_computation.3 | async-start | bytes 8388608
  93.0 3.7 %slice-start.1 = ((s8[5242880]{0:T(1024)(128)(4,1)}), s8[1048576]{0:T(1024)(128)(4,1)S(1)}, s32[]{:S(2)}) async-start(s8[5242880]{0:T(1024)(128)(4,1)} %bitcast.120), calls=%async_computation.4 | async-start | bytes 2097152
  98.1 2.4 %copy-start.1 = (f32[4,80,16,256]{3,2,1,0:T(8,128)}, f32[4,80,16,256]{3,2,1,0:T(8,128)S(1)}, u32[]{:S(2)}) copy-start(f32[4,80,16,256]{3,2,1,0:T(8,128)S(1)} %bitcast_add_fusion) | copy-start | bytes 15728644
  105.2 1.3 collective-permute-start.2
  106.5 4.1 %collective-permute-start.3 = (f32[80,80]{0,1:T(8,128)S(1)}, f32[80,80]{0,1:T(8,128)S(1)}, u32[]{:S(2)}, u32[]{:S(2)}) collective-permute-start(f32[80,80]{0,1:T(8,128)S(1)} %fusion.116), channel_id=1, source_target_pairs={{0,2},{1,3},{2,0},{3,1},{4,6},{5,7},{6,4},{7,5},{8,10},{9,11},{10,... | collective-permute-start | bytes 76808 | tf_op jit(solution)/shard_map/ppermute | solution.py:39
  110.6 4.5 %collective-permute-start.4 = (f32[80,80]{0,1:T(8,128)S(1)}, f32[80,80]{0,1:T(8,128)S(1)}, u32[]{:S(2)}, u32[]{:S(2)}) collective-permute-start(f32[80,80]{0,1:T(8,128)S(1)} %add.149), channel_id=1, source_target_pairs={{0,4},{4,0},{8,12},{12,8},{16,20},{20,16},{24,28},{28,24},{1,5},{5... | collective-permute-start | bytes 76808 | tf_op jit(solution)/shard_map/ppermute | solution.py:39
  115.1 4.0 %collective-permute-start.5 = (f32[80,80]{0,1:T(8,128)S(1)}, f32[80,80]{0,1:T(8,128)S(1)}, u32[]{:S(2)}, u32[]{:S(2)}) collective-permute-start(f32[80,80]{0,1:T(8,128)S(1)} %add.150), channel_id=1, source_target_pairs={{0,8},{4,12},{8,0},{12,4},{16,24},{20,28},{24,16},{28,20},{1,9},{5... | collective-permute-start | bytes 76808 | tf_op jit(solution)/shard_map/ppermute | solution.py:39
  119.1 4.9 %collective-permute-start.6 = (f32[80,80]{0,1:T(8,128)S(1)}, f32[80,80]{0,1:T(8,128)S(1)}, u32[]{:S(2)}, u32[]{:S(2)}) collective-permute-start(f32[80,80]{0,1:T(8,128)S(1)} %add.151), channel_id=1, source_target_pairs={{0,16},{4,20},{8,24},{12,28},{16,0},{20,4},{24,8},{28,12},{1,17},{... | collective-permute-start | bytes 76808 | tf_op jit(solution)/shard_map/ppermute | solution.py:39
